TPU v7x, 32 devices: a whole 2x2x4 slice. The times are simulated.
32 devices in a mesh: groups: 2 (over y), ctx: 4 (over z), head: 2 (over x), sub: 2 (over core).
Axes of the slice: x: 2, y: 2, z: 4, core: 2. Of those that a mesh axis runs over, the one named last changes fastest.
Arguments:
- x_raw: bfloat16 [8192, 8192], P(('groups', 'ctx'), 'head'), parts along dimension 0, may hold values from -6 to 6
- bc_raw: bfloat16 [2, 8, 128, 8192], P(None, 'head', 'sub', ('groups', 'ctx')), parts along dimension 3, may hold values from -6 to 6
- z_gate: bfloat16 [8192, 8192], P(('groups', 'ctx', 'sub'), 'head'), parts along dimension 0, may hold values from -31 to 31
- dt_raw: float32 [128, 8192], P('head', ('groups', 'ctx')), parts along dimension 1, may hold values from -2.3 to 11
- conv_x_w: float32 [4, 8192], P(None, 'head'), may hold values from -3 to 3
- conv_x_b: float32 [8192], P('head'), may hold values from -3 to 3
- conv_bc_w: float32 [4, 2, 8, 128], P(None, None, 'head'), may hold values from -3 to 3
- conv_bc_b: float32 [2, 8, 128], P(None, 'head'), may hold values from -3 to 3
- dt_bias: float32 [128], P('head'), may hold values from -10 to 0
- a_log: float32 [128], P('head'), may hold values from -3 to 0.7
- d_skip: float32 [128], P('head'), may hold values from 0.1 to 1
- norm_w: float32 [8192], P('head'), may hold values from 0.5 to 1.5
Outputs:
- out: bfloat16 [8192, 8192], P(('groups', 'ctx', 'sub'), 'head'), parts along dimension 0
There are 2 independent parts, one for each index of `groups`. A program takes and returns all parts, laid end to end along the dimension named above; an argument that names none is the same for every part. Nothing has to cross between parts.
All inputs are finite; a program needn't handle non-finite values.
Results may differ from a plain program's by a relative error of at most 0.001.
Values may be sent and summed in bfloat16 or wider, within the bound.
No kernel may reach another device: no remote copies, remote signals or barrier semaphores. Data moves between devices by JAX's collectives and lax.ppermute only.
A program may use at most 192 MiB of HBM per device.

v0:
```python
import jax
import jax.numpy as jnp
from jax import lax
from jax.sharding import PartitionSpec as P

HEADS = 128
HEAD_DIM = 64
GROUPS = 8
CONV_K = 4


HIGHEST = lax.Precision.HIGHEST


def passed_along(x, axis, by):
    length = lax.axis_size(axis)
    pairs = [(i, i + by) for i in range(length) if 0 <= i + by < length]
    return lax.ppermute(x, axis, pairs)


def conv_rows(padded, weights, bias_row):
    sequence_length = padded.shape[0] - (CONV_K - 1)
    total = jnp.zeros((sequence_length, padded.shape[1]), jnp.float32) + bias_row[None, :]
    for tap_index in range(CONV_K):
        total = total + weights[tap_index][None, :] * padded[
            tap_index : tap_index + sequence_length
        ].astype(jnp.float32)
    return jax.nn.silu(total)


def conv_cols(padded, weights, bias_block):
    sequence_length = padded.shape[-1] - (CONV_K - 1)
    total = jnp.zeros(padded.shape[:-1] + (sequence_length,), jnp.float32) + bias_block[..., None]
    for tap_index in range(CONV_K):
        total = total + weights[tap_index][..., None] * padded[
            ..., tap_index : tap_index + sequence_length
        ].astype(jnp.float32)
    return jax.nn.silu(total)


def block_heads(carried, x_block, step_block, decay_block, b_block, c_block):
    cumulative = jnp.cumsum(decay_block, axis=-1)
    block_len = decay_block.shape[-1]
    row_ids = lax.broadcasted_iota(jnp.int32, (block_len, block_len), 0)
    col_ids = lax.broadcasted_iota(jnp.int32, (block_len, block_len), 1)
    gaps = cumulative[..., :, None] - cumulative[..., None, :]
    decays = jnp.exp(jnp.where(row_ids >= col_ids, gaps, -jnp.inf))
    scores = jnp.einsum("gnq,gnk->gqk", c_block, b_block, precision=HIGHEST)
    weights = scores[:, None] * decays * step_block[..., None, :]
    outputs = jnp.einsum("grqk,grkp->grqp", weights, x_block, precision=HIGHEST)
    inside = jnp.einsum("gnq,grnp->grqp", c_block, carried, precision=HIGHEST)
    outputs = outputs + inside * jnp.exp(cumulative)[..., None]
    to_end = jnp.exp(cumulative[..., -1:] - cumulative) * step_block
    x_scaled = x_block * to_end[..., None]
    new_state = carried * jnp.exp(cumulative[..., -1])[..., None, None]
    new_state = new_state + jnp.einsum("gnk,grkp->grnp", b_block, x_scaled, precision=HIGHEST)
    return (new_state, outputs)


def local_heads(x_heads, step_sizes, log_decay, b_rows, c_rows, block_limit):
    sequence_length = x_heads.shape[2]
    block_len = min(block_limit, sequence_length)
    num_blocks = sequence_length // block_len
    state = jnp.zeros(
        (x_heads.shape[0], x_heads.shape[1], b_rows.shape[1], x_heads.shape[3]), jnp.float32
    )
    pieces = []
    for block_index in range(num_blocks):
        low = block_index * block_len
        high = low + block_len
        state, outputs = block_heads(
            state,
            x_heads[:, :, low:high],
            step_sizes[..., low:high],
            log_decay[..., low:high],
            b_rows[..., low:high],
            c_rows[..., low:high],
        )
        pieces.append(outputs)
    return (jnp.concatenate(pieces, 2), state)


def per_device(
    x_raw,
    bc_raw,
    z_gate,
    dt_raw,
    conv_x_w,
    conv_x_b,
    conv_bc_w,
    conv_bc_b,
    dt_bias,
    a_log,
    d_skip,
    norm_w,
):
    sequence_length = x_raw.shape[0]
    heads_dev = dt_raw.shape[0]
    per_group = HEADS // GROUPS
    sub_index = lax.axis_index("sub")
    hidden_portion = bc_raw.shape[2]
    bc_weights = lax.dynamic_slice_in_dim(conv_bc_w, sub_index * hidden_portion, hidden_portion, 3)
    bc_bias = lax.dynamic_slice_in_dim(conv_bc_b, sub_index * hidden_portion, hidden_portion, 2)
    channels = heads_dev * HEAD_DIM
    rim_len = CONV_K - 1
    x_rim, bc_rim = passed_along(
        (x_raw[sequence_length - rim_len :], bc_raw[..., sequence_length - rim_len :]), "ctx", 1
    )
    x_conv = conv_rows(jnp.concatenate([x_rim, x_raw], 0), conv_x_w, conv_x_b)
    bc_conv = conv_cols(jnp.concatenate([bc_rim, bc_raw], 3), bc_weights, bc_bias)
    set_groups = max(1, heads_dev // per_group)
    per_set = heads_dev // set_groups
    b_rows = bc_conv[0]
    c_rows = bc_conv[1]
    set_shape = (set_groups, per_set, sequence_length)
    step_sizes = jax.nn.softplus(dt_raw + dt_bias[:, None]).reshape(set_shape)
    log_decay = (-jnp.exp(a_log)[:, None] * step_sizes.reshape(heads_dev, sequence_length)).reshape(
        set_shape
    )
    x_heads = x_conv.reshape(sequence_length, set_groups, per_set, HEAD_DIM).transpose(1, 2, 0, 3)
    device_result, end_states = local_heads(x_heads, step_sizes, log_decay, b_rows, c_rows, 256)
    running = jnp.cumsum(log_decay, axis=-1)
    totals = running[..., -1]

    def pass_state(step_index, incoming):
        outgoing = end_states + jnp.exp(totals)[..., None, None] * incoming
        return passed_along(outgoing, "ctx", 1)

    carried = lax.fori_loop(0, lax.axis_size("ctx") - 1, pass_state, jnp.zeros_like(end_states))
    inflow = jnp.einsum("gnq,grnp->grqp", c_rows, carried, precision=HIGHEST)
    full_heads = device_result + inflow * jnp.exp(running)[..., None]
    token_major = full_heads.transpose(2, 0, 1, 3).reshape(sequence_length, channels)
    summed = lax.psum_scatter(token_major, "sub", scatter_dimension=0, tiled=True)
    row_count = summed.shape[0]
    own_rows = lax.dynamic_slice_in_dim(x_conv, sub_index * row_count, row_count, 0)
    mixed_out = summed + own_rows * jnp.repeat(d_skip, HEAD_DIM)[None, :]
    gated_output = mixed_out * jax.nn.silu(z_gate.astype(jnp.float32))
    group_width = per_group * HEAD_DIM
    grouped = gated_output.reshape(
        gated_output.shape[0], gated_output.shape[1] // group_width, group_width
    )
    mean_square = jnp.mean(grouped * grouped, axis=-1, keepdims=True)
    normed = grouped * lax.rsqrt(mean_square + 1e-05) * norm_w.reshape(1, -1, group_width)
    return normed.reshape(gated_output.shape).astype(jnp.bfloat16)


def solution(mesh):
    in_specs = (
        P(("groups", "ctx"), "head"),
        P(None, "head", "sub", ("groups", "ctx")),
        P(("groups", "ctx", "sub"), "head"),
        P("head", ("groups", "ctx")),
        P(None, "head"),
        P("head"),
        P(None, None, "head", None),
        P(None, "head", None),
        P("head"),
        P("head"),
        P("head"),
        P("head"),
    )
    out_specs = P(("groups", "ctx", "sub"), "head")
    return jax.shard_map(
        per_device, mesh=mesh, in_specs=in_specs, out_specs=out_specs, check_vma=False
    )
```

profile of v0, /device:TPU:0, one launch (start us, length us, event | category | flops | bytes accessed | tf_op | source)
XLA Modules:
  0.0 501.3 jit_solution(4747440389072690896)
XLA Ops:
  7.4 4.9 collective-permute-start.2
  13.4 3.5 collective-permute-start.1
  33.0 18.0 %reduce-window.46 = f32[4,16,8,128]{3,2,1,0:T(8,128)S(1)} reduce-window(f32[4,16,8,128]{3,2,1,0:T(8,128)S(1)} %bitcast.193, f32[]{:T(128)} %constant.45.clone.1), window={size=1x1x1x128 pad=0_0x0_0x0_0x127_0}, to_apply=%region_8.9 | reduce-window | flops 8323072 | bytes 524292 | tf_op jit(solution)/shard_map/reduce-window.8
  61.8 4.9 fusion.103
  68.8 13.0 %divide_multiply_fusion = f32[1024,4096]{1,0:T(8,128)} fusion(bf16[1024,4096]{1,0:T(8,128)(2,1)S(1)} %bitcast.190, bf16[3,4096]{1,0:T(4,128)(2,1)S(1)} %collective-permute-done.2, f32[4096]{0:T(1024)S(1)} %bitcast.200, f32[4096]{0:T(1024)S(1)} %bitcast.201, f32[4096]{0:T(1024)S(1)} %bitcast.199, f32[4096]{0:T(1024)S(1)} %bitcast.198, f32[4096]{0:T(1024)S(1)} %copy-done.27), kind=kLoop, calls=%fused_computation.20 | loop fusion | flops 104857600 | bytes 25272320 | tf_op jit(solution)/shard_map/jit(silu)/mul | solution.py:28
  81.8 17.4 %copy.128 = f32[1024,4096]{0,1:T(8,128)} copy(f32[1024,4096]{1,0:T(8,128)} %divide_multiply_fusion) | data formatting | bytes 33554432 | tf_op jit(solution)/shard_map/jit(silu)/mul | solution.py:28
  99.2 5.7 %fusion.60 = f32[4,16,64,64]{3,2,1,0:T(8,128)S(1)} fusion(f32[4,16,1024,64]{2,3,1,0:T(8,128)} %bitcast.174, f32[4,16,256]{2,1,0:T(8,128)S(1)} %get-tuple-element.89, f32[4,64,1024]{2,1,0:T(8,128)S(1)} %get-tuple-element.87), kind=kOutput, calls=%fused_computation.73 | convolution fusion | flops 806354944 | bytes 5570560 | tf_op jit(solution)/shard_map/gnk,grkp->grnp/dot_general | solution.py:56
  104.9 5.0 %fusion.70 = f32[4,16,64,256]{3,2,1,0:T(8,128)} fusion(f32[4,16,64,64]{3,2,1,0:T(8,128)S(1)} %fusion.60, f32[4,16]{1,0:T(4,128)S(1)} %exponential_multiply_fusion.4, f32[4,64,1024]{2,1,0:T(8,128)S(1)} %get-tuple-element.86), kind=kOutput, calls=%fused_computation.87 | convolution fusion | flops 805568512 | bytes 6555648 | tf_op jit(solution)/shard_map/gnq,grnp->grqp/dot_general | solution.py:51
  109.9 6.3 %bitcast_add_fusion.6 = f32[4,16,64,64]{2,3,1,0:T(8,128)S(1)} fusion(f32[4,16,64,64]{3,2,1,0:T(8,128)S(1)} %fusion.60, f32[4,16,1024,64]{2,3,1,0:T(8,128)} %bitcast.175, f32[4,16,256]{2,1,0:T(8,128)S(1)} %get-tuple-element.90, f32[4,16]{1,0:T(4,128)S(1)} %exp.132, f32[4,16]{1,0:T(4,128)S(1)} %exponential_multiply_fusion.4, ...), kind=kOutput, calls=%fused_computation.85 | convolution fusion | flops 807141376 | bytes 7671808 | tf_op jit(solution)/shard_map/gnk,grkp->grnp/dot_general | solution.py:56
  116.2 5.0 fusion.110
  121.2 4.0 bitcast_add_fusion.5
  125.3 5.3 %fusion.107 = f32[4,16,64,256]{3,2,1,0:T(8,128)} fusion(f32[4,16,64,64]{2,3,1,0:T(8,128)S(1)} %bitcast_add_fusion.5, f32[4,64,1024]{2,1,0:T(8,128)S(1)} %get-tuple-element.86), kind=kOutput, calls=%fused_computation.112 | convolution fusion | flops 805306368 | bytes 6553600 | tf_op jit(solution)/shard_map/gnq,grnp->grqp/dot_general | solution.py:51
  130.6 4.0 bitcast_add_fusion.4
  136.5 23.3 %bitcast_add_fusion = f32[4,16,256,64]{2,3,1,0:T(8,128)} fusion(f32[4,16,64,256]{3,2,1,0:T(8,128)} %fusion.107, f32[4,16,256]{2,1,0:T(8,128)} %get-tuple-element.103, f32[4,16,1024,64]{2,3,1,0:T(8,128)} %bitcast.176, f32[4,16,256]{2,1,0:T(8,128)} %get-tuple-element.92, f32[4,16,256]{2,1,0:T(8,128)S(1)} %copy-done.13, f32[4,256,256]{2,1,0:T(8,128)S(1)} %copy-done.11, ...), kind=kOutput, calls=%fused_computation.63 | convolution fusion | flops 3240099840 | bytes 13959168 | tf_op jit(solution)/shard_map/grqk,grkp->grqp/dot_general | solution.py:50
  160.0 23.1 %bitcast_add_fusion.1 = f32[4,16,256,64]{2,3,1,0:T(8,128)} fusion(f32[4,16,64,256]{3,2,1,0:T(8,128)S(1)} %copy-done.6, f32[4,16,256]{2,1,0:T(8,128)S(1)} %copy-done.24, f32[4,16,1024,64]{2,3,1,0:T(8,128)} %bitcast.177, f32[4,16,256]{2,1,0:T(8,128)S(1)} %copy-done.23, f32[4,16,256]{2,1,0:T(8,128)S(1)} %copy-done.17, f32[4,256,256]{2,1,0:T(8,128)S(1)} %copy-done.10, ...), kind=kOutput, calls=%fused_computation.64 | convolution fusion | flops 3240099840 | bytes 13959168 | tf_op jit(solution)/shard_map/grqk,grkp->grqp/dot_general | solution.py:50
  183.2 21.5 %bitcast_add_fusion.2 = f32[4,16,256,64]{2,3,1,0:T(8,128)} fusion(f32[4,16,64,256]{3,2,1,0:T(8,128)S(1)} %copy-done.4, f32[4,16,256]{2,1,0:T(8,128)S(1)} %copy-done.22, f32[4,16,1024,64]{2,3,1,0:T(8,128)S(1)} %bitcast.182, f32[4,16,256]{2,1,0:T(8,128)S(1)} %copy-done.21, f32[4,16,256]{2,1,0:T(8,128)S(1)} %copy-done.15, f32[4,256,256]{2,1,0:T(8,128)S(1)} %copy-done.9, ...), kind=kOutput, calls=%fused_computation.65 | convolution fusion | flops 3240099840 | bytes 13959168 | tf_op jit(solution)/shard_map/grqk,grkp->grqp/dot_general | solution.py:50
  204.7 21.8 %bitcast_add_fusion.3 = f32[4,16,256,64]{2,3,1,0:T(8,128)} fusion(f32[4,16,64,256]{3,2,1,0:T(8,128)S(1)} %copy-done.5, f32[4,16,256]{2,1,0:T(8,128)S(1)} %copy-done.20, f32[4,16,1024,64]{2,3,1,0:T(8,128)S(1)} %bitcast.183, f32[4,16,256]{2,1,0:T(8,128)S(1)} %copy-done.19, f32[4,16,256]{2,1,0:T(8,128)S(1)} %copy_bitcast_fusion.3, ...), kind=kOutput, calls=%fused_computation.66 | convolution fusion | flops 3240099840 | bytes 13959168 | tf_op jit(solution)/shard_map/grqk,grkp->grqp/dot_general | solution.py:50
  226.8 152.8 %while.12 = (s32[]{:T(128)}, f32[4,16,64,64]{3,2,1,0:T(8,128)S(1)}, f32[4,16,1,1]{1,0,3,2:T(4,128)S(1)}, f32[4,16,64,64]{3,2,1,0:T(8,128)}, s32[]{:T(128)}) while((s32[]{:T(128)}, f32[4,16,64,64]{3,2,1,0:T(8,128)S(1)}, f32[4,16,1,1]{1,0,3,2:T(4,128)S(1)}, f32[4,16,64,64]{3,2,1,0:T(8,128)}, s32[]{:T(128)}) %tuple.59), condition=%wide.region_11.12_spmd, body=%wide.region_10.11_spmd.sunk | while | flops 524290 | bytes 7340389 | solution.py:129
  230.0 3.6 collective-permute-start
  233.6 44.5 %collective-permute-done = f32[4,16,64,64]{3,2,1,0:T(8,128)S(1)} collective-permute-done((f32[4,16,64,64]{3,2,1,0:T(8,128)}, f32[4,16,64,64]{3,2,1,0:T(8,128)S(1)}, u32[]{:S(2)}, u32[]{:S(2)}) %collective-permute-start) | collective-permute-done | bytes 1048608 | tf_op jit(solution)/shard_map/while/body/eval_jaxpr/ppermute | solution.py:18
  281.3 4.4 collective-permute-start
  285.7 43.6 %collective-permute-done = f32[4,16,64,64]{3,2,1,0:T(8,128)S(1)} collective-permute-done((f32[4,16,64,64]{3,2,1,0:T(8,128)}, f32[4,16,64,64]{3,2,1,0:T(8,128)S(1)}, u32[]{:S(2)}, u32[]{:S(2)}) %collective-permute-start) | collective-permute-done | bytes 1048608 | tf_op jit(solution)/shard_map/while/body/eval_jaxpr/ppermute | solution.py:18
  332.5 4.4 collective-permute-start
  336.9 42.7 %collective-permute-done = f32[4,16,64,64]{3,2,1,0:T(8,128)S(1)} collective-permute-done((f32[4,16,64,64]{3,2,1,0:T(8,128)}, f32[4,16,64,64]{3,2,1,0:T(8,128)S(1)}, u32[]{:S(2)}, u32[]{:S(2)}) %collective-permute-start) | collective-permute-done | bytes 1048608 | tf_op jit(solution)/shard_map/while/body/eval_jaxpr/ppermute | solution.py:18
  379.6 19.3 %maximum_add_fusion = f32[4,16,1024,64]{2,3,1,0:T(8,128)} fusion(f32[4,16,256,64]{2,3,1,0:T(8,128)} %bitcast_add_fusion, f32[4,16,256,64]{2,3,1,0:T(8,128)} %bitcast_add_fusion.1, f32[4,16,256,64]{2,3,1,0:T(8,128)} %bitcast_add_fusion.2, f32[4,16,256,64]{2,3,1,0:T(8,128)} %bitcast_add_fusion.3, f32[4,16,64,64]{3,2,1,0:T(8,128)S(1)} %get-tuple-element.55, ...), kind=kOutput, calls=%fused_computation.1 | convolution fusion | flops 3242196992 | bytes 35913728 | tf_op jit(solution)/shard_map/gnq,grnp->grqp/dot_general | solution.py:130
  398.9 17.5 %copy.147 = f32[1024,4096]{1,0:T(8,128)} copy(f32[1024,4096]{0,1:T(8,128)} %bitcast.184) | data formatting | bytes 33554432 | tf_op jit(solution)/shard_map/reshape | solution.py:132
  417.2 26.3 %reduce-scatter.2.cloned.1.call-done = f32[512,4096]{1,0:T(8,128)} async-done(((f32[1024,4096]{1,0:T(8,128)}), f32[512,4096]{1,0:T(8,128)}) %reduce-scatter.2.cloned.1.call-update) | async-done | bytes 8388624 | tf_op jit(solution)/shard_map/reduce_scatter | solution.py:133
  443.5 11.5 %fusion.153 = f32[512,4096]{1,0:T(8,128)} fusion(bf16[512,4096]{1,0:T(8,128)(2,1)} %param.16, f32[512,4096]{1,0:T(8,128)} %reduce-scatter.2.cloned.1.call-done, f32[4096]{0:T(1024)S(1)} %mul.434, f32[1024,4096]{1,0:T(8,128)} %divide_multiply_fusion, s32[]{:T(128)S(6)} %select_n.30), kind=kLoop, calls=%fused_computation.193 | loop fusion | flops 18874368 | bytes 29376516 | tf_op jit(solution)/shard_map/mul | solution.py:142
  455.0 11.1 %mul.440 = f32[512,4,1024]{2,1,0:T(4,128)} reshape(f32[512,4096]{1,0:T(8,128)} %fusion.153) | data formatting | bytes 16777216 | tf_op jit(solution)/shard_map/mul | solution.py:142
  466.1 4.6 reduce_sum.9
  471.9 11.4 %copy.171 = f32[64,8,4,1024]{3,1,2,0:T(8,128)} copy(f32[64,8,4,1024]{3,2,1,0:T(4,128)S(1)} %bitcast.187) | data formatting | bytes 16777216
  483.3 10.7 %multiply_convert_fusion = bf16[512,4096]{1,0:T(8,128)(2,1)} fusion(f32[512,4096]{1,0:T(8,128)} %bitcast.188, f32[4096]{0:T(1024)S(1)} %copy-done.25, bf16[512,4096]{1,0:T(8,128)(2,1)} %param.16, f32[512,4096]{1,0:T(8,128)S(1)} %bitcast.186, f32[4096]{0:T(1024)S(1)} %mul.434, f32[1024,4096]{1,0:T(8,128)} %divide_multiply_fusion, s32[]{:T(128)S(6)} %select_n.30), kind=kLoop, calls=%fused_computation.38 | loop fusion | flops 23068672 | bytes 33587204 | tf_op jit(solution)/shard_map/convert_element_type | solution.py:144
  (155 shorter events, 44.5 us)
Async XLA Ops:
  6.5 46.3 %copy-start = (f32[2,4,128]{2,1,0:T(4,128)S(1)}, f32[2,4,128]{2,1,0:T(4,128)}, u32[]{:S(2)}) copy-start(f32[2,4,128]{2,1,0:T(4,128)} %param.21) | copy-start | bytes 12292
  6.5 437.0 %reduce-scatter.2.cloned.1.call-start = ((), (), s32[]{:S(2)}) async-start(), calls=%async_computation.1 | async-start | bytes 25165824 | tf_op jit(solution)/shard_map/reduce_scatter | solution.py:133
  7.4 61.3 %collective-permute-start.2 = (bf16[3,4096]{1,0:T(4,128)(2,1)S(1)}, bf16[3,4096]{1,0:T(4,128)(2,1)S(1)}, u32[]{:S(2)}, u32[]{:S(2)}) collective-permute-start(bf16[3,4096]{1,0:T(4,128)(2,1)S(1)} %slice.180), channel_id=1, source_target_pairs={{0,4},{4,8},{8,12},{1,5},{5,9},{9,13},{2,6},{6,10},{10,14},{3,7},{... | collective-permute-start | bytes 73736 | tf_op jit(solution)/shard_map/ppermute | solution.py:18
  13.4 39.7 %collective-permute-start.1 = (bf16[2,4,64,3]{3,2,1,0:T(8,128)(2,1)S(1)}, bf16[2,4,64,3]{3,2,1,0:T(8,128)(2,1)S(1)}, u32[]{:S(2)}, u32[]{:S(2)}) collective-permute-start(bf16[2,4,64,3]{3,2,1,0:T(8,128)(2,1)S(1)} %slice.164), channel_id=1, source_target_pairs={{0,4},{4,8},{8,12},{1,5},{5,9},{9,13},{2,6},{6,10},{10,14},{3,7},{... | collective-permute-start | bytes 9224 | tf_op jit(solution)/shard_map/ppermute | solution.py:18
  19.2 33.5 %copy-start.26 = (f32[4,2,4,128]{3,2,1,0:T(4,128)S(1)}, f32[4,2,4,128]{3,2,1,0:T(4,128)}, u32[]{:S(2)}) copy-start(f32[4,2,4,128]{3,2,1,0:T(4,128)} %param.20) | copy-start | bytes 49156
  20.4 32.7 %copy-start.7 = (bf16[2,4,64,1024]{3,2,1,0:T(8,128)(2,1)S(1)}, bf16[2,4,64,1024]{3,2,1,0:T(8,128)(2,1)}, u32[]{:S(2)}) copy-start(bf16[2,4,64,1024]{3,2,1,0:T(8,128)(2,1)} %param.15) | copy-start | bytes 3145732
  53.1 15.6 %slice-start.6 = ((s8[8388608]{0:T(1024)(128)(4,1)}), s8[4194304]{0:T(1024)(128)(4,1)S(1)}, s32[]{:S(2)}) async-start(s8[8388608]{0:T(1024)(128)(4,1)} %bitcast.189), calls=%async_computation.8 | async-start | bytes 8388608
  104.9 16.3 %copy-start.2 = (f32[1024,4096]{0,1:T(8,128)S(1)}, f32[1024,4096]{0,1:T(8,128)}, u32[]{:S(2)}) copy-start(f32[1024,4096]{0,1:T(8,128)} %copy.128) | copy-start | bytes 50331652
  136.5 23.4 %copy-start.6 = (f32[4,16,64,256]{3,2,1,0:T(8,128)S(1)}, f32[4,16,64,256]{3,2,1,0:T(8,128)}, u32[]{:S(2)}) copy-start(f32[4,16,64,256]{3,2,1,0:T(8,128)} %fusion.110) | copy-start | bytes 12582916
  136.5 23.4 %copy-start.10 = (f32[4,256,256]{2,1,0:T(8,128)S(1)}, f32[4,256,256]{2,1,0:T(8,128)}, u32[]{:S(2)}) copy-start(f32[4,256,256]{2,1,0:T(8,128)} %fusion.122) | copy-start | bytes 3145732
  136.5 23.4 %copy-start.17 = (f32[4,16,256]{2,1,0:T(8,128)S(1)}, f32[4,16,256]{2,1,0:T(8,128)}, u32[]{:S(2)}) copy-start(f32[4,16,256]{2,1,0:T(8,128)} %copy-done.16) | copy-start | bytes 196612
  136.5 23.4 %copy-start.18 = (pred[256,256]{1,0:T(8,128)(4,1)S(1)}, pred[256,256]{1,0:T(8,128)(4,1)}, u32[]{:S(2)}) copy-start(pred[256,256]{1,0:T(8,128)(4,1)} %iota_compare_fusion) | copy-start | bytes 196612
  136.5 23.4 %copy-start.23 = (f32[4,16,256]{2,1,0:T(8,128)S(1)}, f32[4,16,256]{2,1,0:T(8,128)}, u32[]{:S(2)}) copy-start(f32[4,16,256]{2,1,0:T(8,128)} %get-tuple-element.93) | copy-start | bytes 196612
  136.5 23.4 %copy-start.24 = (f32[4,16,256]{2,1,0:T(8,128)S(1)}, f32[4,16,256]{2,1,0:T(8,128)}, u32[]{:S(2)}) copy-start(f32[4,16,256]{2,1,0:T(8,128)} %get-tuple-element.100) | copy-start | bytes 196612
  136.5 46.6 %slice-start = ((s8[16777216]{0:T(1024)(128)(4,1)}), s8[4194304]{0:T(1024)(128)(4,1)S(1)}, s32[]{:S(2)}) async-start(s8[16777216]{0:T(1024)(128)(4,1)} %bitcast.180), calls=%async_computation.2 | async-start | bytes 8388608
  136.5 46.6 %slice-start.1 = ((s8[16777216]{0:T(1024)(128)(4,1)}), s8[4194304]{0:T(1024)(128)(4,1)S(1)}, s32[]{:S(2)}) async-start(s8[16777216]{0:T(1024)(128)(4,1)} %bitcast.180), calls=%async_computation.3 | async-start | bytes 8388608
  159.9 23.2 %slice-start.2 = ((s8[16777216]{0:T(1024)(128)(4,1)}), s8[4194304]{0:T(1024)(128)(4,1)S(1)}, s32[]{:S(2)}) async-start(s8[16777216]{0:T(1024)(128)(4,1)} %bitcast.180), calls=%async_computation.4 | async-start | bytes 8388608
  159.9 23.2 %slice-start.3 = ((s8[16777216]{0:T(1024)(128)(4,1)}), s8[4194304]{0:T(1024)(128)(4,1)S(1)}, s32[]{:S(2)}) async-start(s8[16777216]{0:T(1024)(128)(4,1)} %bitcast.180), calls=%async_computation.5 | async-start | bytes 8388608
  159.9 23.2 %copy-start.4 = (f32[4,16,64,256]{3,2,1,0:T(8,128)S(1)}, f32[4,16,64,256]{3,2,1,0:T(8,128)}, u32[]{:S(2)}) copy-start(f32[4,16,64,256]{3,2,1,0:T(8,128)} %fusion.70) | copy-start | bytes 12582916
  159.9 23.2 %copy-start.9 = (f32[4,256,256]{2,1,0:T(8,128)S(1)}, f32[4,256,256]{2,1,0:T(8,128)}, u32[]{:S(2)}) copy-start(f32[4,256,256]{2,1,0:T(8,128)} %fusion.127) | copy-start | bytes 3145732
  159.9 23.2 %copy-start.15 = (f32[4,16,256]{2,1,0:T(8,128)S(1)}, f32[4,16,256]{2,1,0:T(8,128)}, u32[]{:S(2)}) copy-start(f32[4,16,256]{2,1,0:T(8,128)} %copy-done.14) | copy-start | bytes 196612
  160.0 23.2 %copy-start.21 = (f32[4,16,256]{2,1,0:T(8,128)S(1)}, f32[4,16,256]{2,1,0:T(8,128)}, u32[]{:S(2)}) copy-start(f32[4,16,256]{2,1,0:T(8,128)} %get-tuple-element.94) | copy-start | bytes 196612
  160.0 23.2 %copy-start.22 = (f32[4,16,256]{2,1,0:T(8,128)S(1)}, f32[4,16,256]{2,1,0:T(8,128)}, u32[]{:S(2)}) copy-start(f32[4,16,256]{2,1,0:T(8,128)} %get-tuple-element.101) | copy-start | bytes 196612
  183.2 21.5 %copy-start.5 = (f32[4,16,64,256]{3,2,1,0:T(8,128)S(1)}, f32[4,16,64,256]{3,2,1,0:T(8,128)}, u32[]{:S(2)}) copy-start(f32[4,16,64,256]{3,2,1,0:T(8,128)} %fusion.103) | copy-start | bytes 12582916
  183.2 21.5 %copy-start.8 = (f32[4,256,256]{2,1,0:T(8,128)S(1)}, f32[4,256,256]{2,1,0:T(8,128)}, u32[]{:S(2)}) copy-start(f32[4,256,256]{2,1,0:T(8,128)} %fusion.132) | copy-start | bytes 3145732
  183.2 21.5 %copy-start.19 = (f32[4,16,256]{2,1,0:T(8,128)S(1)}, f32[4,16,256]{2,1,0:T(8,128)}, u32[]{:S(2)}) copy-start(f32[4,16,256]{2,1,0:T(8,128)} %get-tuple-element.95) | copy-start | bytes 196612
  183.2 21.5 %copy-start.20 = (f32[4,16,256]{2,1,0:T(8,128)S(1)}, f32[4,16,256]{2,1,0:T(8,128)}, u32[]{:S(2)}) copy-start(f32[4,16,256]{2,1,0:T(8,128)} %get-tuple-element.102) | copy-start | bytes 196612
  230.0 48.1 %collective-permute-start = (f32[4,16,64,64]{3,2,1,0:T(8,128)}, f32[4,16,64,64]{3,2,1,0:T(8,128)S(1)}, u32[]{:S(2)}, u32[]{:S(2)}) collective-permute-start(f32[4,16,64,64]{3,2,1,0:T(8,128)} %multiply_add_fusion.2), channel_id=1, source_target_pairs={{0,4},{4,8},{8,12},{1,5},{5,9},{9,13},{2,6},{6,10},{10,14},{3,7},{... | collective-permute-start | bytes 3145736 | tf_op jit(solution)/shard_map/while/body/eval_jaxpr/ppermute | solution.py:18
  281.3 48.0 %collective-permute-start = (f32[4,16,64,64]{3,2,1,0:T(8,128)}, f32[4,16,64,64]{3,2,1,0:T(8,128)S(1)}, u32[]{:S(2)}, u32[]{:S(2)}) collective-permute-start(f32[4,16,64,64]{3,2,1,0:T(8,128)} %multiply_add_fusion.2), channel_id=1, source_target_pairs={{0,4},{4,8},{8,12},{1,5},{5,9},{9,13},{2,6},{6,10},{10,14},{3,7},{... | collective-permute-start | bytes 3145736 | tf_op jit(solution)/shard_map/while/body/eval_jaxpr/ppermute | solution.py:18
  332.5 47.1 %collective-permute-start = (f32[4,16,64,64]{3,2,1,0:T(8,128)}, f32[4,16,64,64]{3,2,1,0:T(8,128)S(1)}, u32[]{:S(2)}, u32[]{:S(2)}) collective-permute-start(f32[4,16,64,64]{3,2,1,0:T(8,128)} %multiply_add_fusion.2), channel_id=1, source_target_pairs={{0,4},{4,8},{8,12},{1,5},{5,9},{9,13},{2,6},{6,10},{10,14},{3,7},{... | collective-permute-start | bytes 3145736 | tf_op jit(solution)/shard_map/while/body/eval_jaxpr/ppermute | solution.py:18
  470.7 12.6 %slice-start.4 = ((s8[8388608]{0:T(1024)(128)(4,1)}), s8[4194304]{0:T(1024)(128)(4,1)S(1)}, s32[]{:S(2)}) async-start(s8[8388608]{0:T(1024)(128)(4,1)} %bitcast.185), calls=%async_computation.6 | async-start | bytes 8388608
  471.9 11.4 %slice-start.5 = ((s8[8388608]{0:T(1024)(128)(4,1)}), s8[4194304]{0:T(1024)(128)(4,1)S(1)}, s32[]{:S(2)}) async-start(s8[8388608]{0:T(1024)(128)(4,1)} %bitcast.185), calls=%async_computation.7 | async-start | bytes 8388608
  (11 other events, 54.9 us)
Sparse Core Ops, SparseCore 0:
  416.5 26.8 reduce-scatter.1
where the time goes:
time: 511 us; the launch traced here: 501 us
  matrix products  158 us (31%)
  waiting for transfers between devices  157 us (31%)
  other arithmetic  82.8 us (16%)
  local copies, waits for them, and re-layouts  68.6 us (13%)
  starting transfers between devices  20.8 us (4%)
  between operations  14.5 us (3%)
    ppermute x5, waiting for transfers between devices, passed_along(): return lax.ppermute(x, axis, pairs)  131 us
    dot_general x4, matrix products, block_heads(): outputs = jnp.einsum('grqk,grkp->grqp', weights, x_block, precision=HIGHEST)  89.7 us
    another operation x15, other arithmetic  27.7 us
    reduce_scatter x1, waiting for transfers between devices, per_device(): lax.psum_scatter(token_major, 'sub', scatter_dimension=0, tiled=True)  26.3 us
    ppermute x5, starting transfers between devices, passed_along(): return lax.ppermute(x, axis, pairs)  20.8 us
    dot_general x4, matrix products, block_heads(): inside = jnp.einsum('gnq,grnp->grqp', c_block, carried, precision=HIGHEST)  20.2 us
    dot_general x4, matrix products, block_heads(): jnp.einsum('gnk,grkp->grnp', b_block, x_scaled, precision=HIGHEST)  20 us
    dot_general x1, matrix products, per_device(): inflow = jnp.einsum('gnq,grnp->grqp', c_rows, carried, precision=HIGHEST)  19.3 us
  transfers between devices with their start and end apart: 6, of which 4 were waited for; matrix products, arithmetic and copies ran while one was open for 10% of the time, Pallas kernels for 0%

commit v1 on v0

v1 whole, which is shorter than its diff:
```python
import jax
import jax.numpy as jnp
from jax import lax
from jax.experimental import pallas as pl
from jax.experimental.pallas import tpu as pltpu
from jax.sharding import PartitionSpec as P

HEADS = 128
HEAD_DIM = 64
GROUPS = 8
CONV_K = 4


HIGHEST = lax.Precision.HIGHEST
F32 = jnp.float32


def passed_along(x, axis, by):
    length = lax.axis_size(axis)
    pairs = [(i, i + by) for i in range(length) if 0 <= i + by < length]
    return lax.ppermute(x, axis, pairs)


def swapped(x, axis):
    return lax.ppermute(x, axis, [(0, 1), (1, 0)])


def conv_rows(padded, weights, bias_row):
    sequence_length = padded.shape[0] - (CONV_K - 1)
    total = jnp.zeros((sequence_length, padded.shape[1]), jnp.float32) + bias_row[None, :]
    for tap_index in range(CONV_K):
        total = total + weights[tap_index][None, :] * padded[
            tap_index : tap_index + sequence_length
        ].astype(jnp.float32)
    return jax.nn.silu(total)


def conv_cols(padded, weights, bias_block):
    sequence_length = padded.shape[-1] - (CONV_K - 1)
    total = jnp.zeros(padded.shape[:-1] + (sequence_length,), jnp.float32) + bias_block[..., None]
    for tap_index in range(CONV_K):
        total = total + weights[tap_index][..., None] * padded[
            ..., tap_index : tap_index + sequence_length
        ].astype(jnp.float32)
    return jax.nn.silu(total)


def dot(a, b):
    return jnp.dot(a, b, precision=HIGHEST, preferred_element_type=F32)


def pair_picker(heads, pair):
    rows = lax.broadcasted_iota(jnp.int32, (heads, 128), 0)
    lanes = lax.broadcasted_iota(jnp.int32, (heads, 128), 1)
    target = jnp.where(lanes < HEAD_DIM, 2 * pair, 2 * pair + 1)
    return (rows == target).astype(F32)


def scan_kernel(xc_ref, ct_ref, b_ref, cumr_ref, cumc_ref, stp_ref, dsk_ref, y_ref, e_ref):
    chunk = pl.program_id(1)
    block_len = xc_ref.shape[0]
    pairs = e_ref.shape[1]
    heads = 2 * pairs

    @pl.when(chunk == 0)
    def _():
        e_ref[...] = jnp.zeros_like(e_ref)

    ct = ct_ref[0]
    bm = b_ref[0]
    scores = dot(ct, bm)
    rows = lax.broadcasted_iota(jnp.int32, (block_len, block_len), 0)
    cols = lax.broadcasted_iota(jnp.int32, (block_len, block_len), 1)
    causal = rows >= cols
    cumr = cumr_ref[0]
    cumc = cumc_ref[0]
    stp = stp_ref[0]
    head_rows = lax.broadcasted_iota(jnp.int32, (heads, block_len), 0)
    left = lax.broadcasted_iota(jnp.int32, (1, 128), 1) < HEAD_DIM
    for pair in range(pairs):
        lanes = slice(pair * 128, (pair + 1) * 128)
        xp = xc_ref[:, lanes]
        s_old = e_ref[0, pair]
        ys = []
        us = []
        for side in range(2):
            head = 2 * pair + side
            dq = dot(cumc, (head_rows == head).astype(F32))
            ck = cumr[head : head + 1, :]
            sk = stp[head : head + 1, :]
            dec = jnp.exp(jnp.where(causal, dq - ck, -jnp.inf))
            ys.append(dot(scores * dec * sk, xp))
            wk = jnp.exp(dq[block_len - 1 : block_len, :] - ck) * sk
            us.append(dot(bm * wk, xp))
        cq = dot(cumc, pair_picker(heads, pair))
        inflow = dot(ct, s_old) * jnp.exp(cq)
        y = jnp.where(left, ys[0], ys[1]) + inflow
        y_ref[:, lanes] = y + xp * dsk_ref[:, lanes]
        e_ref[0, pair] = jnp.exp(cq[block_len - 1 : block_len, :]) * s_old + jnp.where(
            left, us[0], us[1]
        )


def out_kernel(y_ref, ct_ref, cumc_ref, v_ref, z_ref, nw_ref, o_ref, g_ref):
    pairs = v_ref.shape[1]
    heads = 2 * pairs
    ct = ct_ref[0]
    cumc = cumc_ref[0]
    total = jnp.zeros((y_ref.shape[0], 1), F32)
    for pair in range(pairs):
        lanes = slice(pair * 128, (pair + 1) * 128)
        cq = dot(cumc, pair_picker(heads, pair))
        y = y_ref[:, lanes] + dot(ct, v_ref[0, pair]) * jnp.exp(cq)
        z = z_ref[:, lanes].astype(F32)
        gated = y * (z / (1.0 + jnp.exp(-z)))
        g_ref[:, lanes] = gated
        total = total + jnp.sum(gated * gated, axis=-1, keepdims=True)
    mean_square = total / g_ref.shape[1]
    o_ref[...] = (g_ref[...] * lax.rsqrt(mean_square + 1e-05) * nw_ref[...]).astype(o_ref.dtype)


def per_device(
    x_raw,
    bc_raw,
    z_gate,
    dt_raw,
    conv_x_w,
    conv_x_b,
    conv_bc_w,
    conv_bc_b,
    dt_bias,
    a_log,
    d_skip,
    norm_w,
):
    tokens = x_raw.shape[0]
    heads_dev = dt_raw.shape[0]
    per_group = HEADS // GROUPS
    set_groups = heads_dev // per_group
    pairs = per_group // 2
    group_width = per_group * HEAD_DIM
    nsub = lax.axis_size("sub")
    sub_index = lax.axis_index("sub")
    own = tokens // nsub
    half = bc_raw.shape[2]
    state = half * nsub
    channels = heads_dev * HEAD_DIM
    rim_len = CONV_K - 1

    x_rim, bc_rim = passed_along(
        (x_raw[tokens - rim_len :], bc_raw[..., tokens - rim_len :]), "ctx", 1
    )
    x_pad = jnp.concatenate([x_rim, x_raw], 0)
    x_own = conv_rows(
        lax.dynamic_slice_in_dim(x_pad, sub_index * own, own + rim_len, 0), conv_x_w, conv_x_b
    )
    bc_weights = lax.dynamic_slice_in_dim(conv_bc_w, sub_index * half, half, 3)
    bc_bias = lax.dynamic_slice_in_dim(conv_bc_b, sub_index * half, half, 2)
    bc_conv = conv_cols(jnp.concatenate([bc_rim, bc_raw], 3), bc_weights, bc_bias)
    bc_own = lax.all_to_all(bc_conv, "sub", 3, 2, tiled=True)
    b_rows = bc_own[0]
    c_cols = bc_own[1].transpose(0, 2, 1)

    step_sizes = jax.nn.softplus(dt_raw + dt_bias[:, None])
    log_decay = -jnp.exp(a_log)[:, None] * step_sizes
    half_totals = jnp.exp(log_decay.reshape(heads_dev, nsub, own).sum(-1))
    step_own = lax.dynamic_slice_in_dim(step_sizes, sub_index * own, own, 1)
    decay_own = lax.dynamic_slice_in_dim(log_decay, sub_index * own, own, 1)
    block_len = min(256, own)
    blocks = own // block_len
    upper = (
        lax.broadcasted_iota(jnp.int32, (block_len, block_len), 0)
        <= lax.broadcasted_iota(jnp.int32, (block_len, block_len), 1)
    ).astype(F32)
    cum_local = jnp.einsum(
        "hct,tu->hcu", decay_own.reshape(heads_dev, blocks, block_len), upper, precision=HIGHEST
    )
    block_totals = cum_local[..., -1]
    offsets = jnp.cumsum(block_totals, axis=-1) - block_totals
    cum_device = (cum_local + offsets[..., None]).reshape(set_groups, per_group, own)
    cum_rows = cum_local.reshape(set_groups, per_group, own)
    cum_cols = cum_rows.transpose(0, 2, 1)
    step_rows = step_own.reshape(set_groups, per_group, own)
    skip_row = jnp.repeat(d_skip, HEAD_DIM)[None, :]

    y_local, end_state = pl.pallas_call(
        scan_kernel,
        grid=(set_groups, blocks),
        in_specs=[
            pl.BlockSpec((block_len, group_width), lambda g, c: (c, g)),
            pl.BlockSpec((1, block_len, state), lambda g, c: (g, c, 0)),
            pl.BlockSpec((1, state, block_len), lambda g, c: (g, 0, c)),
            pl.BlockSpec((1, per_group, block_len), lambda g, c: (g, 0, c)),
            pl.BlockSpec((1, block_len, per_group), lambda g, c: (g, c, 0)),
            pl.BlockSpec((1, per_group, block_len), lambda g, c: (g, 0, c)),
            pl.BlockSpec((1, group_width), lambda g, c: (0, g)),
        ],
        out_specs=[
            pl.BlockSpec((block_len, group_width), lambda g, c: (c, g)),
            pl.BlockSpec((1, pairs, state, 128), lambda g, c: (g, 0, 0, 0)),
        ],
        out_shape=[
            jax.ShapeDtypeStruct((own, channels), F32),
            jax.ShapeDtypeStruct((set_groups, pairs, state, 128), F32),
        ],
    )(x_own, c_cols, b_rows, cum_rows, cum_cols, step_rows, skip_row)

    def pair_layout(values):
        return jnp.repeat(values.reshape(set_groups, pairs, 2), HEAD_DIM, axis=-1)[:, :, None, :]

    decay_first = pair_layout(half_totals[:, 0])
    decay_second = pair_layout(half_totals[:, 1])
    halves = end_state.reshape(set_groups, pairs, nsub, half, 128)
    mine = lax.dynamic_index_in_dim(halves, sub_index, 2, keepdims=False)
    theirs = swapped(lax.dynamic_index_in_dim(halves, 1 - sub_index, 2, keepdims=False), "sub")
    first_end = jnp.where(sub_index == 0, mine, theirs)
    second_end = jnp.where(sub_index == 0, theirs, mine)
    chip_end = decay_second * first_end + second_end
    chip_decay = decay_first * decay_second
    carried = jnp.zeros_like(chip_end)
    for _ in range(lax.axis_size("ctx") - 1):
        carried = passed_along(chip_end + chip_decay * carried, "ctx", 1)
    into_second = decay_first * carried + first_end
    keep = jnp.where(sub_index == 0, carried, into_second)
    got = swapped(jnp.where(sub_index == 0, into_second, carried), "sub")
    low = jnp.where(sub_index == 0, keep, got)
    high = jnp.where(sub_index == 0, got, keep)
    incoming = jnp.stack([low, high], 2).reshape(set_groups, pairs, state, 128)

    out_len = min(256, own)
    return pl.pallas_call(
        out_kernel,
        grid=(set_groups, own // out_len),
        in_specs=[
            pl.BlockSpec((out_len, group_width), lambda g, c: (c, g)),
            pl.BlockSpec((1, out_len, state), lambda g, c: (g, c, 0)),
            pl.BlockSpec((1, out_len, per_group), lambda g, c: (g, c, 0)),
            pl.BlockSpec((1, pairs, state, 128), lambda g, c: (g, 0, 0, 0)),
            pl.BlockSpec((out_len, group_width), lambda g, c: (c, g)),
            pl.BlockSpec((1, group_width), lambda g, c: (0, g)),
        ],
        out_specs=pl.BlockSpec((out_len, group_width), lambda g, c: (c, g)),
        out_shape=jax.ShapeDtypeStruct((own, channels), jnp.bfloat16),
        scratch_shapes=[pltpu.VMEM((out_len, group_width), F32)],
    )(y_local, c_cols, cum_device.transpose(0, 2, 1), incoming, z_gate, norm_w[None, :])


def solution(mesh):
    in_specs = (
        P(("groups", "ctx"), "head"),
        P(None, "head", "sub", ("groups", "ctx")),
        P(("groups", "ctx", "sub"), "head"),
        P("head", ("groups", "ctx")),
        P(None, "head"),
        P("head"),
        P(None, None, "head", None),
        P(None, "head", None),
        P("head"),
        P("head"),
        P("head"),
        P("head"),
    )
    out_specs = P(("groups", "ctx", "sub"), "head")
    return jax.shard_map(
        per_device, mesh=mesh, in_specs=in_specs, out_specs=out_specs, check_vma=False
    )
```

time: 511 us -> 290 us (0.57); the launches traced: 501 us -> 290 us
  matrix products: 158 us -> 0.23 us
  Pallas kernels: 0 us -> 125 us
  waiting for transfers between devices: 157 us -> 67.3 us
  other arithmetic: 82.8 us -> 30.8 us
  local copies, waits for them, and re-layouts: 68.6 us -> 38.1 us
  between operations: 14.5 us -> 0.36 us
  blocking collectives: 0 us -> 6.29 us
    dot_general x17 -> x1, matrix products: 158 us -> 0.23 us  [per_device(): jnp.einsum('hct,tu->hcu', decay_own.reshape(heads_dev, blocks, block_len)...]
    pallas_call x0 -> x2, Pallas kernels: none -> 125 us  [the longest x1 107 us: per_device(): pl.pallas_call(scan_kernel, grid=(set_groups, blocks), in_specs=[pl.Block...]
    ppermute x5, waiting for transfers between devices: 131 us -> 66.3 us  [passed_along(): return lax.ppermute(x, axis, pairs)]
    mul x4 -> x2, local copies, waits for them, and re-layouts: 29.7 us -> 3.22 us  [the longest x1 3.13 us: conv_cols(): return jax.nn.silu(total)]
    reduce_scatter x1 -> x0, waiting for transfers between devices: 26.3 us -> none  [per_device(): lax.psum_scatter(token_major, 'sub', scatter_dimension=0, tiled=True)]
    another operation x16 -> x3, other arithmetic: 27.7 us -> 3.31 us  [the longest x2 3.13 us: per_device(): incoming = jnp.stack([low, high], 2).reshape(set_groups, pairs, state, 128)]
    reshape x1 -> x5, local copies, waits for them, and re-layouts: 17.5 us -> 3.8 us  [the longest x2 1.45 us: per_device(): cum_rows = cum_local.reshape(set_groups, per_group, own)]
    mul x3 -> x2, other arithmetic: 13.6 us -> 1.18 us  [the longest x1 1.18 us: per_device(): log_decay = -jnp.exp(a_log)[:, None] * step_sizes]
  transfers between devices with their start and end apart: 6 -> 7, of which waited for: 4 -> 4; matrix products, arithmetic and copies ran while one was open for 10% -> 17% of each run, Pallas kernels for 0% -> 0%
where the time goes in v1:
time: 290 us
  Pallas kernels  125 us (43%)
  waiting for transfers between devices  67.3 us (23%)
  local copies, waits for them, and re-layouts  38.1 us (13%)
  other arithmetic  30.8 us (11%)
  starting transfers between devices  21.2 us (7%)
  blocking collectives  6.29 us (2%)
    pallas_call x1, Pallas kernels, per_device(): pl.pallas_call(scan_kernel, grid=(set_groups, blocks), in_specs=[pl.Block...  107 us
    ppermute x5, waiting for transfers between devices, passed_along(): return lax.ppermute(x, axis, pairs)  66.3 us
    ppermute x5, starting transfers between devices, passed_along(): return lax.ppermute(x, axis, pairs)  20.8 us
    pallas_call x1, Pallas kernels, per_device(): pl.pallas_call(out_kernel, grid=(set_groups, own // out_len), in_specs=[p...  18.7 us
    unnamed x28, local copies, waits for them, and re-layouts  11.7 us
    all_to_all x1, other arithmetic, per_device(): bc_own = lax.all_to_all(bc_conv, 'sub', 3, 2, tiled=True)  8.58 us
    mul x1, other arithmetic, conv_rows(): return jax.nn.silu(total)  6.81 us
    all_to_all x1, blocking collectives, per_device(): bc_own = lax.all_to_all(bc_conv, 'sub', 3, 2, tiled=True)  6.29 us
  transfers between devices with their start and end apart: 7, of which 4 were waited for; matrix products, arithmetic and copies ran while one was open for 17% of the time, Pallas kernels for 0%

profile of v1, /device:TPU:0, one launch (start us, length us, event | category | flops | bytes accessed | tf_op | source)
XLA Modules:
  0.0 289.6 jit_solution(963816445319067396)
XLA Ops:
  0.0 1.1 slice.78
  1.1 4.9 %collective-permute-start.1 = (bf16[2,4,64,3]{3,2,1,0:T(8,128)(2,1)S(1)}, bf16[2,4,64,3]{3,2,1,0:T(8,128)(2,1)S(1)}, u32[]{:S(2)}, u32[]{:S(2)}) collective-permute-start(bf16[2,4,64,3]{3,2,1,0:T(8,128)(2,1)S(1)} %slice.78), channel_id=1, source_target_pairs={{0,4},{4,8},{8,12},{1,5},{5,9},{9,13},{2,6},{6,10},{10,14},{3,7},{... | collective-permute-start | bytes 9224 | tf_op jit(solution)/shard_map/ppermute | solution.py:21
  6.1 1.5 slice.69
  7.5 4.1 %collective-permute-start = (bf16[3,4096]{1,0:T(4,128)(2,1)}, bf16[3,4096]{1,0:T(4,128)(2,1)}, u32[]{:S(2)}, u32[]{:S(2)}) collective-permute-start(bf16[3,4096]{1,0:T(4,128)(2,1)} %slice.69), channel_id=1, source_target_pairs={{0,4},{4,8},{8,12},{1,5},{5,9},{9,13},{2,6},{6,10},{10,14},{3,7},{... | collective-permute-start | bytes 73736 | tf_op jit(solution)/shard_map/ppermute | solution.py:21
  11.6 1.7 fusion.14
  13.9 1.2 broadcast_multiply_fusion
  16.0 1.4 dynamic-slice_bitcast_fusion.4
  18.3 1.3 copy.67
  21.1 3.2 %divide_multiply_fusion.1 = f32[2,4,64,1024]{3,2,1,0:T(8,128)S(1)} fusion(bf16[2,4,64,1024]{3,2,1,0:T(8,128)(2,1)S(1)} %copy-done.3, bf16[2,4,64,3]{3,2,1,0:T(8,128)(2,1)} %copy-done.6, f32[2,4,64]{2,1,0:T(4,128)} %get-tuple-element.29, f32[2,4,64]{2,1,0:T(4,128)S(1)} %get-tuple-element.27, f32[2,4,64]{2,1,0:T(4,128)S(1)} %get-tuple-element.28, ...), kind=kLoop, calls=%fused_computation.5 | loop fusion | flops 13107200 | bytes 3159040 | tf_op jit(solution)/shard_map/jit(silu)/mul | solution.py:45
  24.3 3.1 %copy.60 = f32[2,4,64,1024]{2,1,0,3:T(4,128)} copy(f32[2,4,64,1024]{3,2,1,0:T(8,128)S(1)} %divide_multiply_fusion.1) | data formatting | bytes 4194304 | tf_op jit(solution)/shard_map/jit(silu)/mul | solution.py:45
  27.4 5.5 %reshape.62 = f32[2,1,262144]{2,1,0:T(1,128)S(1)} reshape(f32[1024,2,4,64]{3,2,1,0:T(4,128)} %bitcast.47) | data formatting | bytes 4194304
  32.9 6.3 %all_to_all.15 = f32[2,1,262144]{2,1,0:T(1,128)} all-to-all(f32[2,1,262144]{2,1,0:T(1,128)S(1)} %reshape.62), channel_id=1, replica_groups=mesh['groups'=2,'ctx'=4,'head'=2,'sub'=2] {'sub'}, dimensions={0} | all-to-all | bytes 4194304 | tf_op jit(solution)/shard_map/all_to_all | solution.py:160
  39.7 8.6 %reduce.6 = f32[2,262144]{1,0:T(2,128)S(1)} reduce(f32[2,1,262144]{2,1,0:T(1,128)} %all_to_all.15, f32[]{:T(128)} %broadcast.13), dimensions={1}, to_apply=%all_to_all.11.reduce_sub_computation | reduce | bytes 4194308 | tf_op jit(solution)/shard_map/all_to_all | solution.py:160
  48.3 5.5 %reshape.63 = f32[1024,2,4,64]{3,2,1,0:T(4,128)} reshape(f32[2,262144]{1,0:T(2,128)S(1)} %reduce.6) | data formatting | bytes 4194304
  53.8 5.4 %copy.71 = f32[2,4,64,2,512]{4,3,2,1,0:T(2,128)S(1)} copy(f32[2,4,64,2,512]{2,1,0,4,3:T(4,128)} %bitcast.48) | data formatting | bytes 4194304 | tf_op jit(solution)/shard_map/all_to_all | solution.py:160
  60.2 1.3 copy.63
  61.5 1.2 copy.64
  62.7 3.6 %fusion = bf16[515,4096]{1,0:T(8,128)(2,1)S(1)} fusion(s32[]{:T(128)S(6)} %select_n.50, bf16[3,4096]{1,0:T(4,128)(2,1)} %collective-permute-done, bf16[1024,4096]{1,0:T(8,128)(2,1)} %param.12), kind=kLoop, calls=%fused_computation.3 | loop fusion | flops 8437760 | bytes 12632068 | tf_op jit(solution)/shard_map/concatenate | solution.py:153
  66.4 6.8 %divide_multiply_fusion.xc_ref = f32[512,4096]{1,0:T(8,128)} fusion(bf16[515,4096]{1,0:T(8,128)(2,1)S(1)} %fusion, f32[4096]{0:T(1024)S(1)} %bitcast.63, f32[4096]{0:T(1024)S(1)} %bitcast.64, f32[4096]{0:T(1024)S(1)} %bitcast.62, f32[4096]{0:T(1024)S(1)} %bitcast.61, f32[4096]{0:T(1024)S(1)} %copy-done.11), kind=kLoop, calls=%fused_computation.2 | loop fusion | flops 33554432 | bytes 25247744 | tf_op jit(solution)/shard_map/jit(silu)/mul | solution.py:35
  73.2 106.7 %shard_map.118 = (f32[512,4096]{1,0:T(8,128)}, f32[4,8,128,128]{3,2,1,0:T(8,128)}) custom-call(f32[512,4096]{1,0:T(8,128)} %divide_multiply_fusion.xc_ref, f32[4,512,128]{2,1,0:T(8,128)} %bitcast.49, f32[4,128,512]{2,1,0:T(8,128)} %bitcast.54, f32[4,16,512]{2,1,0:T(8,128)} %copy-done.4, f32[4,512,16]{2,1,0:T(8,128)} %bitcast.53, f32[4,16,512]{2,1,0:T(8,128)} %bitcast.59, ...), custom_call_target="tpu_custom_call" | custom-call | tf_op jit(solution)/shard_map/pallas_call | solution.py:186
  179.9 1.5 dynamic-slice_bitcast_fusion
  184.4 1.6 broadcast_add_fusion
  186.0 2.9 %collective-permute-start.3 = (f32[4,8,64,128]{3,2,1,0:T(8,128)S(1)}, f32[4,8,64,128]{3,2,1,0:T(8,128)S(1)}, u32[]{:S(2)}, u32[]{:S(2)}) collective-permute-start(f32[4,8,64,128]{3,2,1,0:T(8,128)S(1)} %get-tuple-element.11), channel_id=1, source_target_pairs={{0,4},{4,8},{8,12},{1,5},{5,9},{9,13},{2,6},{6,10},{10,14},{3,7},{... | collective-permute-start | bytes 3145736 | tf_op jit(solution)/shard_map/ppermute | solution.py:21
  188.9 22.9 %collective-permute-done.3 = f32[4,8,64,128]{3,2,1,0:T(8,128)S(1)} collective-permute-done((f32[4,8,64,128]{3,2,1,0:T(8,128)S(1)}, f32[4,8,64,128]{3,2,1,0:T(8,128)S(1)}, u32[]{:S(2)}, u32[]{:S(2)}) %collective-permute-start.3) | collective-permute-done | bytes 1048608 | tf_op jit(solution)/shard_map/ppermute | solution.py:21
  212.1 4.5 %collective-permute-start.4 = (f32[4,8,64,128]{3,2,1,0:T(8,128)S(1)}, f32[4,8,64,128]{3,2,1,0:T(8,128)S(1)}, u32[]{:S(2)}, u32[]{:S(2)}) collective-permute-start(f32[4,8,64,128]{3,2,1,0:T(8,128)S(1)} %multiply_add_fusion.2), channel_id=1, source_target_pairs={{0,4},{4,8},{8,12},{1,5},{5,9},{9,13},{2,6},{6,10},{10,14},{3,7},{... | collective-permute-start | bytes 3145736 | tf_op jit(solution)/shard_map/ppermute | solution.py:21
  216.6 22.1 %collective-permute-done.4 = f32[4,8,64,128]{3,2,1,0:T(8,128)S(1)} collective-permute-done((f32[4,8,64,128]{3,2,1,0:T(8,128)S(1)}, f32[4,8,64,128]{3,2,1,0:T(8,128)S(1)}, u32[]{:S(2)}, u32[]{:S(2)}) %collective-permute-start.4) | collective-permute-done | bytes 1048608 | tf_op jit(solution)/shard_map/ppermute | solution.py:21
  238.9 4.5 %collective-permute-start.5 = (f32[4,8,64,128]{3,2,1,0:T(8,128)S(1)}, f32[4,8,64,128]{3,2,1,0:T(8,128)S(1)}, u32[]{:S(2)}, u32[]{:S(2)}) collective-permute-start(f32[4,8,64,128]{3,2,1,0:T(8,128)S(1)} %multiply_add_fusion.1), channel_id=1, source_target_pairs={{0,4},{4,8},{8,12},{1,5},{5,9},{9,13},{2,6},{6,10},{10,14},{3,7},{... | collective-permute-start | bytes 3145736 | tf_op jit(solution)/shard_map/ppermute | solution.py:21
  243.4 21.2 %collective-permute-done.5 = f32[4,8,64,128]{3,2,1,0:T(8,128)S(1)} collective-permute-done((f32[4,8,64,128]{3,2,1,0:T(8,128)S(1)}, f32[4,8,64,128]{3,2,1,0:T(8,128)S(1)}, u32[]{:S(2)}, u32[]{:S(2)}) %collective-permute-start.5) | collective-permute-done | bytes 1048608 | tf_op jit(solution)/shard_map/ppermute | solution.py:21
  265.5 1.3 copy.69
  267.8 1.6 select_bitcast_fusion.1
  269.4 1.5 pad_maximum_fusion
  270.9 18.7 %shard_map.119 = bf16[512,4096]{1,0:T(8,128)(2,1)} custom-call(f32[512,4096]{1,0:T(8,128)} %get-tuple-element.7.y_ref, f32[4,512,128]{2,1,0:T(8,128)} %bitcast.50, f32[4,512,16]{2,1,0:T(8,128)} %bitcast.55, f32[4,8,128,128]{3,2,1,0:T(8,128)} %bitcast.51, bf16[512,4096]{1,0:T(8,128)(2,1)} %z_ref.1, f32[1,4096]{1,0:T(1,128)} %bitcast.65), custom_call_target="tpu_custom_call" | custom-call | tf_op jit(solution)/shard_map/pallas_call | solution.py:231
  (62 shorter events, 10.6 us)
Async XLA Ops:
  0.0 17.4 %copy-start = (f32[2,4,128]{2,1,0:T(4,128)S(1)}, f32[2,4,128]{2,1,0:T(4,128)}, u32[]{:S(2)}) copy-start(f32[2,4,128]{2,1,0:T(4,128)} %param.19) | copy-start | bytes 12292
  0.0 21.1 %copy-start.3 = (bf16[2,4,64,1024]{3,2,1,0:T(8,128)(2,1)S(1)}, bf16[2,4,64,1024]{3,2,1,0:T(8,128)(2,1)}, u32[]{:S(2)}) copy-start(bf16[2,4,64,1024]{3,2,1,0:T(8,128)(2,1)} %param.13) | copy-start | bytes 3145732
  0.0 19.7 %copy-start.12 = (f32[64]{0:T(128)S(1)}, f32[64]{0:T(128)}, u32[]{:S(2)}) copy-start(f32[64]{0:T(128)} %param.22) | copy-start | bytes 772
  1.1 19.3 %collective-permute-start.1 = (bf16[2,4,64,3]{3,2,1,0:T(8,128)(2,1)S(1)}, bf16[2,4,64,3]{3,2,1,0:T(8,128)(2,1)S(1)}, u32[]{:S(2)}, u32[]{:S(2)}) collective-permute-start(bf16[2,4,64,3]{3,2,1,0:T(8,128)(2,1)S(1)} %slice.78), channel_id=1, source_target_pairs={{0,4},{4,8},{8,12},{1,5},{5,9},{9,13},{2,6},{6,10},{10,14},{3,7},{... | collective-permute-start | bytes 9224 | tf_op jit(solution)/shard_map/ppermute | solution.py:21
  7.5 55.2 %collective-permute-start = (bf16[3,4096]{1,0:T(4,128)(2,1)}, bf16[3,4096]{1,0:T(4,128)(2,1)}, u32[]{:S(2)}, u32[]{:S(2)}) collective-permute-start(bf16[3,4096]{1,0:T(4,128)(2,1)} %slice.69), channel_id=1, source_target_pairs={{0,4},{4,8},{8,12},{1,5},{5,9},{9,13},{2,6},{6,10},{10,14},{3,7},{... | collective-permute-start | bytes 73736 | tf_op jit(solution)/shard_map/ppermute | solution.py:21
  18.3 2.1 copy-start.4
  20.4 0.7 copy-start.6
  62.7 3.6 %copy-start.7 = (f32[1,4096]{1,0:T(1,128)S(1)}, f32[1,4096]{1,0:T(1,128)}, u32[]{:S(2)}) copy-start(f32[1,4096]{1,0:T(1,128)} %get-tuple-element.22) | copy-start | bytes 49156
  62.7 3.6 %copy-start.8 = (f32[1,4096]{1,0:T(1,128)S(1)}, f32[1,4096]{1,0:T(1,128)}, u32[]{:S(2)}) copy-start(f32[1,4096]{1,0:T(1,128)} %get-tuple-element.23) | copy-start | bytes 49156
  62.7 3.6 %copy-start.9 = (f32[1,4096]{1,0:T(1,128)S(1)}, f32[1,4096]{1,0:T(1,128)}, u32[]{:S(2)}) copy-start(f32[1,4096]{1,0:T(1,128)} %get-tuple-element.24) | copy-start | bytes 49156
  62.7 3.7 %copy-start.10 = (f32[1,4096]{1,0:T(1,128)S(1)}, f32[1,4096]{1,0:T(1,128)}, u32[]{:S(2)}) copy-start(f32[1,4096]{1,0:T(1,128)} %get-tuple-element.25) | copy-start | bytes 49156
  62.7 3.7 %copy-start.11 = (f32[4096]{0:T(1024)S(1)}, f32[4096]{0:T(1024)}, u32[]{:S(2)}) copy-start(f32[4096]{0:T(1024)} %param.17) | copy-start | bytes 49156
  179.8 4.6 %copy-start.2 = (f32[4,8,128,128]{3,2,1,0:T(8,128)S(1)}, f32[4,8,128,128]{3,2,1,0:T(8,128)}, u32[]{:S(2)}) copy-start(f32[4,8,128,128]{3,2,1,0:T(8,128)} %get-tuple-element.8) | copy-start | bytes 6291460
  181.3 3.1 %collective-permute-start.2 = (f32[4,8,64,128]{3,2,1,0:T(8,128)S(1)}, f32[4,8,64,128]{3,2,1,0:T(8,128)}, u32[]{:S(2)}, u32[]{:S(2)}) collective-permute-start(f32[4,8,64,128]{3,2,1,0:T(8,128)S(1)} %dynamic-slice_bitcast_fusion), channel_id=1, source_target_pairs={{0,1},{1,0},{2,3},{3,2},{4,5},{5,4},{6,7},{7,6},{8,9},{9,8},{10,11... | collective-permute-start | bytes 3145736 | tf_op jit(solution)/shard_map/ppermute | solution.py:25
  184.1 80.5 %copy-start.5 = (f32[4,8,128]{2,1,0:T(8,128)}, f32[4,8,128]{2,1,0:T(8,128)S(1)}, u32[]{:S(2)}) copy-start(f32[4,8,128]{2,1,0:T(8,128)S(1)} %broadcast_in_dim_reshape.8) | copy-start | bytes 49156
  186.0 25.8 %collective-permute-start.3 = (f32[4,8,64,128]{3,2,1,0:T(8,128)S(1)}, f32[4,8,64,128]{3,2,1,0:T(8,128)S(1)}, u32[]{:S(2)}, u32[]{:S(2)}) collective-permute-start(f32[4,8,64,128]{3,2,1,0:T(8,128)S(1)} %get-tuple-element.11), channel_id=1, source_target_pairs={{0,4},{4,8},{8,12},{1,5},{5,9},{9,13},{2,6},{6,10},{10,14},{3,7},{... | collective-permute-start | bytes 3145736 | tf_op jit(solution)/shard_map/ppermute | solution.py:21
  212.1 26.6 %collective-permute-start.4 = (f32[4,8,64,128]{3,2,1,0:T(8,128)S(1)}, f32[4,8,64,128]{3,2,1,0:T(8,128)S(1)}, u32[]{:S(2)}, u32[]{:S(2)}) collective-permute-start(f32[4,8,64,128]{3,2,1,0:T(8,128)S(1)} %multiply_add_fusion.2), channel_id=1, source_target_pairs={{0,4},{4,8},{8,12},{1,5},{5,9},{9,13},{2,6},{6,10},{10,14},{3,7},{... | collective-permute-start | bytes 3145736 | tf_op jit(solution)/shard_map/ppermute | solution.py:21
  238.9 25.7 %collective-permute-start.5 = (f32[4,8,64,128]{3,2,1,0:T(8,128)S(1)}, f32[4,8,64,128]{3,2,1,0:T(8,128)S(1)}, u32[]{:S(2)}, u32[]{:S(2)}) collective-permute-start(f32[4,8,64,128]{3,2,1,0:T(8,128)S(1)} %multiply_add_fusion.1), channel_id=1, source_target_pairs={{0,4},{4,8},{8,12},{1,5},{5,9},{9,13},{2,6},{6,10},{10,14},{3,7},{... | collective-permute-start | bytes 3145736 | tf_op jit(solution)/shard_map/ppermute | solution.py:21
  264.9 2.9 collective-permute-start.6
  270.9 18.7 %copy-start.1 = (f32[2,4,128]{2,1,0:T(4,128)S(1)}, f32[2,4,128]{2,1,0:T(4,128)}, u32[]{:S(2)}) copy-start(f32[2,4,128]{2,1,0:T(4,128)} %param.19) | copy-start | bytes 12292

commit v2 on v1

--- a/solution.py
+++ b/solution.py
@@ -49,11 +49,25 @@
     return jnp.dot(a, b, precision=HIGHEST, preferred_element_type=F32)
 
 
-def pair_picker(heads, pair):
-    rows = lax.broadcasted_iota(jnp.int32, (heads, 128), 0)
-    lanes = lax.broadcasted_iota(jnp.int32, (heads, 128), 1)
-    target = jnp.where(lanes < HEAD_DIM, 2 * pair, 2 * pair + 1)
-    return (rows == target).astype(F32)
+def split(a):
+    high = a.astype(jnp.bfloat16)
+    return high, (a - high.astype(F32)).astype(jnp.bfloat16)
+
+
+def dot3(a_parts, b_parts):
+    a_high, a_low = a_parts
+    b_high, b_low = b_parts
+    flat = lambda u, v: jnp.dot(u, v, preferred_element_type=F32)
+    return flat(a_high, b_high) + (flat(a_high, b_low) + flat(a_low, b_high))
+
+
+def pair_columns(cumc, pair, rows):
+    left = lax.broadcasted_iota(jnp.int32, (1, 128), 1) < HEAD_DIM
+    return jnp.where(
+        left,
+        jnp.broadcast_to(cumc[:, 2 * pair : 2 * pair + 1], (rows, 128)),
+        jnp.broadcast_to(cumc[:, 2 * pair + 1 : 2 * pair + 2], (rows, 128)),
+    )
 
 
 def scan_kernel(xc_ref, ct_ref, b_ref, cumr_ref, cumc_ref, stp_ref, dsk_ref, y_ref, e_ref):
@@ -66,34 +80,34 @@
     def _():
         e_ref[...] = jnp.zeros_like(e_ref)
 
-    ct = ct_ref[0]
+    ct = split(ct_ref[0])
     bm = b_ref[0]
-    scores = dot(ct, bm)
+    scores = dot3(ct, split(bm))
     rows = lax.broadcasted_iota(jnp.int32, (block_len, block_len), 0)
     cols = lax.broadcasted_iota(jnp.int32, (block_len, block_len), 1)
     causal = rows >= cols
     cumr = cumr_ref[0]
     cumc = cumc_ref[0]
     stp = stp_ref[0]
-    head_rows = lax.broadcasted_iota(jnp.int32, (heads, block_len), 0)
     left = lax.broadcasted_iota(jnp.int32, (1, 128), 1) < HEAD_DIM
     for pair in range(pairs):
         lanes = slice(pair * 128, (pair + 1) * 128)
         xp = xc_ref[:, lanes]
+        xs = split(xp)
         s_old = e_ref[0, pair]
         ys = []
         us = []
         for side in range(2):
             head = 2 * pair + side
-            dq = dot(cumc, (head_rows == head).astype(F32))
+            dq = jnp.broadcast_to(cumc[:, head : head + 1], (block_len, block_len))
             ck = cumr[head : head + 1, :]
             sk = stp[head : head + 1, :]
             dec = jnp.exp(jnp.where(causal, dq - ck, -jnp.inf))
-            ys.append(dot(scores * dec * sk, xp))
+            ys.append(dot3(split(scores * dec * sk), xs))
             wk = jnp.exp(dq[block_len - 1 : block_len, :] - ck) * sk
-            us.append(dot(bm * wk, xp))
-        cq = dot(cumc, pair_picker(heads, pair))
-        inflow = dot(ct, s_old) * jnp.exp(cq)
+            us.append(dot3(split(bm * wk), xs))
+        cq = pair_columns(cumc, pair, block_len)
+        inflow = dot3(ct, split(s_old)) * jnp.exp(cq)
         y = jnp.where(left, ys[0], ys[1]) + inflow
         y_ref[:, lanes] = y + xp * dsk_ref[:, lanes]
         e_ref[0, pair] = jnp.exp(cq[block_len - 1 : block_len, :]) * s_old + jnp.where(
@@ -104,13 +118,13 @@
 def out_kernel(y_ref, ct_ref, cumc_ref, v_ref, z_ref, nw_ref, o_ref, g_ref):
     pairs = v_ref.shape[1]
     heads = 2 * pairs
-    ct = ct_ref[0]
+    ct = split(ct_ref[0])
     cumc = cumc_ref[0]
     total = jnp.zeros((y_ref.shape[0], 1), F32)
     for pair in range(pairs):
         lanes = slice(pair * 128, (pair + 1) * 128)
-        cq = dot(cumc, pair_picker(heads, pair))
-        y = y_ref[:, lanes] + dot(ct, v_ref[0, pair]) * jnp.exp(cq)
+        cq = pair_columns(cumc, pair, y_ref.shape[0])
+        y = y_ref[:, lanes] + dot3(ct, split(v_ref[0, pair])) * jnp.exp(cq)
         z = z_ref[:, lanes].astype(F32)
         gated = y * (z / (1.0 + jnp.exp(-z)))
         g_ref[:, lanes] = gated

time: 290 us -> 215 us (0.74)
  Pallas kernels: 125 us -> 50 us
    pallas_call x1, Pallas kernels: 107 us -> 34.8 us  [per_device(): pl.pallas_call(scan_kernel, grid=(set_groups, blocks), in_specs=[pl.Block...]
    pallas_call x1, Pallas kernels: 18.7 us -> 15.3 us  [per_device(): pl.pallas_call(out_kernel, grid=(set_groups, own // out_len), in_specs=[p...]
  transfers between devices with their start and end apart: 7 -> 7, of which waited for: 4 -> 4; matrix products, arithmetic and copies ran while one was open for 17% -> 23% of each run, Pallas kernels for 0% -> 0%
where the time goes in v2:
time: 215 us; the launch traced here: 214 us
  waiting for transfers between devices  67 us (31%)
  Pallas kernels  50 us (23%)
  local copies, waits for them, and re-layouts  38.1 us (18%)
  other arithmetic  30.8 us (14%)
  starting transfers between devices  21.2 us (10%)
  blocking collectives  6.29 us (3%)
    ppermute x5, waiting for transfers between devices, passed_along(): return lax.ppermute(x, axis, pairs)  66 us
    pallas_call x1, Pallas kernels, per_device(): pl.pallas_call(scan_kernel, grid=(set_groups, blocks), in_specs=[pl.Block...  34.8 us
    ppermute x5, starting transfers between devices, passed_along(): return lax.ppermute(x, axis, pairs)  20.9 us
    pallas_call x1, Pallas kernels, per_device(): pl.pallas_call(out_kernel, grid=(set_groups, own // out_len), in_specs=[p...  15.3 us
    unnamed x28, local copies, waits for them, and re-layouts  11.7 us
    all_to_all x1, other arithmetic, per_device(): bc_own = lax.all_to_all(bc_conv, 'sub', 3, 2, tiled=True)  8.58 us
    mul x1, other arithmetic, conv_rows(): return jax.nn.silu(total)  6.81 us
    all_to_all x1, blocking collectives, per_device(): bc_own = lax.all_to_all(bc_conv, 'sub', 3, 2, tiled=True)  6.29 us
  transfers between devices with their start and end apart: 7, of which 4 were waited for; matrix products, arithmetic and copies ran while one was open for 23% of the time, Pallas kernels for 0%

profile of v2, /device:TPU:0, one launch (start us, length us, event | category | flops | bytes accessed | tf_op | source)
XLA Modules:
  0.0 214.0 jit_solution(8688274145419812407)
XLA Ops:
  0.0 1.1 slice.78
  1.1 4.9 %collective-permute-start.1 = (bf16[2,4,64,3]{3,2,1,0:T(8,128)(2,1)S(1)}, bf16[2,4,64,3]{3,2,1,0:T(8,128)(2,1)S(1)}, u32[]{:S(2)}, u32[]{:S(2)}) collective-permute-start(bf16[2,4,64,3]{3,2,1,0:T(8,128)(2,1)S(1)} %slice.78), channel_id=1, source_target_pairs={{0,4},{4,8},{8,12},{1,5},{5,9},{9,13},{2,6},{6,10},{10,14},{3,7},{... | collective-permute-start | bytes 9224 | tf_op jit(solution)/shard_map/ppermute | solution.py:21
  6.1 1.5 slice.69
  7.5 4.1 %collective-permute-start = (bf16[3,4096]{1,0:T(4,128)(2,1)}, bf16[3,4096]{1,0:T(4,128)(2,1)}, u32[]{:S(2)}, u32[]{:S(2)}) collective-permute-start(bf16[3,4096]{1,0:T(4,128)(2,1)} %slice.69), channel_id=1, source_target_pairs={{0,4},{4,8},{8,12},{1,5},{5,9},{9,13},{2,6},{6,10},{10,14},{3,7},{... | collective-permute-start | bytes 73736 | tf_op jit(solution)/shard_map/ppermute | solution.py:21
  11.6 1.7 fusion.14
  13.9 1.2 broadcast_multiply_fusion
  16.0 1.4 dynamic-slice_bitcast_fusion.4
  18.3 1.3 copy.67
  21.1 3.2 %divide_multiply_fusion.1 = f32[2,4,64,1024]{3,2,1,0:T(8,128)S(1)} fusion(bf16[2,4,64,1024]{3,2,1,0:T(8,128)(2,1)S(1)} %copy-done.3, bf16[2,4,64,3]{3,2,1,0:T(8,128)(2,1)} %copy-done.6, f32[2,4,64]{2,1,0:T(4,128)} %get-tuple-element.29, f32[2,4,64]{2,1,0:T(4,128)S(1)} %get-tuple-element.27, f32[2,4,64]{2,1,0:T(4,128)S(1)} %get-tuple-element.28, ...), kind=kLoop, calls=%fused_computation.5 | loop fusion | flops 13107200 | bytes 3159040 | tf_op jit(solution)/shard_map/jit(silu)/mul | solution.py:45
  24.3 3.1 %copy.60 = f32[2,4,64,1024]{2,1,0,3:T(4,128)} copy(f32[2,4,64,1024]{3,2,1,0:T(8,128)S(1)} %divide_multiply_fusion.1) | data formatting | bytes 4194304 | tf_op jit(solution)/shard_map/jit(silu)/mul | solution.py:45
  27.4 5.5 %reshape.62 = f32[2,1,262144]{2,1,0:T(1,128)S(1)} reshape(f32[1024,2,4,64]{3,2,1,0:T(4,128)} %bitcast.47) | data formatting | bytes 4194304
  32.9 6.3 %all_to_all.15 = f32[2,1,262144]{2,1,0:T(1,128)} all-to-all(f32[2,1,262144]{2,1,0:T(1,128)S(1)} %reshape.62), channel_id=1, replica_groups=mesh['groups'=2,'ctx'=4,'head'=2,'sub'=2] {'sub'}, dimensions={0} | all-to-all | bytes 4194304 | tf_op jit(solution)/shard_map/all_to_all | solution.py:174
  39.7 8.6 %reduce.6 = f32[2,262144]{1,0:T(2,128)S(1)} reduce(f32[2,1,262144]{2,1,0:T(1,128)} %all_to_all.15, f32[]{:T(128)} %broadcast.13), dimensions={1}, to_apply=%all_to_all.11.reduce_sub_computation | reduce | bytes 4194308 | tf_op jit(solution)/shard_map/all_to_all | solution.py:174
  48.3 5.5 %reshape.63 = f32[1024,2,4,64]{3,2,1,0:T(4,128)} reshape(f32[2,262144]{1,0:T(2,128)S(1)} %reduce.6) | data formatting | bytes 4194304
  53.8 5.4 %copy.71 = f32[2,4,64,2,512]{4,3,2,1,0:T(2,128)S(1)} copy(f32[2,4,64,2,512]{2,1,0,4,3:T(4,128)} %bitcast.48) | data formatting | bytes 4194304 | tf_op jit(solution)/shard_map/all_to_all | solution.py:174
  60.2 1.3 copy.63
  61.5 1.2 copy.64
  62.7 3.6 %fusion = bf16[515,4096]{1,0:T(8,128)(2,1)S(1)} fusion(s32[]{:T(128)S(6)} %select_n.50, bf16[3,4096]{1,0:T(4,128)(2,1)} %collective-permute-done, bf16[1024,4096]{1,0:T(8,128)(2,1)} %param.12), kind=kLoop, calls=%fused_computation.3 | loop fusion | flops 8437760 | bytes 12632068 | tf_op jit(solution)/shard_map/concatenate | solution.py:167
  66.4 6.8 %divide_multiply_fusion.xc_ref = f32[512,4096]{1,0:T(8,128)} fusion(bf16[515,4096]{1,0:T(8,128)(2,1)S(1)} %fusion, f32[4096]{0:T(1024)S(1)} %bitcast.63, f32[4096]{0:T(1024)S(1)} %bitcast.64, f32[4096]{0:T(1024)S(1)} %bitcast.62, f32[4096]{0:T(1024)S(1)} %bitcast.61, f32[4096]{0:T(1024)S(1)} %copy-done.11), kind=kLoop, calls=%fused_computation.2 | loop fusion | flops 33554432 | bytes 25247744 | tf_op jit(solution)/shard_map/jit(silu)/mul | solution.py:35
  73.2 34.8 %shard_map.118 = (f32[512,4096]{1,0:T(8,128)}, f32[4,8,128,128]{3,2,1,0:T(8,128)}) custom-call(f32[512,4096]{1,0:T(8,128)} %divide_multiply_fusion.xc_ref, f32[4,512,128]{2,1,0:T(8,128)} %bitcast.49, f32[4,128,512]{2,1,0:T(8,128)} %bitcast.54, f32[4,16,512]{2,1,0:T(8,128)} %copy-done.4, f32[4,512,16]{2,1,0:T(8,128)} %bitcast.53, f32[4,16,512]{2,1,0:T(8,128)} %bitcast.59, ...), custom_call_target="tpu_custom_call" | custom-call | tf_op jit(solution)/shard_map/pallas_call | solution.py:200
  107.9 1.5 dynamic-slice_bitcast_fusion
  112.5 1.6 broadcast_add_fusion
  114.1 3.0 %collective-permute-start.3 = (f32[4,8,64,128]{3,2,1,0:T(8,128)S(1)}, f32[4,8,64,128]{3,2,1,0:T(8,128)S(1)}, u32[]{:S(2)}, u32[]{:S(2)}) collective-permute-start(f32[4,8,64,128]{3,2,1,0:T(8,128)S(1)} %get-tuple-element.11), channel_id=1, source_target_pairs={{0,4},{4,8},{8,12},{1,5},{5,9},{9,13},{2,6},{6,10},{10,14},{3,7},{... | collective-permute-start | bytes 3145736 | tf_op jit(solution)/shard_map/ppermute | solution.py:21
  117.0 22.9 %collective-permute-done.3 = f32[4,8,64,128]{3,2,1,0:T(8,128)S(1)} collective-permute-done((f32[4,8,64,128]{3,2,1,0:T(8,128)S(1)}, f32[4,8,64,128]{3,2,1,0:T(8,128)S(1)}, u32[]{:S(2)}, u32[]{:S(2)}) %collective-permute-start.3) | collective-permute-done | bytes 1048608 | tf_op jit(solution)/shard_map/ppermute | solution.py:21
  140.1 4.5 %collective-permute-start.4 = (f32[4,8,64,128]{3,2,1,0:T(8,128)S(1)}, f32[4,8,64,128]{3,2,1,0:T(8,128)S(1)}, u32[]{:S(2)}, u32[]{:S(2)}) collective-permute-start(f32[4,8,64,128]{3,2,1,0:T(8,128)S(1)} %multiply_add_fusion.2), channel_id=1, source_target_pairs={{0,4},{4,8},{8,12},{1,5},{5,9},{9,13},{2,6},{6,10},{10,14},{3,7},{... | collective-permute-start | bytes 3145736 | tf_op jit(solution)/shard_map/ppermute | solution.py:21
  144.6 22.0 %collective-permute-done.4 = f32[4,8,64,128]{3,2,1,0:T(8,128)S(1)} collective-permute-done((f32[4,8,64,128]{3,2,1,0:T(8,128)S(1)}, f32[4,8,64,128]{3,2,1,0:T(8,128)S(1)}, u32[]{:S(2)}, u32[]{:S(2)}) %collective-permute-start.4) | collective-permute-done | bytes 1048608 | tf_op jit(solution)/shard_map/ppermute | solution.py:21
  166.8 4.5 %collective-permute-start.5 = (f32[4,8,64,128]{3,2,1,0:T(8,128)S(1)}, f32[4,8,64,128]{3,2,1,0:T(8,128)S(1)}, u32[]{:S(2)}, u32[]{:S(2)}) collective-permute-start(f32[4,8,64,128]{3,2,1,0:T(8,128)S(1)} %multiply_add_fusion.1), channel_id=1, source_target_pairs={{0,4},{4,8},{8,12},{1,5},{5,9},{9,13},{2,6},{6,10},{10,14},{3,7},{... | collective-permute-start | bytes 3145736 | tf_op jit(solution)/shard_map/ppermute | solution.py:21
  171.3 21.1 %collective-permute-done.5 = f32[4,8,64,128]{3,2,1,0:T(8,128)S(1)} collective-permute-done((f32[4,8,64,128]{3,2,1,0:T(8,128)S(1)}, f32[4,8,64,128]{3,2,1,0:T(8,128)S(1)}, u32[]{:S(2)}, u32[]{:S(2)}) %collective-permute-start.5) | collective-permute-done | bytes 1048608 | tf_op jit(solution)/shard_map/ppermute | solution.py:21
  193.3 1.3 copy.69
  195.6 1.6 select_bitcast_fusion.1
  197.2 1.5 pad_maximum_fusion
  198.7 15.3 %shard_map.119 = bf16[512,4096]{1,0:T(8,128)(2,1)} custom-call(f32[512,4096]{1,0:T(8,128)} %get-tuple-element.7.y_ref, f32[4,512,128]{2,1,0:T(8,128)} %bitcast.50, f32[4,512,16]{2,1,0:T(8,128)} %bitcast.55, f32[4,8,128,128]{3,2,1,0:T(8,128)} %bitcast.51, bf16[512,4096]{1,0:T(8,128)(2,1)} %z_ref.1, f32[1,4096]{1,0:T(1,128)} %bitcast.65), custom_call_target="tpu_custom_call" | custom-call | tf_op jit(solution)/shard_map/pallas_call | solution.py:245
  (62 shorter events, 10.5 us)
Async XLA Ops:
  0.0 17.4 %copy-start = (f32[2,4,128]{2,1,0:T(4,128)S(1)}, f32[2,4,128]{2,1,0:T(4,128)}, u32[]{:S(2)}) copy-start(f32[2,4,128]{2,1,0:T(4,128)} %param.19) | copy-start | bytes 12292
  0.0 21.1 %copy-start.3 = (bf16[2,4,64,1024]{3,2,1,0:T(8,128)(2,1)S(1)}, bf16[2,4,64,1024]{3,2,1,0:T(8,128)(2,1)}, u32[]{:S(2)}) copy-start(bf16[2,4,64,1024]{3,2,1,0:T(8,128)(2,1)} %param.13) | copy-start | bytes 3145732
  0.0 19.7 %copy-start.12 = (f32[64]{0:T(128)S(1)}, f32[64]{0:T(128)}, u32[]{:S(2)}) copy-start(f32[64]{0:T(128)} %param.22) | copy-start | bytes 772
  1.1 19.3 %collective-permute-start.1 = (bf16[2,4,64,3]{3,2,1,0:T(8,128)(2,1)S(1)}, bf16[2,4,64,3]{3,2,1,0:T(8,128)(2,1)S(1)}, u32[]{:S(2)}, u32[]{:S(2)}) collective-permute-start(bf16[2,4,64,3]{3,2,1,0:T(8,128)(2,1)S(1)} %slice.78), channel_id=1, source_target_pairs={{0,4},{4,8},{8,12},{1,5},{5,9},{9,13},{2,6},{6,10},{10,14},{3,7},{... | collective-permute-start | bytes 9224 | tf_op jit(solution)/shard_map/ppermute | solution.py:21
  7.5 55.2 %collective-permute-start = (bf16[3,4096]{1,0:T(4,128)(2,1)}, bf16[3,4096]{1,0:T(4,128)(2,1)}, u32[]{:S(2)}, u32[]{:S(2)}) collective-permute-start(bf16[3,4096]{1,0:T(4,128)(2,1)} %slice.69), channel_id=1, source_target_pairs={{0,4},{4,8},{8,12},{1,5},{5,9},{9,13},{2,6},{6,10},{10,14},{3,7},{... | collective-permute-start | bytes 73736 | tf_op jit(solution)/shard_map/ppermute | solution.py:21
  18.3 2.1 copy-start.4
  20.4 0.7 copy-start.6
  62.7 3.6 %copy-start.7 = (f32[1,4096]{1,0:T(1,128)S(1)}, f32[1,4096]{1,0:T(1,128)}, u32[]{:S(2)}) copy-start(f32[1,4096]{1,0:T(1,128)} %get-tuple-element.22) | copy-start | bytes 49156
  62.7 3.6 %copy-start.8 = (f32[1,4096]{1,0:T(1,128)S(1)}, f32[1,4096]{1,0:T(1,128)}, u32[]{:S(2)}) copy-start(f32[1,4096]{1,0:T(1,128)} %get-tuple-element.23) | copy-start | bytes 49156
  62.7 3.6 %copy-start.9 = (f32[1,4096]{1,0:T(1,128)S(1)}, f32[1,4096]{1,0:T(1,128)}, u32[]{:S(2)}) copy-start(f32[1,4096]{1,0:T(1,128)} %get-tuple-element.24) | copy-start | bytes 49156
  62.7 3.7 %copy-start.10 = (f32[1,4096]{1,0:T(1,128)S(1)}, f32[1,4096]{1,0:T(1,128)}, u32[]{:S(2)}) copy-start(f32[1,4096]{1,0:T(1,128)} %get-tuple-element.25) | copy-start | bytes 49156
  62.7 3.7 %copy-start.11 = (f32[4096]{0:T(1024)S(1)}, f32[4096]{0:T(1024)}, u32[]{:S(2)}) copy-start(f32[4096]{0:T(1024)} %param.17) | copy-start | bytes 49156
  107.9 4.5 %copy-start.2 = (f32[4,8,128,128]{3,2,1,0:T(8,128)S(1)}, f32[4,8,128,128]{3,2,1,0:T(8,128)}, u32[]{:S(2)}) copy-start(f32[4,8,128,128]{3,2,1,0:T(8,128)} %get-tuple-element.8) | copy-start | bytes 6291460
  109.4 3.0 %collective-permute-start.2 = (f32[4,8,64,128]{3,2,1,0:T(8,128)S(1)}, f32[4,8,64,128]{3,2,1,0:T(8,128)}, u32[]{:S(2)}, u32[]{:S(2)}) collective-permute-start(f32[4,8,64,128]{3,2,1,0:T(8,128)S(1)} %dynamic-slice_bitcast_fusion), channel_id=1, source_target_pairs={{0,1},{1,0},{2,3},{3,2},{4,5},{5,4},{6,7},{7,6},{8,9},{9,8},{10,11... | collective-permute-start | bytes 3145736 | tf_op jit(solution)/shard_map/ppermute | solution.py:25
  112.1 80.3 %copy-start.5 = (f32[4,8,128]{2,1,0:T(8,128)}, f32[4,8,128]{2,1,0:T(8,128)S(1)}, u32[]{:S(2)}) copy-start(f32[4,8,128]{2,1,0:T(8,128)S(1)} %broadcast_in_dim_reshape.8) | copy-start | bytes 49156
  114.1 25.8 %collective-permute-start.3 = (f32[4,8,64,128]{3,2,1,0:T(8,128)S(1)}, f32[4,8,64,128]{3,2,1,0:T(8,128)S(1)}, u32[]{:S(2)}, u32[]{:S(2)}) collective-permute-start(f32[4,8,64,128]{3,2,1,0:T(8,128)S(1)} %get-tuple-element.11), channel_id=1, source_target_pairs={{0,4},{4,8},{8,12},{1,5},{5,9},{9,13},{2,6},{6,10},{10,14},{3,7},{... | collective-permute-start | bytes 3145736 | tf_op jit(solution)/shard_map/ppermute | solution.py:21
  140.1 26.5 %collective-permute-start.4 = (f32[4,8,64,128]{3,2,1,0:T(8,128)S(1)}, f32[4,8,64,128]{3,2,1,0:T(8,128)S(1)}, u32[]{:S(2)}, u32[]{:S(2)}) collective-permute-start(f32[4,8,64,128]{3,2,1,0:T(8,128)S(1)} %multiply_add_fusion.2), channel_id=1, source_target_pairs={{0,4},{4,8},{8,12},{1,5},{5,9},{9,13},{2,6},{6,10},{10,14},{3,7},{... | collective-permute-start | bytes 3145736 | tf_op jit(solution)/shard_map/ppermute | solution.py:21
  166.8 25.6 %collective-permute-start.5 = (f32[4,8,64,128]{3,2,1,0:T(8,128)S(1)}, f32[4,8,64,128]{3,2,1,0:T(8,128)S(1)}, u32[]{:S(2)}, u32[]{:S(2)}) collective-permute-start(f32[4,8,64,128]{3,2,1,0:T(8,128)S(1)} %multiply_add_fusion.1), channel_id=1, source_target_pairs={{0,4},{4,8},{8,12},{1,5},{5,9},{9,13},{2,6},{6,10},{10,14},{3,7},{... | collective-permute-start | bytes 3145736 | tf_op jit(solution)/shard_map/ppermute | solution.py:21
  192.7 2.9 %collective-permute-start.6 = (f32[4,8,64,128]{3,2,1,0:T(8,128)S(1)}, f32[4,8,64,128]{3,2,1,0:T(8,128)}, u32[]{:S(2)}, u32[]{:S(2)}) collective-permute-start(f32[4,8,64,128]{3,2,1,0:T(8,128)S(1)} %fusion.4), channel_id=1, source_target_pairs={{0,1},{1,0},{2,3},{3,2},{4,5},{5,4},{6,7},{7,6},{8,9},{9,8},{10,11... | collective-permute-start | bytes 3145736 | tf_op jit(solution)/shard_map/ppermute | solution.py:25
  198.7 15.3 %copy-start.1 = (f32[2,4,128]{2,1,0:T(4,128)S(1)}, f32[2,4,128]{2,1,0:T(4,128)}, u32[]{:S(2)}) copy-start(f32[2,4,128]{2,1,0:T(4,128)} %param.19) | copy-start | bytes 12292

commit v3 on v2

--- a/solution.py
+++ b/solution.py
@@ -73,7 +73,7 @@
 def scan_kernel(xc_ref, ct_ref, b_ref, cumr_ref, cumc_ref, stp_ref, dsk_ref, y_ref, e_ref):
     chunk = pl.program_id(1)
     block_len = xc_ref.shape[0]
-    pairs = e_ref.shape[1]
+    pairs = e_ref.shape[0]
     heads = 2 * pairs
 
     @pl.when(chunk == 0)
@@ -94,7 +94,7 @@
         lanes = slice(pair * 128, (pair + 1) * 128)
         xp = xc_ref[:, lanes]
         xs = split(xp)
-        s_old = e_ref[0, pair]
+        s_old = e_ref[pair]
         ys = []
         us = []
         for side in range(2):
@@ -110,9 +110,22 @@
         inflow = dot3(ct, split(s_old)) * jnp.exp(cq)
         y = jnp.where(left, ys[0], ys[1]) + inflow
         y_ref[:, lanes] = y + xp * dsk_ref[:, lanes]
-        e_ref[0, pair] = jnp.exp(cq[block_len - 1 : block_len, :]) * s_old + jnp.where(
+        e_ref[pair] = jnp.exp(cq[block_len - 1 : block_len, :]) * s_old + jnp.where(
             left, us[0], us[1]
         )
+
+
+def end_kernel(xc_ref, b_ref, wk_ref, e_ref):
+    pairs = e_ref.shape[1]
+    bm = b_ref[0]
+    wk = wk_ref[0]
+    left = lax.broadcasted_iota(jnp.int32, (1, 128), 1) < HEAD_DIM
+    for pair in range(pairs):
+        xs = split(xc_ref[:, pair * 128 : (pair + 1) * 128])
+        us = [
+            dot3(split(bm * wk[2 * pair + side : 2 * pair + side + 1, :]), xs) for side in range(2)
+        ]
+        e_ref[0, pair] = jnp.where(left, us[0], us[1])
 
 
 def out_kernel(y_ref, ct_ref, cumc_ref, v_ref, z_ref, nw_ref, o_ref, g_ref):
@@ -171,7 +184,18 @@
     bc_weights = lax.dynamic_slice_in_dim(conv_bc_w, sub_index * half, half, 3)
     bc_bias = lax.dynamic_slice_in_dim(conv_bc_b, sub_index * half, half, 2)
     bc_conv = conv_cols(jnp.concatenate([bc_rim, bc_raw], 3), bc_weights, bc_bias)
-    bc_own = lax.all_to_all(bc_conv, "sub", 3, 2, tiled=True)
+    bc_halves = bc_conv.reshape(2, set_groups, half, nsub, own)
+    bc_mine = lax.dynamic_index_in_dim(bc_halves, sub_index, 3, keepdims=False)
+    bc_theirs = swapped(
+        lax.dynamic_index_in_dim(bc_halves, 1 - sub_index, 3, keepdims=False), "sub"
+    )
+    bc_own = jnp.stack(
+        [
+            jnp.where(sub_index == 0, bc_mine, bc_theirs),
+            jnp.where(sub_index == 0, bc_theirs, bc_mine),
+        ],
+        2,
+    ).reshape(2, set_groups, state, own)
     b_rows = bc_own[0]
     c_cols = bc_own[1].transpose(0, 2, 1)
 
@@ -197,7 +221,35 @@
     step_rows = step_own.reshape(set_groups, per_group, own)
     skip_row = jnp.repeat(d_skip, HEAD_DIM)[None, :]
 
-    y_local, end_state = pl.pallas_call(
+    to_end = jnp.exp(cum_device[..., own - 1 :] - cum_device) * step_rows
+    end_state = pl.pallas_call(
+        end_kernel,
+        grid=(set_groups,),
+        in_specs=[
+            pl.BlockSpec((own, group_width), lambda g: (0, g)),
+            pl.BlockSpec((1, state, own), lambda g: (g, 0, 0)),
+            pl.BlockSpec((1, per_group, own), lambda g: (g, 0, 0)),
+        ],
+        out_specs=pl.BlockSpec((1, pairs, state, 128), lambda g: (g, 0, 0, 0)),
+        out_shape=jax.ShapeDtypeStruct((set_groups, pairs, state, 128), F32),
+    )(x_own, b_rows, to_end)
+
+    def pair_layout(values):
+        return jnp.repeat(values.reshape(set_groups, pairs, 2), HEAD_DIM, axis=-1)[:, :, None, :]
+
+    decay_first = pair_layout(half_totals[:, 0])
+    decay_second = pair_layout(half_totals[:, 1])
+    halves = end_state.reshape(set_groups, pairs, nsub, half, 128)
+    mine = lax.dynamic_index_in_dim(halves, sub_index, 2, keepdims=False)
+    theirs = swapped(lax.dynamic_index_in_dim(halves, 1 - sub_index, 2, keepdims=False), "sub")
+    first_end = jnp.where(sub_index == 0, mine, theirs)
+    second_end = jnp.where(sub_index == 0, theirs, mine)
+    chip_end = decay_second * first_end + second_end
+    chip_decay = decay_first * decay_second
+    ctx_index = lax.axis_index("ctx")
+    packed = jnp.concatenate([chip_end, chip_decay], 2)
+    packed, x_held = lax.optimization_barrier((packed, x_own))
+    y_local = pl.pallas_call(
         scan_kernel,
         grid=(set_groups, blocks),
         in_specs=[
@@ -209,31 +261,20 @@
             pl.BlockSpec((1, per_group, block_len), lambda g, c: (g, 0, c)),
             pl.BlockSpec((1, group_width), lambda g, c: (0, g)),
         ],
-        out_specs=[
-            pl.BlockSpec((block_len, group_width), lambda g, c: (c, g)),
-            pl.BlockSpec((1, pairs, state, 128), lambda g, c: (g, 0, 0, 0)),
-        ],
-        out_shape=[
-            jax.ShapeDtypeStruct((own, channels), F32),
-            jax.ShapeDtypeStruct((set_groups, pairs, state, 128), F32),
-        ],
-    )(x_own, c_cols, b_rows, cum_rows, cum_cols, step_rows, skip_row)
-
-    def pair_layout(values):
-        return jnp.repeat(values.reshape(set_groups, pairs, 2), HEAD_DIM, axis=-1)[:, :, None, :]
-
-    decay_first = pair_layout(half_totals[:, 0])
-    decay_second = pair_layout(half_totals[:, 1])
-    halves = end_state.reshape(set_groups, pairs, nsub, half, 128)
-    mine = lax.dynamic_index_in_dim(halves, sub_index, 2, keepdims=False)
-    theirs = swapped(lax.dynamic_index_in_dim(halves, 1 - sub_index, 2, keepdims=False), "sub")
-    first_end = jnp.where(sub_index == 0, mine, theirs)
-    second_end = jnp.where(sub_index == 0, theirs, mine)
-    chip_end = decay_second * first_end + second_end
-    chip_decay = decay_first * decay_second
+        out_specs=pl.BlockSpec((block_len, group_width), lambda g, c: (c, g)),
+        out_shape=jax.ShapeDtypeStruct((own, channels), F32),
+        scratch_shapes=[pltpu.VMEM((pairs, state, 128), F32)],
+    )(x_held, c_cols, b_rows, cum_rows, cum_cols, step_rows, skip_row)
+
+    gathered = lax.all_gather(packed, "ctx")
+    gathered, y_local = lax.optimization_barrier((gathered, y_local))
+    all_ends = gathered[:, :, :, :half]
+    all_decays = gathered[:, :, :, half:]
     carried = jnp.zeros_like(chip_end)
-    for _ in range(lax.axis_size("ctx") - 1):
-        carried = passed_along(chip_end + chip_decay * carried, "ctx", 1)
+    for earlier in range(lax.axis_size("ctx") - 1):
+        carried = jnp.where(
+            earlier < ctx_index, all_ends[earlier] + all_decays[earlier] * carried, carried
+        )
     into_second = decay_first * carried + first_end
     keep = jnp.where(sub_index == 0, carried, into_second)
     got = swapped(jnp.where(sub_index == 0, into_second, carried), "sub")

time: 215 us -> 181 us (0.84)
  waiting for transfers between devices: 67 us -> 42.9 us
  between operations: 0.35 us -> 13.8 us
  local copies, waits for them, and re-layouts: 38.1 us -> 25.4 us
  starting transfers between devices: 21.2 us -> 9.57 us
  Pallas kernels: 50 us -> 60.7 us
  blocking collectives: 6.29 us -> 0 us
  other arithmetic: 30.8 us -> 28.2 us
    ppermute x5 -> x2, waiting for transfers between devices: 66 us -> 0.01 us  [passed_along(): return lax.ppermute(x, axis, pairs)]
    all_gather x0 -> x1, waiting for transfers between devices: none -> 41.3 us  [per_device(): gathered = lax.all_gather(packed, 'ctx')]
    ppermute x5 -> x2, starting transfers between devices: 20.9 us -> 9.01 us  [passed_along(): return lax.ppermute(x, axis, pairs)]
    unnamed x28 -> x35, local copies, waits for them, and re-layouts: 11.7 us -> 0.81 us
    pallas_call x0 -> x1, Pallas kernels: none -> 10.6 us  [per_device(): pl.pallas_call(end_kernel, grid=(set_groups,), in_specs=[pl.BlockSpec((ow...]
    all_to_all x1 -> x0, other arithmetic: 8.58 us -> none  [per_device(): bc_own = lax.all_to_all(bc_conv, 'sub', 3, 2, tiled=True)]
    dynamic_slice x1 -> x3, local copies, waits for them, and re-layouts: 0.02 us -> 7.64 us  [the longest x1 4.38 us: per_device(): bc_mine = lax.dynamic_index_in_dim(bc_halves, sub_index, 3, keepdims=False)]
    all_to_all x1 -> x0, blocking collectives: 6.29 us -> none  [per_device(): bc_own = lax.all_to_all(bc_conv, 'sub', 3, 2, tiled=True)]
  transfers between devices with their start and end apart: 7 -> 6, of which waited for: 4 -> 2; matrix products, arithmetic and copies ran while one was open for 23% -> 20% of each run, Pallas kernels for 0% -> 19%
where the time goes in v3:
time: 181 us
  Pallas kernels  60.7 us (34%)
  waiting for transfers between devices  42.9 us (24%)
  other arithmetic  28.2 us (16%)
  local copies, waits for them, and re-layouts  25.4 us (14%)
  between operations  13.8 us (8%)
  starting transfers between devices  9.57 us (5%)
    all_gather x1, waiting for transfers between devices, per_device(): gathered = lax.all_gather(packed, 'ctx')  41.3 us
    pallas_call x1, Pallas kernels, per_device(): pl.pallas_call(scan_kernel, grid=(set_groups, blocks), in_specs=[pl.Block...  34.8 us
    pallas_call x1, Pallas kernels, per_device(): pl.pallas_call(out_kernel, grid=(set_groups, own // out_len), in_specs=[p...  15.3 us
    pallas_call x1, Pallas kernels, per_device(): pl.pallas_call(end_kernel, grid=(set_groups,), in_specs=[pl.BlockSpec((ow...  10.6 us
    ppermute x2, starting transfers between devices, passed_along(): return lax.ppermute(x, axis, pairs)  9.01 us
    mul x1, other arithmetic, conv_rows(): return jax.nn.silu(total)  6.82 us
    dynamic_slice x1, local copies, waits for them, and re-layouts, per_device(): bc_mine = lax.dynamic_index_in_dim(bc_halves, sub_index, 3, keepdims=False)  4.38 us
    select_n x1, other arithmetic, per_device(): got = swapped(jnp.where(sub_index == 0, into_second, carried), 'sub')  4.29 us
  transfers between devices with their start and end apart: 6, of which 2 were waited for; matrix products, arithmetic and copies ran while one was open for 20% of the time, Pallas kernels for 19%

profile of v3, /device:TPU:0, one launch (start us, length us, event | category | flops | bytes accessed | tf_op | source)
XLA Modules:
  0.0 180.7 jit_solution(2813595899803595267)
XLA Ops:
  6.6 1.1 slice.108
  7.7 4.9 %collective-permute-start.1 = (bf16[2,4,64,3]{3,2,1,0:T(8,128)(2,1)S(1)}, bf16[2,4,64,3]{3,2,1,0:T(8,128)(2,1)S(1)}, u32[]{:S(2)}, u32[]{:S(2)}) collective-permute-start(bf16[2,4,64,3]{3,2,1,0:T(8,128)(2,1)S(1)} %slice.108), channel_id=1, source_target_pairs={{0,4},{4,8},{8,12},{1,5},{5,9},{9,13},{2,6},{6,10},{10,14},{3,7},{... | collective-permute-start | bytes 9224 | tf_op jit(solution)/shard_map/ppermute | solution.py:21
  12.6 1.5 slice.99
  14.1 4.1 %collective-permute-start = (bf16[3,4096]{1,0:T(4,128)(2,1)}, bf16[3,4096]{1,0:T(4,128)(2,1)}, u32[]{:S(2)}, u32[]{:S(2)}) collective-permute-start(bf16[3,4096]{1,0:T(4,128)(2,1)} %slice.99), channel_id=1, source_target_pairs={{0,4},{4,8},{8,12},{1,5},{5,9},{9,13},{2,6},{6,10},{10,14},{3,7},{... | collective-permute-start | bytes 73736 | tf_op jit(solution)/shard_map/ppermute | solution.py:21
  18.8 1.2 broadcast_multiply_fusion
  21.6 0.7 exponential_multiply_fusion.wk_ref
  22.4 0.7 dynamic-slice_bitcast_fusion.3
  24.4 3.2 %divide_multiply_fusion.1 = f32[2,4,64,1024]{3,2,1,0:T(8,128)S(1)} fusion(bf16[2,4,64,1024]{3,2,1,0:T(8,128)(2,1)S(1)} %copy-done.4, bf16[2,4,64,3]{3,2,1,0:T(8,128)(2,1)} %copy-done.8, f32[2,4,64]{2,1,0:T(4,128)} %get-tuple-element.39, f32[2,4,64]{2,1,0:T(4,128)S(1)} %get-tuple-element.37, f32[2,4,64]{2,1,0:T(4,128)S(1)} %get-tuple-element.38, ...), kind=kLoop, calls=%fused_computation.7 | loop fusion | flops 13107200 | bytes 3159040 | tf_op jit(solution)/shard_map/jit(silu)/mul | solution.py:45
  27.6 2.8 %reshape.70 = f32[2,4,64,2,512]{4,3,2,1,0:T(2,128)} reshape(f32[2,4,64,1024]{3,2,1,0:T(8,128)S(1)} %divide_multiply_fusion.1) | data formatting | bytes 4194304 | tf_op jit(solution)/shard_map/reshape | solution.py:187
  30.3 4.4 %constant_dynamic-slice_fusion.5 = (f32[2,4,64,1,512]{4,3,2,1,0:T(1,128)S(1)}, f32[2,4,64,1,512]{4,3,2,1,0:T(1,128)S(1)}) fusion(f32[2,4,64,2,512]{4,3,2,1,0:T(2,128)} %reshape.70, s32[]{:T(128)S(6)} %select_n.88, s32[]{:T(128)S(6)} %select_n.89), kind=kLoop, calls=%fused_computation.63 | loop fusion | bytes 4194312 | tf_op jit(solution)/shard_map/jit(dynamic_index_in_dim)/dynamic_slice | solution.py:188
  35.0 3.6 %fusion = bf16[515,4096]{1,0:T(8,128)(2,1)S(1)} fusion(s32[]{:T(128)S(6)} %select_n.85, bf16[3,4096]{1,0:T(4,128)(2,1)} %collective-permute-done, bf16[1024,4096]{1,0:T(8,128)(2,1)} %param.12), kind=kLoop, calls=%fused_computation.3 | loop fusion | flops 8437760 | bytes 12632068 | tf_op jit(solution)/shard_map/concatenate | solution.py:180
  38.6 6.8 %divide_multiply_fusion.xc_ref = f32[512,4096]{1,0:T(8,128)} fusion(bf16[515,4096]{1,0:T(8,128)(2,1)S(1)} %fusion, f32[4096]{0:T(1024)S(1)} %bitcast.107, f32[4096]{0:T(1024)S(1)} %bitcast.108, f32[4096]{0:T(1024)S(1)} %bitcast.106, f32[4096]{0:T(1024)S(1)} %bitcast.105, f32[4096]{0:T(1024)S(1)} %copy-done.15), kind=kLoop, calls=%fused_computation.2 | loop fusion | flops 33554432 | bytes 25247744 | tf_op jit(solution)/shard_map/jit(silu)/mul | solution.py:35
  45.7 1.2 pad_maximum_fusion.2
  46.9 10.6 %shard_map.118 = f32[4,8,128,128]{3,2,1,0:T(8,128)} custom-call(f32[512,4096]{1,0:T(8,128)} %divide_multiply_fusion.xc_ref, f32[4,128,512]{2,1,0:T(8,128)} %bitcast.92, f32[4,16,512]{2,1,0:T(8,128)} %exponential_multiply_fusion.wk_ref), custom_call_target="tpu_custom_call" | custom-call | tf_op jit(solution)/shard_map/pallas_call | solution.py:225
  57.5 1.7 constant_dynamic-slice_fusion.1
  59.2 1.6 copy.77
  61.3 0.9 reshape.69
  62.2 1.1 reduce_sum.9
  64.8 1.0 pad_maximum_fusion.1
  66.1 1.3 copy.50
  67.5 0.7 broadcast_in_dim_reshape.2.dsk_ref
  68.2 0.8 broadcast_in_dim.29
  69.1 1.3 copy.48
  70.4 34.8 %shard_map.119.y_ref = f32[512,4096]{1,0:T(8,128)} custom-call(f32[512,4096]{1,0:T(8,128)} %divide_multiply_fusion.xc_ref, f32[4,512,128]{2,1,0:T(8,128)} %bitcast.90, f32[4,128,512]{2,1,0:T(8,128)} %bitcast.93, f32[4,16,512]{2,1,0:T(8,128)} %copy-done.6, f32[4,512,16]{2,1,0:T(8,128)} %bitcast.97, f32[4,16,512]{2,1,0:T(8,128)} %bitcast.102, ...), custom_call_target="tpu_custom_call" | custom-call | tf_op jit(solution)/shard_map/pallas_call | solution.py:252
  105.2 41.3 %all-gather.3.cloned.1.call-done = f32[16,8,65,128]{3,1,2,0:T(8,128)} async-done(((f32[4,8,65,128]{3,1,2,0:T(8,128)}), f32[16,8,65,128]{3,1,2,0:T(8,128)}) %all-gather.3.cloned.1.call-update) | async-done | bytes 4259856 | tf_op jit(solution)/shard_map/all_gather | solution.py:269
  146.5 0.8 slice_bitcast_fusion.1
  147.2 4.3 %fusion.8 = (f32[4,8,64,128]{3,1,2,0:T(8,128)}, f32[4,8,64,128]{3,1,2,0:T(8,128)}) fusion(f32[4,8,64,128]{3,1,2,0:T(8,128)S(1)} %collective-permute-done.3, f32[4,8,1,64,128]{4,3,2,1,0:T(8,128)S(1)} %get-tuple-element.26, f32[4,8,128]{2,1,0:T(8,128)S(1)} %mul.220, pred[]{:T(512)S(6)} %eq.2, f32[4,8,128]{2,1,0:T(8,128)S(1)} %get-tuple-element.23, ...), kind=kLoop, calls=%fused_computation.34 | loop fusion | flops 3145728 | bytes 7405572 | tf_op jit(solution)/shard_map/jit(_where)/select_n | solution.py:280
  151.5 1.3 copy.51
  152.9 1.5 collective-permute-done.4
  154.4 2.1 %select_bitcast_fusion.1 = (f32[4,8,1,64,128]{4,1,3,0,2:T(8,128)S(1)}, f32[4,8,64,128]{3,1,2,0:T(8,128)S(1)}) fusion(f32[4,8,64,128]{3,1,2,0:T(8,128)S(1)} %collective-permute-done.4, pred[]{:T(512)S(6)} %eq.2, f32[4,8,64,128]{3,1,2,0:T(8,128)} %get-tuple-element.18, f32[4,8,64,128]{3,1,2,0:T(8,128)S(1)} %collective-permute-done.3, ...), kind=kLoop, calls=%fused_computation.32 | loop fusion | flops 1310720 | bytes 6307841 | tf_op jit(solution)/shard_map/stack | solution.py:283
  156.8 1.7 copy.52
  158.6 15.3 %shard_map.120 = bf16[512,4096]{1,0:T(8,128)(2,1)} custom-call(f32[512,4096]{1,0:T(8,128)} %shard_map.119.y_ref, f32[4,512,128]{2,1,0:T(8,128)} %bitcast.91, f32[4,512,16]{2,1,0:T(8,128)} %bitcast.96, f32[4,8,128,128]{3,2,1,0:T(8,128)} %bitcast.94, bf16[512,4096]{1,0:T(8,128)(2,1)} %z_ref.1, f32[1,4096]{1,0:T(1,128)} %bitcast.109), custom_call_target="tpu_custom_call" | custom-call | tf_op jit(solution)/shard_map/pallas_call | solution.py:286
  (71 shorter events, 6.7 us)
Async XLA Ops:
  6.5 16.5 %copy-start = (f32[2,4,128]{2,1,0:T(4,128)S(1)}, f32[2,4,128]{2,1,0:T(4,128)}, u32[]{:S(2)}) copy-start(f32[2,4,128]{2,1,0:T(4,128)} %param.19) | copy-start | bytes 12292
  6.5 17.8 %copy-start.4 = (bf16[2,4,64,1024]{3,2,1,0:T(8,128)(2,1)S(1)}, bf16[2,4,64,1024]{3,2,1,0:T(8,128)(2,1)}, u32[]{:S(2)}) copy-start(bf16[2,4,64,1024]{3,2,1,0:T(8,128)(2,1)} %param.13) | copy-start | bytes 3145732
  6.5 14.4 %copy-start.9 = (f32[4,4096]{1,0:T(4,128)S(1)}, f32[4,4096]{1,0:T(4,128)}, u32[]{:S(2)}) copy-start(f32[4,4096]{1,0:T(4,128)} %param.16) | copy-start | bytes 196612
  6.5 15.8 %copy-start.14 = (f32[4,2,4,128]{3,2,1,0:T(4,128)S(1)}, f32[4,2,4,128]{3,2,1,0:T(4,128)}, u32[]{:S(2)}) copy-start(f32[4,2,4,128]{3,2,1,0:T(4,128)} %param.18) | copy-start | bytes 49156
  6.5 139.9 %all-gather.3.cloned.1.call-start = ((), (), s32[]{:S(2)}) async-start(), calls=%async_computation | async-start | bytes 5324800 | tf_op jit(solution)/shard_map/all_gather | solution.py:269
  7.7 16.0 %collective-permute-start.1 = (bf16[2,4,64,3]{3,2,1,0:T(8,128)(2,1)S(1)}, bf16[2,4,64,3]{3,2,1,0:T(8,128)(2,1)S(1)}, u32[]{:S(2)}, u32[]{:S(2)}) collective-permute-start(bf16[2,4,64,3]{3,2,1,0:T(8,128)(2,1)S(1)} %slice.108), channel_id=1, source_target_pairs={{0,4},{4,8},{8,12},{1,5},{5,9},{9,13},{2,6},{6,10},{10,14},{3,7},{... | collective-permute-start | bytes 9224 | tf_op jit(solution)/shard_map/ppermute | solution.py:21
  14.1 20.9 %collective-permute-start = (bf16[3,4096]{1,0:T(4,128)(2,1)}, bf16[3,4096]{1,0:T(4,128)(2,1)}, u32[]{:S(2)}, u32[]{:S(2)}) collective-permute-start(bf16[3,4096]{1,0:T(4,128)(2,1)} %slice.99), channel_id=1, source_target_pairs={{0,4},{4,8},{8,12},{1,5},{5,9},{9,13},{2,6},{6,10},{10,14},{3,7},{... | collective-permute-start | bytes 73736 | tf_op jit(solution)/shard_map/ppermute | solution.py:21
  20.0 3.7 %copy-start.5 = (f32[64,512]{1,0:T(8,128)}, f32[64,512]{1,0:T(8,128)S(1)}, u32[]{:S(2)}) copy-start(f32[64,512]{1,0:T(8,128)S(1)} %get-tuple-element.40) | copy-start | bytes 393220
  20.8 2.9 %copy-start.2 = (f32[4,16,512]{2,1,0:T(8,128)}, f32[4,16,512]{2,1,0:T(8,128)S(1)}, u32[]{:S(2)}) copy-start(f32[4,16,512]{2,1,0:T(8,128)S(1)} %reshape.72) | copy-start | bytes 393220
  23.7 0.7 copy-start.8
  34.8 3.7 %copy-start.10 = (f32[1,4096]{1,0:T(1,128)S(1)}, f32[1,4096]{1,0:T(1,128)}, u32[]{:S(2)}) copy-start(f32[1,4096]{1,0:T(1,128)} %get-tuple-element.32) | copy-start | bytes 49156
  34.8 3.7 %copy-start.11 = (f32[1,4096]{1,0:T(1,128)S(1)}, f32[1,4096]{1,0:T(1,128)}, u32[]{:S(2)}) copy-start(f32[1,4096]{1,0:T(1,128)} %get-tuple-element.33) | copy-start | bytes 49156
  34.8 3.7 %copy-start.12 = (f32[1,4096]{1,0:T(1,128)S(1)}, f32[1,4096]{1,0:T(1,128)}, u32[]{:S(2)}) copy-start(f32[1,4096]{1,0:T(1,128)} %get-tuple-element.34) | copy-start | bytes 49156
  34.9 3.7 %copy-start.13 = (f32[1,4096]{1,0:T(1,128)S(1)}, f32[1,4096]{1,0:T(1,128)}, u32[]{:S(2)}) copy-start(f32[1,4096]{1,0:T(1,128)} %get-tuple-element.35) | copy-start | bytes 49156
  34.9 3.7 %copy-start.15 = (f32[4096]{0:T(1024)S(1)}, f32[4096]{0:T(1024)}, u32[]{:S(2)}) copy-start(f32[4096]{0:T(1024)} %param.17) | copy-start | bytes 49156
  34.9 10.5 %collective-permute-start.2 = (f32[2,4,64,512]{3,2,1,0:T(8,128)S(1)}, f32[2,4,64,512]{3,2,1,0:T(8,128)S(1)}, u32[]{:S(2)}, u32[]{:S(2)}) collective-permute-start(f32[2,4,64,512]{3,2,1,0:T(8,128)S(1)} %bitcast.103), channel_id=1, source_target_pairs={{0,1},{1,0},{2,3},{3,2},{4,5},{5,4},{6,7},{7,6},{8,9},{9,8},{10,11... | collective-permute-start | bytes 3145736 | tf_op jit(solution)/shard_map/ppermute | solution.py:25
  60.8 3.3 %collective-permute-start.3 = (f32[4,8,64,128]{3,1,2,0:T(8,128)}, f32[4,8,64,128]{3,1,2,0:T(8,128)S(1)}, u32[]{:S(2)}, u32[]{:S(2)}) collective-permute-start(f32[4,8,64,128]{3,1,2,0:T(8,128)} %bitcast.89), channel_id=1, source_target_pairs={{0,1},{1,0},{2,3},{3,2},{4,5},{5,4},{6,7},{7,6},{8,9},{9,8},{10,11... | collective-permute-start | bytes 3145736 | tf_op jit(solution)/shard_map/ppermute | solution.py:25
  63.9 1.9 %copy-start.7 = (f32[4,8,2]{2,1,0:T(8,128)}, f32[4,8,2]{2,1,0:T(8,128)S(1)}, u32[]{:S(2)}) copy-start(f32[4,8,2]{2,1,0:T(8,128)S(1)} %reshape_squeeze.7) | copy-start | bytes 772
  64.8 2.6 %copy-start.16 = (f32[64]{0:T(128)S(1)}, f32[64]{0:T(128)}, u32[]{:S(2)}) copy-start(f32[64]{0:T(128)} %param.22) | copy-start | bytes 772
  66.1 4.3 %copy-start.6 = (f32[4,16,512]{2,1,0:T(8,128)}, f32[4,16,512]{2,1,0:T(8,128)S(1)}, u32[]{:S(2)}) copy-start(f32[4,16,512]{2,1,0:T(8,128)S(1)} %reshape.75.cumr_ref) | copy-start | bytes 393220
  147.2 4.3 %copy-start.3 = (f32[4,16,512]{2,1,0:T(8,128)S(1)}, f32[4,16,512]{2,1,0:T(8,128)}, u32[]{:S(2)}) copy-start(f32[4,16,512]{2,1,0:T(8,128)} %copy-done.2) | copy-start | bytes 393220
  151.5 2.9 %collective-permute-start.4 = (f32[4,8,64,128]{3,1,2,0:T(8,128)}, f32[4,8,64,128]{3,1,2,0:T(8,128)S(1)}, u32[]{:S(2)}, u32[]{:S(2)}) collective-permute-start(f32[4,8,64,128]{3,1,2,0:T(8,128)} %get-tuple-element.17), channel_id=1, source_target_pairs={{0,1},{1,0},{2,3},{3,2},{4,5},{5,4},{6,7},{7,6},{8,9},{9,8},{10,11... | collective-permute-start | bytes 3145736 | tf_op jit(solution)/shard_map/ppermute | solution.py:25
  158.6 15.3 %copy-start.1 = (f32[2,4,128]{2,1,0:T(4,128)S(1)}, f32[2,4,128]{2,1,0:T(4,128)}, u32[]{:S(2)}) copy-start(f32[2,4,128]{2,1,0:T(4,128)} %param.19) | copy-start | bytes 12292
Sparse Core Ops, SparseCore 0:
  66.0 80.4 all-gather.2

commit v4 on v3

--- a/solution.py
+++ b/solution.py
@@ -174,13 +174,18 @@
     channels = heads_dev * HEAD_DIM
     rim_len = CONV_K - 1
 
-    x_rim, bc_rim = passed_along(
-        (x_raw[tokens - rim_len :], bc_raw[..., tokens - rim_len :]), "ctx", 1
-    )
+    bc_tail = bc_raw[..., tokens - rim_len :]
+    rims = passed_along(
+        jnp.concatenate(
+            [x_raw[tokens - rim_len :], bc_tail.reshape(-1, rim_len).transpose(1, 0)], 1
+        ),
+        "ctx",
+        1,
+    )
+    x_rim = rims[:, :channels]
+    bc_rim = rims[:, channels:].transpose(1, 0).reshape(bc_tail.shape)
     x_pad = jnp.concatenate([x_rim, x_raw], 0)
-    x_own = conv_rows(
-        lax.dynamic_slice_in_dim(x_pad, sub_index * own, own + rim_len, 0), conv_x_w, conv_x_b
-    )
+    x_all = conv_rows(x_pad, conv_x_w, conv_x_b)
     bc_weights = lax.dynamic_slice_in_dim(conv_bc_w, sub_index * half, half, 3)
     bc_bias = lax.dynamic_slice_in_dim(conv_bc_b, sub_index * half, half, 2)
     bc_conv = conv_cols(jnp.concatenate([bc_rim, bc_raw], 3), bc_weights, bc_bias)
@@ -221,34 +226,44 @@
     step_rows = step_own.reshape(set_groups, per_group, own)
     skip_row = jnp.repeat(d_skip, HEAD_DIM)[None, :]
 
-    to_end = jnp.exp(cum_device[..., own - 1 :] - cum_device) * step_rows
-    end_state = pl.pallas_call(
+    cum_all = jnp.einsum(
+        "hjct,tu->hjcu",
+        log_decay.reshape(heads_dev, nsub, blocks, block_len),
+        upper,
+        precision=HIGHEST,
+    )
+    all_totals = cum_all[..., -1]
+    cum_all = (cum_all + (jnp.cumsum(all_totals, axis=-1) - all_totals)[..., None]).reshape(
+        heads_dev, nsub, own
+    )
+    to_end = jnp.exp(cum_all[..., own - 1 :] - cum_all) * step_sizes.reshape(heads_dev, nsub, own)
+    to_end = to_end.reshape(set_groups, per_group, tokens)
+    ends = pl.pallas_call(
         end_kernel,
-        grid=(set_groups,),
+        grid=(nsub, set_groups),
         in_specs=[
-            pl.BlockSpec((own, group_width), lambda g: (0, g)),
-            pl.BlockSpec((1, state, own), lambda g: (g, 0, 0)),
-            pl.BlockSpec((1, per_group, own), lambda g: (g, 0, 0)),
+            pl.BlockSpec((own, group_width), lambda j, g: (j, g)),
+            pl.BlockSpec((1, half, own), lambda j, g: (g, 0, j)),
+            pl.BlockSpec((1, per_group, own), lambda j, g: (g, 0, j)),
         ],
-        out_specs=pl.BlockSpec((1, pairs, state, 128), lambda g: (g, 0, 0, 0)),
-        out_shape=jax.ShapeDtypeStruct((set_groups, pairs, state, 128), F32),
-    )(x_own, b_rows, to_end)
+        out_specs=pl.BlockSpec((1, pairs, half, 128), lambda j, g: (j * set_groups + g, 0, 0, 0)),
+        out_shape=jax.ShapeDtypeStruct((nsub * set_groups, pairs, half, 128), F32),
+    )(x_all, bc_conv[0], to_end)
+    ends = ends.reshape(nsub, set_groups, pairs, half, 128)
 
     def pair_layout(values):
         return jnp.repeat(values.reshape(set_groups, pairs, 2), HEAD_DIM, axis=-1)[:, :, None, :]
 
     decay_first = pair_layout(half_totals[:, 0])
     decay_second = pair_layout(half_totals[:, 1])
-    halves = end_state.reshape(set_groups, pairs, nsub, half, 128)
-    mine = lax.dynamic_index_in_dim(halves, sub_index, 2, keepdims=False)
-    theirs = swapped(lax.dynamic_index_in_dim(halves, 1 - sub_index, 2, keepdims=False), "sub")
-    first_end = jnp.where(sub_index == 0, mine, theirs)
-    second_end = jnp.where(sub_index == 0, theirs, mine)
+    first_end = ends[0]
+    second_end = ends[1]
     chip_end = decay_second * first_end + second_end
     chip_decay = decay_first * decay_second
     ctx_index = lax.axis_index("ctx")
     packed = jnp.concatenate([chip_end, chip_decay], 2)
-    packed, x_held = lax.optimization_barrier((packed, x_own))
+    packed, x_held = lax.optimization_barrier((packed, x_all))
+    x_own = lax.dynamic_slice_in_dim(x_held, sub_index * own, own, 0)
     y_local = pl.pallas_call(
         scan_kernel,
         grid=(set_groups, blocks),
@@ -264,7 +279,7 @@
         out_specs=pl.BlockSpec((block_len, group_width), lambda g, c: (c, g)),
         out_shape=jax.ShapeDtypeStruct((own, channels), F32),
         scratch_shapes=[pltpu.VMEM((pairs, state, 128), F32)],
-    )(x_held, c_cols, b_rows, cum_rows, cum_cols, step_rows, skip_row)
+    )(x_own, c_cols, b_rows, cum_rows, cum_cols, step_rows, skip_row)
 
     gathered = lax.all_gather(packed, "ctx")
     gathered, y_local = lax.optimization_barrier((gathered, y_local))

time: 181 us -> 184 us (1.017)
  waiting for transfers between devices: 42.9 us -> 25.6 us
  other arithmetic: 28.2 us -> 40.1 us
  local copies, waits for them, and re-layouts: 25.4 us -> 33.5 us
  starting transfers between devices: 9.57 us -> 4.94 us
  Pallas kernels: 60.7 us -> 64.4 us
    all_gather x1, waiting for transfers between devices: 41.3 us -> 24.4 us  [per_device(): gathered = lax.all_gather(packed, 'ctx')]
    mul x1, other arithmetic: 6.82 us -> 23 us  [conv_rows(): return jax.nn.silu(total)]
    dynamic_slice x2 -> x1, local copies, waits for them, and re-layouts: 3.26 us -> 7.59 us  [per_device(): x_own = lax.dynamic_slice_in_dim(x_held, sub_index * own, own, 0)]
    ppermute x2 -> x1, starting transfers between devices: 9.01 us -> 4.93 us  [passed_along(): return lax.ppermute(x, axis, pairs)]
    pallas_call x1, Pallas kernels: 10.6 us -> 14.5 us  [per_device(): pl.pallas_call(end_kernel, grid=(nsub, set_groups), in_specs=[pl.BlockSpe...]
    concatenate x1, other arithmetic: 3.56 us -> 0.02 us  [per_device(): jnp.concatenate([x_raw[tokens - rim_len:], bc_tail.reshape(-1, rim_len).t...]
    all_gather x0 -> x1, local copies, waits for them, and re-layouts: none -> 3 us  [per_device(): gathered = lax.all_gather(packed, 'ctx')]
    select_n x1, other arithmetic: 4.29 us -> 1.41 us  [per_device(): got = swapped(jnp.where(sub_index == 0, into_second, carried), 'sub')]
  transfers between devices with their start and end apart: 6 -> 4, of which waited for: 2 -> 2; matrix products, arithmetic and copies ran while one was open for 20% -> 17% of each run, Pallas kernels for 19% -> 19%
where the time goes in v4:
time: 184 us; the launch traced here: 183 us
  Pallas kernels  64.4 us (35%)
  other arithmetic  40.1 us (22%)
  local copies, waits for them, and re-layouts  33.5 us (18%)
  waiting for transfers between devices  25.6 us (14%)
  between operations  13.8 us (8%)
  starting transfers between devices  4.94 us (3%)
    pallas_call x1, Pallas kernels, per_device(): pl.pallas_call(scan_kernel, grid=(set_groups, blocks), in_specs=[pl.Block...  34.6 us
    all_gather x1, waiting for transfers between devices, per_device(): gathered = lax.all_gather(packed, 'ctx')  24.4 us
    mul x1, other arithmetic, conv_rows(): return jax.nn.silu(total)  23 us
    pallas_call x1, Pallas kernels, per_device(): pl.pallas_call(out_kernel, grid=(set_groups, own // out_len), in_specs=[p...  15.3 us
    pallas_call x1, Pallas kernels, per_device(): pl.pallas_call(end_kernel, grid=(nsub, set_groups), in_specs=[pl.BlockSpe...  14.5 us
    dynamic_slice x1, local copies, waits for them, and re-layouts, per_device(): x_own = lax.dynamic_slice_in_dim(x_held, sub_index * own, own, 0)  7.59 us
    mul x1, other arithmetic, conv_cols(): return jax.nn.silu(total)  5.91 us
    ppermute x1, starting transfers between devices, passed_along(): return lax.ppermute(x, axis, pairs)  4.93 us
  transfers between devices with their start and end apart: 4, of which 2 were waited for; matrix products, arithmetic and copies ran while one was open for 17% of the time, Pallas kernels for 19%

profile of v4, /device:TPU:0, one launch (start us, length us, event | category | flops | bytes accessed | tf_op | source)
XLA Modules:
  0.0 182.9 jit_solution(8834294824669380809)
XLA Ops:
  6.5 1.0 slice.117
  7.7 0.9 slice.116
  8.6 4.9 %collective-permute-start = (bf16[3,4608]{1,0:T(4,128)(2,1)S(1)}, bf16[3,4608]{1,0:T(4,128)(2,1)S(1)}, u32[]{:S(2)}, u32[]{:S(2)}) collective-permute-start(bf16[3,4608]{1,0:T(4,128)(2,1)S(1)} %pad_maximum_fusion.5), channel_id=1, source_target_pairs={{0,4},{4,8},{8,12},{1,5},{5,9},{9,13},{2,6},{6,10},{10,14},{3,7},{... | collective-permute-start | bytes 82952 | tf_op jit(solution)/shard_map/ppermute | solution.py:21
  13.5 0.7 exponential_negate_fusion
  14.2 1.2 broadcast_multiply_fusion
  16.7 0.5 copy.71
  18.4 0.8 exponential_multiply_fusion.wk_ref
  20.1 5.9 %divide_multiply_fusion.1 = f32[2,4,64,1024]{3,2,1,0:T(8,128)S(1)} fusion(bf16[2,4,64,1024]{3,2,1,0:T(8,128)(2,1)} %param.13, bf16[2,4,64,3]{3,2,1,0:T(8,128)(2,1)S(1)} %bitcast.100, f32[2,4,64]{2,1,0:T(4,128)S(1)} %get-tuple-element.37, f32[2,4,64]{2,1,0:T(4,128)S(1)} %get-tuple-element.35, f32[2,4,64]{2,1,0:T(4,128)S(1)} %get-tuple-element.36, ...), kind=kLoop, calls=%fused_computation.9 | loop fusion | flops 13107200 | bytes 3159040 | tf_op jit(solution)/shard_map/jit(silu)/mul | solution.py:45
  26.0 1.0 slice_bitcast_fusion.b_ref
  27.1 23.0 %divide_multiply_fusion.xc_ref = f32[1024,4096]{1,0:T(8,128)} fusion(bf16[1024,4096]{1,0:T(8,128)(2,1)} %param.12, bf16[3,4096]{1,0:T(4,128)(2,1)S(1)} %slice.149, f32[4096]{0:T(1024)S(1)} %bitcast.110, f32[4096]{0:T(1024)S(1)} %bitcast.111, f32[4096]{0:T(1024)S(1)} %bitcast.109, f32[4096]{0:T(1024)S(1)} %bitcast.108, f32[4096]{0:T(1024)S(1)} %copy-done.6), kind=kLoop, calls=%fused_computation | loop fusion | flops 104857600 | bytes 25272320 | tf_op jit(solution)/shard_map/jit(silu)/mul | solution.py:35
  50.1 14.5 %shard_map.118 = f32[8,8,64,128]{3,2,1,0:T(8,128)} custom-call(f32[1024,4096]{1,0:T(8,128)} %divide_multiply_fusion.xc_ref, f32[4,64,1024]{2,1,0:T(8,128)} %slice_bitcast_fusion.b_ref, f32[4,16,1024]{2,1,0:T(8,128)} %exponential_multiply_fusion.wk_ref), custom_call_target="tpu_custom_call" | custom-call | tf_op jit(solution)/shard_map/pallas_call | solution.py:241
  64.6 1.8 slice_add_fusion
  66.4 1.2 copy.58
  67.6 2.8 %reshape.102 = f32[2,4,64,2,512]{4,3,2,1,0:T(2,128)} reshape(f32[2,4,64,1024]{3,2,1,0:T(8,128)S(1)} %divide_multiply_fusion.1) | data formatting | bytes 4194304 | tf_op jit(solution)/shard_map/reshape | solution.py:192
  70.4 4.4 %constant_dynamic-slice_fusion.3 = (f32[2,4,64,1,512]{4,3,2,1,0:T(1,128)S(1)}, f32[2,4,64,1,512]{4,3,2,1,0:T(1,128)S(1)}) fusion(f32[2,4,64,2,512]{4,3,2,1,0:T(2,128)} %reshape.102, s32[]{:T(128)S(6)} %select_n.74, s32[]{:T(128)S(6)} %select_n.75), kind=kLoop, calls=%fused_computation.67 | loop fusion | bytes 4194312 | tf_op jit(solution)/shard_map/jit(dynamic_index_in_dim)/dynamic_slice | solution.py:193
  74.8 1.1 copy.85
  75.9 0.7 constant_dynamic-slice_fusion
  77.0 1.3 copy.64
  78.4 0.7 broadcast_in_dim_reshape.2.dsk_ref
  79.3 7.6 %constant_dynamic-slice_fusion.4.xc_ref = f32[512,4096]{1,0:T(8,128)} fusion(f32[1024,4096]{1,0:T(8,128)} %divide_multiply_fusion.xc_ref, s32[]{:T(128)S(6)} %select_n.72), kind=kLoop, calls=%fused_computation.68 | loop fusion | bytes 16777220 | tf_op jit(solution)/shard_map/dynamic_slice | solution.py:266
  86.9 1.5 fusion.6
  88.4 1.2 pad_maximum_fusion.3
  89.6 1.3 copy.61
  90.9 34.6 %shard_map.119.y_ref = f32[512,4096]{1,0:T(8,128)} custom-call(f32[512,4096]{1,0:T(8,128)} %constant_dynamic-slice_fusion.4.xc_ref, f32[4,512,128]{2,1,0:T(8,128)} %bitcast.91, f32[4,128,512]{2,1,0:T(8,128)} %bitcast.96, f32[4,16,512]{2,1,0:T(8,128)} %copy-done.3, f32[4,512,16]{2,1,0:T(8,128)} %bitcast.94, f32[4,16,512]{2,1,0:T(8,128)} %bitcast.99, ...), custom_call_target="tpu_custom_call" | custom-call | tf_op jit(solution)/shard_map/pallas_call | solution.py:267
  125.5 24.4 %all-gather.3.cloned.1.call-done = f32[16,8,65,128]{3,1,2,0:T(8,128)} async-done(((f32[4,8,65,128]{3,1,2,0:T(8,128)}), f32[16,8,65,128]{3,1,2,0:T(8,128)}) %all-gather.3.cloned.1.call-update) | async-done | bytes 4259856 | tf_op jit(solution)/shard_map/all_gather | solution.py:284
  149.9 3.0 %copy.59 = f32[16,8,65,128]{3,2,1,0:T(8,128)S(1)} copy(f32[16,8,65,128]{3,1,2,0:T(8,128)} %all-gather.3.cloned.1.call-done) | data formatting | bytes 8519680 | tf_op jit(solution)/shard_map/all_gather | solution.py:284
  153.0 1.4 fusion.10
  154.9 1.3 copy.66
  156.2 1.2 collective-permute-done.2
  157.4 1.6 select_bitcast_fusion.1
  159.3 1.5 copy.67
  160.8 15.3 %shard_map.120 = bf16[512,4096]{1,0:T(8,128)(2,1)} custom-call(f32[512,4096]{1,0:T(8,128)} %shard_map.119.y_ref, f32[4,512,128]{2,1,0:T(8,128)} %bitcast.92, f32[4,512,16]{2,1,0:T(8,128)} %bitcast.95, f32[4,8,128,128]{3,2,1,0:T(8,128)} %bitcast.93, bf16[512,4096]{1,0:T(8,128)(2,1)} %z_ref.1, f32[1,4096]{1,0:T(1,128)} %bitcast.113), custom_call_target="tpu_custom_call" | custom-call | tf_op jit(solution)/shard_map/pallas_call | solution.py:301
  (65 shorter events, 5.0 us)
Async XLA Ops:
  6.5 12.7 %copy-start = (f32[2,4,128]{2,1,0:T(4,128)S(1)}, f32[2,4,128]{2,1,0:T(4,128)}, u32[]{:S(2)}) copy-start(f32[2,4,128]{2,1,0:T(4,128)} %param.19) | copy-start | bytes 12292
  6.5 143.4 %all-gather.3.cloned.1.call-start = ((), (), s32[]{:S(2)}) async-start(), calls=%async_computation | async-start | bytes 5324800 | tf_op jit(solution)/shard_map/all_gather | solution.py:284
  8.6 11.3 %collective-permute-start = (bf16[3,4608]{1,0:T(4,128)(2,1)S(1)}, bf16[3,4608]{1,0:T(4,128)(2,1)S(1)}, u32[]{:S(2)}, u32[]{:S(2)}) collective-permute-start(bf16[3,4608]{1,0:T(4,128)(2,1)S(1)} %pad_maximum_fusion.5), channel_id=1, source_target_pairs={{0,4},{4,8},{8,12},{1,5},{5,9},{9,13},{2,6},{6,10},{10,14},{3,7},{... | collective-permute-start | bytes 82952 | tf_op jit(solution)/shard_map/ppermute | solution.py:21
  16.1 1.9 %copy-start.4 = (f32[4,4096]{1,0:T(4,128)S(1)}, f32[4,4096]{1,0:T(4,128)}, u32[]{:S(2)}) copy-start(f32[4,4096]{1,0:T(4,128)} %param.16) | copy-start | bytes 196612
  16.5 2.6 %copy-start.5 = (f32[4,2,4,128]{3,2,1,0:T(4,128)S(1)}, f32[4,2,4,128]{3,2,1,0:T(4,128)}, u32[]{:S(2)}) copy-start(f32[4,2,4,128]{3,2,1,0:T(4,128)} %param.18) | copy-start | bytes 49156
  20.1 7.0 %copy-start.6 = (f32[4096]{0:T(1024)S(1)}, f32[4096]{0:T(1024)}, u32[]{:S(2)}) copy-start(f32[4096]{0:T(1024)} %param.17) | copy-start | bytes 49156
  74.8 3.5 %copy-start.7 = (f32[64]{0:T(128)S(1)}, f32[64]{0:T(128)}, u32[]{:S(2)}) copy-start(f32[64]{0:T(128)} %param.22) | copy-start | bytes 772
  75.9 11.0 %collective-permute-start.1 = (f32[2,4,64,512]{3,2,1,0:T(8,128)}, f32[2,4,64,512]{3,2,1,0:T(8,128)}, u32[]{:S(2)}, u32[]{:S(2)}) collective-permute-start(f32[2,4,64,512]{3,2,1,0:T(8,128)} %bitcast.88), channel_id=1, source_target_pairs={{0,1},{1,0},{2,3},{3,2},{4,5},{5,4},{6,7},{7,6},{8,9},{9,8},{10,11... | collective-permute-start | bytes 3145736 | tf_op jit(solution)/shard_map/ppermute | solution.py:25
  77.0 9.9 %copy-start.3 = (f32[4,16,512]{2,1,0:T(8,128)}, f32[4,16,512]{2,1,0:T(8,128)S(1)}, u32[]{:S(2)}) copy-start(f32[4,16,512]{2,1,0:T(8,128)S(1)} %reshape.104.cumr_ref) | copy-start | bytes 393220
  125.5 27.5 %copy-start.2 = (f32[8,8,64,128]{3,2,1,0:T(8,128)S(1)}, f32[8,8,64,128]{3,2,1,0:T(8,128)}, u32[]{:S(2)}) copy-start(f32[8,8,64,128]{3,2,1,0:T(8,128)} %shard_map.118) | copy-start | bytes 6291460
  154.4 3.0 %collective-permute-start.2 = (f32[4,8,64,128]{3,2,1,0:T(8,128)}, f32[4,8,64,128]{3,2,1,0:T(8,128)}, u32[]{:S(2)}, u32[]{:S(2)}) collective-permute-start(f32[4,8,64,128]{3,2,1,0:T(8,128)} %get-tuple-element.15), channel_id=1, source_target_pairs={{0,1},{1,0},{2,3},{3,2},{4,5},{5,4},{6,7},{7,6},{8,9},{9,8},{10,11... | collective-permute-start | bytes 3145736 | tf_op jit(solution)/shard_map/ppermute | solution.py:25
  160.8 15.3 %copy-start.1 = (f32[2,4,128]{2,1,0:T(4,128)S(1)}, f32[2,4,128]{2,1,0:T(4,128)}, u32[]{:S(2)}) copy-start(f32[2,4,128]{2,1,0:T(4,128)} %param.19) | copy-start | bytes 12292
Sparse Core Ops, SparseCore 0:
  67.8 82.1 all-gather.2

commit v5 on v4

--- a/solution.py
+++ b/solution.py
@@ -261,35 +261,70 @@
     chip_end = decay_second * first_end + second_end
     chip_decay = decay_first * decay_second
     ctx_index = lax.axis_index("ctx")
-    packed = jnp.concatenate([chip_end, chip_decay], 2)
-    packed, x_held = lax.optimization_barrier((packed, x_all))
-    x_own = lax.dynamic_slice_in_dim(x_held, sub_index * own, own, 0)
-    y_local = pl.pallas_call(
-        scan_kernel,
-        grid=(set_groups, blocks),
-        in_specs=[
-            pl.BlockSpec((block_len, group_width), lambda g, c: (c, g)),
-            pl.BlockSpec((1, block_len, state), lambda g, c: (g, c, 0)),
-            pl.BlockSpec((1, state, block_len), lambda g, c: (g, 0, c)),
-            pl.BlockSpec((1, per_group, block_len), lambda g, c: (g, 0, c)),
-            pl.BlockSpec((1, block_len, per_group), lambda g, c: (g, c, 0)),
-            pl.BlockSpec((1, per_group, block_len), lambda g, c: (g, 0, c)),
-            pl.BlockSpec((1, group_width), lambda g, c: (0, g)),
-        ],
-        out_specs=pl.BlockSpec((block_len, group_width), lambda g, c: (c, g)),
-        out_shape=jax.ShapeDtypeStruct((own, channels), F32),
-        scratch_shapes=[pltpu.VMEM((pairs, state, 128), F32)],
-    )(x_own, c_cols, b_rows, cum_rows, cum_cols, step_rows, skip_row)
-
-    gathered = lax.all_gather(packed, "ctx")
-    gathered, y_local = lax.optimization_barrier((gathered, y_local))
-    all_ends = gathered[:, :, :, :half]
-    all_decays = gathered[:, :, :, half:]
-    carried = jnp.zeros_like(chip_end)
-    for earlier in range(lax.axis_size("ctx") - 1):
-        carried = jnp.where(
-            earlier < ctx_index, all_ends[earlier] + all_decays[earlier] * carried, carried
+    ctx_size = lax.axis_size("ctx")
+    x_own = lax.dynamic_slice_in_dim(x_all, sub_index * own, own, 0)
+    scan_inputs = (x_own, c_cols, b_rows, cum_rows, cum_cols, step_rows, skip_row)
+
+    def scan_group(group, inputs, target):
+        extra = {} if target is None else {"input_output_aliases": {len(inputs): 0}}
+        in_specs = [
+            pl.BlockSpec((block_len, group_width), lambda g, c: (c, group)),
+            pl.BlockSpec((1, block_len, state), lambda g, c: (group, c, 0)),
+            pl.BlockSpec((1, state, block_len), lambda g, c: (group, 0, c)),
+            pl.BlockSpec((1, per_group, block_len), lambda g, c: (group, 0, c)),
+            pl.BlockSpec((1, block_len, per_group), lambda g, c: (group, c, 0)),
+            pl.BlockSpec((1, per_group, block_len), lambda g, c: (group, 0, c)),
+            pl.BlockSpec((1, group_width), lambda g, c: (0, group)),
+        ]
+        operands = tuple(inputs)
+        if target is not None:
+            in_specs.append(pl.BlockSpec(memory_space=pl.ANY))
+            operands = operands + (target,)
+        kernel = scan_kernel if target is None else (lambda *refs: scan_kernel(*refs[:7], *refs[8:]))
+        return pl.pallas_call(
+            kernel,
+            grid=(1, blocks),
+            in_specs=in_specs,
+            out_specs=pl.BlockSpec((block_len, group_width), lambda g, c: (c, group)),
+            out_shape=jax.ShapeDtypeStruct((own, channels), F32),
+            scratch_shapes=[pltpu.VMEM((pairs, state, 128), F32)],
+            **extra,
+        )(*operands)
+
+    pieces = 2 if (set_groups * pairs) % 2 == 0 else 1
+    rounds = ctx_size + pieces - 2
+    piece_shape = (pieces, set_groups * pairs // pieces, half, 128)
+    end_pieces = chip_end.reshape(piece_shape)
+    decay_pieces = jnp.broadcast_to(chip_decay, chip_end.shape).reshape(piece_shape)
+    received = jnp.zeros(piece_shape, F32)
+    y_local = None
+    placed = [min(group, max(rounds, 1) - 1) for group in range(set_groups)]
+    for step_index in range(max(rounds, 1)):
+        send_at = jnp.clip(step_index - ctx_index, 0, pieces - 1)
+        outgoing = lax.dynamic_index_in_dim(
+            end_pieces, send_at, 0, keepdims=False
+        ) + lax.dynamic_index_in_dim(decay_pieces, send_at, 0, keepdims=False) * (
+            lax.dynamic_index_in_dim(received, send_at, 0, keepdims=False)
         )
+        held = scan_inputs
+        if any(p == step_index for p in placed):
+            outgoing, held = lax.optimization_barrier((outgoing, scan_inputs))
+        if rounds > 0:
+            arrived = passed_along(outgoing, "ctx", 1)
+        for group in range(set_groups):
+            if placed[group] == step_index:
+                y_local = scan_group(group, held, y_local)
+        if rounds == 0:
+            break
+        if any(p == step_index for p in placed):
+            arrived, y_local = lax.optimization_barrier((arrived, y_local))
+        recv_at = step_index - ctx_index + 1
+        valid = (recv_at >= 0) & (recv_at < pieces) & (ctx_index > 0)
+        updated = lax.dynamic_update_index_in_dim(
+            received, arrived, jnp.clip(recv_at, 0, pieces - 1), 0
+        )
+        received = jnp.where(valid, updated, received)
+    carried = received.reshape(chip_end.shape)
     into_second = decay_first * carried + first_end
     keep = jnp.where(sub_index == 0, carried, into_second)
     got = swapped(jnp.where(sub_index == 0, into_second, carried), "sub")

time: 184 us -> 172 us (0.935)
  waiting for transfers between devices: 25.6 us -> 2.92 us
  starting transfers between devices: 4.94 us -> 21.9 us
  between operations: 13.8 us -> 0.61 us
  Pallas kernels: 64.4 us -> 71.9 us
    all_gather x1 -> x0, waiting for transfers between devices: 24.4 us -> none  [per_device(): gathered = lax.all_gather(packed, 'ctx')]
    ppermute x1 -> x5, starting transfers between devices: 4.93 us -> 21.9 us  [passed_along(): return lax.ppermute(x, axis, pairs)]
    pallas_call x1 -> x4, Pallas kernels: 34.6 us -> 42.1 us  [scan_group(): pl.pallas_call(kernel, grid=(1, blocks), in_specs=in_specs, out_specs=pl....]
    all_gather x1 -> x0, local copies, waits for them, and re-layouts: 3 us -> none  [per_device(): gathered = lax.all_gather(packed, 'ctx')]
    mul x1, other arithmetic: 5.91 us -> 2.92 us  [conv_cols(): return jax.nn.silu(total)]
    add x0 -> x4, other arithmetic: none -> 1.91 us  [per_device(): lax.dynamic_index_in_dim(end_pieces, send_at, 0, keepdims=False)]
    dynamic_slice x1 -> x2, local copies, waits for them, and re-layouts: 7.59 us -> 7.61 us  [the longest x1 7.6 us: per_device(): x_own = lax.dynamic_slice_in_dim(x_all, sub_index * own, own, 0)]
  transfers between devices with their start and end apart: 4 -> 7, of which waited for: 2 -> 3; matrix products, arithmetic and copies ran while one was open for 17% -> 28% of each run, Pallas kernels for 19% -> 33%
where the time goes in v5:
time: 172 us; the launch traced here: 171 us
  Pallas kernels  71.9 us (42%)
  other arithmetic  39.4 us (23%)
  local copies, waits for them, and re-layouts  33.5 us (19%)
  starting transfers between devices  21.9 us (13%)
  waiting for transfers between devices  2.92 us (2%)
    pallas_call x4, Pallas kernels, scan_group(): pl.pallas_call(kernel, grid=(1, blocks), in_specs=in_specs, out_specs=pl....  42.1 us
    mul x1, other arithmetic, conv_rows(): return jax.nn.silu(total)  22.7 us
    ppermute x5, starting transfers between devices, passed_along(): return lax.ppermute(x, axis, pairs)  21.9 us
    pallas_call x1, Pallas kernels, per_device(): pl.pallas_call(out_kernel, grid=(set_groups, own // out_len), in_specs=[p...  15.3 us
    pallas_call x1, Pallas kernels, per_device(): pl.pallas_call(end_kernel, grid=(nsub, set_groups), in_specs=[pl.BlockSpe...  14.5 us
    dynamic_slice x1, local copies, waits for them, and re-layouts, per_device(): x_own = lax.dynamic_slice_in_dim(x_all, sub_index * own, own, 0)  7.6 us
    dynamic_slice x1, local copies, waits for them, and re-layouts, per_device(): bc_mine = lax.dynamic_index_in_dim(bc_halves, sub_index, 3, keepdims=False)  4.45 us
  transfers between devices with their start and end apart: 7, of which 3 were waited for; matrix products, arithmetic and copies ran while one was open for 28% of the time, Pallas kernels for 33%

profile of v5, /device:TPU:0, one launch (start us, length us, event | category | flops | bytes accessed | tf_op | source)
XLA Modules:
  0.0 170.8 jit_solution(15445331859273200964)
XLA Ops:
  0.0 1.0 slice.91
  2.0 4.9 %collective-permute-start = (bf16[3,4608]{1,0:T(4,128)(2,1)S(1)}, bf16[3,4608]{1,0:T(4,128)(2,1)S(1)}, u32[]{:S(2)}, u32[]{:S(2)}) collective-permute-start(bf16[3,4608]{1,0:T(4,128)(2,1)S(1)} %pad_maximum_fusion.4), channel_id=1, source_target_pairs={{0,4},{4,8},{8,12},{1,5},{5,9},{9,13},{2,6},{6,10},{10,14},{3,7},{... | collective-permute-start | bytes 82952 | tf_op jit(solution)/shard_map/ppermute | solution.py:21
  7.6 1.2 broadcast_multiply_fusion
  10.0 1.7 fusion.30
  18.6 1.4 copy.68
  21.3 2.9 %divide_multiply_fusion.1 = f32[2,4,64,1024]{3,2,1,0:T(8,128)S(1)} fusion(bf16[2,4,64,1024]{3,2,1,0:T(8,128)(2,1)S(1)} %copy-done.4, bf16[2,4,64,3]{3,2,1,0:T(8,128)(2,1)S(1)} %bitcast.137, f32[2,4,64]{2,1,0:T(4,128)} %get-tuple-element.108, f32[2,4,64]{2,1,0:T(4,128)} %get-tuple-element.106, f32[2,4,64]{2,1,0:T(4,128)} %get-tuple-element.107, ...), kind=kLoop, calls=%fused_computation.9 | loop fusion | flops 13107200 | bytes 3159040 | tf_op jit(solution)/shard_map/jit(silu)/mul | solution.py:45
  24.3 1.1 slice_bitcast_fusion.b_ref
  25.3 2.8 %reshape.106 = f32[2,4,64,2,512]{4,3,2,1,0:T(2,128)} reshape(f32[2,4,64,1024]{3,2,1,0:T(8,128)S(1)} %divide_multiply_fusion.1) | data formatting | bytes 4194304 | tf_op jit(solution)/shard_map/reshape | solution.py:192
  28.1 4.5 %constant_dynamic-slice_fusion.5 = (f32[2,4,64,1,512]{4,3,2,1,0:T(1,128)S(1)}, f32[2,4,64,1,512]{4,3,2,1,0:T(1,128)S(1)}) fusion(f32[2,4,64,2,512]{4,3,2,1,0:T(2,128)} %reshape.106, s32[]{:T(128)S(6)} %select_n.117, s32[]{:T(128)S(6)} %select_n.118), kind=kLoop, calls=%fused_computation.74 | loop fusion | bytes 4194312 | tf_op jit(solution)/shard_map/jit(dynamic_index_in_dim)/dynamic_slice | solution.py:193
  32.6 1.1 copy.89
  33.7 22.7 %divide_multiply_fusion.xc_ref = f32[1024,4096]{1,0:T(8,128)} fusion(bf16[1024,4096]{1,0:T(8,128)(2,1)} %param.12, bf16[3,4096]{1,0:T(4,128)(2,1)S(1)} %slice-done, f32[4096]{0:T(1024)S(1)} %bitcast.144, f32[4096]{0:T(1024)S(1)} %bitcast.145, f32[4096]{0:T(1024)S(1)} %bitcast.143, f32[4096]{0:T(1024)S(1)} %bitcast.142, f32[4096]{0:T(1024)S(1)} %copy-done.18), kind=kLoop, calls=%fused_computation | loop fusion | flops 104857600 | bytes 25272320 | tf_op jit(solution)/shard_map/jit(silu)/mul | solution.py:35
  56.5 14.5 %shard_map.118 = f32[8,8,64,128]{3,2,1,0:T(8,128)} custom-call(f32[1024,4096]{1,0:T(8,128)} %divide_multiply_fusion.xc_ref, f32[4,64,1024]{2,1,0:T(8,128)} %slice_bitcast_fusion.b_ref, f32[4,16,1024]{2,1,0:T(8,128)} %exponential_multiply_fusion.wk_ref), custom_call_target="tpu_custom_call" | custom-call | tf_op jit(solution)/shard_map/pallas_call | solution.py:241
  71.0 1.8 %slice_add_fusion = f32[4,8,64,128]{3,2,1,0:T(8,128)S(1)} fusion(f32[8,8,64,128]{3,2,1,0:T(8,128)} %shard_map.118, f32[4,8,128]{2,1,0:T(8,128)S(1)} %copy-done.9), kind=kLoop, calls=%fused_computation.20 | loop fusion | flops 524288 | bytes 3162112 | tf_op jit(solution)/shard_map/add | solution.py:261
  73.6 7.6 %constant_dynamic-slice_fusion.6.xc_ref.refs_0_ = f32[512,4096]{1,0:T(8,128)} fusion(f32[1024,4096]{1,0:T(8,128)} %divide_multiply_fusion.xc_ref, s32[]{:T(128)S(6)} %select_n.115), kind=kLoop, calls=%fused_computation.75 | loop fusion | bytes 16777220 | tf_op jit(solution)/shard_map/dynamic_slice | solution.py:265
  81.5 1.3 pad_maximum_fusion.2
  82.8 1.3 copy.65
  84.1 3.5 %collective-permute-start.2 = (f32[16,64,128]{2,1,0:T(8,128)S(1)}, f32[16,64,128]{2,1,0:T(8,128)S(1)}, u32[]{:S(2)}, u32[]{:S(2)}) collective-permute-start(f32[16,64,128]{2,1,0:T(8,128)S(1)} %copy-done.5), channel_id=1, source_target_pairs={{0,4},{4,8},{8,12},{1,5},{5,9},{9,13},{2,6},{6,10},{10,14},{3,7},{... | collective-permute-start | bytes 1572872 | tf_op jit(solution)/shard_map/ppermute | solution.py:21
  87.6 10.6 %shard_map.119.refs_7_ = f32[512,4096]{1,0:T(8,128)} custom-call(f32[512,4096]{1,0:T(8,128)} %constant_dynamic-slice_fusion.6.xc_ref.refs_0_, f32[4,512,128]{2,1,0:T(8,128)} %bitcast.110, f32[4,128,512]{2,1,0:T(8,128)} %bitcast.121, f32[4,16,512]{2,1,0:T(8,128)} %copy-done.3, f32[4,512,16]{2,1,0:T(8,128)} %bitcast.117, f32[4,16,512]{2,1,0:T(8,128)} %bitcast.132, ...), custom_call_target="tpu_custom_call" | custom-call | tf_op jit(solution)/shard_map/pallas_call | solution.py:284
  98.2 1.2 collective-permute-done.2
  99.7 4.4 %collective-permute-start.3 = (f32[16,64,128]{2,1,0:T(8,128)S(1)}, f32[16,64,128]{2,1,0:T(8,128)S(1)}, u32[]{:S(2)}, u32[]{:S(2)}) collective-permute-start(f32[16,64,128]{2,1,0:T(8,128)S(1)} %fusion.14), channel_id=1, source_target_pairs={{0,4},{4,8},{8,12},{1,5},{5,9},{9,13},{2,6},{6,10},{10,14},{3,7},{... | collective-permute-start | bytes 1572872 | tf_op jit(solution)/shard_map/ppermute | solution.py:21
  104.1 10.4 %shard_map.120.refs_7_ = f32[512,4096]{1,0:T(8,128)} custom-call(f32[512,4096]{1,0:T(8,128)} %constant_dynamic-slice_fusion.6.xc_ref.refs_0_, f32[4,512,128]{2,1,0:T(8,128)} %bitcast.111, f32[4,128,512]{2,1,0:T(8,128)} %bitcast.122, f32[4,16,512]{2,1,0:T(8,128)} %copy-done.3, f32[4,512,16]{2,1,0:T(8,128)} %bitcast.118, ...), custom_call_target="tpu_custom_call", output_to_operand_aliasing={{}: (7, {})} | custom-call | tf_op jit(solution)/shard_map/pallas_call | solution.py:284
  115.3 4.4 %collective-permute-start.4 = (f32[16,64,128]{2,1,0:T(8,128)S(1)}, f32[16,64,128]{2,1,0:T(8,128)S(1)}, u32[]{:S(2)}, u32[]{:S(2)}) collective-permute-start(f32[16,64,128]{2,1,0:T(8,128)S(1)} %fusion.12), channel_id=1, source_target_pairs={{0,4},{4,8},{8,12},{1,5},{5,9},{9,13},{2,6},{6,10},{10,14},{3,7},{... | collective-permute-start | bytes 1572872 | tf_op jit(solution)/shard_map/ppermute | solution.py:21
  119.8 10.6 %shard_map.121.refs_7_ = f32[512,4096]{1,0:T(8,128)} custom-call(f32[512,4096]{1,0:T(8,128)} %constant_dynamic-slice_fusion.6.xc_ref.refs_0_, f32[4,512,128]{2,1,0:T(8,128)} %bitcast.112, f32[4,128,512]{2,1,0:T(8,128)} %bitcast.123, f32[4,16,512]{2,1,0:T(8,128)} %copy-done.3, f32[4,512,16]{2,1,0:T(8,128)} %bitcast.119, ...), custom_call_target="tpu_custom_call", output_to_operand_aliasing={{}: (7, {})} | custom-call | tf_op jit(solution)/shard_map/pallas_call | solution.py:284
  131.4 4.7 %collective-permute-start.5 = (f32[16,64,128]{2,1,0:T(8,128)}, f32[16,64,128]{2,1,0:T(8,128)}, u32[]{:S(2)}, u32[]{:S(2)}) collective-permute-start(f32[16,64,128]{2,1,0:T(8,128)} %fusion.10), channel_id=1, source_target_pairs={{0,4},{4,8},{8,12},{1,5},{5,9},{9,13},{2,6},{6,10},{10,14},{3,7},{... | collective-permute-start | bytes 1572872 | tf_op jit(solution)/shard_map/ppermute | solution.py:21
  136.2 10.5 %shard_map.122.y_ref = f32[512,4096]{1,0:T(8,128)} custom-call(f32[512,4096]{1,0:T(8,128)} %constant_dynamic-slice_fusion.6.xc_ref.refs_0_, f32[4,512,128]{2,1,0:T(8,128)} %bitcast.113, f32[4,128,512]{2,1,0:T(8,128)} %bitcast.124, f32[4,16,512]{2,1,0:T(8,128)} %copy-done.3, f32[4,512,16]{2,1,0:T(8,128)} %bitcast.120, ...), custom_call_target="tpu_custom_call", output_to_operand_aliasing={{}: (7, {})} | custom-call | tf_op jit(solution)/shard_map/pallas_call | solution.py:284
  146.7 1.2 fusion.9
  147.9 1.2 fusion.7
  149.6 1.3 copy.70
  151.0 1.1 collective-permute-done.6
  152.1 1.6 select_bitcast_fusion.1
  154.0 1.5 copy.71
  155.5 15.3 %shard_map.123 = bf16[512,4096]{1,0:T(8,128)(2,1)} custom-call(f32[512,4096]{1,0:T(8,128)} %shard_map.122.y_ref, f32[4,512,128]{2,1,0:T(8,128)} %bitcast.114, f32[4,512,16]{2,1,0:T(8,128)} %bitcast.130, f32[4,8,128,128]{3,2,1,0:T(8,128)} %bitcast.129, bf16[512,4096]{1,0:T(8,128)(2,1)} %z_ref.1, f32[1,4096]{1,0:T(1,128)} %bitcast.147), custom_call_target="tpu_custom_call" | custom-call | tf_op jit(solution)/shard_map/pallas_call | solution.py:336
  (105 shorter events, 14.9 us)
Async XLA Ops:
  0.0 16.9 %copy-start = (f32[2,4,128]{2,1,0:T(4,128)S(1)}, f32[2,4,128]{2,1,0:T(4,128)}, u32[]{:S(2)}) copy-start(f32[2,4,128]{2,1,0:T(4,128)} %param.19) | copy-start | bytes 12292
  2.0 18.7 %collective-permute-start = (bf16[3,4608]{1,0:T(4,128)(2,1)S(1)}, bf16[3,4608]{1,0:T(4,128)(2,1)S(1)}, u32[]{:S(2)}, u32[]{:S(2)}) collective-permute-start(bf16[3,4608]{1,0:T(4,128)(2,1)S(1)} %pad_maximum_fusion.4), channel_id=1, source_target_pairs={{0,4},{4,8},{8,12},{1,5},{5,9},{9,13},{2,6},{6,10},{10,14},{3,7},{... | collective-permute-start | bytes 82952 | tf_op jit(solution)/shard_map/ppermute | solution.py:21
  8.8 6.8 %copy-start.17 = (f32[4,2,4,128]{3,2,1,0:T(4,128)S(1)}, f32[4,2,4,128]{3,2,1,0:T(4,128)}, u32[]{:S(2)}) copy-start(f32[4,2,4,128]{3,2,1,0:T(4,128)} %param.18) | copy-start | bytes 49156
  9.7 10.3 %copy-start.19 = (f32[64]{0:T(128)S(1)}, f32[64]{0:T(128)}, u32[]{:S(2)}) copy-start(f32[64]{0:T(128)} %param.22) | copy-start | bytes 772
  9.7 11.6 %copy-start.4 = (bf16[2,4,64,1024]{3,2,1,0:T(8,128)(2,1)S(1)}, bf16[2,4,64,1024]{3,2,1,0:T(8,128)(2,1)}, u32[]{:S(2)}) copy-start(bf16[2,4,64,1024]{3,2,1,0:T(8,128)(2,1)} %param.13) | copy-start | bytes 3145732
  13.7 7.2 %copy-start.6 = (f32[4,8,2]{2,1,0:T(8,128)}, f32[4,8,2]{2,1,0:T(8,128)S(1)}, u32[]{:S(2)}) copy-start(f32[4,8,2]{2,1,0:T(8,128)S(1)} %reshape_squeeze.7) | copy-start | bytes 772
  18.6 9.5 %copy-start.3 = (f32[4,16,512]{2,1,0:T(8,128)}, f32[4,16,512]{2,1,0:T(8,128)S(1)}, u32[]{:S(2)}) copy-start(f32[4,16,512]{2,1,0:T(8,128)S(1)} %reshape.108.cumr_ref.refs_3_) | copy-start | bytes 393220
  20.7 0.6 copy-start.8
  28.1 5.6 %slice-start = ((bf16[3,4608]{1,0:T(4,128)(2,1)}), bf16[3,4096]{1,0:T(4,128)(2,1)S(1)}, s32[]{:S(2)}) async-start(bf16[3,4608]{1,0:T(4,128)(2,1)} %copy-done.8), calls=%async_computation | async-start | bytes 65536 | tf_op jit(solution)/shard_map/slice | solution.py:185
  28.1 5.6 %copy-start.10 = (f32[1,4096]{1,0:T(1,128)S(1)}, f32[1,4096]{1,0:T(1,128)}, u32[]{:S(2)}) copy-start(f32[1,4096]{1,0:T(1,128)} %get-tuple-element.97) | copy-start | bytes 49156
  28.1 5.6 %copy-start.11 = (f32[1,4096]{1,0:T(1,128)S(1)}, f32[1,4096]{1,0:T(1,128)}, u32[]{:S(2)}) copy-start(f32[1,4096]{1,0:T(1,128)} %get-tuple-element.98) | copy-start | bytes 49156
  28.1 5.6 %copy-start.12 = (f32[1,4096]{1,0:T(1,128)S(1)}, f32[1,4096]{1,0:T(1,128)}, u32[]{:S(2)}) copy-start(f32[1,4096]{1,0:T(1,128)} %get-tuple-element.99) | copy-start | bytes 49156
  28.1 5.6 %copy-start.13 = (f32[1,4096]{1,0:T(1,128)S(1)}, f32[1,4096]{1,0:T(1,128)}, u32[]{:S(2)}) copy-start(f32[1,4096]{1,0:T(1,128)} %get-tuple-element.100) | copy-start | bytes 49156
  28.1 5.6 %copy-start.18 = (f32[4096]{0:T(1024)S(1)}, f32[4096]{0:T(1024)}, u32[]{:S(2)}) copy-start(f32[4096]{0:T(1024)} %param.17) | copy-start | bytes 49156
  33.7 47.6 %collective-permute-start.1 = (f32[2,4,64,512]{3,2,1,0:T(8,128)}, f32[2,4,64,512]{3,2,1,0:T(8,128)S(1)}, u32[]{:S(2)}, u32[]{:S(2)}) collective-permute-start(f32[2,4,64,512]{3,2,1,0:T(8,128)} %bitcast.109), channel_id=1, source_target_pairs={{0,1},{1,0},{2,3},{3,2},{4,5},{5,4},{6,7},{7,6},{8,9},{9,8},{10,11... | collective-permute-start | bytes 3145736 | tf_op jit(solution)/shard_map/ppermute | solution.py:25
  56.5 14.5 %copy-start.9 = (f32[4,8,128]{2,1,0:T(8,128)S(1)}, f32[4,8,128]{2,1,0:T(8,128)}, u32[]{:S(2)}) copy-start(f32[4,8,128]{2,1,0:T(8,128)} %mul.159) | copy-start | bytes 49156
  56.5 16.3 %copy-start.16 = (f32[16,128]{1,0:T(8,128)S(1)}, f32[16,128]{1,0:T(8,128)}, u32[]{:S(2)}) copy-start(f32[16,128]{1,0:T(8,128)} %get-tuple-element.104) | copy-start | bytes 24580
  81.5 2.6 %copy-start.5 = (f32[16,64,128]{2,1,0:T(8,128)S(1)}, f32[16,64,128]{2,1,0:T(8,128)}, u32[]{:S(2)}) copy-start(f32[16,64,128]{2,1,0:T(8,128)} %bitcast_add_fusion) | copy-start | bytes 1572868
  84.1 15.3 %collective-permute-start.2 = (f32[16,64,128]{2,1,0:T(8,128)S(1)}, f32[16,64,128]{2,1,0:T(8,128)S(1)}, u32[]{:S(2)}, u32[]{:S(2)}) collective-permute-start(f32[16,64,128]{2,1,0:T(8,128)S(1)} %copy-done.5), channel_id=1, source_target_pairs={{0,4},{4,8},{8,12},{1,5},{5,9},{9,13},{2,6},{6,10},{10,14},{3,7},{... | collective-permute-start | bytes 1572872 | tf_op jit(solution)/shard_map/ppermute | solution.py:21
  87.6 12.0 %copy-start.15 = (f32[16,128]{1,0:T(8,128)S(1)}, f32[16,128]{1,0:T(8,128)}, u32[]{:S(2)}) copy-start(f32[16,128]{1,0:T(8,128)} %get-tuple-element.103) | copy-start | bytes 24580
  99.7 15.4 %collective-permute-start.3 = (f32[16,64,128]{2,1,0:T(8,128)S(1)}, f32[16,64,128]{2,1,0:T(8,128)S(1)}, u32[]{:S(2)}, u32[]{:S(2)}) collective-permute-start(f32[16,64,128]{2,1,0:T(8,128)S(1)} %fusion.14), channel_id=1, source_target_pairs={{0,4},{4,8},{8,12},{1,5},{5,9},{9,13},{2,6},{6,10},{10,14},{3,7},{... | collective-permute-start | bytes 1572872 | tf_op jit(solution)/shard_map/ppermute | solution.py:21
  104.1 11.1 %copy-start.14 = (f32[16,128]{1,0:T(8,128)S(1)}, f32[16,128]{1,0:T(8,128)}, u32[]{:S(2)}) copy-start(f32[16,128]{1,0:T(8,128)} %get-tuple-element.102) | copy-start | bytes 24580
  115.3 15.1 %collective-permute-start.4 = (f32[16,64,128]{2,1,0:T(8,128)S(1)}, f32[16,64,128]{2,1,0:T(8,128)S(1)}, u32[]{:S(2)}, u32[]{:S(2)}) collective-permute-start(f32[16,64,128]{2,1,0:T(8,128)S(1)} %fusion.12), channel_id=1, source_target_pairs={{0,4},{4,8},{8,12},{1,5},{5,9},{9,13},{2,6},{6,10},{10,14},{3,7},{... | collective-permute-start | bytes 1572872 | tf_op jit(solution)/shard_map/ppermute | solution.py:21
  119.8 16.3 %copy-start.7 = (f32[4,8,2]{2,1,0:T(8,128)S(1)}, f32[4,8,2]{2,1,0:T(8,128)}, u32[]{:S(2)}) copy-start(f32[4,8,2]{2,1,0:T(8,128)} %copy-done.6) | copy-start | bytes 772
  131.4 15.3 %collective-permute-start.5 = (f32[16,64,128]{2,1,0:T(8,128)}, f32[16,64,128]{2,1,0:T(8,128)}, u32[]{:S(2)}, u32[]{:S(2)}) collective-permute-start(f32[16,64,128]{2,1,0:T(8,128)} %fusion.10), channel_id=1, source_target_pairs={{0,4},{4,8},{8,12},{1,5},{5,9},{9,13},{2,6},{6,10},{10,14},{3,7},{... | collective-permute-start | bytes 1572872 | tf_op jit(solution)/shard_map/ppermute | solution.py:21
  136.2 11.7 %copy-start.2 = (f32[8,8,64,128]{3,2,1,0:T(8,128)S(1)}, f32[8,8,64,128]{3,2,1,0:T(8,128)}, u32[]{:S(2)}) copy-start(f32[8,8,64,128]{3,2,1,0:T(8,128)} %shard_map.118) | copy-start | bytes 6291460
  149.1 3.0 %collective-permute-start.6 = (f32[4,8,64,128]{3,2,1,0:T(8,128)}, f32[4,8,64,128]{3,2,1,0:T(8,128)}, u32[]{:S(2)}, u32[]{:S(2)}) collective-permute-start(f32[4,8,64,128]{3,2,1,0:T(8,128)} %fusion.7), channel_id=1, source_target_pairs={{0,1},{1,0},{2,3},{3,2},{4,5},{5,4},{6,7},{7,6},{8,9},{9,8},{10,11... | collective-permute-start | bytes 3145736 | tf_op jit(solution)/shard_map/ppermute | solution.py:25
  155.5 15.3 %copy-start.1 = (f32[2,4,128]{2,1,0:T(4,128)S(1)}, f32[2,4,128]{2,1,0:T(4,128)}, u32[]{:S(2)}) copy-start(f32[2,4,128]{2,1,0:T(4,128)} %param.19) | copy-start | bytes 12292

commit v6 on v5

--- a/solution.py
+++ b/solution.py
@@ -72,7 +72,7 @@
 
 def scan_kernel(xc_ref, ct_ref, b_ref, cumr_ref, cumc_ref, stp_ref, dsk_ref, y_ref, e_ref):
     chunk = pl.program_id(1)
-    block_len = xc_ref.shape[0]
+    block_len = xc_ref.shape[1]
     pairs = e_ref.shape[0]
     heads = 2 * pairs
 
@@ -92,8 +92,8 @@
     left = lax.broadcasted_iota(jnp.int32, (1, 128), 1) < HEAD_DIM
     for pair in range(pairs):
         lanes = slice(pair * 128, (pair + 1) * 128)
-        xp = xc_ref[:, lanes]
-        xs = split(xp)
+        xs = (xc_ref[0, :, lanes], xc_ref[1, :, lanes])
+        xp = xs[0].astype(F32) + xs[1].astype(F32)
         s_old = e_ref[pair]
         ys = []
         us = []
@@ -115,13 +115,32 @@
         )
 
 
+def conv_kernel(flag_ref, rim_ref, x_ref, w_ref, b_ref, all_ref, own_ref):
+    rows = x_ref.shape[0]
+    own = own_ref.shape[1]
+    lead = rim_ref.shape[0] - (CONV_K - 1)
+    padded = jnp.concatenate([rim_ref[...].astype(F32), x_ref[...].astype(F32)], 0)
+    total = b_ref[...] + w_ref[0:1, :] * padded[lead : lead + rows]
+    for tap_index in range(1, CONV_K):
+        total = total + w_ref[tap_index : tap_index + 1, :] * padded[
+            lead + tap_index : lead + tap_index + rows
+        ]
+    high, low = split(total / (1.0 + jnp.exp(-total)))
+    all_ref[0] = high
+    all_ref[1] = low
+    first = flag_ref[0:1, 0:1] > 0.5
+    own_ref[0] = jnp.where(first, high[:own], high[own:])
+    own_ref[1] = jnp.where(first, low[:own], low[own:])
+
+
 def end_kernel(xc_ref, b_ref, wk_ref, e_ref):
     pairs = e_ref.shape[1]
     bm = b_ref[0]
     wk = wk_ref[0]
     left = lax.broadcasted_iota(jnp.int32, (1, 128), 1) < HEAD_DIM
     for pair in range(pairs):
-        xs = split(xc_ref[:, pair * 128 : (pair + 1) * 128])
+        lanes = slice(pair * 128, (pair + 1) * 128)
+        xs = (xc_ref[0, :, lanes], xc_ref[1, :, lanes])
         us = [
             dot3(split(bm * wk[2 * pair + side : 2 * pair + side + 1, :]), xs) for side in range(2)
         ]
@@ -184,8 +203,28 @@
     )
     x_rim = rims[:, :channels]
     bc_rim = rims[:, channels:].transpose(1, 0).reshape(bc_tail.shape)
-    x_pad = jnp.concatenate([x_rim, x_raw], 0)
-    x_all = conv_rows(x_pad, conv_x_w, conv_x_b)
+    rim_block = jnp.concatenate([jnp.zeros((8 - rim_len, channels), x_raw.dtype), x_rim], 0)
+    first_flag = jnp.full((8, 128), sub_index == 0, F32)
+    conv_width = min(512, channels)
+    x_all, x_own = pl.pallas_call(
+        conv_kernel,
+        grid=(channels // conv_width,),
+        in_specs=[
+            pl.BlockSpec((8, 128), lambda i: (0, 0)),
+            pl.BlockSpec((8, conv_width), lambda i: (0, i)),
+            pl.BlockSpec((tokens, conv_width), lambda i: (0, i)),
+            pl.BlockSpec((CONV_K, conv_width), lambda i: (0, i)),
+            pl.BlockSpec((1, conv_width), lambda i: (0, i)),
+        ],
+        out_specs=[
+            pl.BlockSpec((2, tokens, conv_width), lambda i: (0, 0, i)),
+            pl.BlockSpec((2, own, conv_width), lambda i: (0, 0, i)),
+        ],
+        out_shape=[
+            jax.ShapeDtypeStruct((2, tokens, channels), jnp.bfloat16),
+            jax.ShapeDtypeStruct((2, own, channels), jnp.bfloat16),
+        ],
+    )(first_flag, rim_block, x_raw, conv_x_w, conv_x_b[None, :])
     bc_weights = lax.dynamic_slice_in_dim(conv_bc_w, sub_index * half, half, 3)
     bc_bias = lax.dynamic_slice_in_dim(conv_bc_b, sub_index * half, half, 2)
     bc_conv = conv_cols(jnp.concatenate([bc_rim, bc_raw], 3), bc_weights, bc_bias)
@@ -242,7 +281,7 @@
         end_kernel,
         grid=(nsub, set_groups),
         in_specs=[
-            pl.BlockSpec((own, group_width), lambda j, g: (j, g)),
+            pl.BlockSpec((2, own, group_width), lambda j, g: (0, j, g)),
             pl.BlockSpec((1, half, own), lambda j, g: (g, 0, j)),
             pl.BlockSpec((1, per_group, own), lambda j, g: (g, 0, j)),
         ],
@@ -262,13 +301,12 @@
     chip_decay = decay_first * decay_second
     ctx_index = lax.axis_index("ctx")
     ctx_size = lax.axis_size("ctx")
-    x_own = lax.dynamic_slice_in_dim(x_all, sub_index * own, own, 0)
     scan_inputs = (x_own, c_cols, b_rows, cum_rows, cum_cols, step_rows, skip_row)
 
     def scan_group(group, inputs, target):
         extra = {} if target is None else {"input_output_aliases": {len(inputs): 0}}
         in_specs = [
-            pl.BlockSpec((block_len, group_width), lambda g, c: (c, group)),
+            pl.BlockSpec((2, block_len, group_width), lambda g, c: (0, c, group)),
             pl.BlockSpec((1, block_len, state), lambda g, c: (group, c, 0)),
             pl.BlockSpec((1, state, block_len), lambda g, c: (group, 0, c)),
             pl.BlockSpec((1, per_group, block_len), lambda g, c: (group, 0, c)),

time: 172 us -> 195 us (1.13)
  Pallas kernels: 71.9 us -> 106 us
  other arithmetic: 39.4 us -> 20.6 us
  local copies, waits for them, and re-layouts: 33.5 us -> 41.4 us
    pallas_call x0 -> x1, Pallas kernels: none -> 33.7 us  [per_device(): pl.pallas_call(conv_kernel, grid=(channels // conv_width,), in_specs=[pl....]
    mul x1 -> x0, other arithmetic: 22.7 us -> none  [conv_rows(): return jax.nn.silu(total)]
    dynamic_slice x2 -> x0, local copies, waits for them, and re-layouts: 7.61 us -> none  [the longest x1 7.6 us: per_device(): x_own = lax.dynamic_slice_in_dim(x_all, sub_index * own, own, 0)]
    sub x3, local copies, waits for them, and re-layouts: 0.86 us -> 5.39 us  [per_device(): cum_all[..., own - 1:] - cum_all]
    reshape x2, local copies, waits for them, and re-layouts: 0.23 us -> 2.84 us  [per_device(): (cum_all + (jnp.cumsum(all_totals, axis=-1) - all_totals)[..., None]).res...]
  transfers between devices with their start and end apart: 7 -> 7, of which waited for: 3 -> 3; matrix products, arithmetic and copies ran while one was open for 28% -> 19% of each run, Pallas kernels for 33% -> 47%
where the time goes in v6:
time: 195 us; the launch traced here: 193 us
  Pallas kernels  106 us (54%)
  local copies, waits for them, and re-layouts  41.4 us (21%)
  starting transfers between devices  21.8 us (11%)
  other arithmetic  20.6 us (11%)
  waiting for transfers between devices  2.92 us (1%)
    pallas_call x4, Pallas kernels, scan_group(): pl.pallas_call(kernel, grid=(1, blocks), in_specs=in_specs, out_specs=pl....  42.5 us
    pallas_call x1, Pallas kernels, per_device(): pl.pallas_call(conv_kernel, grid=(channels // conv_width,), in_specs=[pl....  33.7 us
    ppermute x5, starting transfers between devices, passed_along(): return lax.ppermute(x, axis, pairs)  21.8 us
    pallas_call x1, Pallas kernels, per_device(): pl.pallas_call(out_kernel, grid=(set_groups, own // out_len), in_specs=[p...  15.3 us
    pallas_call x1, Pallas kernels, per_device(): pl.pallas_call(end_kernel, grid=(nsub, set_groups), in_specs=[pl.BlockSpe...  14.3 us
    sub x3, local copies, waits for them, and re-layouts, per_device(): cum_all[..., own - 1:] - cum_all  5.39 us
    dynamic_slice x1, local copies, waits for them, and re-layouts, per_device(): bc_mine = lax.dynamic_index_in_dim(bc_halves, sub_index, 3, keepdims=False)  4.38 us
  transfers between devices with their start and end apart: 7, of which 3 were waited for; matrix products, arithmetic and copies ran while one was open for 19% of the time, Pallas kernels for 47%

profile of v6, /device:TPU:0, one launch (start us, length us, event | category | flops | bytes accessed | tf_op | source)
XLA Modules:
  0.0 193.5 jit_solution(4641203939548617300)
XLA Ops:
  2.0 4.9 %collective-permute-start = (bf16[3,4608]{1,0:T(4,128)(2,1)S(1)}, bf16[3,4608]{1,0:T(4,128)(2,1)S(1)}, u32[]{:S(2)}, u32[]{:S(2)}) collective-permute-start(bf16[3,4608]{1,0:T(4,128)(2,1)S(1)} %pad_maximum_fusion.3), channel_id=1, source_target_pairs={{0,4},{4,8},{8,12},{1,5},{5,9},{9,13},{2,6},{6,10},{10,14},{3,7},{... | collective-permute-start | bytes 82952 | tf_op jit(solution)/shard_map/ppermute | solution.py:21
  15.9 3.2 %divide_multiply_fusion = f32[2,4,64,1024]{3,2,1,0:T(8,128)S(1)} fusion(bf16[2,4,64,1024]{3,2,1,0:T(8,128)(2,1)S(1)} %copy-done.6, bf16[2,4,64,3]{3,2,1,0:T(8,128)(2,1)} %bitcast.134, f32[2,4,64]{2,1,0:T(4,128)} %get-tuple-element.108, f32[2,4,64]{2,1,0:T(4,128)S(1)} %get-tuple-element.106, f32[2,4,64]{2,1,0:T(4,128)S(1)} %get-tuple-element.107, ...), kind=kLoop, calls=%fused_computation.3 | loop fusion | flops 13107200 | bytes 3159040 | tf_op jit(solution)/shard_map/jit(silu)/mul | solution.py:45
  19.1 2.8 %reshape.105 = f32[2,4,64,2,512]{4,3,2,1,0:T(2,128)} reshape(f32[2,4,64,1024]{3,2,1,0:T(8,128)S(1)} %divide_multiply_fusion) | data formatting | bytes 4194304 | tf_op jit(solution)/shard_map/reshape | solution.py:231
  21.9 4.4 %constant_dynamic-slice_fusion.5 = (f32[2,4,64,1,512]{4,3,2,1,0:T(1,128)S(1)}, f32[2,4,64,1,512]{4,3,2,1,0:T(1,128)S(1)}) fusion(f32[2,4,64,2,512]{4,3,2,1,0:T(2,128)} %reshape.105, s32[]{:T(128)S(6)} %select_n.115, s32[]{:T(128)S(6)} %select_n.116), kind=kLoop, calls=%fused_computation.68 | loop fusion | bytes 4194312 | tf_op jit(solution)/shard_map/jit(dynamic_index_in_dim)/dynamic_slice | solution.py:232
  29.7 1.9 copy.74
  31.6 1.6 sub.38
  33.2 1.9 sub.39
  35.1 1.9 copy.63
  36.9 1.9 reshape.102
  38.8 1.4 broadcast_in_dim.45
  40.2 1.4 mul.114
  43.4 1.4 copy.68
  45.5 1.4 broadcast_in_dim_reshape.2.dsk_ref.refs_6_
  47.0 1.8 exponential_multiply_fusion.wk_ref
  50.8 33.7 %shard_map.118 = (bf16[2,1024,4096]{2,1,0:T(8,128)(2,1)}, bf16[2,512,4096]{2,1,0:T(8,128)(2,1)}) custom-call(f32[8,128]{1,0:T(8,128)} %broadcast_in_dim.46.flag_ref, bf16[8,4096]{1,0:T(8,128)(2,1)} %concatenate.10.rim_ref, bf16[1024,4096]{1,0:T(8,128)(2,1)} %x_ref.1, f32[4,4096]{1,0:T(4,128)} %w_ref.1, f32[1,4096]{1,0:T(1,128)} %bitcast.139), custom_call_target="tpu_custom_call" | custom-call | tf_op jit(solution)/shard_map/pallas_call | solution.py:209
  85.5 14.3 %shard_map.119 = f32[8,8,64,128]{3,2,1,0:T(8,128)} custom-call(bf16[2,1024,4096]{2,1,0:T(8,128)(2,1)} %get-tuple-element.47.xc_ref, f32[4,64,1024]{2,1,0:T(8,128)} %slice_bitcast_fusion.b_ref, f32[4,16,1024]{2,1,0:T(8,128)} %exponential_multiply_fusion.wk_ref), custom_call_target="tpu_custom_call" | custom-call | tf_op jit(solution)/shard_map/pallas_call | solution.py:280
  99.8 1.8 slice_add_fusion
  102.5 1.5 fusion.4
  105.3 1.3 copy.65
  106.6 3.5 %collective-permute-start.2 = (f32[16,64,128]{2,1,0:T(8,128)S(1)}, f32[16,64,128]{2,1,0:T(8,128)S(1)}, u32[]{:S(2)}, u32[]{:S(2)}) collective-permute-start(f32[16,64,128]{2,1,0:T(8,128)S(1)} %copy-done.7), channel_id=1, source_target_pairs={{0,4},{4,8},{8,12},{1,5},{5,9},{9,13},{2,6},{6,10},{10,14},{3,7},{... | collective-permute-start | bytes 1572872 | tf_op jit(solution)/shard_map/ppermute | solution.py:21
  110.1 10.5 %shard_map.120.refs_7_ = f32[512,4096]{1,0:T(8,128)} custom-call(bf16[2,512,4096]{2,1,0:T(8,128)(2,1)} %get-tuple-element.79.xc_ref.refs_0_, f32[4,512,128]{2,1,0:T(8,128)} %bitcast.107, f32[4,128,512]{2,1,0:T(8,128)} %bitcast.118, f32[4,16,512]{2,1,0:T(8,128)} %copy-done.3, f32[4,512,16]{2,1,0:T(8,128)} %bitcast.114, f32[4,16,512]{2,1,0:T(8,128)} %bitcast.129, ...), custom_call_target="tpu_custom_call" | custom-call | tf_op jit(solution)/shard_map/pallas_call | solution.py:322
  120.6 1.3 collective-permute-done.2
  122.2 4.4 %collective-permute-start.3 = (f32[16,64,128]{2,1,0:T(8,128)S(1)}, f32[16,64,128]{2,1,0:T(8,128)S(1)}, u32[]{:S(2)}, u32[]{:S(2)}) collective-permute-start(f32[16,64,128]{2,1,0:T(8,128)S(1)} %fusion.12), channel_id=1, source_target_pairs={{0,4},{4,8},{8,12},{1,5},{5,9},{9,13},{2,6},{6,10},{10,14},{3,7},{... | collective-permute-start | bytes 1572872 | tf_op jit(solution)/shard_map/ppermute | solution.py:21
  126.6 10.5 %shard_map.121.refs_7_ = f32[512,4096]{1,0:T(8,128)} custom-call(bf16[2,512,4096]{2,1,0:T(8,128)(2,1)} %get-tuple-element.79.xc_ref.refs_0_, f32[4,512,128]{2,1,0:T(8,128)} %bitcast.108, f32[4,128,512]{2,1,0:T(8,128)} %bitcast.119, f32[4,16,512]{2,1,0:T(8,128)} %copy-done.3, f32[4,512,16]{2,1,0:T(8,128)} %bitcast.115, ...), custom_call_target="tpu_custom_call", output_to_operand_aliasing={{}: (7, {})} | custom-call | tf_op jit(solution)/shard_map/pallas_call | solution.py:322
  137.8 4.4 %collective-permute-start.4 = (f32[16,64,128]{2,1,0:T(8,128)S(1)}, f32[16,64,128]{2,1,0:T(8,128)S(1)}, u32[]{:S(2)}, u32[]{:S(2)}) collective-permute-start(f32[16,64,128]{2,1,0:T(8,128)S(1)} %fusion.10), channel_id=1, source_target_pairs={{0,4},{4,8},{8,12},{1,5},{5,9},{9,13},{2,6},{6,10},{10,14},{3,7},{... | collective-permute-start | bytes 1572872 | tf_op jit(solution)/shard_map/ppermute | solution.py:21
  142.2 10.8 %shard_map.122.refs_7_ = f32[512,4096]{1,0:T(8,128)} custom-call(bf16[2,512,4096]{2,1,0:T(8,128)(2,1)} %get-tuple-element.79.xc_ref.refs_0_, f32[4,512,128]{2,1,0:T(8,128)} %bitcast.109, f32[4,128,512]{2,1,0:T(8,128)} %bitcast.120, f32[4,16,512]{2,1,0:T(8,128)} %copy-done.3, f32[4,512,16]{2,1,0:T(8,128)} %bitcast.116, ...), custom_call_target="tpu_custom_call", output_to_operand_aliasing={{}: (7, {})} | custom-call | tf_op jit(solution)/shard_map/pallas_call | solution.py:322
  154.0 4.5 %collective-permute-start.5 = (f32[16,64,128]{2,1,0:T(8,128)}, f32[16,64,128]{2,1,0:T(8,128)}, u32[]{:S(2)}, u32[]{:S(2)}) collective-permute-start(f32[16,64,128]{2,1,0:T(8,128)} %fusion.8), channel_id=1, source_target_pairs={{0,4},{4,8},{8,12},{1,5},{5,9},{9,13},{2,6},{6,10},{10,14},{3,7},{... | collective-permute-start | bytes 1572872 | tf_op jit(solution)/shard_map/ppermute | solution.py:21
  158.7 10.7 %shard_map.123.y_ref = f32[512,4096]{1,0:T(8,128)} custom-call(bf16[2,512,4096]{2,1,0:T(8,128)(2,1)} %get-tuple-element.79.xc_ref.refs_0_, f32[4,512,128]{2,1,0:T(8,128)} %bitcast.110, f32[4,128,512]{2,1,0:T(8,128)} %bitcast.121, f32[4,16,512]{2,1,0:T(8,128)} %copy-done.3, f32[4,512,16]{2,1,0:T(8,128)} %bitcast.117, ...), custom_call_target="tpu_custom_call", output_to_operand_aliasing={{}: (7, {})} | custom-call | tf_op jit(solution)/shard_map/pallas_call | solution.py:322
  172.3 1.3 copy.70
  174.8 1.6 select_bitcast_fusion.1
  176.7 1.5 copy.71
  178.2 15.3 %shard_map.124 = bf16[512,4096]{1,0:T(8,128)(2,1)} custom-call(f32[512,4096]{1,0:T(8,128)} %shard_map.123.y_ref, f32[4,512,128]{2,1,0:T(8,128)} %bitcast.111, f32[4,512,16]{2,1,0:T(8,128)} %bitcast.127, f32[4,8,128,128]{3,2,1,0:T(8,128)} %bitcast.126, bf16[512,4096]{1,0:T(8,128)(2,1)} %z_ref.1, f32[1,4096]{1,0:T(1,128)} %bitcast.141), custom_call_target="tpu_custom_call" | custom-call | tf_op jit(solution)/shard_map/pallas_call | solution.py:374
  (101 shorter events, 28.2 us)
Async XLA Ops:
  0.0 13.4 %copy-start = (f32[2,4,128]{2,1,0:T(4,128)S(1)}, f32[2,4,128]{2,1,0:T(4,128)}, u32[]{:S(2)}) copy-start(f32[2,4,128]{2,1,0:T(4,128)} %param.19) | copy-start | bytes 12292
  2.0 13.1 %collective-permute-start = (bf16[3,4608]{1,0:T(4,128)(2,1)S(1)}, bf16[3,4608]{1,0:T(4,128)(2,1)S(1)}, u32[]{:S(2)}, u32[]{:S(2)}) collective-permute-start(bf16[3,4608]{1,0:T(4,128)(2,1)S(1)} %pad_maximum_fusion.3), channel_id=1, source_target_pairs={{0,4},{4,8},{8,12},{1,5},{5,9},{9,13},{2,6},{6,10},{10,14},{3,7},{... | collective-permute-start | bytes 82952 | tf_op jit(solution)/shard_map/ppermute | solution.py:21
  8.8 3.9 %copy-start.17 = (f32[4,2,4,128]{3,2,1,0:T(4,128)S(1)}, f32[4,2,4,128]{3,2,1,0:T(4,128)}, u32[]{:S(2)}) copy-start(f32[4,2,4,128]{3,2,1,0:T(4,128)} %param.18) | copy-start | bytes 49156
  8.8 7.1 %copy-start.6 = (bf16[2,4,64,1024]{3,2,1,0:T(8,128)(2,1)S(1)}, bf16[2,4,64,1024]{3,2,1,0:T(8,128)(2,1)}, u32[]{:S(2)}) copy-start(bf16[2,4,64,1024]{3,2,1,0:T(8,128)(2,1)} %param.13) | copy-start | bytes 3145732
  12.7 29.0 %copy-start.4 = (f32[64,2,256]{2,0,1:T(8,128)}, f32[64,2,256]{2,0,1:T(8,128)S(1)}, u32[]{:S(2)}) copy-start(f32[64,2,256]{2,0,1:T(8,128)S(1)} %fusion.18) | copy-start | bytes 393220
  14.2 1.8 copy-start.10
  14.3 1.6 copy-start.8
  15.1 0.8 copy-start.13
  26.3 1.1 copy-start.11
  27.4 75.1 %collective-permute-start.1 = (f32[2,4,64,512]{3,2,1,0:T(8,128)}, f32[2,4,64,512]{3,2,1,0:T(8,128)}, u32[]{:S(2)}, u32[]{:S(2)}) collective-permute-start(f32[2,4,64,512]{3,2,1,0:T(8,128)} %bitcast.106), channel_id=1, source_target_pairs={{0,1},{1,0},{2,3},{3,2},{4,5},{5,4},{6,7},{7,6},{8,9},{9,8},{10,11... | collective-permute-start | bytes 3145736 | tf_op jit(solution)/shard_map/ppermute | solution.py:25
  28.0 16.9 %copy-start.18 = (f32[64]{0:T(128)S(1)}, f32[64]{0:T(128)}, u32[]{:S(2)}) copy-start(f32[64]{0:T(128)} %param.22) | copy-start | bytes 772
  43.4 41.0 %copy-start.3 = (f32[4,16,512]{2,1,0:T(8,128)}, f32[4,16,512]{2,1,0:T(8,128)S(1)}, u32[]{:S(2)}) copy-start(f32[4,16,512]{2,1,0:T(8,128)S(1)} %reshape.107.cumr_ref.refs_3_) | copy-start | bytes 393220
  85.5 14.3 %copy-start.12 = (f32[4,8,128]{2,1,0:T(8,128)S(1)}, f32[4,8,128]{2,1,0:T(8,128)}, u32[]{:S(2)}) copy-start(f32[4,8,128]{2,1,0:T(8,128)} %mul.114) | copy-start | bytes 49156
  99.8 1.8 copy-start.16
  105.3 1.3 copy-start.7
  106.6 15.3 %collective-permute-start.2 = (f32[16,64,128]{2,1,0:T(8,128)S(1)}, f32[16,64,128]{2,1,0:T(8,128)S(1)}, u32[]{:S(2)}, u32[]{:S(2)}) collective-permute-start(f32[16,64,128]{2,1,0:T(8,128)S(1)} %copy-done.7), channel_id=1, source_target_pairs={{0,4},{4,8},{8,12},{1,5},{5,9},{9,13},{2,6},{6,10},{10,14},{3,7},{... | collective-permute-start | bytes 1572872 | tf_op jit(solution)/shard_map/ppermute | solution.py:21
  120.6 1.5 copy-start.15
  122.2 15.5 %collective-permute-start.3 = (f32[16,64,128]{2,1,0:T(8,128)S(1)}, f32[16,64,128]{2,1,0:T(8,128)S(1)}, u32[]{:S(2)}, u32[]{:S(2)}) collective-permute-start(f32[16,64,128]{2,1,0:T(8,128)S(1)} %fusion.12), channel_id=1, source_target_pairs={{0,4},{4,8},{8,12},{1,5},{5,9},{9,13},{2,6},{6,10},{10,14},{3,7},{... | collective-permute-start | bytes 1572872 | tf_op jit(solution)/shard_map/ppermute | solution.py:21
  126.6 11.1 %copy-start.14 = (f32[16,128]{1,0:T(8,128)S(1)}, f32[16,128]{1,0:T(8,128)}, u32[]{:S(2)}) copy-start(f32[16,128]{1,0:T(8,128)} %get-tuple-element.102) | copy-start | bytes 24580
  137.8 15.2 %collective-permute-start.4 = (f32[16,64,128]{2,1,0:T(8,128)S(1)}, f32[16,64,128]{2,1,0:T(8,128)S(1)}, u32[]{:S(2)}, u32[]{:S(2)}) collective-permute-start(f32[16,64,128]{2,1,0:T(8,128)S(1)} %fusion.10), channel_id=1, source_target_pairs={{0,4},{4,8},{8,12},{1,5},{5,9},{9,13},{2,6},{6,10},{10,14},{3,7},{... | collective-permute-start | bytes 1572872 | tf_op jit(solution)/shard_map/ppermute | solution.py:21
  153.0 5.5 %copy-start.9 = (f32[4,8,2]{2,1,0:T(8,128)S(1)}, f32[4,8,2]{2,1,0:T(8,128)}, u32[]{:S(2)}) copy-start(f32[4,8,2]{2,1,0:T(8,128)} %copy-done.8) | copy-start | bytes 772
  154.0 15.4 %collective-permute-start.5 = (f32[16,64,128]{2,1,0:T(8,128)}, f32[16,64,128]{2,1,0:T(8,128)}, u32[]{:S(2)}, u32[]{:S(2)}) collective-permute-start(f32[16,64,128]{2,1,0:T(8,128)} %fusion.8), channel_id=1, source_target_pairs={{0,4},{4,8},{8,12},{1,5},{5,9},{9,13},{2,6},{6,10},{10,14},{3,7},{... | collective-permute-start | bytes 1572872 | tf_op jit(solution)/shard_map/ppermute | solution.py:21
  158.7 11.9 %copy-start.2 = (f32[8,8,64,128]{3,2,1,0:T(8,128)S(1)}, f32[8,8,64,128]{3,2,1,0:T(8,128)}, u32[]{:S(2)}) copy-start(f32[8,8,64,128]{3,2,1,0:T(8,128)} %shard_map.119) | copy-start | bytes 6291460
  169.4 2.4 %copy-start.5 = (f32[64,2,256]{2,0,1:T(8,128)S(1)}, f32[64,2,256]{2,0,1:T(8,128)}, u32[]{:S(2)}) copy-start(f32[64,2,256]{2,0,1:T(8,128)} %copy-done.4) | copy-start | bytes 393220
  171.8 3.0 %collective-permute-start.6 = (f32[4,8,64,128]{3,2,1,0:T(8,128)}, f32[4,8,64,128]{3,2,1,0:T(8,128)}, u32[]{:S(2)}, u32[]{:S(2)}) collective-permute-start(f32[4,8,64,128]{3,2,1,0:T(8,128)} %fusion.5), channel_id=1, source_target_pairs={{0,1},{1,0},{2,3},{3,2},{4,5},{5,4},{6,7},{7,6},{8,9},{9,8},{10,11... | collective-permute-start | bytes 3145736 | tf_op jit(solution)/shard_map/ppermute | solution.py:25
  178.2 15.3 %copy-start.1 = (f32[2,4,128]{2,1,0:T(4,128)S(1)}, f32[2,4,128]{2,1,0:T(4,128)}, u32[]{:S(2)}) copy-start(f32[2,4,128]{2,1,0:T(4,128)} %param.19) | copy-start | bytes 12292

commit v7 on v5

--- a/solution.py
+++ b/solution.py
@@ -185,7 +185,14 @@
     x_rim = rims[:, :channels]
     bc_rim = rims[:, channels:].transpose(1, 0).reshape(bc_tail.shape)
     x_pad = jnp.concatenate([x_rim, x_raw], 0)
-    x_all = conv_rows(x_pad, conv_x_w, conv_x_b)
+    x_own = conv_rows(
+        lax.dynamic_slice_in_dim(x_pad, sub_index * own, own + rim_len, 0), conv_x_w, conv_x_b
+    )
+    x_other = conv_rows(
+        lax.dynamic_slice_in_dim(x_pad, (1 - sub_index) * own, own + rim_len, 0),
+        conv_x_w,
+        conv_x_b,
+    )
     bc_weights = lax.dynamic_slice_in_dim(conv_bc_w, sub_index * half, half, 3)
     bc_bias = lax.dynamic_slice_in_dim(conv_bc_b, sub_index * half, half, 2)
     bc_conv = conv_cols(jnp.concatenate([bc_rim, bc_raw], 3), bc_weights, bc_bias)
@@ -209,7 +216,7 @@
     half_totals = jnp.exp(log_decay.reshape(heads_dev, nsub, own).sum(-1))
     step_own = lax.dynamic_slice_in_dim(step_sizes, sub_index * own, own, 1)
     decay_own = lax.dynamic_slice_in_dim(log_decay, sub_index * own, own, 1)
-    block_len = min(256, own)
+    block_len = min(128, own)
     blocks = own // block_len
     upper = (
         lax.broadcasted_iota(jnp.int32, (block_len, block_len), 0)
@@ -238,31 +245,38 @@
     )
     to_end = jnp.exp(cum_all[..., own - 1 :] - cum_all) * step_sizes.reshape(heads_dev, nsub, own)
     to_end = to_end.reshape(set_groups, per_group, tokens)
-    ends = pl.pallas_call(
-        end_kernel,
-        grid=(nsub, set_groups),
-        in_specs=[
-            pl.BlockSpec((own, group_width), lambda j, g: (j, g)),
-            pl.BlockSpec((1, half, own), lambda j, g: (g, 0, j)),
-            pl.BlockSpec((1, per_group, own), lambda j, g: (g, 0, j)),
-        ],
-        out_specs=pl.BlockSpec((1, pairs, half, 128), lambda j, g: (j * set_groups + g, 0, 0, 0)),
-        out_shape=jax.ShapeDtypeStruct((nsub * set_groups, pairs, half, 128), F32),
-    )(x_all, bc_conv[0], to_end)
-    ends = ends.reshape(nsub, set_groups, pairs, half, 128)
+
+    def end_states(x_half, at):
+        return pl.pallas_call(
+            end_kernel,
+            grid=(set_groups,),
+            in_specs=[
+                pl.BlockSpec((own, group_width), lambda g: (0, g)),
+                pl.BlockSpec((1, half, own), lambda g: (g, 0, 0)),
+                pl.BlockSpec((1, per_group, own), lambda g: (g, 0, 0)),
+            ],
+            out_specs=pl.BlockSpec((1, pairs, half, 128), lambda g: (g, 0, 0, 0)),
+            out_shape=jax.ShapeDtypeStruct((set_groups, pairs, half, 128), F32),
+        )(
+            x_half,
+            lax.dynamic_slice_in_dim(bc_conv[0], at * own, own, 2),
+            lax.dynamic_slice_in_dim(to_end, at * own, own, 2),
+        )
+
+    own_end = end_states(x_own, sub_index)
+    other_end = end_states(x_other, 1 - sub_index)
 
     def pair_layout(values):
         return jnp.repeat(values.reshape(set_groups, pairs, 2), HEAD_DIM, axis=-1)[:, :, None, :]
 
     decay_first = pair_layout(half_totals[:, 0])
     decay_second = pair_layout(half_totals[:, 1])
-    first_end = ends[0]
-    second_end = ends[1]
+    first_end = jnp.where(sub_index == 0, own_end, other_end)
+    second_end = jnp.where(sub_index == 0, other_end, own_end)
     chip_end = decay_second * first_end + second_end
     chip_decay = decay_first * decay_second
     ctx_index = lax.axis_index("ctx")
     ctx_size = lax.axis_size("ctx")
-    x_own = lax.dynamic_slice_in_dim(x_all, sub_index * own, own, 0)
     scan_inputs = (x_own, c_cols, b_rows, cum_rows, cum_cols, step_rows, skip_row)
 
     def scan_group(group, inputs, target):

time: 172 us -> 165 us (0.959)
  Pallas kernels: 71.9 us -> 62.9 us
  local copies, waits for them, and re-layouts: 33.5 us -> 25.2 us
  waiting for transfers between devices: 2.92 us -> 10.3 us
  starting transfers between devices: 21.9 us -> 25.8 us
    pallas_call x4, Pallas kernels: 42.1 us -> 31 us  [scan_group(): pl.pallas_call(kernel, grid=(1, blocks), in_specs=in_specs, out_specs=pl....]
    mul x1, other arithmetic: 22.7 us -> 12.4 us  [conv_rows(): return jax.nn.silu(total)]
    ppermute x5, waiting for transfers between devices: 1.76 us -> 9.14 us  [passed_along(): return lax.ppermute(x, axis, pairs)]
    dynamic_slice x2, local copies, waits for them, and re-layouts: 7.61 us -> 1.85 us  [the longest x1 1.11 us: end_states(): lax.dynamic_slice_in_dim(bc_conv[0], at * own, own, 2)]
    concatenate x0 -> x1, other arithmetic: none -> 5 us  [per_device(): x_pad = jnp.concatenate([x_rim, x_raw], 0)]
    ppermute x5, starting transfers between devices: 21.9 us -> 25.8 us  [passed_along(): return lax.ppermute(x, axis, pairs)]
    select_n x4, other arithmetic: 1.42 us -> 3.56 us  [per_device(): received = jnp.where(valid, updated, received)]
    pallas_call x1 -> x2, Pallas kernels: 14.5 us -> 16.6 us  [end_states(): pl.pallas_call(end_kernel, grid=(set_groups,), in_specs=[pl.BlockSpec((ow...]
  transfers between devices with their start and end apart: 7 -> 7, of which waited for: 3 -> 5; matrix products, arithmetic and copies ran while one was open for 28% -> 21% of each run, Pallas kernels for 33% -> 29%
where the time goes in v7:
time: 165 us; the launch traced here: 164 us
  Pallas kernels  62.9 us (38%)
  other arithmetic  38.5 us (23%)
  starting transfers between devices  25.8 us (16%)
  local copies, waits for them, and re-layouts  25.2 us (15%)
  waiting for transfers between devices  10.3 us (6%)
    pallas_call x4, Pallas kernels, scan_group(): pl.pallas_call(kernel, grid=(1, blocks), in_specs=in_specs, out_specs=pl....  31 us
    ppermute x5, starting transfers between devices, passed_along(): return lax.ppermute(x, axis, pairs)  25.8 us
    pallas_call x2, Pallas kernels, end_states(): pl.pallas_call(end_kernel, grid=(set_groups,), in_specs=[pl.BlockSpec((ow...  16.6 us
    pallas_call x1, Pallas kernels, per_device(): pl.pallas_call(out_kernel, grid=(set_groups, own // out_len), in_specs=[p...  15.3 us
    mul x1, other arithmetic, conv_rows(): return jax.nn.silu(total)  12.4 us
    ppermute x5, waiting for transfers between devices, passed_along(): return lax.ppermute(x, axis, pairs)  9.14 us
    concatenate x1, other arithmetic, per_device(): x_pad = jnp.concatenate([x_rim, x_raw], 0)  5 us
    dynamic_slice x1, local copies, waits for them, and re-layouts, per_device(): bc_mine = lax.dynamic_index_in_dim(bc_halves, sub_index, 3, keepdims=False)  4.38 us
  transfers between devices with their start and end apart: 7, of which 5 were waited for; matrix products, arithmetic and copies ran while one was open for 21% of the time, Pallas kernels for 29%

profile of v7, /device:TPU:0, one launch (start us, length us, event | category | flops | bytes accessed | tf_op | source)
XLA Modules:
  0.0 163.8 jit_solution(15170903756636369035)
XLA Ops:
  2.1 4.9 %collective-permute-start = (bf16[3,4608]{1,0:T(4,128)(2,1)S(1)}, bf16[3,4608]{1,0:T(4,128)(2,1)S(1)}, u32[]{:S(2)}, u32[]{:S(2)}) collective-permute-start(bf16[3,4608]{1,0:T(4,128)(2,1)S(1)} %pad_maximum_fusion.3), channel_id=1, source_target_pairs={{0,4},{4,8},{8,12},{1,5},{5,9},{9,13},{2,6},{6,10},{10,14},{3,7},{... | collective-permute-start | bytes 82952 | tf_op jit(solution)/shard_map/ppermute | solution.py:21
  7.7 1.2 broadcast_multiply_fusion
  17.4 1.3 copy.74
  20.1 2.9 %divide_multiply_fusion.2 = f32[2,4,64,1024]{3,2,1,0:T(8,128)S(1)} fusion(bf16[2,4,64,1024]{3,2,1,0:T(8,128)(2,1)S(1)} %copy-done.5, bf16[2,4,64,3]{3,2,1,0:T(8,128)(2,1)S(1)} %bitcast.143, f32[2,4,64]{2,1,0:T(4,128)} %get-tuple-element.116, f32[2,4,64]{2,1,0:T(4,128)} %get-tuple-element.114, f32[2,4,64]{2,1,0:T(4,128)} %get-tuple-element.115, ...), kind=kLoop, calls=%fused_computation.11 | loop fusion | flops 13107200 | bytes 3159040 | tf_op jit(solution)/shard_map/jit(silu)/mul | solution.py:45
  23.1 2.8 %reshape.103 = f32[2,4,64,2,512]{4,3,2,1,0:T(2,128)} reshape(f32[2,4,64,1024]{3,2,1,0:T(8,128)S(1)} %divide_multiply_fusion.2) | data formatting | bytes 4194304 | tf_op jit(solution)/shard_map/reshape | solution.py:199
  25.9 4.4 %constant_dynamic-slice_fusion.7 = (f32[2,4,64,1,512]{4,3,2,1,0:T(1,128)S(1)}, f32[2,4,64,1,512]{4,3,2,1,0:T(1,128)S(1)}) fusion(f32[2,4,64,2,512]{4,3,2,1,0:T(2,128)} %reshape.103, s32[]{:T(128)S(6)} %select_n.142, s32[]{:T(128)S(6)} %select_n.143), kind=kLoop, calls=%fused_computation.77 | loop fusion | bytes 4194312 | tf_op jit(solution)/shard_map/jit(dynamic_index_in_dim)/dynamic_slice | solution.py:200
  31.4 5.0 %fusion.1 = (bf16[515,4096]{1,0:T(8,128)(2,1)S(1)}, bf16[515,4096]{1,0:T(8,128)(2,1)S(1)}) fusion(s32[]{:T(128)S(6)} %select_n.133, bf16[1024,4096]{1,0:T(8,128)(2,1)} %param.12, bf16[3,4096]{1,0:T(4,128)(2,1)S(1)} %slice-done, s32[]{:T(128)S(6)} %select_n.136), kind=kLoop, calls=%fused_computation.7 | loop fusion | flops 16875520 | bytes 16850952 | tf_op jit(solution)/shard_map/concatenate | solution.py:187
  36.4 12.4 %divide_multiply_fusion.1 = (f32[512,4096]{1,0:T(8,128)}, f32[512,4096]{1,0:T(8,128)}) fusion(bf16[515,4096]{1,0:T(8,128)(2,1)S(1)} %get-tuple-element.91, f32[4096]{0:T(1024)S(1)} %bitcast.148, f32[4096]{0:T(1024)S(1)} %bitcast.149, f32[4096]{0:T(1024)S(1)} %bitcast.147, f32[4096]{0:T(1024)S(1)} %bitcast.146, f32[4096]{0:T(1024)S(1)} %copy-done.18, ...), kind=kLoop, calls=%fused_computation.3 | loop fusion | flops 67108864 | bytes 50413568 | tf_op jit(solution)/shard_map/jit(silu)/mul | solution.py:35
  50.0 8.3 %shard_map.119 = f32[4,8,64,128]{3,2,1,0:T(8,128)} custom-call(f32[512,4096]{1,0:T(8,128)} %get-tuple-element.104.xc_ref, f32[4,64,512]{2,1,0:T(8,128)} %get-tuple-element.100.b_ref, f32[4,16,512]{2,1,0:T(8,128)} %get-tuple-element.102.wk_ref), custom_call_target="tpu_custom_call" | custom-call | tf_op jit(solution)/shard_map/pallas_call | solution.py:250
  58.3 8.4 %shard_map.118 = f32[4,8,64,128]{3,2,1,0:T(8,128)} custom-call(f32[512,4096]{1,0:T(8,128)} %get-tuple-element.75.xc_ref.refs_0_, f32[4,64,512]{2,1,0:T(8,128)} %get-tuple-element.99.b_ref, f32[4,16,512]{2,1,0:T(8,128)} %get-tuple-element.101.wk_ref), custom_call_target="tpu_custom_call" | custom-call | tf_op jit(solution)/shard_map/pallas_call | solution.py:250
  66.6 1.5 select_add_fusion
  69.0 1.5 select_bitcast_fusion.2
  70.5 1.2 pad_maximum_fusion.1
  71.7 1.3 copy.71
  73.0 4.3 %collective-permute-start.2 = (f32[16,64,128]{2,1,0:T(8,128)}, f32[16,64,128]{2,1,0:T(8,128)}, u32[]{:S(2)}, u32[]{:S(2)}) collective-permute-start(f32[16,64,128]{2,1,0:T(8,128)} %bitcast_add_fusion), channel_id=1, source_target_pairs={{0,4},{4,8},{8,12},{1,5},{5,9},{9,13},{2,6},{6,10},{10,14},{3,7},{... | collective-permute-start | bytes 1572872 | tf_op jit(solution)/shard_map/ppermute | solution.py:21
  77.3 7.7 %shard_map.120.refs_7_ = f32[512,4096]{1,0:T(8,128)} custom-call(f32[512,4096]{1,0:T(8,128)} %get-tuple-element.75.xc_ref.refs_0_, f32[4,512,128]{2,1,0:T(8,128)} %bitcast.116, f32[4,128,512]{2,1,0:T(8,128)} %bitcast.127, f32[4,16,512]{2,1,0:T(8,128)} %copy-done.4, f32[4,512,16]{2,1,0:T(8,128)} %bitcast.123, f32[4,16,512]{2,1,0:T(8,128)} %bitcast.138, ...), custom_call_target="tpu_custom_call" | custom-call | tf_op jit(solution)/shard_map/pallas_call | solution.py:298
  85.0 3.6 %collective-permute-done.2 = f32[16,64,128]{2,1,0:T(8,128)} collective-permute-done((f32[16,64,128]{2,1,0:T(8,128)}, f32[16,64,128]{2,1,0:T(8,128)}, u32[]{:S(2)}, u32[]{:S(2)}) %collective-permute-start.2) | collective-permute-done | bytes 524320 | tf_op jit(solution)/shard_map/ppermute | solution.py:21
  89.7 6.2 %collective-permute-start.3 = (f32[16,64,128]{2,1,0:T(8,128)}, f32[16,64,128]{2,1,0:T(8,128)}, u32[]{:S(2)}, u32[]{:S(2)}) collective-permute-start(f32[16,64,128]{2,1,0:T(8,128)} %fusion.12), channel_id=1, source_target_pairs={{0,4},{4,8},{8,12},{1,5},{5,9},{9,13},{2,6},{6,10},{10,14},{3,7},{... | collective-permute-start | bytes 1572872 | tf_op jit(solution)/shard_map/ppermute | solution.py:21
  95.9 7.7 %shard_map.121.refs_7_ = f32[512,4096]{1,0:T(8,128)} custom-call(f32[512,4096]{1,0:T(8,128)} %get-tuple-element.75.xc_ref.refs_0_, f32[4,512,128]{2,1,0:T(8,128)} %bitcast.117, f32[4,128,512]{2,1,0:T(8,128)} %bitcast.128, f32[4,16,512]{2,1,0:T(8,128)} %copy-done.4, f32[4,512,16]{2,1,0:T(8,128)} %bitcast.124, ...), custom_call_target="tpu_custom_call", output_to_operand_aliasing={{}: (7, {})} | custom-call | tf_op jit(solution)/shard_map/pallas_call | solution.py:298
  103.7 2.8 %collective-permute-done.3 = f32[16,64,128]{2,1,0:T(8,128)} collective-permute-done((f32[16,64,128]{2,1,0:T(8,128)}, f32[16,64,128]{2,1,0:T(8,128)}, u32[]{:S(2)}, u32[]{:S(2)}) %collective-permute-start.3) | collective-permute-done | bytes 524320 | tf_op jit(solution)/shard_map/ppermute | solution.py:21
  108.6 5.2 %collective-permute-start.4 = (f32[16,64,128]{2,1,0:T(8,128)}, f32[16,64,128]{2,1,0:T(8,128)}, u32[]{:S(2)}, u32[]{:S(2)}) collective-permute-start(f32[16,64,128]{2,1,0:T(8,128)} %fusion.10), channel_id=1, source_target_pairs={{0,4},{4,8},{8,12},{1,5},{5,9},{9,13},{2,6},{6,10},{10,14},{3,7},{... | collective-permute-start | bytes 1572872 | tf_op jit(solution)/shard_map/ppermute | solution.py:21
  113.7 7.7 %shard_map.122.refs_7_ = f32[512,4096]{1,0:T(8,128)} custom-call(f32[512,4096]{1,0:T(8,128)} %get-tuple-element.75.xc_ref.refs_0_, f32[4,512,128]{2,1,0:T(8,128)} %bitcast.118, f32[4,128,512]{2,1,0:T(8,128)} %bitcast.129, f32[4,16,512]{2,1,0:T(8,128)} %copy-done.4, f32[4,512,16]{2,1,0:T(8,128)} %bitcast.125, ...), custom_call_target="tpu_custom_call", output_to_operand_aliasing={{}: (7, {})} | custom-call | tf_op jit(solution)/shard_map/pallas_call | solution.py:298
  121.5 1.9 %collective-permute-done.4 = f32[16,64,128]{2,1,0:T(8,128)} collective-permute-done((f32[16,64,128]{2,1,0:T(8,128)}, f32[16,64,128]{2,1,0:T(8,128)}, u32[]{:S(2)}, u32[]{:S(2)}) %collective-permute-start.4) | collective-permute-done | bytes 524320 | tf_op jit(solution)/shard_map/ppermute | solution.py:21
  125.5 5.2 %collective-permute-start.5 = (f32[16,64,128]{2,1,0:T(8,128)}, f32[16,64,128]{2,1,0:T(8,128)}, u32[]{:S(2)}, u32[]{:S(2)}) collective-permute-start(f32[16,64,128]{2,1,0:T(8,128)} %fusion.8), channel_id=1, source_target_pairs={{0,4},{4,8},{8,12},{1,5},{5,9},{9,13},{2,6},{6,10},{10,14},{3,7},{... | collective-permute-start | bytes 1572872 | tf_op jit(solution)/shard_map/ppermute | solution.py:21
  130.8 7.8 %shard_map.123.y_ref = f32[512,4096]{1,0:T(8,128)} custom-call(f32[512,4096]{1,0:T(8,128)} %get-tuple-element.75.xc_ref.refs_0_, f32[4,512,128]{2,1,0:T(8,128)} %bitcast.119, f32[4,128,512]{2,1,0:T(8,128)} %bitcast.130, f32[4,16,512]{2,1,0:T(8,128)} %copy-done.4, f32[4,512,16]{2,1,0:T(8,128)} %bitcast.126, ...), custom_call_target="tpu_custom_call", output_to_operand_aliasing={{}: (7, {})} | custom-call | tf_op jit(solution)/shard_map/pallas_call | solution.py:298
  139.4 1.2 fusion.7
  140.6 1.3 fusion.5
  142.4 1.3 copy.76
  143.7 1.2 collective-permute-done.6
  145.4 1.4 select_bitcast_fusion
  147.0 1.5 copy.77
  148.5 15.3 %shard_map.124 = bf16[512,4096]{1,0:T(8,128)(2,1)} custom-call(f32[512,4096]{1,0:T(8,128)} %shard_map.123.y_ref, f32[4,512,128]{2,1,0:T(8,128)} %bitcast.120, f32[4,512,16]{2,1,0:T(8,128)} %bitcast.136, f32[4,8,128,128]{3,2,1,0:T(8,128)} %bitcast.135, bf16[512,4096]{1,0:T(8,128)(2,1)} %z_ref.1, f32[1,4096]{1,0:T(1,128)} %bitcast.151), custom_call_target="tpu_custom_call" | custom-call | tf_op jit(solution)/shard_map/pallas_call | solution.py:350
  (109 shorter events, 22.8 us)
Async XLA Ops:
  0.0 15.8 %copy-start = (f32[2,4,128]{2,1,0:T(4,128)S(1)}, f32[2,4,128]{2,1,0:T(4,128)}, u32[]{:S(2)}) copy-start(f32[2,4,128]{2,1,0:T(4,128)} %param.19) | copy-start | bytes 12292
  0.0 10.1 %copy-start.14 = (f32[4,4096]{1,0:T(4,128)S(1)}, f32[4,4096]{1,0:T(4,128)}, u32[]{:S(2)}) copy-start(f32[4,4096]{1,0:T(4,128)} %param.16) | copy-start | bytes 196612
  2.1 17.5 %collective-permute-start = (bf16[3,4608]{1,0:T(4,128)(2,1)S(1)}, bf16[3,4608]{1,0:T(4,128)(2,1)S(1)}, u32[]{:S(2)}, u32[]{:S(2)}) collective-permute-start(bf16[3,4608]{1,0:T(4,128)(2,1)S(1)} %pad_maximum_fusion.3), channel_id=1, source_target_pairs={{0,4},{4,8},{8,12},{1,5},{5,9},{9,13},{2,6},{6,10},{10,14},{3,7},{... | collective-permute-start | bytes 82952 | tf_op jit(solution)/shard_map/ppermute | solution.py:21
  7.7 6.8 %copy-start.19 = (f32[4,2,4,128]{3,2,1,0:T(4,128)S(1)}, f32[4,2,4,128]{3,2,1,0:T(4,128)}, u32[]{:S(2)}) copy-start(f32[4,2,4,128]{3,2,1,0:T(4,128)} %param.18) | copy-start | bytes 49156
  9.6 9.2 %copy-start.20 = (f32[64]{0:T(128)S(1)}, f32[64]{0:T(128)}, u32[]{:S(2)}) copy-start(f32[64]{0:T(128)} %param.22) | copy-start | bytes 772
  9.6 10.5 %copy-start.5 = (bf16[2,4,64,1024]{3,2,1,0:T(8,128)(2,1)S(1)}, bf16[2,4,64,1024]{3,2,1,0:T(8,128)(2,1)}, u32[]{:S(2)}) copy-start(bf16[2,4,64,1024]{3,2,1,0:T(8,128)(2,1)} %param.13) | copy-start | bytes 3145732
  12.6 1.1 copy-start.6
  17.4 8.5 %copy-start.4 = (f32[4,16,512]{2,1,0:T(8,128)}, f32[4,16,512]{2,1,0:T(8,128)S(1)}, u32[]{:S(2)}) copy-start(f32[4,16,512]{2,1,0:T(8,128)S(1)} %reshape.105.cumr_ref.refs_3_) | copy-start | bytes 393220
  19.5 0.6 copy-start.8
  23.1 8.3 %slice-start = ((bf16[3,4608]{1,0:T(4,128)(2,1)}), bf16[3,4096]{1,0:T(4,128)(2,1)S(1)}, s32[]{:S(2)}) async-start(bf16[3,4608]{1,0:T(4,128)(2,1)} %copy-done.8), calls=%async_computation | async-start | bytes 65536 | tf_op jit(solution)/shard_map/slice | solution.py:185
  31.3 37.7 %collective-permute-start.1 = (f32[2,4,64,512]{3,2,1,0:T(8,128)}, f32[2,4,64,512]{3,2,1,0:T(8,128)}, u32[]{:S(2)}, u32[]{:S(2)}) collective-permute-start(f32[2,4,64,512]{3,2,1,0:T(8,128)} %bitcast.115), channel_id=1, source_target_pairs={{0,1},{1,0},{2,3},{3,2},{4,5},{5,4},{6,7},{7,6},{8,9},{9,8},{10,11... | collective-permute-start | bytes 3145736 | tf_op jit(solution)/shard_map/ppermute | solution.py:25
  31.3 5.0 %copy-start.10 = (f32[1,4096]{1,0:T(1,128)S(1)}, f32[1,4096]{1,0:T(1,128)}, u32[]{:S(2)}) copy-start(f32[1,4096]{1,0:T(1,128)} %get-tuple-element.105) | copy-start | bytes 49156
  31.3 5.1 %copy-start.11 = (f32[1,4096]{1,0:T(1,128)S(1)}, f32[1,4096]{1,0:T(1,128)}, u32[]{:S(2)}) copy-start(f32[1,4096]{1,0:T(1,128)} %get-tuple-element.106) | copy-start | bytes 49156
  31.3 5.1 %copy-start.12 = (f32[1,4096]{1,0:T(1,128)S(1)}, f32[1,4096]{1,0:T(1,128)}, u32[]{:S(2)}) copy-start(f32[1,4096]{1,0:T(1,128)} %get-tuple-element.107) | copy-start | bytes 49156
  31.3 5.1 %copy-start.13 = (f32[1,4096]{1,0:T(1,128)S(1)}, f32[1,4096]{1,0:T(1,128)}, u32[]{:S(2)}) copy-start(f32[1,4096]{1,0:T(1,128)} %get-tuple-element.108) | copy-start | bytes 49156
  31.4 5.1 %copy-start.18 = (f32[4096]{0:T(1024)S(1)}, f32[4096]{0:T(1024)}, u32[]{:S(2)}) copy-start(f32[4096]{0:T(1024)} %param.17) | copy-start | bytes 49156
  58.3 8.4 %copy-start.2 = (f32[4,8,64,128]{3,2,1,0:T(8,128)S(1)}, f32[4,8,64,128]{3,2,1,0:T(8,128)}, u32[]{:S(2)}) copy-start(f32[4,8,64,128]{3,2,1,0:T(8,128)} %shard_map.119) | copy-start | bytes 3145732
  58.3 8.4 %copy-start.9 = (f32[4,8,128]{2,1,0:T(8,128)S(1)}, f32[4,8,128]{2,1,0:T(8,128)}, u32[]{:S(2)}) copy-start(f32[4,8,128]{2,1,0:T(8,128)} %mul.193) | copy-start | bytes 49156
  58.3 9.9 %copy-start.17 = (f32[16,128]{1,0:T(8,128)S(1)}, f32[16,128]{1,0:T(8,128)}, u32[]{:S(2)}) copy-start(f32[16,128]{1,0:T(8,128)} %get-tuple-element.112) | copy-start | bytes 24580
  73.0 15.6 %collective-permute-start.2 = (f32[16,64,128]{2,1,0:T(8,128)}, f32[16,64,128]{2,1,0:T(8,128)}, u32[]{:S(2)}, u32[]{:S(2)}) collective-permute-start(f32[16,64,128]{2,1,0:T(8,128)} %bitcast_add_fusion), channel_id=1, source_target_pairs={{0,4},{4,8},{8,12},{1,5},{5,9},{9,13},{2,6},{6,10},{10,14},{3,7},{... | collective-permute-start | bytes 1572872 | tf_op jit(solution)/shard_map/ppermute | solution.py:21
  77.3 11.5 %copy-start.16 = (f32[16,128]{1,0:T(8,128)S(1)}, f32[16,128]{1,0:T(8,128)}, u32[]{:S(2)}) copy-start(f32[16,128]{1,0:T(8,128)} %get-tuple-element.111) | copy-start | bytes 24580
  89.7 16.8 %collective-permute-start.3 = (f32[16,64,128]{2,1,0:T(8,128)}, f32[16,64,128]{2,1,0:T(8,128)}, u32[]{:S(2)}, u32[]{:S(2)}) collective-permute-start(f32[16,64,128]{2,1,0:T(8,128)} %fusion.12), channel_id=1, source_target_pairs={{0,4},{4,8},{8,12},{1,5},{5,9},{9,13},{2,6},{6,10},{10,14},{3,7},{... | collective-permute-start | bytes 1572872 | tf_op jit(solution)/shard_map/ppermute | solution.py:21
  95.9 11.7 %copy-start.15 = (f32[16,128]{1,0:T(8,128)S(1)}, f32[16,128]{1,0:T(8,128)}, u32[]{:S(2)}) copy-start(f32[16,128]{1,0:T(8,128)} %get-tuple-element.110) | copy-start | bytes 24580
  108.6 14.9 %collective-permute-start.4 = (f32[16,64,128]{2,1,0:T(8,128)}, f32[16,64,128]{2,1,0:T(8,128)}, u32[]{:S(2)}, u32[]{:S(2)}) collective-permute-start(f32[16,64,128]{2,1,0:T(8,128)} %fusion.10), channel_id=1, source_target_pairs={{0,4},{4,8},{8,12},{1,5},{5,9},{9,13},{2,6},{6,10},{10,14},{3,7},{... | collective-permute-start | bytes 1572872 | tf_op jit(solution)/shard_map/ppermute | solution.py:21
  113.7 16.9 %copy-start.7 = (f32[4,8,2]{2,1,0:T(8,128)S(1)}, f32[4,8,2]{2,1,0:T(8,128)}, u32[]{:S(2)}) copy-start(f32[4,8,2]{2,1,0:T(8,128)} %copy-done.6) | copy-start | bytes 772
  125.5 13.9 %collective-permute-start.5 = (f32[16,64,128]{2,1,0:T(8,128)}, f32[16,64,128]{2,1,0:T(8,128)}, u32[]{:S(2)}, u32[]{:S(2)}) collective-permute-start(f32[16,64,128]{2,1,0:T(8,128)} %fusion.8), channel_id=1, source_target_pairs={{0,4},{4,8},{8,12},{1,5},{5,9},{9,13},{2,6},{6,10},{10,14},{3,7},{... | collective-permute-start | bytes 1572872 | tf_op jit(solution)/shard_map/ppermute | solution.py:21
  130.8 9.7 %copy-start.3 = (f32[4,8,64,128]{3,2,1,0:T(8,128)S(1)}, f32[4,8,64,128]{3,2,1,0:T(8,128)}, u32[]{:S(2)}) copy-start(f32[4,8,64,128]{3,2,1,0:T(8,128)} %shard_map.118) | copy-start | bytes 3145732
  141.9 3.0 %collective-permute-start.6 = (f32[4,8,64,128]{3,2,1,0:T(8,128)}, f32[4,8,64,128]{3,2,1,0:T(8,128)}, u32[]{:S(2)}, u32[]{:S(2)}) collective-permute-start(f32[4,8,64,128]{3,2,1,0:T(8,128)} %fusion.5), channel_id=1, source_target_pairs={{0,1},{1,0},{2,3},{3,2},{4,5},{5,4},{6,7},{7,6},{8,9},{9,8},{10,11... | collective-permute-start | bytes 3145736 | tf_op jit(solution)/shard_map/ppermute | solution.py:25
  148.5 15.3 %copy-start.1 = (f32[2,4,128]{2,1,0:T(4,128)S(1)}, f32[2,4,128]{2,1,0:T(4,128)}, u32[]{:S(2)}) copy-start(f32[2,4,128]{2,1,0:T(4,128)} %param.19) | copy-start | bytes 12292

commit v8 on v7

--- a/solution.py
+++ b/solution.py
@@ -70,7 +70,7 @@
     )
 
 
-def scan_kernel(xc_ref, ct_ref, b_ref, cumr_ref, cumc_ref, stp_ref, dsk_ref, y_ref, e_ref):
+def scan_kernel(xc_ref, ct_ref, b_ref, cumr_ref, cumc_ref, stp_ref, dsk_ref, z_ref, y_ref, sz_ref, e_ref):
     chunk = pl.program_id(1)
     block_len = xc_ref.shape[0]
     pairs = e_ref.shape[0]
@@ -109,7 +109,10 @@
         cq = pair_columns(cumc, pair, block_len)
         inflow = dot3(ct, split(s_old)) * jnp.exp(cq)
         y = jnp.where(left, ys[0], ys[1]) + inflow
-        y_ref[:, lanes] = y + xp * dsk_ref[:, lanes]
+        z = z_ref[:, lanes].astype(F32)
+        gate = z / (1.0 + jnp.exp(-z))
+        sz_ref[:, lanes] = gate
+        y_ref[:, lanes] = (y + xp * dsk_ref[:, lanes]) * gate
         e_ref[pair] = jnp.exp(cq[block_len - 1 : block_len, :]) * s_old + jnp.where(
             left, us[0], us[1]
         )
@@ -128,7 +131,7 @@
         e_ref[0, pair] = jnp.where(left, us[0], us[1])
 
 
-def out_kernel(y_ref, ct_ref, cumc_ref, v_ref, z_ref, nw_ref, o_ref, g_ref):
+def out_kernel(y_ref, ct_ref, cumc_ref, v_ref, sz_ref, nw_ref, o_ref, g_ref):
     pairs = v_ref.shape[1]
     heads = 2 * pairs
     ct = split(ct_ref[0])
@@ -137,9 +140,7 @@
     for pair in range(pairs):
         lanes = slice(pair * 128, (pair + 1) * 128)
         cq = pair_columns(cumc, pair, y_ref.shape[0])
-        y = y_ref[:, lanes] + dot3(ct, split(v_ref[0, pair])) * jnp.exp(cq)
-        z = z_ref[:, lanes].astype(F32)
-        gated = y * (z / (1.0 + jnp.exp(-z)))
+        gated = y_ref[:, lanes] + dot3(ct, split(v_ref[0, pair])) * jnp.exp(cq) * sz_ref[:, lanes]
         g_ref[:, lanes] = gated
         total = total + jnp.sum(gated * gated, axis=-1, keepdims=True)
     mean_square = total / g_ref.shape[1]
@@ -196,11 +197,8 @@
     bc_weights = lax.dynamic_slice_in_dim(conv_bc_w, sub_index * half, half, 3)
     bc_bias = lax.dynamic_slice_in_dim(conv_bc_b, sub_index * half, half, 2)
     bc_conv = conv_cols(jnp.concatenate([bc_rim, bc_raw], 3), bc_weights, bc_bias)
-    bc_halves = bc_conv.reshape(2, set_groups, half, nsub, own)
-    bc_mine = lax.dynamic_index_in_dim(bc_halves, sub_index, 3, keepdims=False)
-    bc_theirs = swapped(
-        lax.dynamic_index_in_dim(bc_halves, 1 - sub_index, 3, keepdims=False), "sub"
-    )
+    bc_mine = lax.dynamic_slice_in_dim(bc_conv, sub_index * own, own, 3)
+    bc_theirs = swapped(lax.dynamic_slice_in_dim(bc_conv, (1 - sub_index) * own, own, 3), "sub")
     bc_own = jnp.stack(
         [
             jnp.where(sub_index == 0, bc_mine, bc_theirs),
@@ -277,30 +275,34 @@
     chip_decay = decay_first * decay_second
     ctx_index = lax.axis_index("ctx")
     ctx_size = lax.axis_size("ctx")
-    scan_inputs = (x_own, c_cols, b_rows, cum_rows, cum_cols, step_rows, skip_row)
+    scan_inputs = (x_own, c_cols, b_rows, cum_rows, cum_cols, step_rows, skip_row, z_gate)
 
     def scan_group(group, inputs, target):
-        extra = {} if target is None else {"input_output_aliases": {len(inputs): 0}}
+        count = len(inputs)
+        extra = {} if target is None else {"input_output_aliases": {count: 0, count + 1: 1}}
+        tile = pl.BlockSpec((block_len, group_width), lambda g, c: (c, group))
         in_specs = [
-            pl.BlockSpec((block_len, group_width), lambda g, c: (c, group)),
+            tile,
             pl.BlockSpec((1, block_len, state), lambda g, c: (group, c, 0)),
             pl.BlockSpec((1, state, block_len), lambda g, c: (group, 0, c)),
             pl.BlockSpec((1, per_group, block_len), lambda g, c: (group, 0, c)),
             pl.BlockSpec((1, block_len, per_group), lambda g, c: (group, c, 0)),
             pl.BlockSpec((1, per_group, block_len), lambda g, c: (group, 0, c)),
             pl.BlockSpec((1, group_width), lambda g, c: (0, group)),
+            tile,
         ]
         operands = tuple(inputs)
+        kernel = scan_kernel
         if target is not None:
-            in_specs.append(pl.BlockSpec(memory_space=pl.ANY))
-            operands = operands + (target,)
-        kernel = scan_kernel if target is None else (lambda *refs: scan_kernel(*refs[:7], *refs[8:]))
+            in_specs = in_specs + [pl.BlockSpec(memory_space=pl.ANY)] * 2
+            operands = operands + tuple(target)
+            kernel = lambda *refs: scan_kernel(*refs[:count], *refs[count + 2 :])
         return pl.pallas_call(
             kernel,
             grid=(1, blocks),
             in_specs=in_specs,
-            out_specs=pl.BlockSpec((block_len, group_width), lambda g, c: (c, group)),
-            out_shape=jax.ShapeDtypeStruct((own, channels), F32),
+            out_specs=[tile, tile],
+            out_shape=[jax.ShapeDtypeStruct((own, channels), F32)] * 2,
             scratch_shapes=[pltpu.VMEM((pairs, state, 128), F32)],
             **extra,
         )(*operands)
@@ -361,7 +363,7 @@
         out_specs=pl.BlockSpec((out_len, group_width), lambda g, c: (c, g)),
         out_shape=jax.ShapeDtypeStruct((own, channels), jnp.bfloat16),
         scratch_shapes=[pltpu.VMEM((out_len, group_width), F32)],
-    )(y_local, c_cols, cum_device.transpose(0, 2, 1), incoming, z_gate, norm_w[None, :])
+    )(y_local[0], c_cols, cum_device.transpose(0, 2, 1), incoming, y_local[1], norm_w[None, :])
 
 
 def solution(mesh):

time: 165 us -> 160 us (0.970)
  local copies, waits for them, and re-layouts: 25.2 us -> 17.2 us
  Pallas kernels: 62.9 us -> 65.3 us
  other arithmetic: 38.5 us -> 40.5 us
    dynamic_slice x1, local copies, waits for them, and re-layouts: 4.38 us -> 1.08 us  [per_device(): lax.dynamic_slice_in_dim(bc_conv, (1 - sub_index) * own, own, 3)]
    reshape x1 -> x0, local copies, waits for them, and re-layouts: 2.78 us -> none  [per_device(): bc_halves = bc_conv.reshape(2, set_groups, half, nsub, own)]
    mul x1, other arithmetic: 2.93 us -> 5.47 us  [conv_cols(): return jax.nn.silu(total)]
  transfers between devices with their start and end apart: 7 -> 7, of which waited for: 5 -> 5; matrix products, arithmetic and copies ran while one was open for 21% -> 20% of each run, Pallas kernels for 29% -> 31%
where the time goes in v8:
time: 160 us; the launch traced here: 158 us
  Pallas kernels  65.3 us (41%)
  other arithmetic  40.5 us (25%)
  starting transfers between devices  25.1 us (16%)
  local copies, waits for them, and re-layouts  17.2 us (11%)
  waiting for transfers between devices  9.2 us (6%)
    pallas_call x4, Pallas kernels, scan_group(): pl.pallas_call(kernel, grid=(1, blocks), in_specs=in_specs, out_specs=[ti...  32.6 us
    ppermute x5, starting transfers between devices, passed_along(): return lax.ppermute(x, axis, pairs)  25.1 us
    pallas_call x2, Pallas kernels, end_states(): pl.pallas_call(end_kernel, grid=(set_groups,), in_specs=[pl.BlockSpec((ow...  16.6 us
    pallas_call x1, Pallas kernels, per_device(): pl.pallas_call(out_kernel, grid=(set_groups, own // out_len), in_specs=[p...  16 us
    mul x1, other arithmetic, conv_rows(): return jax.nn.silu(total)  12.4 us
    ppermute x5, waiting for transfers between devices, passed_along(): return lax.ppermute(x, axis, pairs)  8.09 us
    mul x1, other arithmetic, conv_cols(): return jax.nn.silu(total)  5.47 us
    concatenate x1, other arithmetic, per_device(): x_pad = jnp.concatenate([x_rim, x_raw], 0)  4.98 us
  transfers between devices with their start and end apart: 7, of which 5 were waited for; matrix products, arithmetic and copies ran while one was open for 20% of the time, Pallas kernels for 31%

profile of v8, /device:TPU:0, one launch (start us, length us, event | category | flops | bytes accessed | tf_op | source)
XLA Modules:
  0.0 158.2 jit_solution(14643595181498765341)
XLA Ops:
  2.1 4.9 %collective-permute-start = (bf16[3,4608]{1,0:T(4,128)(2,1)S(1)}, bf16[3,4608]{1,0:T(4,128)(2,1)S(1)}, u32[]{:S(2)}, u32[]{:S(2)}) collective-permute-start(bf16[3,4608]{1,0:T(4,128)(2,1)S(1)} %pad_maximum_fusion.3), channel_id=1, source_target_pairs={{0,4},{4,8},{8,12},{1,5},{5,9},{9,13},{2,6},{6,10},{10,14},{3,7},{... | collective-permute-start | bytes 82952 | tf_op jit(solution)/shard_map/ppermute | solution.py:21
  7.7 1.2 broadcast_multiply_fusion
  14.4 1.4 copy.69
  16.8 5.5 %divide_multiply_fusion.2 = f32[2,4,64,1024]{3,2,1,0:T(8,128)S(1)} fusion(bf16[2,4,64,1024]{3,2,1,0:T(8,128)(2,1)} %param.13, bf16[2,4,64,3]{3,2,1,0:T(8,128)(2,1)S(1)} %bitcast.132, f32[2,4,64]{2,1,0:T(4,128)S(1)} %get-tuple-element.146, f32[2,4,64]{2,1,0:T(4,128)S(1)} %get-tuple-element.144, f32[2,4,64]{2,1,0:T(4,128)S(1)} %get-tuple-element.145, ...), kind=kLoop, calls=%fused_computation.11 | loop fusion | flops 13107200 | bytes 3159040 | tf_op jit(solution)/shard_map/jit(silu)/mul | solution.py:45
  23.4 5.0 %fusion.1 = (bf16[515,4096]{1,0:T(8,128)(2,1)S(1)}, bf16[515,4096]{1,0:T(8,128)(2,1)S(1)}) fusion(s32[]{:T(128)S(6)} %select_n.128, bf16[1024,4096]{1,0:T(8,128)(2,1)} %param.12, bf16[3,4096]{1,0:T(4,128)(2,1)S(1)} %slice.132, s32[]{:T(128)S(6)} %select_n.131), kind=kLoop, calls=%fused_computation.7 | loop fusion | flops 16875520 | bytes 16850952 | tf_op jit(solution)/shard_map/concatenate | solution.py:188
  28.4 12.4 %divide_multiply_fusion.1 = (f32[512,4096]{1,0:T(8,128)}, f32[512,4096]{1,0:T(8,128)}) fusion(bf16[515,4096]{1,0:T(8,128)(2,1)S(1)} %get-tuple-element.123, f32[4096]{0:T(1024)S(1)} %bitcast.137, f32[4096]{0:T(1024)S(1)} %bitcast.138, f32[4096]{0:T(1024)S(1)} %bitcast.136, f32[4096]{0:T(1024)S(1)} %bitcast.135, f32[4096]{0:T(1024)S(1)} %copy-done.9, ...), kind=kLoop, calls=%fused_computation.3 | loop fusion | flops 67108864 | bytes 50413568 | tf_op jit(solution)/shard_map/jit(silu)/mul | solution.py:35
  41.9 8.3 %shard_map.119 = f32[4,8,64,128]{3,2,1,0:T(8,128)} custom-call(f32[512,4096]{1,0:T(8,128)} %get-tuple-element.134.xc_ref, f32[4,64,512]{2,1,0:T(8,128)} %get-tuple-element.130.b_ref, f32[4,16,512]{2,1,0:T(8,128)} %get-tuple-element.132.wk_ref), custom_call_target="tpu_custom_call" | custom-call | tf_op jit(solution)/shard_map/pallas_call | solution.py:248
  50.2 8.4 %shard_map.118 = f32[4,8,64,128]{3,2,1,0:T(8,128)} custom-call(f32[512,4096]{1,0:T(8,128)} %get-tuple-element.102.xc_ref.refs_0_, f32[4,64,512]{2,1,0:T(8,128)} %get-tuple-element.129.b_ref, f32[4,16,512]{2,1,0:T(8,128)} %get-tuple-element.131.wk_ref), custom_call_target="tpu_custom_call" | custom-call | tf_op jit(solution)/shard_map/pallas_call | solution.py:248
  58.6 1.5 select_add_fusion
  62.0 1.5 select_bitcast_fusion.2
  63.5 1.2 pad_maximum_fusion.1
  64.6 1.3 copy.66
  66.0 3.7 %collective-permute-start.2 = (f32[16,64,128]{2,1,0:T(8,128)}, f32[16,64,128]{2,1,0:T(8,128)S(1)}, u32[]{:S(2)}, u32[]{:S(2)}) collective-permute-start(f32[16,64,128]{2,1,0:T(8,128)} %bitcast_add_fusion), channel_id=1, source_target_pairs={{0,4},{4,8},{8,12},{1,5},{5,9},{9,13},{2,6},{6,10},{10,14},{3,7},{... | collective-permute-start | bytes 1572872 | tf_op jit(solution)/shard_map/ppermute | solution.py:21
  69.7 8.2 %shard_map.120 = (f32[512,4096]{1,0:T(8,128)}, f32[512,4096]{1,0:T(8,128)}) custom-call(f32[512,4096]{1,0:T(8,128)} %get-tuple-element.102.xc_ref.refs_0_, f32[4,512,128]{2,1,0:T(8,128)} %bitcast.107, f32[4,128,512]{2,1,0:T(8,128)} %bitcast.116, f32[4,16,512]{2,1,0:T(8,128)} %copy-done.6, f32[4,512,16]{2,1,0:T(8,128)} %bitcast.112, f32[4,16,512]{2,1,0:T(8,128)} %bitcast.127, ...), custom_call_target="tpu_custom_call" | custom-call | tf_op jit(solution)/shard_map/pallas_call | solution.py:300
  77.9 3.7 %collective-permute-done.2 = f32[16,64,128]{2,1,0:T(8,128)S(1)} collective-permute-done((f32[16,64,128]{2,1,0:T(8,128)}, f32[16,64,128]{2,1,0:T(8,128)S(1)}, u32[]{:S(2)}, u32[]{:S(2)}) %collective-permute-start.2) | collective-permute-done | bytes 524320 | tf_op jit(solution)/shard_map/ppermute | solution.py:21
  83.5 6.1 %collective-permute-start.3 = (f32[16,64,128]{2,1,0:T(8,128)}, f32[16,64,128]{2,1,0:T(8,128)}, u32[]{:S(2)}, u32[]{:S(2)}) collective-permute-start(f32[16,64,128]{2,1,0:T(8,128)} %fusion.12), channel_id=1, source_target_pairs={{0,4},{4,8},{8,12},{1,5},{5,9},{9,13},{2,6},{6,10},{10,14},{3,7},{... | collective-permute-start | bytes 1572872 | tf_op jit(solution)/shard_map/ppermute | solution.py:21
  89.6 8.1 %shard_map.121 = (f32[512,4096]{1,0:T(8,128)}, f32[512,4096]{1,0:T(8,128)}) custom-call(f32[512,4096]{1,0:T(8,128)} %get-tuple-element.102.xc_ref.refs_0_, f32[4,512,128]{2,1,0:T(8,128)} %bitcast.108, f32[4,128,512]{2,1,0:T(8,128)} %bitcast.117, f32[4,16,512]{2,1,0:T(8,128)} %copy-done.6, ...), custom_call_target="tpu_custom_call", output_to_operand_aliasing={{0}: (8, {}), {1}: (9, {})} | custom-call | tf_op jit(solution)/shard_map/pallas_call | solution.py:300
  97.7 2.4 %collective-permute-done.3 = f32[16,64,128]{2,1,0:T(8,128)} collective-permute-done((f32[16,64,128]{2,1,0:T(8,128)}, f32[16,64,128]{2,1,0:T(8,128)}, u32[]{:S(2)}, u32[]{:S(2)}) %collective-permute-start.3) | collective-permute-done | bytes 524320 | tf_op jit(solution)/shard_map/ppermute | solution.py:21
  100.2 1.2 fusion.11
  102.2 5.2 %collective-permute-start.4 = (f32[16,64,128]{2,1,0:T(8,128)}, f32[16,64,128]{2,1,0:T(8,128)}, u32[]{:S(2)}, u32[]{:S(2)}) collective-permute-start(f32[16,64,128]{2,1,0:T(8,128)} %fusion.10), channel_id=1, source_target_pairs={{0,4},{4,8},{8,12},{1,5},{5,9},{9,13},{2,6},{6,10},{10,14},{3,7},{... | collective-permute-start | bytes 1572872 | tf_op jit(solution)/shard_map/ppermute | solution.py:21
  107.4 8.1 %shard_map.122 = (f32[512,4096]{1,0:T(8,128)}, f32[512,4096]{1,0:T(8,128)}) custom-call(f32[512,4096]{1,0:T(8,128)} %get-tuple-element.102.xc_ref.refs_0_, f32[4,512,128]{2,1,0:T(8,128)} %bitcast.109, f32[4,128,512]{2,1,0:T(8,128)} %bitcast.118, f32[4,16,512]{2,1,0:T(8,128)} %copy-done.6, ...), custom_call_target="tpu_custom_call", output_to_operand_aliasing={{0}: (8, {}), {1}: (9, {})} | custom-call | tf_op jit(solution)/shard_map/pallas_call | solution.py:300
  115.5 1.6 collective-permute-done.4
  117.1 1.2 fusion.9
  119.2 5.2 %collective-permute-start.5 = (f32[16,64,128]{2,1,0:T(8,128)}, f32[16,64,128]{2,1,0:T(8,128)}, u32[]{:S(2)}, u32[]{:S(2)}) collective-permute-start(f32[16,64,128]{2,1,0:T(8,128)} %fusion.8), channel_id=1, source_target_pairs={{0,4},{4,8},{8,12},{1,5},{5,9},{9,13},{2,6},{6,10},{10,14},{3,7},{... | collective-permute-start | bytes 1572872 | tf_op jit(solution)/shard_map/ppermute | solution.py:21
  124.5 8.2 %shard_map.123 = (f32[512,4096]{1,0:T(8,128)}, f32[512,4096]{1,0:T(8,128)}) custom-call(f32[512,4096]{1,0:T(8,128)} %get-tuple-element.102.xc_ref.refs_0_, f32[4,512,128]{2,1,0:T(8,128)} %bitcast.110, f32[4,128,512]{2,1,0:T(8,128)} %bitcast.119, f32[4,16,512]{2,1,0:T(8,128)} %copy-done.6, ...), custom_call_target="tpu_custom_call", output_to_operand_aliasing={{0}: (8, {}), {1}: (9, {})} | custom-call | tf_op jit(solution)/shard_map/pallas_call | solution.py:300
  133.1 1.2 fusion.7
  134.3 1.3 fusion.5
  136.1 1.4 copy.71
  137.5 1.1 collective-permute-done.6
  139.1 1.4 select_bitcast_fusion
  140.7 1.5 copy.72
  142.2 16.0 %shard_map.124 = bf16[512,4096]{1,0:T(8,128)(2,1)} custom-call(f32[512,4096]{1,0:T(8,128)} %get-tuple-element.114.y_ref, f32[4,512,128]{2,1,0:T(8,128)} %bitcast.111, f32[4,512,16]{2,1,0:T(8,128)} %bitcast.126, f32[4,8,128,128]{3,2,1,0:T(8,128)} %bitcast.124, f32[512,4096]{1,0:T(8,128)} %get-tuple-element.116.sz_ref, f32[1,4096]{1,0:T(1,128)} %bitcast.140), custom_call_target="tpu_custom_call" | custom-call | tf_op jit(solution)/shard_map/pallas_call | solution.py:352
  (88 shorter events, 18.4 us)
Async XLA Ops:
  0.0 14.0 %copy-start = (f32[2,4,128]{2,1,0:T(4,128)S(1)}, f32[2,4,128]{2,1,0:T(4,128)}, u32[]{:S(2)}) copy-start(f32[2,4,128]{2,1,0:T(4,128)} %param.19) | copy-start | bytes 12292
  0.0 10.1 %copy-start.8 = (f32[4,4096]{1,0:T(4,128)S(1)}, f32[4,4096]{1,0:T(4,128)}, u32[]{:S(2)}) copy-start(f32[4,4096]{1,0:T(4,128)} %param.16) | copy-start | bytes 196612
  2.1 14.6 %collective-permute-start = (bf16[3,4608]{1,0:T(4,128)(2,1)S(1)}, bf16[3,4608]{1,0:T(4,128)(2,1)S(1)}, u32[]{:S(2)}, u32[]{:S(2)}) collective-permute-start(bf16[3,4608]{1,0:T(4,128)(2,1)S(1)} %pad_maximum_fusion.3), channel_id=1, source_target_pairs={{0,4},{4,8},{8,12},{1,5},{5,9},{9,13},{2,6},{6,10},{10,14},{3,7},{... | collective-permute-start | bytes 82952 | tf_op jit(solution)/shard_map/ppermute | solution.py:21
  7.7 6.2 %copy-start.10 = (f32[4,2,4,128]{3,2,1,0:T(4,128)S(1)}, f32[4,2,4,128]{3,2,1,0:T(4,128)}, u32[]{:S(2)}) copy-start(f32[4,2,4,128]{3,2,1,0:T(4,128)} %param.18) | copy-start | bytes 49156
  9.6 6.2 %copy-start.11 = (f32[64]{0:T(128)S(1)}, f32[64]{0:T(128)}, u32[]{:S(2)}) copy-start(f32[64]{0:T(128)} %param.22) | copy-start | bytes 772
  14.4 14.0 %copy-start.6 = (f32[4,16,512]{2,1,0:T(8,128)}, f32[4,16,512]{2,1,0:T(8,128)S(1)}, u32[]{:S(2)}) copy-start(f32[4,16,512]{2,1,0:T(8,128)S(1)} %reshape.101.cumr_ref.refs_3_) | copy-start | bytes 393220
  23.4 38.6 %collective-permute-start.1 = (f32[2,4,64,512]{3,2,1,0:T(8,128)}, f32[2,4,64,512]{3,2,1,0:T(8,128)}, u32[]{:S(2)}, u32[]{:S(2)}) collective-permute-start(f32[2,4,64,512]{3,2,1,0:T(8,128)} %constant_dynamic-slice_fusion.5), channel_id=1, source_target_pairs={{0,1},{1,0},{2,3},{3,2},{4,5},{5,4},{6,7},{7,6},{8,9},{9,8},{10,11... | collective-permute-start | bytes 3145736 | tf_op jit(solution)/shard_map/ppermute | solution.py:25
  23.4 5.0 %copy-start.9 = (f32[4096]{0:T(1024)S(1)}, f32[4096]{0:T(1024)}, u32[]{:S(2)}) copy-start(f32[4096]{0:T(1024)} %param.17) | copy-start | bytes 49156
  50.2 8.4 %copy-start.2 = (f32[4,8,64,128]{3,2,1,0:T(8,128)S(1)}, f32[4,8,64,128]{3,2,1,0:T(8,128)}, u32[]{:S(2)}) copy-start(f32[4,8,64,128]{3,2,1,0:T(8,128)} %shard_map.119) | copy-start | bytes 3145732
  60.1 1.0 copy-start.4
  66.0 15.6 %collective-permute-start.2 = (f32[16,64,128]{2,1,0:T(8,128)}, f32[16,64,128]{2,1,0:T(8,128)S(1)}, u32[]{:S(2)}, u32[]{:S(2)}) collective-permute-start(f32[16,64,128]{2,1,0:T(8,128)} %bitcast_add_fusion), channel_id=1, source_target_pairs={{0,4},{4,8},{8,12},{1,5},{5,9},{9,13},{2,6},{6,10},{10,14},{3,7},{... | collective-permute-start | bytes 1572872 | tf_op jit(solution)/shard_map/ppermute | solution.py:21
  69.7 12.9 %copy-start.5 = (f32[4,8,64,128]{3,2,1,0:T(8,128)S(1)}, f32[4,8,64,128]{3,2,1,0:T(8,128)}, u32[]{:S(2)}) copy-start(f32[4,8,64,128]{3,2,1,0:T(8,128)} %copy-done.4) | copy-start | bytes 3145732
  81.6 0.8 copy-start.7
  83.5 16.7 %collective-permute-start.3 = (f32[16,64,128]{2,1,0:T(8,128)}, f32[16,64,128]{2,1,0:T(8,128)}, u32[]{:S(2)}, u32[]{:S(2)}) collective-permute-start(f32[16,64,128]{2,1,0:T(8,128)} %fusion.12), channel_id=1, source_target_pairs={{0,4},{4,8},{8,12},{1,5},{5,9},{9,13},{2,6},{6,10},{10,14},{3,7},{... | collective-permute-start | bytes 1572872 | tf_op jit(solution)/shard_map/ppermute | solution.py:21
  102.2 14.9 %collective-permute-start.4 = (f32[16,64,128]{2,1,0:T(8,128)}, f32[16,64,128]{2,1,0:T(8,128)}, u32[]{:S(2)}, u32[]{:S(2)}) collective-permute-start(f32[16,64,128]{2,1,0:T(8,128)} %fusion.10), channel_id=1, source_target_pairs={{0,4},{4,8},{8,12},{1,5},{5,9},{9,13},{2,6},{6,10},{10,14},{3,7},{... | collective-permute-start | bytes 1572872 | tf_op jit(solution)/shard_map/ppermute | solution.py:21
  119.2 13.9 %collective-permute-start.5 = (f32[16,64,128]{2,1,0:T(8,128)}, f32[16,64,128]{2,1,0:T(8,128)}, u32[]{:S(2)}, u32[]{:S(2)}) collective-permute-start(f32[16,64,128]{2,1,0:T(8,128)} %fusion.8), channel_id=1, source_target_pairs={{0,4},{4,8},{8,12},{1,5},{5,9},{9,13},{2,6},{6,10},{10,14},{3,7},{... | collective-permute-start | bytes 1572872 | tf_op jit(solution)/shard_map/ppermute | solution.py:21
  124.5 9.7 %copy-start.3 = (f32[4,8,64,128]{3,2,1,0:T(8,128)S(1)}, f32[4,8,64,128]{3,2,1,0:T(8,128)}, u32[]{:S(2)}) copy-start(f32[4,8,64,128]{3,2,1,0:T(8,128)} %shard_map.118) | copy-start | bytes 3145732
  135.6 3.0 %collective-permute-start.6 = (f32[4,8,64,128]{3,2,1,0:T(8,128)}, f32[4,8,64,128]{3,2,1,0:T(8,128)}, u32[]{:S(2)}, u32[]{:S(2)}) collective-permute-start(f32[4,8,64,128]{3,2,1,0:T(8,128)} %fusion.5), channel_id=1, source_target_pairs={{0,1},{1,0},{2,3},{3,2},{4,5},{5,4},{6,7},{7,6},{8,9},{9,8},{10,11... | collective-permute-start | bytes 3145736 | tf_op jit(solution)/shard_map/ppermute | solution.py:25
  142.2 16.0 %copy-start.1 = (f32[2,4,128]{2,1,0:T(4,128)S(1)}, f32[2,4,128]{2,1,0:T(4,128)}, u32[]{:S(2)}) copy-start(f32[2,4,128]{2,1,0:T(4,128)} %param.19) | copy-start | bytes 12292

commit v9 on v8

--- a/solution.py
+++ b/solution.py
@@ -185,18 +185,27 @@
     )
     x_rim = rims[:, :channels]
     bc_rim = rims[:, channels:].transpose(1, 0).reshape(bc_tail.shape)
-    x_pad = jnp.concatenate([x_rim, x_raw], 0)
-    x_own = conv_rows(
-        lax.dynamic_slice_in_dim(x_pad, sub_index * own, own + rim_len, 0), conv_x_w, conv_x_b
-    )
-    x_other = conv_rows(
-        lax.dynamic_slice_in_dim(x_pad, (1 - sub_index) * own, own + rim_len, 0),
-        conv_x_w,
-        conv_x_b,
-    )
+    x_pad = jnp.concatenate([jnp.zeros_like(x_rim), x_raw], 0)
+    x_start = conv_rows(jnp.concatenate([x_rim, x_raw[:rim_len]], 0), conv_x_w, conv_x_b)
+
+    def x_window(at):
+        body = conv_rows(
+            lax.dynamic_slice_in_dim(x_pad, at * own, own + rim_len, 0), conv_x_w, conv_x_b
+        )
+        head_rows = jnp.where(at == 0, x_start, body[:rim_len])
+        return lax.dynamic_update_slice_in_dim(body, head_rows, 0, 0)
+
+    x_own = x_window(sub_index)
+    x_other = x_window(1 - sub_index)
     bc_weights = lax.dynamic_slice_in_dim(conv_bc_w, sub_index * half, half, 3)
     bc_bias = lax.dynamic_slice_in_dim(conv_bc_b, sub_index * half, half, 2)
-    bc_conv = conv_cols(jnp.concatenate([bc_rim, bc_raw], 3), bc_weights, bc_bias)
+    bc_body = conv_cols(
+        jnp.concatenate([jnp.zeros_like(bc_rim), bc_raw], 3), bc_weights, bc_bias
+    )
+    bc_start = conv_cols(
+        jnp.concatenate([bc_rim, bc_raw[..., :rim_len]], 3), bc_weights, bc_bias
+    )
+    bc_conv = lax.dynamic_update_slice_in_dim(bc_body, bc_start, 0, 3)
     bc_mine = lax.dynamic_slice_in_dim(bc_conv, sub_index * own, own, 3)
     bc_theirs = swapped(lax.dynamic_slice_in_dim(bc_conv, (1 - sub_index) * own, own, 3), "sub")
     bc_own = jnp.stack(

time: 160 us -> 177 us (1.11)
  other arithmetic: 40.5 us -> 49.1 us
  local copies, waits for them, and re-layouts: 17.2 us -> 25.4 us
    mul x1, other arithmetic: 12.4 us -> 22.6 us  [conv_rows(): return jax.nn.silu(total)]
    concatenate x1 -> x0, other arithmetic: 4.98 us -> none  [per_device(): x_pad = jnp.concatenate([x_rim, x_raw], 0)]
    dynamic_update_slice x0 -> x3, local copies, waits for them, and re-layouts: none -> 3.93 us  [the longest x2 3.37 us: x_window(): return lax.dynamic_update_slice_in_dim(body, head_rows, 0, 0)]
    select_n x0 -> x2, other arithmetic: none -> 1.98 us  [x_window(): head_rows = jnp.where(at == 0, x_start, body[:rim_len])]
    mul x1 -> x2, other arithmetic: 5.47 us -> 5.68 us  [conv_cols(): return jax.nn.silu(total)]
  transfers between devices with their start and end apart: 7 -> 7, of which waited for: 5 -> 5; matrix products, arithmetic and copies ran while one was open for 20% -> 30% of each run, Pallas kernels for 31% -> 28%
where the time goes in v9:
time: 177 us; the launch traced here: 175 us
  Pallas kernels  65.3 us (37%)
  other arithmetic  49.1 us (28%)
  local copies, waits for them, and re-layouts  25.4 us (14%)
  starting transfers between devices  25 us (14%)
  waiting for transfers between devices  9.33 us (5%)
    pallas_call x4, Pallas kernels, scan_group(): pl.pallas_call(kernel, grid=(1, blocks), in_specs=in_specs, out_specs=[ti...  32.6 us
    ppermute x5, starting transfers between devices, passed_along(): return lax.ppermute(x, axis, pairs)  25 us
    mul x1, other arithmetic, conv_rows(): return jax.nn.silu(total)  22.6 us
    pallas_call x2, Pallas kernels, end_states(): pl.pallas_call(end_kernel, grid=(set_groups,), in_specs=[pl.BlockSpec((ow...  16.6 us
    pallas_call x1, Pallas kernels, per_device(): pl.pallas_call(out_kernel, grid=(set_groups, own // out_len), in_specs=[p...  16 us
    ppermute x5, waiting for transfers between devices, passed_along(): return lax.ppermute(x, axis, pairs)  8.2 us
    mul x2, other arithmetic, conv_cols(): return jax.nn.silu(total)  5.68 us
    select_n x4, other arithmetic, per_device(): received = jnp.where(valid, updated, received)  3.56 us
  transfers between devices with their start and end apart: 7, of which 5 were waited for; matrix products, arithmetic and copies ran while one was open for 30% of the time, Pallas kernels for 28%

profile of v9, /device:TPU:0, one launch (start us, length us, event | category | flops | bytes accessed | tf_op | source)
XLA Modules:
  0.0 175.1 jit_solution(17443880614743090713)
XLA Ops:
  0.0 1.5 fusion.32
  3.4 5.5 %collective-permute-start = (bf16[3,4608]{1,0:T(4,128)(2,1)}, bf16[3,4608]{1,0:T(4,128)(2,1)}, u32[]{:S(2)}, u32[]{:S(2)}) collective-permute-start(bf16[3,4608]{1,0:T(4,128)(2,1)} %pad_maximum_fusion.2), channel_id=1, source_target_pairs={{0,4},{4,8},{8,12},{1,5},{5,9},{9,13},{2,6},{6,10},{10,14},{3,7},{... | collective-permute-start | bytes 82952 | tf_op jit(solution)/shard_map/ppermute | solution.py:21
  9.6 1.2 broadcast_multiply_fusion
  17.3 5.6 %divide_multiply_fusion.2 = f32[2,4,64,1024]{3,2,1,0:T(8,128)S(1)} fusion(bf16[2,4,64,1024]{3,2,1,0:T(8,128)(2,1)} %param.13, f32[2,4,64]{2,1,0:T(4,128)S(1)} %get-tuple-element.150, f32[2,4,64]{2,1,0:T(4,128)S(1)} %get-tuple-element.148, f32[2,4,64]{2,1,0:T(4,128)S(1)} %get-tuple-element.149, f32[2,4,64]{2,1,0:T(4,128)S(1)} %get-tuple-element.147, ...), kind=kLoop, calls=%fused_computation.9 | loop fusion | flops 8388608 | bytes 3155968 | tf_op jit(solution)/shard_map/jit(silu)/mul | solution.py:45
  23.0 22.6 %divide_multiply_fusion.1 = (f32[512,4096]{1,0:T(8,128)}, f32[512,4096]{1,0:T(8,128)}) fusion(s32[]{:T(128)S(6)} %add.268, bf16[1024,4096]{1,0:T(8,128)(2,1)} %param.12, s32[]{:T(128)S(6)} %select_n.142, s32[]{:T(128)S(6)} %add.266, s32[]{:T(128)S(6)} %add.267, f32[4096]{0:T(1024)S(1)} %bitcast.138, f32[4096]{0:T(1024)S(1)} %bitcast.140, ...), kind=kLoop, calls=%fused_computation.1 | loop fusion | flops 67108864 | bytes 25247776 | tf_op jit(solution)/shard_map/jit(silu)/mul | solution.py:35
  47.3 1.4 copy.95
  55.0 1.7 dynamic_update_slice.16.xc_ref
  56.7 1.7 dynamic_update_slice.14.xc_ref.refs_0_
  59.5 8.3 %shard_map.119 = f32[4,8,64,128]{3,2,1,0:T(8,128)} custom-call(f32[512,4096]{1,0:T(8,128)} %dynamic_update_slice.16.xc_ref, f32[4,64,512]{2,1,0:T(8,128)} %get-tuple-element.134.b_ref, f32[4,16,512]{2,1,0:T(8,128)} %get-tuple-element.138.wk_ref), custom_call_target="tpu_custom_call" | custom-call | tf_op jit(solution)/shard_map/pallas_call | solution.py:257
  67.8 8.4 %shard_map.118 = f32[4,8,64,128]{3,2,1,0:T(8,128)} custom-call(f32[512,4096]{1,0:T(8,128)} %dynamic_update_slice.14.xc_ref.refs_0_, f32[4,64,512]{2,1,0:T(8,128)} %get-tuple-element.133.b_ref, f32[4,16,512]{2,1,0:T(8,128)} %get-tuple-element.137.wk_ref), custom_call_target="tpu_custom_call" | custom-call | tf_op jit(solution)/shard_map/pallas_call | solution.py:257
  76.1 1.5 select_add_fusion
  79.5 1.5 select_bitcast_fusion.2
  81.0 1.2 pad_maximum_fusion.1
  82.2 1.3 copy.92
  83.5 2.9 %collective-permute-start.2 = (f32[16,64,128]{2,1,0:T(8,128)}, f32[16,64,128]{2,1,0:T(8,128)S(1)}, u32[]{:S(2)}, u32[]{:S(2)}) collective-permute-start(f32[16,64,128]{2,1,0:T(8,128)} %bitcast_add_fusion), channel_id=1, source_target_pairs={{0,4},{4,8},{8,12},{1,5},{5,9},{9,13},{2,6},{6,10},{10,14},{3,7},{... | collective-permute-start | bytes 1572872 | tf_op jit(solution)/shard_map/ppermute | solution.py:21
  86.5 8.4 %shard_map.120 = (f32[512,4096]{1,0:T(8,128)}, f32[512,4096]{1,0:T(8,128)}) custom-call(f32[512,4096]{1,0:T(8,128)} %dynamic_update_slice.14.xc_ref.refs_0_, f32[4,512,128]{2,1,0:T(8,128)} %bitcast.108, f32[4,128,512]{2,1,0:T(8,128)} %bitcast.117, f32[4,16,512]{2,1,0:T(8,128)} %copy-done.6, f32[4,512,16]{2,1,0:T(8,128)} %bitcast.113, ...), custom_call_target="tpu_custom_call" | custom-call | tf_op jit(solution)/shard_map/pallas_call | solution.py:309
  94.9 3.7 %collective-permute-done.2 = f32[16,64,128]{2,1,0:T(8,128)S(1)} collective-permute-done((f32[16,64,128]{2,1,0:T(8,128)}, f32[16,64,128]{2,1,0:T(8,128)S(1)}, u32[]{:S(2)}, u32[]{:S(2)}) %collective-permute-start.2) | collective-permute-done | bytes 524320 | tf_op jit(solution)/shard_map/ppermute | solution.py:21
  100.5 6.1 %collective-permute-start.3 = (f32[16,64,128]{2,1,0:T(8,128)}, f32[16,64,128]{2,1,0:T(8,128)}, u32[]{:S(2)}, u32[]{:S(2)}) collective-permute-start(f32[16,64,128]{2,1,0:T(8,128)} %fusion.8), channel_id=1, source_target_pairs={{0,4},{4,8},{8,12},{1,5},{5,9},{9,13},{2,6},{6,10},{10,14},{3,7},{... | collective-permute-start | bytes 1572872 | tf_op jit(solution)/shard_map/ppermute | solution.py:21
  106.6 8.1 %shard_map.121 = (f32[512,4096]{1,0:T(8,128)}, f32[512,4096]{1,0:T(8,128)}) custom-call(f32[512,4096]{1,0:T(8,128)} %dynamic_update_slice.14.xc_ref.refs_0_, f32[4,512,128]{2,1,0:T(8,128)} %bitcast.109, f32[4,128,512]{2,1,0:T(8,128)} %bitcast.118, f32[4,16,512]{2,1,0:T(8,128)} %copy-done.6, ...), custom_call_target="tpu_custom_call", output_to_operand_aliasing={{0}: (8, {}), {1}: (9, {})} | custom-call | tf_op jit(solution)/shard_map/pallas_call | solution.py:309
  114.6 2.5 %collective-permute-done.3 = f32[16,64,128]{2,1,0:T(8,128)} collective-permute-done((f32[16,64,128]{2,1,0:T(8,128)}, f32[16,64,128]{2,1,0:T(8,128)}, u32[]{:S(2)}, u32[]{:S(2)}) %collective-permute-start.3) | collective-permute-done | bytes 524320 | tf_op jit(solution)/shard_map/ppermute | solution.py:21
  117.1 1.2 fusion.7
  119.2 5.2 %collective-permute-start.4 = (f32[16,64,128]{2,1,0:T(8,128)}, f32[16,64,128]{2,1,0:T(8,128)}, u32[]{:S(2)}, u32[]{:S(2)}) collective-permute-start(f32[16,64,128]{2,1,0:T(8,128)} %fusion.6), channel_id=1, source_target_pairs={{0,4},{4,8},{8,12},{1,5},{5,9},{9,13},{2,6},{6,10},{10,14},{3,7},{... | collective-permute-start | bytes 1572872 | tf_op jit(solution)/shard_map/ppermute | solution.py:21
  124.4 8.1 %shard_map.122 = (f32[512,4096]{1,0:T(8,128)}, f32[512,4096]{1,0:T(8,128)}) custom-call(f32[512,4096]{1,0:T(8,128)} %dynamic_update_slice.14.xc_ref.refs_0_, f32[4,512,128]{2,1,0:T(8,128)} %bitcast.110, f32[4,128,512]{2,1,0:T(8,128)} %bitcast.119, f32[4,16,512]{2,1,0:T(8,128)} %copy-done.6, ...), custom_call_target="tpu_custom_call", output_to_operand_aliasing={{0}: (8, {}), {1}: (9, {})} | custom-call | tf_op jit(solution)/shard_map/pallas_call | solution.py:309
  132.5 1.6 collective-permute-done.4
  134.0 1.2 fusion.5
  136.1 5.2 %collective-permute-start.5 = (f32[16,64,128]{2,1,0:T(8,128)}, f32[16,64,128]{2,1,0:T(8,128)}, u32[]{:S(2)}, u32[]{:S(2)}) collective-permute-start(f32[16,64,128]{2,1,0:T(8,128)} %fusion.4), channel_id=1, source_target_pairs={{0,4},{4,8},{8,12},{1,5},{5,9},{9,13},{2,6},{6,10},{10,14},{3,7},{... | collective-permute-start | bytes 1572872 | tf_op jit(solution)/shard_map/ppermute | solution.py:21
  141.5 8.1 %shard_map.123 = (f32[512,4096]{1,0:T(8,128)}, f32[512,4096]{1,0:T(8,128)}) custom-call(f32[512,4096]{1,0:T(8,128)} %dynamic_update_slice.14.xc_ref.refs_0_, f32[4,512,128]{2,1,0:T(8,128)} %bitcast.111, f32[4,128,512]{2,1,0:T(8,128)} %bitcast.120, f32[4,16,512]{2,1,0:T(8,128)} %copy-done.6, ...), custom_call_target="tpu_custom_call", output_to_operand_aliasing={{0}: (8, {}), {1}: (9, {})} | custom-call | tf_op jit(solution)/shard_map/pallas_call | solution.py:309
  151.2 1.3 fusion.1
  153.0 1.4 copy.97
  156.0 1.4 select_bitcast_fusion
  157.6 1.5 copy.98
  159.1 16.0 %shard_map.124 = bf16[512,4096]{1,0:T(8,128)(2,1)} custom-call(f32[512,4096]{1,0:T(8,128)} %get-tuple-element.114.y_ref, f32[4,512,128]{2,1,0:T(8,128)} %bitcast.112, f32[4,512,16]{2,1,0:T(8,128)} %bitcast.127, f32[4,8,128,128]{3,2,1,0:T(8,128)} %bitcast.125, f32[512,4096]{1,0:T(8,128)} %get-tuple-element.116.sz_ref, f32[1,4096]{1,0:T(1,128)} %bitcast.144), custom_call_target="tpu_custom_call" | custom-call | tf_op jit(solution)/shard_map/pallas_call | solution.py:361
  (110 shorter events, 27.4 us)
Async XLA Ops:
  0.0 16.4 %copy-start = (f32[2,4,128]{2,1,0:T(4,128)S(1)}, f32[2,4,128]{2,1,0:T(4,128)}, u32[]{:S(2)}) copy-start(f32[2,4,128]{2,1,0:T(4,128)} %param.19) | copy-start | bytes 12292
  0.0 17.2 %copy-start.17 = (f32[4,2,4,128]{3,2,1,0:T(4,128)S(1)}, f32[4,2,4,128]{3,2,1,0:T(4,128)}, u32[]{:S(2)}) copy-start(f32[4,2,4,128]{3,2,1,0:T(4,128)} %param.18) | copy-start | bytes 49156
  0.0 23.0 %copy-start.12 = (f32[4096]{0:T(1024)S(1)}, f32[4096]{0:T(1024)}, u32[]{:S(2)}) copy-start(f32[4096]{0:T(1024)} %param.17) | copy-start | bytes 49156
  3.4 46.1 %collective-permute-start = (bf16[3,4608]{1,0:T(4,128)(2,1)}, bf16[3,4608]{1,0:T(4,128)(2,1)}, u32[]{:S(2)}, u32[]{:S(2)}) collective-permute-start(bf16[3,4608]{1,0:T(4,128)(2,1)} %pad_maximum_fusion.2), channel_id=1, source_target_pairs={{0,4},{4,8},{8,12},{1,5},{5,9},{9,13},{2,6},{6,10},{10,14},{3,7},{... | collective-permute-start | bytes 82952 | tf_op jit(solution)/shard_map/ppermute | solution.py:21
  14.9 0.6 copy-start.8
  23.0 25.8 %copy-start.18 = (f32[64]{0:T(128)S(1)}, f32[64]{0:T(128)}, u32[]{:S(2)}) copy-start(f32[64]{0:T(128)} %param.22) | copy-start | bytes 772
  23.0 29.9 %copy-start.10 = (bf16[3,4096]{1,0:T(4,128)(2,1)S(1)}, bf16[3,4096]{1,0:T(4,128)(2,1)}, u32[]{:S(2)}) copy-start(bf16[3,4096]{1,0:T(4,128)(2,1)} %get-tuple-element.128) | copy-start | bytes 73732
  23.0 29.9 %copy-start.13 = (f32[4096]{0:T(1024)S(1)}, f32[4096]{0:T(1024)}, u32[]{:S(2)}) copy-start(f32[4096]{0:T(1024)} %param.17) | copy-start | bytes 49156
  47.3 20.4 %copy-start.6 = (f32[4,16,512]{2,1,0:T(8,128)}, f32[4,16,512]{2,1,0:T(8,128)S(1)}, u32[]{:S(2)}) copy-start(f32[4,16,512]{2,1,0:T(8,128)S(1)} %reshape.101.cumr_ref.refs_3_) | copy-start | bytes 393220
  52.1 27.4 %collective-permute-start.1 = (f32[2,4,64,512]{3,2,1,0:T(8,128)}, f32[2,4,64,512]{3,2,1,0:T(8,128)}, u32[]{:S(2)}, u32[]{:S(2)}) collective-permute-start(f32[2,4,64,512]{3,2,1,0:T(8,128)} %constant_dynamic-slice_fusion.5), channel_id=1, source_target_pairs={{0,1},{1,0},{2,3},{3,2},{4,5},{5,4},{6,7},{7,6},{8,9},{9,8},{10,11... | collective-permute-start | bytes 3145736 | tf_op jit(solution)/shard_map/ppermute | solution.py:25
  59.5 16.6 %copy-start.11 = (f32[4,8,128]{2,1,0:T(8,128)S(1)}, f32[4,8,128]{2,1,0:T(8,128)}, u32[]{:S(2)}) copy-start(f32[4,8,128]{2,1,0:T(8,128)} %mul.267) | copy-start | bytes 49156
  67.7 8.4 %copy-start.2 = (f32[4,8,64,128]{3,2,1,0:T(8,128)S(1)}, f32[4,8,64,128]{3,2,1,0:T(8,128)}, u32[]{:S(2)}) copy-start(f32[4,8,64,128]{3,2,1,0:T(8,128)} %shard_map.119) | copy-start | bytes 3145732
  67.7 10.9 %copy-start.16 = (f32[16,128]{1,0:T(8,128)S(1)}, f32[16,128]{1,0:T(8,128)}, u32[]{:S(2)}) copy-start(f32[16,128]{1,0:T(8,128)} %get-tuple-element.146) | copy-start | bytes 24580
  77.6 1.0 copy-start.4
  83.5 15.0 %collective-permute-start.2 = (f32[16,64,128]{2,1,0:T(8,128)}, f32[16,64,128]{2,1,0:T(8,128)S(1)}, u32[]{:S(2)}, u32[]{:S(2)}) collective-permute-start(f32[16,64,128]{2,1,0:T(8,128)} %bitcast_add_fusion), channel_id=1, source_target_pairs={{0,4},{4,8},{8,12},{1,5},{5,9},{9,13},{2,6},{6,10},{10,14},{3,7},{... | collective-permute-start | bytes 1572872 | tf_op jit(solution)/shard_map/ppermute | solution.py:21
  86.5 13.1 %copy-start.5 = (f32[4,8,64,128]{3,2,1,0:T(8,128)S(1)}, f32[4,8,64,128]{3,2,1,0:T(8,128)}, u32[]{:S(2)}) copy-start(f32[4,8,64,128]{3,2,1,0:T(8,128)} %copy-done.4) | copy-start | bytes 3145732
  86.5 13.1 %copy-start.15 = (f32[16,128]{1,0:T(8,128)S(1)}, f32[16,128]{1,0:T(8,128)}, u32[]{:S(2)}) copy-start(f32[16,128]{1,0:T(8,128)} %get-tuple-element.145) | copy-start | bytes 24580
  98.6 0.8 copy-start.7
  100.5 16.7 %collective-permute-start.3 = (f32[16,64,128]{2,1,0:T(8,128)}, f32[16,64,128]{2,1,0:T(8,128)}, u32[]{:S(2)}, u32[]{:S(2)}) collective-permute-start(f32[16,64,128]{2,1,0:T(8,128)} %fusion.8), channel_id=1, source_target_pairs={{0,4},{4,8},{8,12},{1,5},{5,9},{9,13},{2,6},{6,10},{10,14},{3,7},{... | collective-permute-start | bytes 1572872 | tf_op jit(solution)/shard_map/ppermute | solution.py:21
  106.6 11.7 %copy-start.14 = (f32[16,128]{1,0:T(8,128)S(1)}, f32[16,128]{1,0:T(8,128)}, u32[]{:S(2)}) copy-start(f32[16,128]{1,0:T(8,128)} %get-tuple-element.144) | copy-start | bytes 24580
  119.2 14.9 %collective-permute-start.4 = (f32[16,64,128]{2,1,0:T(8,128)}, f32[16,64,128]{2,1,0:T(8,128)}, u32[]{:S(2)}, u32[]{:S(2)}) collective-permute-start(f32[16,64,128]{2,1,0:T(8,128)} %fusion.6), channel_id=1, source_target_pairs={{0,4},{4,8},{8,12},{1,5},{5,9},{9,13},{2,6},{6,10},{10,14},{3,7},{... | collective-permute-start | bytes 1572872 | tf_op jit(solution)/shard_map/ppermute | solution.py:21
  124.4 16.9 %copy-start.9 = (f32[4,8,2]{2,1,0:T(8,128)S(1)}, f32[4,8,2]{2,1,0:T(8,128)}, u32[]{:S(2)}) copy-start(f32[4,8,2]{2,1,0:T(8,128)} %copy-done.8) | copy-start | bytes 772
  136.1 13.9 %collective-permute-start.5 = (f32[16,64,128]{2,1,0:T(8,128)}, f32[16,64,128]{2,1,0:T(8,128)}, u32[]{:S(2)}, u32[]{:S(2)}) collective-permute-start(f32[16,64,128]{2,1,0:T(8,128)} %fusion.4), channel_id=1, source_target_pairs={{0,4},{4,8},{8,12},{1,5},{5,9},{9,13},{2,6},{6,10},{10,14},{3,7},{... | collective-permute-start | bytes 1572872 | tf_op jit(solution)/shard_map/ppermute | solution.py:21
  141.5 9.7 %copy-start.3 = (f32[4,8,64,128]{3,2,1,0:T(8,128)S(1)}, f32[4,8,64,128]{3,2,1,0:T(8,128)}, u32[]{:S(2)}) copy-start(f32[4,8,64,128]{3,2,1,0:T(8,128)} %shard_map.118) | copy-start | bytes 3145732
  152.5 3.0 %collective-permute-start.6 = (f32[4,8,64,128]{3,2,1,0:T(8,128)}, f32[4,8,64,128]{3,2,1,0:T(8,128)}, u32[]{:S(2)}, u32[]{:S(2)}) collective-permute-start(f32[4,8,64,128]{3,2,1,0:T(8,128)} %fusion.1), channel_id=1, source_target_pairs={{0,1},{1,0},{2,3},{3,2},{4,5},{5,4},{6,7},{7,6},{8,9},{9,8},{10,11... | collective-permute-start | bytes 3145736 | tf_op jit(solution)/shard_map/ppermute | solution.py:25
  159.1 16.0 %copy-start.1 = (f32[2,4,128]{2,1,0:T(4,128)S(1)}, f32[2,4,128]{2,1,0:T(4,128)}, u32[]{:S(2)}) copy-start(f32[2,4,128]{2,1,0:T(4,128)} %param.19) | copy-start | bytes 12292

commit v10 on v8

--- a/solution.py
+++ b/solution.py
@@ -136,14 +136,14 @@
     heads = 2 * pairs
     ct = split(ct_ref[0])
     cumc = cumc_ref[0]
-    total = jnp.zeros((y_ref.shape[0], 1), F32)
+    total = jnp.zeros((y_ref.shape[0], 128), F32)
     for pair in range(pairs):
         lanes = slice(pair * 128, (pair + 1) * 128)
         cq = pair_columns(cumc, pair, y_ref.shape[0])
         gated = y_ref[:, lanes] + dot3(ct, split(v_ref[0, pair])) * jnp.exp(cq) * sz_ref[:, lanes]
         g_ref[:, lanes] = gated
-        total = total + jnp.sum(gated * gated, axis=-1, keepdims=True)
-    mean_square = total / g_ref.shape[1]
+        total = total + gated * gated
+    mean_square = jnp.sum(total, axis=-1, keepdims=True) / g_ref.shape[1]
     o_ref[...] = (g_ref[...] * lax.rsqrt(mean_square + 1e-05) * nw_ref[...]).astype(o_ref.dtype)
 
 
@@ -186,14 +186,13 @@
     x_rim = rims[:, :channels]
     bc_rim = rims[:, channels:].transpose(1, 0).reshape(bc_tail.shape)
     x_pad = jnp.concatenate([x_rim, x_raw], 0)
-    x_own = conv_rows(
-        lax.dynamic_slice_in_dim(x_pad, sub_index * own, own + rim_len, 0), conv_x_w, conv_x_b
-    )
-    x_other = conv_rows(
-        lax.dynamic_slice_in_dim(x_pad, (1 - sub_index) * own, own + rim_len, 0),
-        conv_x_w,
-        conv_x_b,
-    )
+    windows = lax.optimization_barrier(
+        tuple(
+            lax.dynamic_slice_in_dim(x_pad, at * own, own + rim_len, 0).astype(F32)
+            for at in (sub_index, 1 - sub_index)
+        )
+    )
+    x_own, x_other = (conv_rows(window, conv_x_w, conv_x_b) for window in windows)
     bc_weights = lax.dynamic_slice_in_dim(conv_bc_w, sub_index * half, half, 3)
     bc_bias = lax.dynamic_slice_in_dim(conv_bc_b, sub_index * half, half, 2)
     bc_conv = conv_cols(jnp.concatenate([bc_rim, bc_raw], 3), bc_weights, bc_bias)

time: 160 us -> 179 us (1.12)
  other arithmetic: 40.5 us -> 60 us
  Pallas kernels: 65.3 us -> 62.9 us
  local copies, waits for them, and re-layouts: 17.2 us -> 19.1 us
    mul x1, other arithmetic: 12.4 us -> 29.9 us  [conv_rows(): return jax.nn.silu(total)]
    convert_element_type x0 -> x1, other arithmetic: none -> 9.53 us  [per_device(): lax.dynamic_slice_in_dim(x_pad, at * own, own + rim_len, 0).astype(F32)]
    concatenate x1 -> x0, other arithmetic: 4.98 us -> none  [per_device(): x_pad = jnp.concatenate([x_rim, x_raw], 0)]
    mul x1, other arithmetic: 5.47 us -> 2.84 us  [conv_cols(): return jax.nn.silu(total)]
    pallas_call x1, Pallas kernels: 16 us -> 13.6 us  [per_device(): pl.pallas_call(out_kernel, grid=(set_groups, own // out_len), in_specs=[p...]
  transfers between devices with their start and end apart: 7 -> 7, of which waited for: 5 -> 5; matrix products, arithmetic and copies ran while one was open for 20% -> 26% of each run, Pallas kernels for 31% -> 28%
where the time goes in v10:
time: 179 us; the launch traced here: 177 us
  Pallas kernels  62.9 us (35%)
  other arithmetic  60 us (34%)
  starting transfers between devices  25.1 us (14%)
  local copies, waits for them, and re-layouts  19.1 us (11%)
  waiting for transfers between devices  9.46 us (5%)
    pallas_call x4, Pallas kernels, scan_group(): pl.pallas_call(kernel, grid=(1, blocks), in_specs=in_specs, out_specs=[ti...  32.6 us
    mul x1, other arithmetic, conv_rows(): return jax.nn.silu(total)  29.9 us
    ppermute x5, starting transfers between devices, passed_along(): return lax.ppermute(x, axis, pairs)  25.1 us
    pallas_call x2, Pallas kernels, end_states(): pl.pallas_call(end_kernel, grid=(set_groups,), in_specs=[pl.BlockSpec((ow...  16.7 us
    pallas_call x1, Pallas kernels, per_device(): pl.pallas_call(out_kernel, grid=(set_groups, own // out_len), in_specs=[p...  13.6 us
    convert_element_type x1, other arithmetic, per_device(): lax.dynamic_slice_in_dim(x_pad, at * own, own + rim_len, 0).astype(F32)  9.53 us
    ppermute x5, waiting for transfers between devices, passed_along(): return lax.ppermute(x, axis, pairs)  8.26 us
  transfers between devices with their start and end apart: 7, of which 5 were waited for; matrix products, arithmetic and copies ran while one was open for 26% of the time, Pallas kernels for 28%

profile of v10, /device:TPU:0, one launch (start us, length us, event | category | flops | bytes accessed | tf_op | source)
XLA Modules:
  0.0 177.4 jit_solution(14293562883232151868)
XLA Ops:
  2.1 4.9 %collective-permute-start = (bf16[3,4608]{1,0:T(4,128)(2,1)S(1)}, bf16[3,4608]{1,0:T(4,128)(2,1)S(1)}, u32[]{:S(2)}, u32[]{:S(2)}) collective-permute-start(bf16[3,4608]{1,0:T(4,128)(2,1)S(1)} %pad_maximum_fusion.3), channel_id=1, source_target_pairs={{0,4},{4,8},{8,12},{1,5},{5,9},{9,13},{2,6},{6,10},{10,14},{3,7},{... | collective-permute-start | bytes 82952 | tf_op jit(solution)/shard_map/ppermute | solution.py:21
  7.7 1.2 broadcast_multiply_fusion
  16.5 1.3 copy.69
  18.7 9.5 %fusion.1 = (f32[515,4096]{1,0:T(8,128)}, f32[515,4096]{1,0:T(8,128)}) fusion(s32[]{:T(128)S(6)} %select_n.129, bf16[1024,4096]{1,0:T(8,128)(2,1)} %param.12, bf16[3,4096]{1,0:T(4,128)(2,1)S(1)} %slice.132, s32[]{:T(128)S(6)} %select_n.128), kind=kLoop, calls=%fused_computation.7 | loop fusion | flops 16875520 | bytes 25288712 | tf_op jit(solution)/shard_map/convert_element_type | solution.py:191
  28.4 2.8 %divide_multiply_fusion.2 = f32[2,4,64,1024]{3,2,1,0:T(8,128)S(1)} fusion(bf16[2,4,64,1024]{3,2,1,0:T(8,128)(2,1)S(1)} %copy-done.7, bf16[2,4,64,3]{3,2,1,0:T(8,128)(2,1)S(1)} %bitcast.132, f32[2,4,64]{2,1,0:T(4,128)S(1)} %copy-done.9, f32[2,4,64]{2,1,0:T(4,128)S(1)} %get-tuple-element.148, f32[2,4,64]{2,1,0:T(4,128)S(1)} %get-tuple-element.149, ...), kind=kLoop, calls=%fused_computation.13 | loop fusion | flops 13107200 | bytes 3159040 | tf_op jit(solution)/shard_map/jit(silu)/mul | solution.py:45
  32.3 29.9 %divide_multiply_fusion.1 = (f32[512,4096]{1,0:T(8,128)}, f32[512,4096]{1,0:T(8,128)}) fusion(f32[515,4096]{1,0:T(8,128)} %get-tuple-element.63, f32[4096]{0:T(1024)S(1)} %bitcast.137, f32[4096]{0:T(1024)S(1)} %bitcast.138, f32[4096]{0:T(1024)S(1)} %bitcast.136, f32[4096]{0:T(1024)S(1)} %bitcast.135, f32[4096]{0:T(1024)} %param.17, ...), kind=kLoop, calls=%fused_computation.3 | loop fusion | flops 50331648 | bytes 83968000 | tf_op jit(solution)/shard_map/jit(silu)/mul | solution.py:35
  63.4 8.3 %shard_map.119 = f32[4,8,64,128]{3,2,1,0:T(8,128)} custom-call(f32[512,4096]{1,0:T(8,128)} %get-tuple-element.138.xc_ref, f32[4,64,512]{2,1,0:T(8,128)} %get-tuple-element.134.b_ref, f32[4,16,512]{2,1,0:T(8,128)} %get-tuple-element.136.wk_ref), custom_call_target="tpu_custom_call" | custom-call | tf_op jit(solution)/shard_map/pallas_call | solution.py:247
  71.7 8.4 %shard_map.118 = f32[4,8,64,128]{3,2,1,0:T(8,128)} custom-call(f32[512,4096]{1,0:T(8,128)} %get-tuple-element.106.xc_ref.refs_0_, f32[4,64,512]{2,1,0:T(8,128)} %get-tuple-element.133.b_ref, f32[4,16,512]{2,1,0:T(8,128)} %get-tuple-element.135.wk_ref), custom_call_target="tpu_custom_call" | custom-call | tf_op jit(solution)/shard_map/pallas_call | solution.py:247
  80.1 1.5 select_add_fusion
  83.5 1.5 select_bitcast_fusion.2
  84.9 1.2 pad_maximum_fusion.1
  86.1 1.3 copy.66
  87.5 3.7 %collective-permute-start.2 = (f32[16,64,128]{2,1,0:T(8,128)}, f32[16,64,128]{2,1,0:T(8,128)S(1)}, u32[]{:S(2)}, u32[]{:S(2)}) collective-permute-start(f32[16,64,128]{2,1,0:T(8,128)} %bitcast_add_fusion), channel_id=1, source_target_pairs={{0,4},{4,8},{8,12},{1,5},{5,9},{9,13},{2,6},{6,10},{10,14},{3,7},{... | collective-permute-start | bytes 1572872 | tf_op jit(solution)/shard_map/ppermute | solution.py:21
  91.2 8.2 %shard_map.120 = (f32[512,4096]{1,0:T(8,128)}, f32[512,4096]{1,0:T(8,128)}) custom-call(f32[512,4096]{1,0:T(8,128)} %get-tuple-element.106.xc_ref.refs_0_, f32[4,512,128]{2,1,0:T(8,128)} %bitcast.107, f32[4,128,512]{2,1,0:T(8,128)} %bitcast.116, f32[4,16,512]{2,1,0:T(8,128)} %copy-done.6, f32[4,512,16]{2,1,0:T(8,128)} %bitcast.112, f32[4,16,512]{2,1,0:T(8,128)} %bitcast.127, ...), custom_call_target="tpu_custom_call" | custom-call | tf_op jit(solution)/shard_map/pallas_call | solution.py:299
  99.3 3.8 %collective-permute-done.2 = f32[16,64,128]{2,1,0:T(8,128)S(1)} collective-permute-done((f32[16,64,128]{2,1,0:T(8,128)}, f32[16,64,128]{2,1,0:T(8,128)S(1)}, u32[]{:S(2)}, u32[]{:S(2)}) %collective-permute-start.2) | collective-permute-done | bytes 524320 | tf_op jit(solution)/shard_map/ppermute | solution.py:21
  105.0 6.1 %collective-permute-start.3 = (f32[16,64,128]{2,1,0:T(8,128)}, f32[16,64,128]{2,1,0:T(8,128)}, u32[]{:S(2)}, u32[]{:S(2)}) collective-permute-start(f32[16,64,128]{2,1,0:T(8,128)} %fusion.14), channel_id=1, source_target_pairs={{0,4},{4,8},{8,12},{1,5},{5,9},{9,13},{2,6},{6,10},{10,14},{3,7},{... | collective-permute-start | bytes 1572872 | tf_op jit(solution)/shard_map/ppermute | solution.py:21
  111.1 8.1 %shard_map.121 = (f32[512,4096]{1,0:T(8,128)}, f32[512,4096]{1,0:T(8,128)}) custom-call(f32[512,4096]{1,0:T(8,128)} %get-tuple-element.106.xc_ref.refs_0_, f32[4,512,128]{2,1,0:T(8,128)} %bitcast.108, f32[4,128,512]{2,1,0:T(8,128)} %bitcast.117, f32[4,16,512]{2,1,0:T(8,128)} %copy-done.6, ...), custom_call_target="tpu_custom_call", output_to_operand_aliasing={{0}: (8, {}), {1}: (9, {})} | custom-call | tf_op jit(solution)/shard_map/pallas_call | solution.py:299
  119.2 2.5 %collective-permute-done.3 = f32[16,64,128]{2,1,0:T(8,128)} collective-permute-done((f32[16,64,128]{2,1,0:T(8,128)}, f32[16,64,128]{2,1,0:T(8,128)}, u32[]{:S(2)}, u32[]{:S(2)}) %collective-permute-start.3) | collective-permute-done | bytes 524320 | tf_op jit(solution)/shard_map/ppermute | solution.py:21
  121.7 1.2 fusion.13
  123.8 5.2 %collective-permute-start.4 = (f32[16,64,128]{2,1,0:T(8,128)}, f32[16,64,128]{2,1,0:T(8,128)}, u32[]{:S(2)}, u32[]{:S(2)}) collective-permute-start(f32[16,64,128]{2,1,0:T(8,128)} %fusion.12), channel_id=1, source_target_pairs={{0,4},{4,8},{8,12},{1,5},{5,9},{9,13},{2,6},{6,10},{10,14},{3,7},{... | collective-permute-start | bytes 1572872 | tf_op jit(solution)/shard_map/ppermute | solution.py:21
  129.0 8.1 %shard_map.122 = (f32[512,4096]{1,0:T(8,128)}, f32[512,4096]{1,0:T(8,128)}) custom-call(f32[512,4096]{1,0:T(8,128)} %get-tuple-element.106.xc_ref.refs_0_, f32[4,512,128]{2,1,0:T(8,128)} %bitcast.109, f32[4,128,512]{2,1,0:T(8,128)} %bitcast.118, f32[4,16,512]{2,1,0:T(8,128)} %copy-done.6, ...), custom_call_target="tpu_custom_call", output_to_operand_aliasing={{0}: (8, {}), {1}: (9, {})} | custom-call | tf_op jit(solution)/shard_map/pallas_call | solution.py:299
  137.1 1.6 collective-permute-done.4
  138.7 1.2 fusion.11
  140.8 5.2 %collective-permute-start.5 = (f32[16,64,128]{2,1,0:T(8,128)}, f32[16,64,128]{2,1,0:T(8,128)}, u32[]{:S(2)}, u32[]{:S(2)}) collective-permute-start(f32[16,64,128]{2,1,0:T(8,128)} %fusion.10), channel_id=1, source_target_pairs={{0,4},{4,8},{8,12},{1,5},{5,9},{9,13},{2,6},{6,10},{10,14},{3,7},{... | collective-permute-start | bytes 1572872 | tf_op jit(solution)/shard_map/ppermute | solution.py:21
  146.1 8.2 %shard_map.123 = (f32[512,4096]{1,0:T(8,128)}, f32[512,4096]{1,0:T(8,128)}) custom-call(f32[512,4096]{1,0:T(8,128)} %get-tuple-element.106.xc_ref.refs_0_, f32[4,512,128]{2,1,0:T(8,128)} %bitcast.110, f32[4,128,512]{2,1,0:T(8,128)} %bitcast.119, f32[4,16,512]{2,1,0:T(8,128)} %copy-done.6, ...), custom_call_target="tpu_custom_call", output_to_operand_aliasing={{0}: (8, {}), {1}: (9, {})} | custom-call | tf_op jit(solution)/shard_map/pallas_call | solution.py:299
  154.7 1.2 fusion.9
  155.9 1.3 fusion.7
  157.7 1.3 copy.71
  159.0 1.2 collective-permute-done.6
  160.7 1.4 select_bitcast_fusion
  162.3 1.5 copy.72
  163.8 13.6 %shard_map.124 = bf16[512,4096]{1,0:T(8,128)(2,1)} custom-call(f32[512,4096]{1,0:T(8,128)} %get-tuple-element.118.y_ref, f32[4,512,128]{2,1,0:T(8,128)} %bitcast.111, f32[4,512,16]{2,1,0:T(8,128)} %bitcast.126, f32[4,8,128,128]{3,2,1,0:T(8,128)} %bitcast.124, f32[512,4096]{1,0:T(8,128)} %get-tuple-element.120.sz_ref, f32[1,4096]{1,0:T(1,128)} %bitcast.140), custom_call_target="tpu_custom_call" | custom-call | tf_op jit(solution)/shard_map/pallas_call | solution.py:351
  (88 shorter events, 20.7 us)
Async XLA Ops:
  0.0 15.5 %copy-start = (f32[2,4,128]{2,1,0:T(4,128)S(1)}, f32[2,4,128]{2,1,0:T(4,128)}, u32[]{:S(2)}) copy-start(f32[2,4,128]{2,1,0:T(4,128)} %param.19) | copy-start | bytes 12292
  0.0 14.8 %copy-start.10 = (f32[4,2,4,128]{3,2,1,0:T(4,128)S(1)}, f32[4,2,4,128]{3,2,1,0:T(4,128)}, u32[]{:S(2)}) copy-start(f32[4,2,4,128]{3,2,1,0:T(4,128)} %param.18) | copy-start | bytes 49156
  0.0 17.9 %copy-start.11 = (f32[64]{0:T(128)S(1)}, f32[64]{0:T(128)}, u32[]{:S(2)}) copy-start(f32[64]{0:T(128)} %param.22) | copy-start | bytes 772
  2.1 16.6 %collective-permute-start = (bf16[3,4608]{1,0:T(4,128)(2,1)S(1)}, bf16[3,4608]{1,0:T(4,128)(2,1)S(1)}, u32[]{:S(2)}, u32[]{:S(2)}) collective-permute-start(bf16[3,4608]{1,0:T(4,128)(2,1)S(1)} %pad_maximum_fusion.3), channel_id=1, source_target_pairs={{0,4},{4,8},{8,12},{1,5},{5,9},{9,13},{2,6},{6,10},{10,14},{3,7},{... | collective-permute-start | bytes 82952 | tf_op jit(solution)/shard_map/ppermute | solution.py:21
  16.5 11.7 %copy-start.6 = (f32[4,16,512]{2,1,0:T(8,128)}, f32[4,16,512]{2,1,0:T(8,128)S(1)}, u32[]{:S(2)}) copy-start(f32[4,16,512]{2,1,0:T(8,128)S(1)} %reshape.101.cumr_ref.refs_3_) | copy-start | bytes 393220
  18.7 9.8 %copy-start.7 = (bf16[2,4,64,1024]{3,2,1,0:T(8,128)(2,1)S(1)}, bf16[2,4,64,1024]{3,2,1,0:T(8,128)(2,1)}, u32[]{:S(2)}) copy-start(bf16[2,4,64,1024]{3,2,1,0:T(8,128)(2,1)} %param.13) | copy-start | bytes 3145732
  18.7 9.7 %copy-start.9 = (f32[2,4,64]{2,1,0:T(4,128)S(1)}, f32[2,4,64]{2,1,0:T(4,128)}, u32[]{:S(2)}) copy-start(f32[2,4,64]{2,1,0:T(4,128)} %get-tuple-element.150) | copy-start | bytes 6148
  32.3 51.1 %collective-permute-start.1 = (f32[2,4,64,512]{3,2,1,0:T(8,128)}, f32[2,4,64,512]{3,2,1,0:T(8,128)}, u32[]{:S(2)}, u32[]{:S(2)}) collective-permute-start(f32[2,4,64,512]{3,2,1,0:T(8,128)} %constant_dynamic-slice_fusion.6), channel_id=1, source_target_pairs={{0,1},{1,0},{2,3},{3,2},{4,5},{5,4},{6,7},{7,6},{8,9},{9,8},{10,11... | collective-permute-start | bytes 3145736 | tf_op jit(solution)/shard_map/ppermute | solution.py:25
  71.7 8.4 %copy-start.2 = (f32[4,8,64,128]{3,2,1,0:T(8,128)S(1)}, f32[4,8,64,128]{3,2,1,0:T(8,128)}, u32[]{:S(2)}) copy-start(f32[4,8,64,128]{3,2,1,0:T(8,128)} %shard_map.119) | copy-start | bytes 3145732
  81.6 1.0 copy-start.4
  87.5 15.6 %collective-permute-start.2 = (f32[16,64,128]{2,1,0:T(8,128)}, f32[16,64,128]{2,1,0:T(8,128)S(1)}, u32[]{:S(2)}, u32[]{:S(2)}) collective-permute-start(f32[16,64,128]{2,1,0:T(8,128)} %bitcast_add_fusion), channel_id=1, source_target_pairs={{0,4},{4,8},{8,12},{1,5},{5,9},{9,13},{2,6},{6,10},{10,14},{3,7},{... | collective-permute-start | bytes 1572872 | tf_op jit(solution)/shard_map/ppermute | solution.py:21
  91.2 12.9 %copy-start.5 = (f32[4,8,64,128]{3,2,1,0:T(8,128)S(1)}, f32[4,8,64,128]{3,2,1,0:T(8,128)}, u32[]{:S(2)}) copy-start(f32[4,8,64,128]{3,2,1,0:T(8,128)} %copy-done.4) | copy-start | bytes 3145732
  103.1 0.8 copy-start.8
  105.0 16.7 %collective-permute-start.3 = (f32[16,64,128]{2,1,0:T(8,128)}, f32[16,64,128]{2,1,0:T(8,128)}, u32[]{:S(2)}, u32[]{:S(2)}) collective-permute-start(f32[16,64,128]{2,1,0:T(8,128)} %fusion.14), channel_id=1, source_target_pairs={{0,4},{4,8},{8,12},{1,5},{5,9},{9,13},{2,6},{6,10},{10,14},{3,7},{... | collective-permute-start | bytes 1572872 | tf_op jit(solution)/shard_map/ppermute | solution.py:21
  123.8 14.9 %collective-permute-start.4 = (f32[16,64,128]{2,1,0:T(8,128)}, f32[16,64,128]{2,1,0:T(8,128)}, u32[]{:S(2)}, u32[]{:S(2)}) collective-permute-start(f32[16,64,128]{2,1,0:T(8,128)} %fusion.12), channel_id=1, source_target_pairs={{0,4},{4,8},{8,12},{1,5},{5,9},{9,13},{2,6},{6,10},{10,14},{3,7},{... | collective-permute-start | bytes 1572872 | tf_op jit(solution)/shard_map/ppermute | solution.py:21
  140.8 14.0 %collective-permute-start.5 = (f32[16,64,128]{2,1,0:T(8,128)}, f32[16,64,128]{2,1,0:T(8,128)}, u32[]{:S(2)}, u32[]{:S(2)}) collective-permute-start(f32[16,64,128]{2,1,0:T(8,128)} %fusion.10), channel_id=1, source_target_pairs={{0,4},{4,8},{8,12},{1,5},{5,9},{9,13},{2,6},{6,10},{10,14},{3,7},{... | collective-permute-start | bytes 1572872 | tf_op jit(solution)/shard_map/ppermute | solution.py:21
  146.1 9.8 %copy-start.3 = (f32[4,8,64,128]{3,2,1,0:T(8,128)S(1)}, f32[4,8,64,128]{3,2,1,0:T(8,128)}, u32[]{:S(2)}) copy-start(f32[4,8,64,128]{3,2,1,0:T(8,128)} %shard_map.118) | copy-start | bytes 3145732
  157.2 3.0 %collective-permute-start.6 = (f32[4,8,64,128]{3,2,1,0:T(8,128)}, f32[4,8,64,128]{3,2,1,0:T(8,128)}, u32[]{:S(2)}, u32[]{:S(2)}) collective-permute-start(f32[4,8,64,128]{3,2,1,0:T(8,128)} %fusion.7), channel_id=1, source_target_pairs={{0,1},{1,0},{2,3},{3,2},{4,5},{5,4},{6,7},{7,6},{8,9},{9,8},{10,11... | collective-permute-start | bytes 3145736 | tf_op jit(solution)/shard_map/ppermute | solution.py:25
  163.8 13.6 %copy-start.1 = (f32[2,4,128]{2,1,0:T(4,128)S(1)}, f32[2,4,128]{2,1,0:T(4,128)}, u32[]{:S(2)}) copy-start(f32[2,4,128]{2,1,0:T(4,128)} %param.19) | copy-start | bytes 12292

commit v11 on v8

--- a/solution.py
+++ b/solution.py
@@ -136,14 +136,14 @@
     heads = 2 * pairs
     ct = split(ct_ref[0])
     cumc = cumc_ref[0]
-    total = jnp.zeros((y_ref.shape[0], 1), F32)
+    total = jnp.zeros((y_ref.shape[0], 128), F32)
     for pair in range(pairs):
         lanes = slice(pair * 128, (pair + 1) * 128)
         cq = pair_columns(cumc, pair, y_ref.shape[0])
         gated = y_ref[:, lanes] + dot3(ct, split(v_ref[0, pair])) * jnp.exp(cq) * sz_ref[:, lanes]
         g_ref[:, lanes] = gated
-        total = total + jnp.sum(gated * gated, axis=-1, keepdims=True)
-    mean_square = total / g_ref.shape[1]
+        total = total + gated * gated
+    mean_square = jnp.sum(total, axis=-1, keepdims=True) / g_ref.shape[1]
     o_ref[...] = (g_ref[...] * lax.rsqrt(mean_square + 1e-05) * nw_ref[...]).astype(o_ref.dtype)
 
 

time: 160 us -> 157 us (0.981)
  Pallas kernels: 65.3 us -> 62.9 us
    pallas_call x1, Pallas kernels: 16 us -> 13.6 us  [per_device(): pl.pallas_call(out_kernel, grid=(set_groups, own // out_len), in_specs=[p...]
  transfers between devices with their start and end apart: 7 -> 7, of which waited for: 5 -> 5; matrix products, arithmetic and copies ran while one was open for 20% -> 21% of each run, Pallas kernels for 31% -> 32%
where the time goes in v11:
time: 157 us; the launch traced here: 156 us
  Pallas kernels  62.9 us (40%)
  other arithmetic  40.5 us (26%)
  starting transfers between devices  25.1 us (16%)
  local copies, waits for them, and re-layouts  17.2 us (11%)
  waiting for transfers between devices  9.2 us (6%)
    pallas_call x4, Pallas kernels, scan_group(): pl.pallas_call(kernel, grid=(1, blocks), in_specs=in_specs, out_specs=[ti...  32.6 us
    ppermute x5, starting transfers between devices, passed_along(): return lax.ppermute(x, axis, pairs)  25.1 us
    pallas_call x2, Pallas kernels, end_states(): pl.pallas_call(end_kernel, grid=(set_groups,), in_specs=[pl.BlockSpec((ow...  16.6 us
    pallas_call x1, Pallas kernels, per_device(): pl.pallas_call(out_kernel, grid=(set_groups, own // out_len), in_specs=[p...  13.6 us
    mul x1, other arithmetic, conv_rows(): return jax.nn.silu(total)  12.4 us
    ppermute x5, waiting for transfers between devices, passed_along(): return lax.ppermute(x, axis, pairs)  8.09 us
    mul x1, other arithmetic, conv_cols(): return jax.nn.silu(total)  5.47 us
    concatenate x1, other arithmetic, per_device(): x_pad = jnp.concatenate([x_rim, x_raw], 0)  4.98 us
  transfers between devices with their start and end apart: 7, of which 5 were waited for; matrix products, arithmetic and copies ran while one was open for 21% of the time, Pallas kernels for 32%

profile of v11, /device:TPU:0, one launch (start us, length us, event | category | flops | bytes accessed | tf_op | source)
XLA Modules:
  0.0 155.8 jit_solution(16377170488770134807)
XLA Ops:
  2.1 4.9 %collective-permute-start = (bf16[3,4608]{1,0:T(4,128)(2,1)S(1)}, bf16[3,4608]{1,0:T(4,128)(2,1)S(1)}, u32[]{:S(2)}, u32[]{:S(2)}) collective-permute-start(bf16[3,4608]{1,0:T(4,128)(2,1)S(1)} %pad_maximum_fusion.3), channel_id=1, source_target_pairs={{0,4},{4,8},{8,12},{1,5},{5,9},{9,13},{2,6},{6,10},{10,14},{3,7},{... | collective-permute-start | bytes 82952 | tf_op jit(solution)/shard_map/ppermute | solution.py:21
  7.7 1.2 broadcast_multiply_fusion
  14.4 1.4 copy.69
  16.8 5.5 %divide_multiply_fusion.2 = f32[2,4,64,1024]{3,2,1,0:T(8,128)S(1)} fusion(bf16[2,4,64,1024]{3,2,1,0:T(8,128)(2,1)} %param.13, bf16[2,4,64,3]{3,2,1,0:T(8,128)(2,1)S(1)} %bitcast.132, f32[2,4,64]{2,1,0:T(4,128)S(1)} %get-tuple-element.146, f32[2,4,64]{2,1,0:T(4,128)S(1)} %get-tuple-element.144, f32[2,4,64]{2,1,0:T(4,128)S(1)} %get-tuple-element.145, ...), kind=kLoop, calls=%fused_computation.11 | loop fusion | flops 13107200 | bytes 3159040 | tf_op jit(solution)/shard_map/jit(silu)/mul | solution.py:45
  23.4 5.0 %fusion.1 = (bf16[515,4096]{1,0:T(8,128)(2,1)S(1)}, bf16[515,4096]{1,0:T(8,128)(2,1)S(1)}) fusion(s32[]{:T(128)S(6)} %select_n.128, bf16[1024,4096]{1,0:T(8,128)(2,1)} %param.12, bf16[3,4096]{1,0:T(4,128)(2,1)S(1)} %slice.132, s32[]{:T(128)S(6)} %select_n.131), kind=kLoop, calls=%fused_computation.7 | loop fusion | flops 16875520 | bytes 16850952 | tf_op jit(solution)/shard_map/concatenate | solution.py:188
  28.4 12.4 %divide_multiply_fusion.1 = (f32[512,4096]{1,0:T(8,128)}, f32[512,4096]{1,0:T(8,128)}) fusion(bf16[515,4096]{1,0:T(8,128)(2,1)S(1)} %get-tuple-element.123, f32[4096]{0:T(1024)S(1)} %bitcast.137, f32[4096]{0:T(1024)S(1)} %bitcast.138, f32[4096]{0:T(1024)S(1)} %bitcast.136, f32[4096]{0:T(1024)S(1)} %bitcast.135, f32[4096]{0:T(1024)S(1)} %copy-done.9, ...), kind=kLoop, calls=%fused_computation.3 | loop fusion | flops 67108864 | bytes 50413568 | tf_op jit(solution)/shard_map/jit(silu)/mul | solution.py:35
  41.9 8.3 %shard_map.119 = f32[4,8,64,128]{3,2,1,0:T(8,128)} custom-call(f32[512,4096]{1,0:T(8,128)} %get-tuple-element.134.xc_ref, f32[4,64,512]{2,1,0:T(8,128)} %get-tuple-element.130.b_ref, f32[4,16,512]{2,1,0:T(8,128)} %get-tuple-element.132.wk_ref), custom_call_target="tpu_custom_call" | custom-call | tf_op jit(solution)/shard_map/pallas_call | solution.py:248
  50.2 8.4 %shard_map.118 = f32[4,8,64,128]{3,2,1,0:T(8,128)} custom-call(f32[512,4096]{1,0:T(8,128)} %get-tuple-element.102.xc_ref.refs_0_, f32[4,64,512]{2,1,0:T(8,128)} %get-tuple-element.129.b_ref, f32[4,16,512]{2,1,0:T(8,128)} %get-tuple-element.131.wk_ref), custom_call_target="tpu_custom_call" | custom-call | tf_op jit(solution)/shard_map/pallas_call | solution.py:248
  58.6 1.5 select_add_fusion
  62.0 1.5 select_bitcast_fusion.2
  63.5 1.2 pad_maximum_fusion.1
  64.6 1.3 copy.66
  66.0 3.7 %collective-permute-start.2 = (f32[16,64,128]{2,1,0:T(8,128)}, f32[16,64,128]{2,1,0:T(8,128)S(1)}, u32[]{:S(2)}, u32[]{:S(2)}) collective-permute-start(f32[16,64,128]{2,1,0:T(8,128)} %bitcast_add_fusion), channel_id=1, source_target_pairs={{0,4},{4,8},{8,12},{1,5},{5,9},{9,13},{2,6},{6,10},{10,14},{3,7},{... | collective-permute-start | bytes 1572872 | tf_op jit(solution)/shard_map/ppermute | solution.py:21
  69.7 8.2 %shard_map.120 = (f32[512,4096]{1,0:T(8,128)}, f32[512,4096]{1,0:T(8,128)}) custom-call(f32[512,4096]{1,0:T(8,128)} %get-tuple-element.102.xc_ref.refs_0_, f32[4,512,128]{2,1,0:T(8,128)} %bitcast.107, f32[4,128,512]{2,1,0:T(8,128)} %bitcast.116, f32[4,16,512]{2,1,0:T(8,128)} %copy-done.6, f32[4,512,16]{2,1,0:T(8,128)} %bitcast.112, f32[4,16,512]{2,1,0:T(8,128)} %bitcast.127, ...), custom_call_target="tpu_custom_call" | custom-call | tf_op jit(solution)/shard_map/pallas_call | solution.py:300
  77.9 3.7 %collective-permute-done.2 = f32[16,64,128]{2,1,0:T(8,128)S(1)} collective-permute-done((f32[16,64,128]{2,1,0:T(8,128)}, f32[16,64,128]{2,1,0:T(8,128)S(1)}, u32[]{:S(2)}, u32[]{:S(2)}) %collective-permute-start.2) | collective-permute-done | bytes 524320 | tf_op jit(solution)/shard_map/ppermute | solution.py:21
  83.5 6.1 %collective-permute-start.3 = (f32[16,64,128]{2,1,0:T(8,128)}, f32[16,64,128]{2,1,0:T(8,128)}, u32[]{:S(2)}, u32[]{:S(2)}) collective-permute-start(f32[16,64,128]{2,1,0:T(8,128)} %fusion.12), channel_id=1, source_target_pairs={{0,4},{4,8},{8,12},{1,5},{5,9},{9,13},{2,6},{6,10},{10,14},{3,7},{... | collective-permute-start | bytes 1572872 | tf_op jit(solution)/shard_map/ppermute | solution.py:21
  89.6 8.1 %shard_map.121 = (f32[512,4096]{1,0:T(8,128)}, f32[512,4096]{1,0:T(8,128)}) custom-call(f32[512,4096]{1,0:T(8,128)} %get-tuple-element.102.xc_ref.refs_0_, f32[4,512,128]{2,1,0:T(8,128)} %bitcast.108, f32[4,128,512]{2,1,0:T(8,128)} %bitcast.117, f32[4,16,512]{2,1,0:T(8,128)} %copy-done.6, ...), custom_call_target="tpu_custom_call", output_to_operand_aliasing={{0}: (8, {}), {1}: (9, {})} | custom-call | tf_op jit(solution)/shard_map/pallas_call | solution.py:300
  97.7 2.4 %collective-permute-done.3 = f32[16,64,128]{2,1,0:T(8,128)} collective-permute-done((f32[16,64,128]{2,1,0:T(8,128)}, f32[16,64,128]{2,1,0:T(8,128)}, u32[]{:S(2)}, u32[]{:S(2)}) %collective-permute-start.3) | collective-permute-done | bytes 524320 | tf_op jit(solution)/shard_map/ppermute | solution.py:21
  100.2 1.2 fusion.11
  102.2 5.2 %collective-permute-start.4 = (f32[16,64,128]{2,1,0:T(8,128)}, f32[16,64,128]{2,1,0:T(8,128)}, u32[]{:S(2)}, u32[]{:S(2)}) collective-permute-start(f32[16,64,128]{2,1,0:T(8,128)} %fusion.10), channel_id=1, source_target_pairs={{0,4},{4,8},{8,12},{1,5},{5,9},{9,13},{2,6},{6,10},{10,14},{3,7},{... | collective-permute-start | bytes 1572872 | tf_op jit(solution)/shard_map/ppermute | solution.py:21
  107.4 8.1 %shard_map.122 = (f32[512,4096]{1,0:T(8,128)}, f32[512,4096]{1,0:T(8,128)}) custom-call(f32[512,4096]{1,0:T(8,128)} %get-tuple-element.102.xc_ref.refs_0_, f32[4,512,128]{2,1,0:T(8,128)} %bitcast.109, f32[4,128,512]{2,1,0:T(8,128)} %bitcast.118, f32[4,16,512]{2,1,0:T(8,128)} %copy-done.6, ...), custom_call_target="tpu_custom_call", output_to_operand_aliasing={{0}: (8, {}), {1}: (9, {})} | custom-call | tf_op jit(solution)/shard_map/pallas_call | solution.py:300
  115.5 1.6 %collective-permute-done.4 = f32[16,64,128]{2,1,0:T(8,128)} collective-permute-done((f32[16,64,128]{2,1,0:T(8,128)}, f32[16,64,128]{2,1,0:T(8,128)}, u32[]{:S(2)}, u32[]{:S(2)}) %collective-permute-start.4) | collective-permute-done | bytes 524320 | tf_op jit(solution)/shard_map/ppermute | solution.py:21
  117.1 1.2 fusion.9
  119.2 5.2 %collective-permute-start.5 = (f32[16,64,128]{2,1,0:T(8,128)}, f32[16,64,128]{2,1,0:T(8,128)}, u32[]{:S(2)}, u32[]{:S(2)}) collective-permute-start(f32[16,64,128]{2,1,0:T(8,128)} %fusion.8), channel_id=1, source_target_pairs={{0,4},{4,8},{8,12},{1,5},{5,9},{9,13},{2,6},{6,10},{10,14},{3,7},{... | collective-permute-start | bytes 1572872 | tf_op jit(solution)/shard_map/ppermute | solution.py:21
  124.5 8.2 %shard_map.123 = (f32[512,4096]{1,0:T(8,128)}, f32[512,4096]{1,0:T(8,128)}) custom-call(f32[512,4096]{1,0:T(8,128)} %get-tuple-element.102.xc_ref.refs_0_, f32[4,512,128]{2,1,0:T(8,128)} %bitcast.110, f32[4,128,512]{2,1,0:T(8,128)} %bitcast.119, f32[4,16,512]{2,1,0:T(8,128)} %copy-done.6, ...), custom_call_target="tpu_custom_call", output_to_operand_aliasing={{0}: (8, {}), {1}: (9, {})} | custom-call | tf_op jit(solution)/shard_map/pallas_call | solution.py:300
  133.1 1.2 fusion.7
  134.3 1.3 fusion.5
  136.1 1.4 copy.71
  137.5 1.1 collective-permute-done.6
  139.1 1.4 select_bitcast_fusion
  140.7 1.5 copy.72
  142.2 13.6 %shard_map.124 = bf16[512,4096]{1,0:T(8,128)(2,1)} custom-call(f32[512,4096]{1,0:T(8,128)} %get-tuple-element.114.y_ref, f32[4,512,128]{2,1,0:T(8,128)} %bitcast.111, f32[4,512,16]{2,1,0:T(8,128)} %bitcast.126, f32[4,8,128,128]{3,2,1,0:T(8,128)} %bitcast.124, f32[512,4096]{1,0:T(8,128)} %get-tuple-element.116.sz_ref, f32[1,4096]{1,0:T(1,128)} %bitcast.140), custom_call_target="tpu_custom_call" | custom-call | tf_op jit(solution)/shard_map/pallas_call | solution.py:352
  (88 shorter events, 18.4 us)
Async XLA Ops:
  0.0 14.0 %copy-start = (f32[2,4,128]{2,1,0:T(4,128)S(1)}, f32[2,4,128]{2,1,0:T(4,128)}, u32[]{:S(2)}) copy-start(f32[2,4,128]{2,1,0:T(4,128)} %param.19) | copy-start | bytes 12292
  0.0 10.1 %copy-start.8 = (f32[4,4096]{1,0:T(4,128)S(1)}, f32[4,4096]{1,0:T(4,128)}, u32[]{:S(2)}) copy-start(f32[4,4096]{1,0:T(4,128)} %param.16) | copy-start | bytes 196612
  2.1 14.6 %collective-permute-start = (bf16[3,4608]{1,0:T(4,128)(2,1)S(1)}, bf16[3,4608]{1,0:T(4,128)(2,1)S(1)}, u32[]{:S(2)}, u32[]{:S(2)}) collective-permute-start(bf16[3,4608]{1,0:T(4,128)(2,1)S(1)} %pad_maximum_fusion.3), channel_id=1, source_target_pairs={{0,4},{4,8},{8,12},{1,5},{5,9},{9,13},{2,6},{6,10},{10,14},{3,7},{... | collective-permute-start | bytes 82952 | tf_op jit(solution)/shard_map/ppermute | solution.py:21
  7.7 6.2 %copy-start.10 = (f32[4,2,4,128]{3,2,1,0:T(4,128)S(1)}, f32[4,2,4,128]{3,2,1,0:T(4,128)}, u32[]{:S(2)}) copy-start(f32[4,2,4,128]{3,2,1,0:T(4,128)} %param.18) | copy-start | bytes 49156
  9.6 6.2 %copy-start.11 = (f32[64]{0:T(128)S(1)}, f32[64]{0:T(128)}, u32[]{:S(2)}) copy-start(f32[64]{0:T(128)} %param.22) | copy-start | bytes 772
  14.4 14.0 %copy-start.6 = (f32[4,16,512]{2,1,0:T(8,128)}, f32[4,16,512]{2,1,0:T(8,128)S(1)}, u32[]{:S(2)}) copy-start(f32[4,16,512]{2,1,0:T(8,128)S(1)} %reshape.101.cumr_ref.refs_3_) | copy-start | bytes 393220
  23.4 38.6 %collective-permute-start.1 = (f32[2,4,64,512]{3,2,1,0:T(8,128)}, f32[2,4,64,512]{3,2,1,0:T(8,128)}, u32[]{:S(2)}, u32[]{:S(2)}) collective-permute-start(f32[2,4,64,512]{3,2,1,0:T(8,128)} %constant_dynamic-slice_fusion.5), channel_id=1, source_target_pairs={{0,1},{1,0},{2,3},{3,2},{4,5},{5,4},{6,7},{7,6},{8,9},{9,8},{10,11... | collective-permute-start | bytes 3145736 | tf_op jit(solution)/shard_map/ppermute | solution.py:25
  23.4 5.0 %copy-start.9 = (f32[4096]{0:T(1024)S(1)}, f32[4096]{0:T(1024)}, u32[]{:S(2)}) copy-start(f32[4096]{0:T(1024)} %param.17) | copy-start | bytes 49156
  50.2 8.4 %copy-start.2 = (f32[4,8,64,128]{3,2,1,0:T(8,128)S(1)}, f32[4,8,64,128]{3,2,1,0:T(8,128)}, u32[]{:S(2)}) copy-start(f32[4,8,64,128]{3,2,1,0:T(8,128)} %shard_map.119) | copy-start | bytes 3145732
  60.1 1.0 copy-start.4
  66.0 15.6 %collective-permute-start.2 = (f32[16,64,128]{2,1,0:T(8,128)}, f32[16,64,128]{2,1,0:T(8,128)S(1)}, u32[]{:S(2)}, u32[]{:S(2)}) collective-permute-start(f32[16,64,128]{2,1,0:T(8,128)} %bitcast_add_fusion), channel_id=1, source_target_pairs={{0,4},{4,8},{8,12},{1,5},{5,9},{9,13},{2,6},{6,10},{10,14},{3,7},{... | collective-permute-start | bytes 1572872 | tf_op jit(solution)/shard_map/ppermute | solution.py:21
  69.7 12.9 %copy-start.5 = (f32[4,8,64,128]{3,2,1,0:T(8,128)S(1)}, f32[4,8,64,128]{3,2,1,0:T(8,128)}, u32[]{:S(2)}) copy-start(f32[4,8,64,128]{3,2,1,0:T(8,128)} %copy-done.4) | copy-start | bytes 3145732
  81.6 0.8 copy-start.7
  83.5 16.7 %collective-permute-start.3 = (f32[16,64,128]{2,1,0:T(8,128)}, f32[16,64,128]{2,1,0:T(8,128)}, u32[]{:S(2)}, u32[]{:S(2)}) collective-permute-start(f32[16,64,128]{2,1,0:T(8,128)} %fusion.12), channel_id=1, source_target_pairs={{0,4},{4,8},{8,12},{1,5},{5,9},{9,13},{2,6},{6,10},{10,14},{3,7},{... | collective-permute-start | bytes 1572872 | tf_op jit(solution)/shard_map/ppermute | solution.py:21
  102.2 14.9 %collective-permute-start.4 = (f32[16,64,128]{2,1,0:T(8,128)}, f32[16,64,128]{2,1,0:T(8,128)}, u32[]{:S(2)}, u32[]{:S(2)}) collective-permute-start(f32[16,64,128]{2,1,0:T(8,128)} %fusion.10), channel_id=1, source_target_pairs={{0,4},{4,8},{8,12},{1,5},{5,9},{9,13},{2,6},{6,10},{10,14},{3,7},{... | collective-permute-start | bytes 1572872 | tf_op jit(solution)/shard_map/ppermute | solution.py:21
  119.2 13.9 %collective-permute-start.5 = (f32[16,64,128]{2,1,0:T(8,128)}, f32[16,64,128]{2,1,0:T(8,128)}, u32[]{:S(2)}, u32[]{:S(2)}) collective-permute-start(f32[16,64,128]{2,1,0:T(8,128)} %fusion.8), channel_id=1, source_target_pairs={{0,4},{4,8},{8,12},{1,5},{5,9},{9,13},{2,6},{6,10},{10,14},{3,7},{... | collective-permute-start | bytes 1572872 | tf_op jit(solution)/shard_map/ppermute | solution.py:21
  124.5 9.7 %copy-start.3 = (f32[4,8,64,128]{3,2,1,0:T(8,128)S(1)}, f32[4,8,64,128]{3,2,1,0:T(8,128)}, u32[]{:S(2)}) copy-start(f32[4,8,64,128]{3,2,1,0:T(8,128)} %shard_map.118) | copy-start | bytes 3145732
  135.6 3.0 %collective-permute-start.6 = (f32[4,8,64,128]{3,2,1,0:T(8,128)}, f32[4,8,64,128]{3,2,1,0:T(8,128)}, u32[]{:S(2)}, u32[]{:S(2)}) collective-permute-start(f32[4,8,64,128]{3,2,1,0:T(8,128)} %fusion.5), channel_id=1, source_target_pairs={{0,1},{1,0},{2,3},{3,2},{4,5},{5,4},{6,7},{7,6},{8,9},{9,8},{10,11... | collective-permute-start | bytes 3145736 | tf_op jit(solution)/shard_map/ppermute | solution.py:25
  142.2 13.6 %copy-start.1 = (f32[2,4,128]{2,1,0:T(4,128)S(1)}, f32[2,4,128]{2,1,0:T(4,128)}, u32[]{:S(2)}) copy-start(f32[2,4,128]{2,1,0:T(4,128)} %param.19) | copy-start | bytes 12292

commit v12 on v7

--- a/solution.py
+++ b/solution.py
@@ -133,7 +133,7 @@
     heads = 2 * pairs
     ct = split(ct_ref[0])
     cumc = cumc_ref[0]
-    total = jnp.zeros((y_ref.shape[0], 1), F32)
+    total = jnp.zeros((y_ref.shape[0], 128), F32)
     for pair in range(pairs):
         lanes = slice(pair * 128, (pair + 1) * 128)
         cq = pair_columns(cumc, pair, y_ref.shape[0])
@@ -141,8 +141,8 @@
         z = z_ref[:, lanes].astype(F32)
         gated = y * (z / (1.0 + jnp.exp(-z)))
         g_ref[:, lanes] = gated
-        total = total + jnp.sum(gated * gated, axis=-1, keepdims=True)
-    mean_square = total / g_ref.shape[1]
+        total = total + gated * gated
+    mean_square = jnp.sum(total, axis=-1, keepdims=True) / g_ref.shape[1]
     o_ref[...] = (g_ref[...] * lax.rsqrt(mean_square + 1e-05) * nw_ref[...]).astype(o_ref.dtype)
 
 
@@ -196,11 +196,8 @@
     bc_weights = lax.dynamic_slice_in_dim(conv_bc_w, sub_index * half, half, 3)
     bc_bias = lax.dynamic_slice_in_dim(conv_bc_b, sub_index * half, half, 2)
     bc_conv = conv_cols(jnp.concatenate([bc_rim, bc_raw], 3), bc_weights, bc_bias)
-    bc_halves = bc_conv.reshape(2, set_groups, half, nsub, own)
-    bc_mine = lax.dynamic_index_in_dim(bc_halves, sub_index, 3, keepdims=False)
-    bc_theirs = swapped(
-        lax.dynamic_index_in_dim(bc_halves, 1 - sub_index, 3, keepdims=False), "sub"
-    )
+    bc_mine = lax.dynamic_slice_in_dim(bc_conv, sub_index * own, own, 3)
+    bc_theirs = swapped(lax.dynamic_slice_in_dim(bc_conv, (1 - sub_index) * own, own, 3), "sub")
     bc_own = jnp.stack(
         [
             jnp.where(sub_index == 0, bc_mine, bc_theirs),
@@ -280,9 +277,11 @@
     scan_inputs = (x_own, c_cols, b_rows, cum_rows, cum_cols, step_rows, skip_row)
 
     def scan_group(group, inputs, target):
-        extra = {} if target is None else {"input_output_aliases": {len(inputs): 0}}
+        count = len(inputs)
+        extra = {} if target is None else {"input_output_aliases": {count: 0}}
+        tile = pl.BlockSpec((block_len, group_width), lambda g, c: (c, group))
         in_specs = [
-            pl.BlockSpec((block_len, group_width), lambda g, c: (c, group)),
+            tile,
             pl.BlockSpec((1, block_len, state), lambda g, c: (group, c, 0)),
             pl.BlockSpec((1, state, block_len), lambda g, c: (group, 0, c)),
             pl.BlockSpec((1, per_group, block_len), lambda g, c: (group, 0, c)),
@@ -291,15 +290,16 @@
             pl.BlockSpec((1, group_width), lambda g, c: (0, group)),
         ]
         operands = tuple(inputs)
+        kernel = scan_kernel
         if target is not None:
-            in_specs.append(pl.BlockSpec(memory_space=pl.ANY))
+            in_specs = in_specs + [pl.BlockSpec(memory_space=pl.ANY)]
             operands = operands + (target,)
-        kernel = scan_kernel if target is None else (lambda *refs: scan_kernel(*refs[:7], *refs[8:]))
+            kernel = lambda *refs: scan_kernel(*refs[:count], *refs[count + 1 :])
         return pl.pallas_call(
             kernel,
             grid=(1, blocks),
             in_specs=in_specs,
-            out_specs=pl.BlockSpec((block_len, group_width), lambda g, c: (c, group)),
+            out_specs=tile,
             out_shape=jax.ShapeDtypeStruct((own, channels), F32),
             scratch_shapes=[pltpu.VMEM((pairs, state, 128), F32)],
             **extra,

time: 165 us -> 155 us (0.939)
  local copies, waits for them, and re-layouts: 25.2 us -> 16.2 us
  Pallas kernels: 62.9 us -> 60 us
  other arithmetic: 38.5 us -> 40.5 us
    dynamic_slice x1, local copies, waits for them, and re-layouts: 4.38 us -> 1.08 us  [per_device(): lax.dynamic_slice_in_dim(bc_conv, (1 - sub_index) * own, own, 3)]
    pallas_call x1, Pallas kernels: 15.3 us -> 12.4 us  [per_device(): pl.pallas_call(out_kernel, grid=(set_groups, own // out_len), in_specs=[p...]
    reshape x1 -> x0, local copies, waits for them, and re-layouts: 2.78 us -> none  [per_device(): bc_halves = bc_conv.reshape(2, set_groups, half, nsub, own)]
    mul x1, other arithmetic: 2.93 us -> 5.47 us  [conv_cols(): return jax.nn.silu(total)]
  transfers between devices with their start and end apart: 7 -> 7, of which waited for: 5 -> 5; matrix products, arithmetic and copies ran while one was open for 21% -> 21% of each run, Pallas kernels for 29% -> 31%
where the time goes in v12:
time: 155 us; the launch traced here: 154 us
  Pallas kernels  60 us (39%)
  other arithmetic  40.5 us (26%)
  starting transfers between devices  25.8 us (17%)
  local copies, waits for them, and re-layouts  16.2 us (10%)
  waiting for transfers between devices  10.4 us (7%)
    pallas_call x4, Pallas kernels, scan_group(): pl.pallas_call(kernel, grid=(1, blocks), in_specs=in_specs, out_specs=til...  30.9 us
    ppermute x5, starting transfers between devices, passed_along(): return lax.ppermute(x, axis, pairs)  25.8 us
    pallas_call x2, Pallas kernels, end_states(): pl.pallas_call(end_kernel, grid=(set_groups,), in_specs=[pl.BlockSpec((ow...  16.6 us
    pallas_call x1, Pallas kernels, per_device(): pl.pallas_call(out_kernel, grid=(set_groups, own // out_len), in_specs=[p...  12.4 us
    mul x1, other arithmetic, conv_rows(): return jax.nn.silu(total)  12.4 us
    ppermute x5, waiting for transfers between devices, passed_along(): return lax.ppermute(x, axis, pairs)  9.16 us
    mul x1, other arithmetic, conv_cols(): return jax.nn.silu(total)  5.47 us
    concatenate x1, other arithmetic, per_device(): x_pad = jnp.concatenate([x_rim, x_raw], 0)  4.98 us
  transfers between devices with their start and end apart: 7, of which 5 were waited for; matrix products, arithmetic and copies ran while one was open for 21% of the time, Pallas kernels for 31%

profile of v12, /device:TPU:0, one launch (start us, length us, event | category | flops | bytes accessed | tf_op | source)
XLA Modules:
  0.0 153.7 jit_solution(12836489375091086520)
XLA Ops:
  2.1 4.9 %collective-permute-start = (bf16[3,4608]{1,0:T(4,128)(2,1)S(1)}, bf16[3,4608]{1,0:T(4,128)(2,1)S(1)}, u32[]{:S(2)}, u32[]{:S(2)}) collective-permute-start(bf16[3,4608]{1,0:T(4,128)(2,1)S(1)} %pad_maximum_fusion.3), channel_id=1, source_target_pairs={{0,4},{4,8},{8,12},{1,5},{5,9},{9,13},{2,6},{6,10},{10,14},{3,7},{... | collective-permute-start | bytes 82952 | tf_op jit(solution)/shard_map/ppermute | solution.py:21
  7.7 1.2 broadcast_multiply_fusion
  14.4 1.3 copy.66
  16.7 5.5 %divide_multiply_fusion.2 = f32[2,4,64,1024]{3,2,1,0:T(8,128)S(1)} fusion(bf16[2,4,64,1024]{3,2,1,0:T(8,128)(2,1)} %param.13, bf16[2,4,64,3]{3,2,1,0:T(8,128)(2,1)S(1)} %bitcast.132, f32[2,4,64]{2,1,0:T(4,128)S(1)} %get-tuple-element.114, f32[2,4,64]{2,1,0:T(4,128)S(1)} %get-tuple-element.112, f32[2,4,64]{2,1,0:T(4,128)S(1)} %get-tuple-element.113, ...), kind=kLoop, calls=%fused_computation.11 | loop fusion | flops 13107200 | bytes 3159040 | tf_op jit(solution)/shard_map/jit(silu)/mul | solution.py:45
  23.3 5.0 %fusion.1 = (bf16[515,4096]{1,0:T(8,128)(2,1)S(1)}, bf16[515,4096]{1,0:T(8,128)(2,1)S(1)}) fusion(s32[]{:T(128)S(6)} %select_n.128, bf16[1024,4096]{1,0:T(8,128)(2,1)} %param.12, bf16[3,4096]{1,0:T(4,128)(2,1)S(1)} %slice.132, s32[]{:T(128)S(6)} %select_n.131), kind=kLoop, calls=%fused_computation.7 | loop fusion | flops 16875520 | bytes 16850952 | tf_op jit(solution)/shard_map/concatenate | solution.py:187
  28.3 12.4 %divide_multiply_fusion.1 = (f32[512,4096]{1,0:T(8,128)}, f32[512,4096]{1,0:T(8,128)}) fusion(bf16[515,4096]{1,0:T(8,128)(2,1)S(1)} %get-tuple-element.91, f32[4096]{0:T(1024)S(1)} %bitcast.137, f32[4096]{0:T(1024)S(1)} %bitcast.138, f32[4096]{0:T(1024)S(1)} %bitcast.136, f32[4096]{0:T(1024)S(1)} %bitcast.135, f32[4096]{0:T(1024)S(1)} %copy-done.8, ...), kind=kLoop, calls=%fused_computation.3 | loop fusion | flops 67108864 | bytes 50413568 | tf_op jit(solution)/shard_map/jit(silu)/mul | solution.py:35
  41.9 8.3 %shard_map.119 = f32[4,8,64,128]{3,2,1,0:T(8,128)} custom-call(f32[512,4096]{1,0:T(8,128)} %get-tuple-element.102.xc_ref, f32[4,64,512]{2,1,0:T(8,128)} %get-tuple-element.98.b_ref, f32[4,16,512]{2,1,0:T(8,128)} %get-tuple-element.100.wk_ref), custom_call_target="tpu_custom_call" | custom-call | tf_op jit(solution)/shard_map/pallas_call | solution.py:247
  50.2 8.4 %shard_map.118 = f32[4,8,64,128]{3,2,1,0:T(8,128)} custom-call(f32[512,4096]{1,0:T(8,128)} %get-tuple-element.75.xc_ref.refs_0_, f32[4,64,512]{2,1,0:T(8,128)} %get-tuple-element.97.b_ref, f32[4,16,512]{2,1,0:T(8,128)} %get-tuple-element.99.wk_ref), custom_call_target="tpu_custom_call" | custom-call | tf_op jit(solution)/shard_map/pallas_call | solution.py:247
  58.6 1.5 select_add_fusion
  61.9 1.5 select_bitcast_fusion.2
  63.4 1.2 pad_maximum_fusion.1
  64.6 1.3 copy.63
  65.9 4.3 %collective-permute-start.2 = (f32[16,64,128]{2,1,0:T(8,128)}, f32[16,64,128]{2,1,0:T(8,128)}, u32[]{:S(2)}, u32[]{:S(2)}) collective-permute-start(f32[16,64,128]{2,1,0:T(8,128)} %bitcast_add_fusion), channel_id=1, source_target_pairs={{0,4},{4,8},{8,12},{1,5},{5,9},{9,13},{2,6},{6,10},{10,14},{3,7},{... | collective-permute-start | bytes 1572872 | tf_op jit(solution)/shard_map/ppermute | solution.py:21
  70.2 7.8 %shard_map.120.refs_7_ = f32[512,4096]{1,0:T(8,128)} custom-call(f32[512,4096]{1,0:T(8,128)} %get-tuple-element.75.xc_ref.refs_0_, f32[4,512,128]{2,1,0:T(8,128)} %bitcast.105, f32[4,128,512]{2,1,0:T(8,128)} %bitcast.116, f32[4,16,512]{2,1,0:T(8,128)} %copy-done.6, f32[4,512,16]{2,1,0:T(8,128)} %bitcast.112, f32[4,16,512]{2,1,0:T(8,128)} %bitcast.127, ...), custom_call_target="tpu_custom_call" | custom-call | tf_op jit(solution)/shard_map/pallas_call | solution.py:298
  77.9 3.6 %collective-permute-done.2 = f32[16,64,128]{2,1,0:T(8,128)} collective-permute-done((f32[16,64,128]{2,1,0:T(8,128)}, f32[16,64,128]{2,1,0:T(8,128)}, u32[]{:S(2)}, u32[]{:S(2)}) %collective-permute-start.2) | collective-permute-done | bytes 524320 | tf_op jit(solution)/shard_map/ppermute | solution.py:21
  82.6 6.2 %collective-permute-start.3 = (f32[16,64,128]{2,1,0:T(8,128)}, f32[16,64,128]{2,1,0:T(8,128)}, u32[]{:S(2)}, u32[]{:S(2)}) collective-permute-start(f32[16,64,128]{2,1,0:T(8,128)} %fusion.12), channel_id=1, source_target_pairs={{0,4},{4,8},{8,12},{1,5},{5,9},{9,13},{2,6},{6,10},{10,14},{3,7},{... | collective-permute-start | bytes 1572872 | tf_op jit(solution)/shard_map/ppermute | solution.py:21
  88.8 7.7 %shard_map.121.refs_7_ = f32[512,4096]{1,0:T(8,128)} custom-call(f32[512,4096]{1,0:T(8,128)} %get-tuple-element.75.xc_ref.refs_0_, f32[4,512,128]{2,1,0:T(8,128)} %bitcast.106, f32[4,128,512]{2,1,0:T(8,128)} %bitcast.117, f32[4,16,512]{2,1,0:T(8,128)} %copy-done.6, f32[4,512,16]{2,1,0:T(8,128)} %bitcast.113, ...), custom_call_target="tpu_custom_call", output_to_operand_aliasing={{}: (7, {})} | custom-call | tf_op jit(solution)/shard_map/pallas_call | solution.py:298
  96.5 2.9 %collective-permute-done.3 = f32[16,64,128]{2,1,0:T(8,128)} collective-permute-done((f32[16,64,128]{2,1,0:T(8,128)}, f32[16,64,128]{2,1,0:T(8,128)}, u32[]{:S(2)}, u32[]{:S(2)}) %collective-permute-start.3) | collective-permute-done | bytes 524320 | tf_op jit(solution)/shard_map/ppermute | solution.py:21
  99.3 1.2 fusion.11
  101.4 5.2 %collective-permute-start.4 = (f32[16,64,128]{2,1,0:T(8,128)}, f32[16,64,128]{2,1,0:T(8,128)}, u32[]{:S(2)}, u32[]{:S(2)}) collective-permute-start(f32[16,64,128]{2,1,0:T(8,128)} %fusion.10), channel_id=1, source_target_pairs={{0,4},{4,8},{8,12},{1,5},{5,9},{9,13},{2,6},{6,10},{10,14},{3,7},{... | collective-permute-start | bytes 1572872 | tf_op jit(solution)/shard_map/ppermute | solution.py:21
  106.6 7.7 %shard_map.122.refs_7_ = f32[512,4096]{1,0:T(8,128)} custom-call(f32[512,4096]{1,0:T(8,128)} %get-tuple-element.75.xc_ref.refs_0_, f32[4,512,128]{2,1,0:T(8,128)} %bitcast.107, f32[4,128,512]{2,1,0:T(8,128)} %bitcast.118, f32[4,16,512]{2,1,0:T(8,128)} %copy-done.6, f32[4,512,16]{2,1,0:T(8,128)} %bitcast.114, ...), custom_call_target="tpu_custom_call", output_to_operand_aliasing={{}: (7, {})} | custom-call | tf_op jit(solution)/shard_map/pallas_call | solution.py:298
  114.2 2.0 %collective-permute-done.4 = f32[16,64,128]{2,1,0:T(8,128)} collective-permute-done((f32[16,64,128]{2,1,0:T(8,128)}, f32[16,64,128]{2,1,0:T(8,128)}, u32[]{:S(2)}, u32[]{:S(2)}) %collective-permute-start.4) | collective-permute-done | bytes 524320 | tf_op jit(solution)/shard_map/ppermute | solution.py:21
  116.2 1.2 fusion.9
  118.3 5.2 %collective-permute-start.5 = (f32[16,64,128]{2,1,0:T(8,128)}, f32[16,64,128]{2,1,0:T(8,128)}, u32[]{:S(2)}, u32[]{:S(2)}) collective-permute-start(f32[16,64,128]{2,1,0:T(8,128)} %fusion.8), channel_id=1, source_target_pairs={{0,4},{4,8},{8,12},{1,5},{5,9},{9,13},{2,6},{6,10},{10,14},{3,7},{... | collective-permute-start | bytes 1572872 | tf_op jit(solution)/shard_map/ppermute | solution.py:21
  123.6 7.8 %shard_map.123.y_ref = f32[512,4096]{1,0:T(8,128)} custom-call(f32[512,4096]{1,0:T(8,128)} %get-tuple-element.75.xc_ref.refs_0_, f32[4,512,128]{2,1,0:T(8,128)} %bitcast.108, f32[4,128,512]{2,1,0:T(8,128)} %bitcast.119, f32[4,16,512]{2,1,0:T(8,128)} %copy-done.6, f32[4,512,16]{2,1,0:T(8,128)} %bitcast.115, ...), custom_call_target="tpu_custom_call", output_to_operand_aliasing={{}: (7, {})} | custom-call | tf_op jit(solution)/shard_map/pallas_call | solution.py:298
  132.2 1.2 fusion.7
  133.4 1.3 fusion.5
  135.2 1.3 copy.68
  136.5 1.2 collective-permute-done.6
  138.2 1.4 select_bitcast_fusion
  139.8 1.5 copy.69
  141.3 12.4 %shard_map.124 = bf16[512,4096]{1,0:T(8,128)(2,1)} custom-call(f32[512,4096]{1,0:T(8,128)} %shard_map.123.y_ref, f32[4,512,128]{2,1,0:T(8,128)} %bitcast.109, f32[4,512,16]{2,1,0:T(8,128)} %bitcast.125, f32[4,8,128,128]{3,2,1,0:T(8,128)} %bitcast.124, bf16[512,4096]{1,0:T(8,128)(2,1)} %z_ref.1, f32[1,4096]{1,0:T(1,128)} %bitcast.140), custom_call_target="tpu_custom_call" | custom-call | tf_op jit(solution)/shard_map/pallas_call | solution.py:350
  (86 shorter events, 18.0 us)
Async XLA Ops:
  0.0 14.0 %copy-start = (f32[2,4,128]{2,1,0:T(4,128)S(1)}, f32[2,4,128]{2,1,0:T(4,128)}, u32[]{:S(2)}) copy-start(f32[2,4,128]{2,1,0:T(4,128)} %param.19) | copy-start | bytes 12292
  0.0 10.1 %copy-start.7 = (f32[4,4096]{1,0:T(4,128)S(1)}, f32[4,4096]{1,0:T(4,128)}, u32[]{:S(2)}) copy-start(f32[4,4096]{1,0:T(4,128)} %param.16) | copy-start | bytes 196612
  2.1 14.4 %collective-permute-start = (bf16[3,4608]{1,0:T(4,128)(2,1)S(1)}, bf16[3,4608]{1,0:T(4,128)(2,1)S(1)}, u32[]{:S(2)}, u32[]{:S(2)}) collective-permute-start(bf16[3,4608]{1,0:T(4,128)(2,1)S(1)} %pad_maximum_fusion.3), channel_id=1, source_target_pairs={{0,4},{4,8},{8,12},{1,5},{5,9},{9,13},{2,6},{6,10},{10,14},{3,7},{... | collective-permute-start | bytes 82952 | tf_op jit(solution)/shard_map/ppermute | solution.py:21
  7.7 6.2 %copy-start.9 = (f32[4,2,4,128]{3,2,1,0:T(4,128)S(1)}, f32[4,2,4,128]{3,2,1,0:T(4,128)}, u32[]{:S(2)}) copy-start(f32[4,2,4,128]{3,2,1,0:T(4,128)} %param.18) | copy-start | bytes 49156
  9.6 6.1 %copy-start.10 = (f32[64]{0:T(128)S(1)}, f32[64]{0:T(128)}, u32[]{:S(2)}) copy-start(f32[64]{0:T(128)} %param.22) | copy-start | bytes 772
  14.4 13.9 %copy-start.6 = (f32[4,16,512]{2,1,0:T(8,128)}, f32[4,16,512]{2,1,0:T(8,128)S(1)}, u32[]{:S(2)}) copy-start(f32[4,16,512]{2,1,0:T(8,128)S(1)} %reshape.101.cumr_ref.refs_3_) | copy-start | bytes 393220
  23.2 38.7 %collective-permute-start.1 = (f32[2,4,64,512]{3,2,1,0:T(8,128)}, f32[2,4,64,512]{3,2,1,0:T(8,128)}, u32[]{:S(2)}, u32[]{:S(2)}) collective-permute-start(f32[2,4,64,512]{3,2,1,0:T(8,128)} %constant_dynamic-slice_fusion.5), channel_id=1, source_target_pairs={{0,1},{1,0},{2,3},{3,2},{4,5},{5,4},{6,7},{7,6},{8,9},{9,8},{10,11... | collective-permute-start | bytes 3145736 | tf_op jit(solution)/shard_map/ppermute | solution.py:25
  23.3 5.0 %copy-start.8 = (f32[4096]{0:T(1024)S(1)}, f32[4096]{0:T(1024)}, u32[]{:S(2)}) copy-start(f32[4096]{0:T(1024)} %param.17) | copy-start | bytes 49156
  50.2 8.4 %copy-start.2 = (f32[4,8,64,128]{3,2,1,0:T(8,128)S(1)}, f32[4,8,64,128]{3,2,1,0:T(8,128)}, u32[]{:S(2)}) copy-start(f32[4,8,64,128]{3,2,1,0:T(8,128)} %shard_map.119) | copy-start | bytes 3145732
  60.1 1.0 copy-start.4
  65.9 15.6 %collective-permute-start.2 = (f32[16,64,128]{2,1,0:T(8,128)}, f32[16,64,128]{2,1,0:T(8,128)}, u32[]{:S(2)}, u32[]{:S(2)}) collective-permute-start(f32[16,64,128]{2,1,0:T(8,128)} %bitcast_add_fusion), channel_id=1, source_target_pairs={{0,4},{4,8},{8,12},{1,5},{5,9},{9,13},{2,6},{6,10},{10,14},{3,7},{... | collective-permute-start | bytes 1572872 | tf_op jit(solution)/shard_map/ppermute | solution.py:21
  70.2 11.5 %copy-start.5 = (f32[4,8,64,128]{3,2,1,0:T(8,128)S(1)}, f32[4,8,64,128]{3,2,1,0:T(8,128)}, u32[]{:S(2)}) copy-start(f32[4,8,64,128]{3,2,1,0:T(8,128)} %copy-done.4) | copy-start | bytes 3145732
  82.6 16.8 %collective-permute-start.3 = (f32[16,64,128]{2,1,0:T(8,128)}, f32[16,64,128]{2,1,0:T(8,128)}, u32[]{:S(2)}, u32[]{:S(2)}) collective-permute-start(f32[16,64,128]{2,1,0:T(8,128)} %fusion.12), channel_id=1, source_target_pairs={{0,4},{4,8},{8,12},{1,5},{5,9},{9,13},{2,6},{6,10},{10,14},{3,7},{... | collective-permute-start | bytes 1572872 | tf_op jit(solution)/shard_map/ppermute | solution.py:21
  101.4 14.8 %collective-permute-start.4 = (f32[16,64,128]{2,1,0:T(8,128)}, f32[16,64,128]{2,1,0:T(8,128)}, u32[]{:S(2)}, u32[]{:S(2)}) collective-permute-start(f32[16,64,128]{2,1,0:T(8,128)} %fusion.10), channel_id=1, source_target_pairs={{0,4},{4,8},{8,12},{1,5},{5,9},{9,13},{2,6},{6,10},{10,14},{3,7},{... | collective-permute-start | bytes 1572872 | tf_op jit(solution)/shard_map/ppermute | solution.py:21
  118.3 13.9 %collective-permute-start.5 = (f32[16,64,128]{2,1,0:T(8,128)}, f32[16,64,128]{2,1,0:T(8,128)}, u32[]{:S(2)}, u32[]{:S(2)}) collective-permute-start(f32[16,64,128]{2,1,0:T(8,128)} %fusion.8), channel_id=1, source_target_pairs={{0,4},{4,8},{8,12},{1,5},{5,9},{9,13},{2,6},{6,10},{10,14},{3,7},{... | collective-permute-start | bytes 1572872 | tf_op jit(solution)/shard_map/ppermute | solution.py:21
  123.6 9.7 %copy-start.3 = (f32[4,8,64,128]{3,2,1,0:T(8,128)S(1)}, f32[4,8,64,128]{3,2,1,0:T(8,128)}, u32[]{:S(2)}) copy-start(f32[4,8,64,128]{3,2,1,0:T(8,128)} %shard_map.118) | copy-start | bytes 3145732
  134.7 3.0 %collective-permute-start.6 = (f32[4,8,64,128]{3,2,1,0:T(8,128)}, f32[4,8,64,128]{3,2,1,0:T(8,128)}, u32[]{:S(2)}, u32[]{:S(2)}) collective-permute-start(f32[4,8,64,128]{3,2,1,0:T(8,128)} %fusion.5), channel_id=1, source_target_pairs={{0,1},{1,0},{2,3},{3,2},{4,5},{5,4},{6,7},{7,6},{8,9},{9,8},{10,11... | collective-permute-start | bytes 3145736 | tf_op jit(solution)/shard_map/ppermute | solution.py:25
  141.3 12.4 %copy-start.1 = (f32[2,4,128]{2,1,0:T(4,128)S(1)}, f32[2,4,128]{2,1,0:T(4,128)}, u32[]{:S(2)}) copy-start(f32[2,4,128]{2,1,0:T(4,128)} %param.19) | copy-start | bytes 12292

commit v13 on v12

--- a/solution.py
+++ b/solution.py
@@ -167,6 +167,7 @@
     pairs = per_group // 2
     group_width = per_group * HEAD_DIM
     nsub = lax.axis_size("sub")
+    ctx_size = lax.axis_size("ctx")
     sub_index = lax.axis_index("sub")
     own = tokens // nsub
     half = bc_raw.shape[2]
@@ -243,37 +244,42 @@
     to_end = jnp.exp(cum_all[..., own - 1 :] - cum_all) * step_sizes.reshape(heads_dev, nsub, own)
     to_end = to_end.reshape(set_groups, per_group, tokens)
 
-    def end_states(x_half, at):
+    def end_states(x_half, at, start, count):
         return pl.pallas_call(
             end_kernel,
-            grid=(set_groups,),
+            grid=(count,),
             in_specs=[
-                pl.BlockSpec((own, group_width), lambda g: (0, g)),
-                pl.BlockSpec((1, half, own), lambda g: (g, 0, 0)),
-                pl.BlockSpec((1, per_group, own), lambda g: (g, 0, 0)),
+                pl.BlockSpec((own, group_width), lambda g: (0, g + start)),
+                pl.BlockSpec((1, half, own), lambda g: (g + start, 0, 0)),
+                pl.BlockSpec((1, per_group, own), lambda g: (g + start, 0, 0)),
             ],
             out_specs=pl.BlockSpec((1, pairs, half, 128), lambda g: (g, 0, 0, 0)),
-            out_shape=jax.ShapeDtypeStruct((set_groups, pairs, half, 128), F32),
+            out_shape=jax.ShapeDtypeStruct((count, pairs, half, 128), F32),
         )(
             x_half,
             lax.dynamic_slice_in_dim(bc_conv[0], at * own, own, 2),
             lax.dynamic_slice_in_dim(to_end, at * own, own, 2),
         )
 
-    own_end = end_states(x_own, sub_index)
-    other_end = end_states(x_other, 1 - sub_index)
-
     def pair_layout(values):
         return jnp.repeat(values.reshape(set_groups, pairs, 2), HEAD_DIM, axis=-1)[:, :, None, :]
 
     decay_first = pair_layout(half_totals[:, 0])
     decay_second = pair_layout(half_totals[:, 1])
-    first_end = jnp.where(sub_index == 0, own_end, other_end)
-    second_end = jnp.where(sub_index == 0, other_end, own_end)
-    chip_end = decay_second * first_end + second_end
     chip_decay = decay_first * decay_second
+
+    def chip_ends(x_pair, start, count):
+        own_end = end_states(x_pair[0], sub_index, start, count)
+        other_end = end_states(x_pair[1], 1 - sub_index, start, count)
+        first = jnp.where(sub_index == 0, own_end, other_end)
+        second = jnp.where(sub_index == 0, other_end, own_end)
+        return first, decay_second[start : start + count] * first + second
+
+    pieces = 2 if (set_groups * pairs) % 2 == 0 else 1
+    rounds = ctx_size + pieces - 2
+    early = set_groups // 2 if (pieces == 2 and set_groups % 2 == 0 and rounds > 0) else set_groups
+    first_end, chip_end = chip_ends((x_own, x_other), 0, early)
     ctx_index = lax.axis_index("ctx")
-    ctx_size = lax.axis_size("ctx")
     scan_inputs = (x_own, c_cols, b_rows, cum_rows, cum_cols, step_rows, skip_row)
 
     def scan_group(group, inputs, target):
@@ -305,11 +311,13 @@
             **extra,
         )(*operands)
 
-    pieces = 2 if (set_groups * pairs) % 2 == 0 else 1
-    rounds = ctx_size + pieces - 2
     piece_shape = (pieces, set_groups * pairs // pieces, half, 128)
-    end_pieces = chip_end.reshape(piece_shape)
-    decay_pieces = jnp.broadcast_to(chip_decay, chip_end.shape).reshape(piece_shape)
+    full_shape = (set_groups, pairs, half, 128)
+    decay_pieces = jnp.broadcast_to(chip_decay, full_shape).reshape(piece_shape)
+    if early == set_groups:
+        end_pieces = chip_end.reshape(piece_shape)
+    else:
+        end_pieces = chip_end.reshape((1,) + piece_shape[1:])
     received = jnp.zeros(piece_shape, F32)
     y_local = None
     placed = [min(group, max(rounds, 1) - 1) for group in range(set_groups)]
@@ -321,24 +329,32 @@
             lax.dynamic_index_in_dim(received, send_at, 0, keepdims=False)
         )
         held = scan_inputs
+        x_pair = (x_own, x_other)
         if any(p == step_index for p in placed):
-            outgoing, held = lax.optimization_barrier((outgoing, scan_inputs))
+            outgoing, held, x_pair = lax.optimization_barrier((outgoing, scan_inputs, x_pair))
         if rounds > 0:
             arrived = passed_along(outgoing, "ctx", 1)
         for group in range(set_groups):
             if placed[group] == step_index:
                 y_local = scan_group(group, held, y_local)
+        late = None
+        if step_index == 0 and early < set_groups:
+            late = chip_ends(x_pair, early, set_groups - early)
         if rounds == 0:
             break
         if any(p == step_index for p in placed):
-            arrived, y_local = lax.optimization_barrier((arrived, y_local))
+            arrived, y_local, late = lax.optimization_barrier((arrived, y_local, late))
+        if late is not None:
+            first_end = jnp.concatenate([first_end, late[0]], 0)
+            chip_end = jnp.concatenate([chip_end, late[1]], 0)
+            end_pieces = chip_end.reshape(piece_shape)
         recv_at = step_index - ctx_index + 1
         valid = (recv_at >= 0) & (recv_at < pieces) & (ctx_index > 0)
         updated = lax.dynamic_update_index_in_dim(
             received, arrived, jnp.clip(recv_at, 0, pieces - 1), 0
         )
         received = jnp.where(valid, updated, received)
-    carried = received.reshape(chip_end.shape)
+    carried = received.reshape(full_shape)
     into_second = decay_first * carried + first_end
     keep = jnp.where(sub_index == 0, carried, into_second)
     got = swapped(jnp.where(sub_index == 0, into_second, carried), "sub")

time: 155 us -> 149 us (0.961)
  other arithmetic: 40.5 us -> 36.7 us
  Pallas kernels: 60 us -> 63.6 us
  starting transfers between devices: 25.8 us -> 22.8 us
  waiting for transfers between devices: 10.4 us -> 8.07 us
    pallas_call x2 -> x4, Pallas kernels: 16.6 us -> 20.3 us  [end_states(): pl.pallas_call(end_kernel, grid=(count,), in_specs=[pl.BlockSpec((own, gr...]
    ppermute x5, starting transfers between devices: 25.8 us -> 22.7 us  [passed_along(): return lax.ppermute(x, axis, pairs)]
    add x4, other arithmetic: 3.5 us -> 1.13 us  [per_device(): lax.dynamic_index_in_dim(end_pieces, send_at, 0, keepdims=False)]
    ppermute x5, waiting for transfers between devices: 9.16 us -> 7.1 us  [passed_along(): return lax.ppermute(x, axis, pairs)]
  transfers between devices with their start and end apart: 7 -> 7, of which waited for: 5 -> 4; matrix products, arithmetic and copies ran while one was open for 21% -> 23% of each run, Pallas kernels for 31% -> 35%
where the time goes in v13:
time: 149 us; the launch traced here: 148 us
  Pallas kernels  63.6 us (43%)
  other arithmetic  36.7 us (25%)
  starting transfers between devices  22.8 us (15%)
  local copies, waits for them, and re-layouts  15.7 us (11%)
  waiting for transfers between devices  8.07 us (5%)
    pallas_call x4, Pallas kernels, scan_group(): pl.pallas_call(kernel, grid=(1, blocks), in_specs=in_specs, out_specs=til...  30.9 us
    ppermute x5, starting transfers between devices, passed_along(): return lax.ppermute(x, axis, pairs)  22.7 us
    pallas_call x4, Pallas kernels, end_states(): pl.pallas_call(end_kernel, grid=(count,), in_specs=[pl.BlockSpec((own, gr...  20.3 us
    pallas_call x1, Pallas kernels, per_device(): pl.pallas_call(out_kernel, grid=(set_groups, own // out_len), in_specs=[p...  12.4 us
    mul x1, other arithmetic, conv_rows(): return jax.nn.silu(total)  12.4 us
    ppermute x5, waiting for transfers between devices, passed_along(): return lax.ppermute(x, axis, pairs)  7.1 us
    mul x1, other arithmetic, conv_cols(): return jax.nn.silu(total)  5.59 us
    concatenate x1, other arithmetic, per_device(): x_pad = jnp.concatenate([x_rim, x_raw], 0)  4.98 us
  transfers between devices with their start and end apart: 7, of which 4 were waited for; matrix products, arithmetic and copies ran while one was open for 23% of the time, Pallas kernels for 35%

profile of v13, /device:TPU:0, one launch (start us, length us, event | category | flops | bytes accessed | tf_op | source)
XLA Modules:
  0.0 147.8 jit_solution(9885065365201433091)
XLA Ops:
  2.1 4.9 %collective-permute-start = (bf16[3,4608]{1,0:T(4,128)(2,1)S(1)}, bf16[3,4608]{1,0:T(4,128)(2,1)S(1)}, u32[]{:S(2)}, u32[]{:S(2)}) collective-permute-start(bf16[3,4608]{1,0:T(4,128)(2,1)S(1)} %pad_maximum_fusion.4), channel_id=1, source_target_pairs={{0,4},{4,8},{8,12},{1,5},{5,9},{9,13},{2,6},{6,10},{10,14},{3,7},{... | collective-permute-start | bytes 82952 | tf_op jit(solution)/shard_map/ppermute | solution.py:21
  7.7 1.2 broadcast_multiply_fusion
  14.6 1.3 copy.66
  16.9 5.6 %divide_multiply_fusion.2 = f32[2,4,64,1024]{3,2,1,0:T(8,128)S(1)} fusion(bf16[2,4,64,1024]{3,2,1,0:T(8,128)(2,1)} %param.13, bf16[2,4,64,3]{3,2,1,0:T(8,128)(2,1)S(1)} %bitcast.131, f32[2,4,64]{2,1,0:T(4,128)S(1)} %get-tuple-element.128, f32[2,4,64]{2,1,0:T(4,128)S(1)} %get-tuple-element.126, f32[2,4,64]{2,1,0:T(4,128)S(1)} %get-tuple-element.127, ...), kind=kLoop, calls=%fused_computation.11 | loop fusion | flops 13107200 | bytes 3159040 | tf_op jit(solution)/shard_map/jit(silu)/mul | solution.py:45
  22.5 1.1 constant_dynamic-slice_fusion.7
  23.6 5.0 %fusion.1 = (bf16[515,4096]{1,0:T(8,128)(2,1)S(1)}, bf16[515,4096]{1,0:T(8,128)(2,1)S(1)}) fusion(s32[]{:T(128)S(6)} %select_n.145, bf16[1024,4096]{1,0:T(8,128)(2,1)} %param.12, bf16[3,4096]{1,0:T(4,128)(2,1)S(1)} %slice.156, s32[]{:T(128)S(6)} %select_n.148), kind=kLoop, calls=%fused_computation.7 | loop fusion | flops 16875520 | bytes 16850952 | tf_op jit(solution)/shard_map/concatenate | solution.py:188
  28.6 12.4 %divide_multiply_fusion.1 = (f32[512,4096]{1,0:T(8,128)}, f32[512,4096]{1,0:T(8,128)}) fusion(bf16[515,4096]{1,0:T(8,128)(2,1)S(1)} %get-tuple-element.99, f32[4096]{0:T(1024)S(1)} %bitcast.136, f32[4096]{0:T(1024)S(1)} %bitcast.137, f32[4096]{0:T(1024)S(1)} %bitcast.135, f32[4096]{0:T(1024)S(1)} %bitcast.134, f32[4096]{0:T(1024)S(1)} %copy-done.7, ...), kind=kLoop, calls=%fused_computation.3 | loop fusion | flops 67108864 | bytes 50413568 | tf_op jit(solution)/shard_map/jit(silu)/mul | solution.py:35
  42.2 5.1 %shard_map.118 = f32[2,8,64,128]{3,2,1,0:T(8,128)} custom-call(f32[512,4096]{1,0:T(8,128)} %get-tuple-element.82.xc_ref.refs_0_, f32[4,64,512]{2,1,0:T(8,128)} %get-tuple-element.111.b_ref, f32[4,16,512]{2,1,0:T(8,128)} %get-tuple-element.113.wk_ref), custom_call_target="tpu_custom_call" | custom-call | tf_op jit(solution)/shard_map/pallas_call | solution.py:248
  47.2 5.1 %shard_map.119 = f32[2,8,64,128]{3,2,1,0:T(8,128)} custom-call(f32[512,4096]{1,0:T(8,128)} %get-tuple-element.58.xc_ref, f32[4,64,512]{2,1,0:T(8,128)} %get-tuple-element.112.b_ref, f32[4,16,512]{2,1,0:T(8,128)} %get-tuple-element.114.wk_ref), custom_call_target="tpu_custom_call" | custom-call | tf_op jit(solution)/shard_map/pallas_call | solution.py:248
  52.3 1.3 broadcast_select_fusion.1
  54.5 1.5 %select_bitcast_fusion.2 = (f32[2,4,1,64,512]{4,3,2,1,0:T(8,128)S(1)}, f32[2,4,1,64,512]{4,3,2,1,0:T(8,128)S(1)}) fusion(f32[2,4,64,512]{3,2,1,0:T(8,128)} %collective-permute-done.1, f32[2,4,64,1024]{3,2,1,0:T(8,128)S(1)} %divide_multiply_fusion.2, s32[]{:T(128)S(6)} %select_n.147, pred[]{:T(512)S(6)} %eq.2), kind=kLoop, calls=%fused_computation.29 | loop fusion | flops 524288 | bytes 4194309 | tf_op jit(solution)/shard_map/stack | solution.py:202
  56.0 1.2 pad_maximum_fusion.1
  57.2 1.4 copy.63
  58.6 3.7 %collective-permute-start.2 = (f32[16,64,128]{2,1,0:T(8,128)}, f32[16,64,128]{2,1,0:T(8,128)S(1)}, u32[]{:S(2)}, u32[]{:S(2)}) collective-permute-start(f32[16,64,128]{2,1,0:T(8,128)} %bitcast_add_fusion), channel_id=1, source_target_pairs={{0,4},{4,8},{8,12},{1,5},{5,9},{9,13},{2,6},{6,10},{10,14},{3,7},{... | collective-permute-start | bytes 1572872 | tf_op jit(solution)/shard_map/ppermute | solution.py:21
  62.5 5.1 %shard_map.122 = f32[2,8,64,128]{3,2,1,0:T(8,128)} custom-call(f32[512,4096]{1,0:T(8,128)} %get-tuple-element.58.xc_ref, f32[4,64,512]{2,1,0:T(8,128)} %get-tuple-element.112.b_ref, f32[4,16,512]{2,1,0:T(8,128)} %get-tuple-element.114.wk_ref), custom_call_target="tpu_custom_call" | custom-call | tf_op jit(solution)/shard_map/pallas_call | solution.py:248
  67.6 5.1 %shard_map.121 = f32[2,8,64,128]{3,2,1,0:T(8,128)} custom-call(f32[512,4096]{1,0:T(8,128)} %get-tuple-element.82.xc_ref.refs_0_, f32[4,64,512]{2,1,0:T(8,128)} %get-tuple-element.111.b_ref, f32[4,16,512]{2,1,0:T(8,128)} %get-tuple-element.113.wk_ref), custom_call_target="tpu_custom_call" | custom-call | tf_op jit(solution)/shard_map/pallas_call | solution.py:248
  72.7 7.7 %shard_map.120.refs_7_ = f32[512,4096]{1,0:T(8,128)} custom-call(f32[512,4096]{1,0:T(8,128)} %get-tuple-element.82.xc_ref.refs_0_, f32[4,512,128]{2,1,0:T(8,128)} %bitcast.105, f32[4,128,512]{2,1,0:T(8,128)} %bitcast.116, f32[4,16,512]{2,1,0:T(8,128)} %copy-done.2, f32[4,512,16]{2,1,0:T(8,128)} %bitcast.112, f32[4,16,512]{2,1,0:T(8,128)} %bitcast.126, ...), custom_call_target="tpu_custom_call" | custom-call | tf_op jit(solution)/shard_map/pallas_call | solution.py:304
  81.7 4.2 %collective-permute-start.3 = (f32[16,64,128]{2,1,0:T(8,128)S(1)}, f32[16,64,128]{2,1,0:T(8,128)}, u32[]{:S(2)}, u32[]{:S(2)}) collective-permute-start(f32[16,64,128]{2,1,0:T(8,128)S(1)} %fusion.12), channel_id=1, source_target_pairs={{0,4},{4,8},{8,12},{1,5},{5,9},{9,13},{2,6},{6,10},{10,14},{3,7},{... | collective-permute-start | bytes 1572872 | tf_op jit(solution)/shard_map/ppermute | solution.py:21
  86.0 7.7 %shard_map.123.refs_7_ = f32[512,4096]{1,0:T(8,128)} custom-call(f32[512,4096]{1,0:T(8,128)} %get-tuple-element.82.xc_ref.refs_0_, f32[4,512,128]{2,1,0:T(8,128)} %bitcast.106, f32[4,128,512]{2,1,0:T(8,128)} %bitcast.117, f32[4,16,512]{2,1,0:T(8,128)} %copy-done.2, f32[4,512,16]{2,1,0:T(8,128)} %bitcast.113, ...), custom_call_target="tpu_custom_call", output_to_operand_aliasing={{}: (7, {})} | custom-call | tf_op jit(solution)/shard_map/pallas_call | solution.py:304
  93.7 3.0 %collective-permute-done.3 = f32[16,64,128]{2,1,0:T(8,128)} collective-permute-done((f32[16,64,128]{2,1,0:T(8,128)S(1)}, f32[16,64,128]{2,1,0:T(8,128)}, u32[]{:S(2)}, u32[]{:S(2)}) %collective-permute-start.3) | collective-permute-done | bytes 524320 | tf_op jit(solution)/shard_map/ppermute | solution.py:21
  96.7 1.2 fusion.11
  98.0 5.3 %collective-permute-start.4 = (f32[16,64,128]{2,1,0:T(8,128)S(1)}, f32[16,64,128]{2,1,0:T(8,128)}, u32[]{:S(2)}, u32[]{:S(2)}) collective-permute-start(f32[16,64,128]{2,1,0:T(8,128)S(1)} %fusion.10), channel_id=1, source_target_pairs={{0,4},{4,8},{8,12},{1,5},{5,9},{9,13},{2,6},{6,10},{10,14},{3,7},{... | collective-permute-start | bytes 1572872 | tf_op jit(solution)/shard_map/ppermute | solution.py:21
  103.3 7.7 %shard_map.124.refs_7_ = f32[512,4096]{1,0:T(8,128)} custom-call(f32[512,4096]{1,0:T(8,128)} %get-tuple-element.82.xc_ref.refs_0_, f32[4,512,128]{2,1,0:T(8,128)} %bitcast.107, f32[4,128,512]{2,1,0:T(8,128)} %bitcast.118, f32[4,16,512]{2,1,0:T(8,128)} %copy-done.2, f32[4,512,16]{2,1,0:T(8,128)} %bitcast.114, ...), custom_call_target="tpu_custom_call", output_to_operand_aliasing={{}: (7, {})} | custom-call | tf_op jit(solution)/shard_map/pallas_call | solution.py:304
  110.9 2.2 %collective-permute-done.4 = f32[16,64,128]{2,1,0:T(8,128)} collective-permute-done((f32[16,64,128]{2,1,0:T(8,128)S(1)}, f32[16,64,128]{2,1,0:T(8,128)}, u32[]{:S(2)}, u32[]{:S(2)}) %collective-permute-start.4) | collective-permute-done | bytes 524320 | tf_op jit(solution)/shard_map/ppermute | solution.py:21
  113.2 1.2 fusion.9
  114.4 4.5 %collective-permute-start.5 = (f32[16,64,128]{2,1,0:T(8,128)S(1)}, f32[16,64,128]{2,1,0:T(8,128)S(1)}, u32[]{:S(2)}, u32[]{:S(2)}) collective-permute-start(f32[16,64,128]{2,1,0:T(8,128)S(1)} %fusion.8), channel_id=1, source_target_pairs={{0,4},{4,8},{8,12},{1,5},{5,9},{9,13},{2,6},{6,10},{10,14},{3,7},{... | collective-permute-start | bytes 1572872 | tf_op jit(solution)/shard_map/ppermute | solution.py:21
  119.2 7.7 %shard_map.125.y_ref = f32[512,4096]{1,0:T(8,128)} custom-call(f32[512,4096]{1,0:T(8,128)} %get-tuple-element.82.xc_ref.refs_0_, f32[4,512,128]{2,1,0:T(8,128)} %bitcast.108, f32[4,128,512]{2,1,0:T(8,128)} %bitcast.119, f32[4,16,512]{2,1,0:T(8,128)} %copy-done.2, f32[4,512,16]{2,1,0:T(8,128)} %bitcast.115, ...), custom_call_target="tpu_custom_call", output_to_operand_aliasing={{}: (7, {})} | custom-call | tf_op jit(solution)/shard_map/pallas_call | solution.py:304
  126.9 1.8 %collective-permute-done.5 = f32[16,64,128]{2,1,0:T(8,128)S(1)} collective-permute-done((f32[16,64,128]{2,1,0:T(8,128)S(1)}, f32[16,64,128]{2,1,0:T(8,128)S(1)}, u32[]{:S(2)}, u32[]{:S(2)}) %collective-permute-start.5) | collective-permute-done | bytes 524320 | tf_op jit(solution)/shard_map/ppermute | solution.py:21
  129.7 1.3 copy.68
  132.0 1.6 %select_bitcast_fusion.1 = (f32[4,8,1,64,128]{4,3,1,0,2:T(8,128)S(1)}, f32[4,8,1,64,128]{4,3,1,0,2:T(8,128)S(1)}) fusion(f32[4,8,64,128]{3,2,1,0:T(8,128)} %collective-permute-done.6, pred[]{:T(512)S(6)} %eq.2, f32[4,8,64,128]{3,2,1,0:T(8,128)S(1)} %bitcast.111, f32[2,8,64,128]{3,2,1,0:T(8,128)S(1)} %copy-done.3, ...), kind=kLoop, calls=%fused_computation.26 | loop fusion | flops 1572864 | bytes 5259265 | tf_op jit(solution)/shard_map/stack | solution.py:363
  133.9 1.5 %copy.69 = f32[4,8,2,64,128]{4,3,2,1,0:T(8,128)} copy(f32[4,8,2,64,128]{4,3,1,0,2:T(8,128)S(1)} %pad_maximum_fusion) | data formatting | bytes 4194304 | tf_op jit(solution)/shard_map/stack | solution.py:363
  135.4 12.4 %shard_map.126 = bf16[512,4096]{1,0:T(8,128)(2,1)} custom-call(f32[512,4096]{1,0:T(8,128)} %shard_map.125.y_ref, f32[4,512,128]{2,1,0:T(8,128)} %bitcast.109, f32[4,512,16]{2,1,0:T(8,128)} %bitcast.124, f32[4,8,128,128]{3,2,1,0:T(8,128)} %bitcast.120, bf16[512,4096]{1,0:T(8,128)(2,1)} %z_ref.1, f32[1,4096]{1,0:T(1,128)} %bitcast.139), custom_call_target="tpu_custom_call" | custom-call | tf_op jit(solution)/shard_map/pallas_call | solution.py:366
  (92 shorter events, 15.3 us)
Async XLA Ops:
  0.0 14.1 %copy-start = (f32[2,4,128]{2,1,0:T(4,128)S(1)}, f32[2,4,128]{2,1,0:T(4,128)}, u32[]{:S(2)}) copy-start(f32[2,4,128]{2,1,0:T(4,128)} %param.19) | copy-start | bytes 12292
  0.0 10.7 %copy-start.6 = (f32[4,4096]{1,0:T(4,128)S(1)}, f32[4,4096]{1,0:T(4,128)}, u32[]{:S(2)}) copy-start(f32[4,4096]{1,0:T(4,128)} %param.16) | copy-start | bytes 196612
  2.1 14.7 %collective-permute-start = (bf16[3,4608]{1,0:T(4,128)(2,1)S(1)}, bf16[3,4608]{1,0:T(4,128)(2,1)S(1)}, u32[]{:S(2)}, u32[]{:S(2)}) collective-permute-start(bf16[3,4608]{1,0:T(4,128)(2,1)S(1)} %pad_maximum_fusion.4), channel_id=1, source_target_pairs={{0,4},{4,8},{8,12},{1,5},{5,9},{9,13},{2,6},{6,10},{10,14},{3,7},{... | collective-permute-start | bytes 82952 | tf_op jit(solution)/shard_map/ppermute | solution.py:21
  7.7 6.4 %copy-start.8 = (f32[4,2,4,128]{3,2,1,0:T(4,128)S(1)}, f32[4,2,4,128]{3,2,1,0:T(4,128)}, u32[]{:S(2)}) copy-start(f32[4,2,4,128]{3,2,1,0:T(4,128)} %param.18) | copy-start | bytes 49156
  9.6 6.4 %copy-start.9 = (f32[64]{0:T(128)S(1)}, f32[64]{0:T(128)}, u32[]{:S(2)}) copy-start(f32[64]{0:T(128)} %param.22) | copy-start | bytes 772
  14.6 14.0 %copy-start.2 = (f32[4,16,512]{2,1,0:T(8,128)}, f32[4,16,512]{2,1,0:T(8,128)S(1)}, u32[]{:S(2)}) copy-start(f32[4,16,512]{2,1,0:T(8,128)S(1)} %reshape.107.cumr_ref.refs_3_) | copy-start | bytes 393220
  23.6 30.9 %collective-permute-start.1 = (f32[2,4,64,512]{3,2,1,0:T(8,128)}, f32[2,4,64,512]{3,2,1,0:T(8,128)}, u32[]{:S(2)}, u32[]{:S(2)}) collective-permute-start(f32[2,4,64,512]{3,2,1,0:T(8,128)} %constant_dynamic-slice_fusion.7), channel_id=1, source_target_pairs={{0,1},{1,0},{2,3},{3,2},{4,5},{5,4},{6,7},{7,6},{8,9},{9,8},{10,11... | collective-permute-start | bytes 3145736 | tf_op jit(solution)/shard_map/ppermute | solution.py:25
  23.6 5.0 %copy-start.7 = (f32[4096]{0:T(1024)S(1)}, f32[4096]{0:T(1024)}, u32[]{:S(2)}) copy-start(f32[4096]{0:T(1024)} %param.17) | copy-start | bytes 49156
  58.6 22.8 %collective-permute-start.2 = (f32[16,64,128]{2,1,0:T(8,128)}, f32[16,64,128]{2,1,0:T(8,128)S(1)}, u32[]{:S(2)}, u32[]{:S(2)}) collective-permute-start(f32[16,64,128]{2,1,0:T(8,128)} %bitcast_add_fusion), channel_id=1, source_target_pairs={{0,4},{4,8},{8,12},{1,5},{5,9},{9,13},{2,6},{6,10},{10,14},{3,7},{... | collective-permute-start | bytes 1572872 | tf_op jit(solution)/shard_map/ppermute | solution.py:21
  72.7 7.7 %copy-start.4 = (f32[2,8,64,128]{3,2,1,0:T(8,128)S(1)}, f32[2,8,64,128]{3,2,1,0:T(8,128)}, u32[]{:S(2)}) copy-start(f32[2,8,64,128]{3,2,1,0:T(8,128)} %shard_map.122) | copy-start | bytes 1572868
  72.7 7.7 %copy-start.5 = (f32[2,8,64,128]{3,2,1,0:T(8,128)S(1)}, f32[2,8,64,128]{3,2,1,0:T(8,128)}, u32[]{:S(2)}) copy-start(f32[2,8,64,128]{3,2,1,0:T(8,128)} %shard_map.121) | copy-start | bytes 1572868
  81.7 15.0 %collective-permute-start.3 = (f32[16,64,128]{2,1,0:T(8,128)S(1)}, f32[16,64,128]{2,1,0:T(8,128)}, u32[]{:S(2)}, u32[]{:S(2)}) collective-permute-start(f32[16,64,128]{2,1,0:T(8,128)S(1)} %fusion.12), channel_id=1, source_target_pairs={{0,4},{4,8},{8,12},{1,5},{5,9},{9,13},{2,6},{6,10},{10,14},{3,7},{... | collective-permute-start | bytes 1572872 | tf_op jit(solution)/shard_map/ppermute | solution.py:21
  98.0 15.2 %collective-permute-start.4 = (f32[16,64,128]{2,1,0:T(8,128)S(1)}, f32[16,64,128]{2,1,0:T(8,128)}, u32[]{:S(2)}, u32[]{:S(2)}) collective-permute-start(f32[16,64,128]{2,1,0:T(8,128)S(1)} %fusion.10), channel_id=1, source_target_pairs={{0,4},{4,8},{8,12},{1,5},{5,9},{9,13},{2,6},{6,10},{10,14},{3,7},{... | collective-permute-start | bytes 1572872 | tf_op jit(solution)/shard_map/ppermute | solution.py:21
  114.4 14.3 %collective-permute-start.5 = (f32[16,64,128]{2,1,0:T(8,128)S(1)}, f32[16,64,128]{2,1,0:T(8,128)S(1)}, u32[]{:S(2)}, u32[]{:S(2)}) collective-permute-start(f32[16,64,128]{2,1,0:T(8,128)S(1)} %fusion.8), channel_id=1, source_target_pairs={{0,4},{4,8},{8,12},{1,5},{5,9},{9,13},{2,6},{6,10},{10,14},{3,7},{... | collective-permute-start | bytes 1572872 | tf_op jit(solution)/shard_map/ppermute | solution.py:21
  119.2 9.7 %copy-start.3 = (f32[2,8,64,128]{3,2,1,0:T(8,128)S(1)}, f32[2,8,64,128]{3,2,1,0:T(8,128)}, u32[]{:S(2)}) copy-start(f32[2,8,64,128]{3,2,1,0:T(8,128)} %get-tuple-element.92) | copy-start | bytes 1572868
  129.2 2.9 %collective-permute-start.6 = (f32[4,8,64,128]{3,2,1,0:T(8,128)S(1)}, f32[4,8,64,128]{3,2,1,0:T(8,128)}, u32[]{:S(2)}, u32[]{:S(2)}) collective-permute-start(f32[4,8,64,128]{3,2,1,0:T(8,128)S(1)} %fusion.5), channel_id=1, source_target_pairs={{0,1},{1,0},{2,3},{3,2},{4,5},{5,4},{6,7},{7,6},{8,9},{9,8},{10,11... | collective-permute-start | bytes 3145736 | tf_op jit(solution)/shard_map/ppermute | solution.py:25
  135.4 12.4 %copy-start.1 = (f32[2,4,128]{2,1,0:T(4,128)S(1)}, f32[2,4,128]{2,1,0:T(4,128)}, u32[]{:S(2)}) copy-start(f32[2,4,128]{2,1,0:T(4,128)} %param.19) | copy-start | bytes 12292

commit v14 on v13

--- a/solution.py
+++ b/solution.py
@@ -128,6 +128,11 @@
         e_ref[0, pair] = jnp.where(left, us[0], us[1])
 
 
+def end_pair_kernel(xa_ref, xb_ref, ba_ref, bb_ref, wa_ref, wb_ref, ea_ref, eb_ref):
+    end_kernel(xa_ref, ba_ref, wa_ref, ea_ref)
+    end_kernel(xb_ref, bb_ref, wb_ref, eb_ref)
+
+
 def out_kernel(y_ref, ct_ref, cumc_ref, v_ref, z_ref, nw_ref, o_ref, g_ref):
     pairs = v_ref.shape[1]
     heads = 2 * pairs
@@ -244,21 +249,27 @@
     to_end = jnp.exp(cum_all[..., own - 1 :] - cum_all) * step_sizes.reshape(heads_dev, nsub, own)
     to_end = to_end.reshape(set_groups, per_group, tokens)
 
-    def end_states(x_half, at, start, count):
+    def end_states(x_pair, start, count):
+        x_spec = pl.BlockSpec((own, group_width), lambda g: (0, g + start))
+        b_spec = pl.BlockSpec((1, half, own), lambda g: (g + start, 0, 0))
+        w_spec = pl.BlockSpec((1, per_group, own), lambda g: (g + start, 0, 0))
+        e_spec = pl.BlockSpec((1, pairs, half, 128), lambda g: (g, 0, 0, 0))
         return pl.pallas_call(
-            end_kernel,
+            end_pair_kernel,
             grid=(count,),
-            in_specs=[
-                pl.BlockSpec((own, group_width), lambda g: (0, g + start)),
-                pl.BlockSpec((1, half, own), lambda g: (g + start, 0, 0)),
-                pl.BlockSpec((1, per_group, own), lambda g: (g + start, 0, 0)),
-            ],
-            out_specs=pl.BlockSpec((1, pairs, half, 128), lambda g: (g, 0, 0, 0)),
-            out_shape=jax.ShapeDtypeStruct((count, pairs, half, 128), F32),
+            in_specs=[x_spec, x_spec, b_spec, b_spec, w_spec, w_spec],
+            out_specs=[e_spec, e_spec],
+            out_shape=[jax.ShapeDtypeStruct((count, pairs, half, 128), F32)] * 2,
         )(
-            x_half,
-            lax.dynamic_slice_in_dim(bc_conv[0], at * own, own, 2),
-            lax.dynamic_slice_in_dim(to_end, at * own, own, 2),
+            *x_pair,
+            *(
+                lax.dynamic_slice_in_dim(bc_conv[0], at * own, own, 2)
+                for at in (sub_index, 1 - sub_index)
+            ),
+            *(
+                lax.dynamic_slice_in_dim(to_end, at * own, own, 2)
+                for at in (sub_index, 1 - sub_index)
+            ),
         )
 
     def pair_layout(values):
@@ -269,8 +280,7 @@
     chip_decay = decay_first * decay_second
 
     def chip_ends(x_pair, start, count):
-        own_end = end_states(x_pair[0], sub_index, start, count)
-        other_end = end_states(x_pair[1], 1 - sub_index, start, count)
+        own_end, other_end = end_states(x_pair, start, count)
         first = jnp.where(sub_index == 0, own_end, other_end)
         second = jnp.where(sub_index == 0, other_end, own_end)
         return first, decay_second[start : start + count] * first + second

time: 149 us -> 144 us (0.966)
  Pallas kernels: 63.6 us -> 59.4 us
    pallas_call x4 -> x2, Pallas kernels: 20.3 us -> 16.1 us  [end_states(): pl.pallas_call(end_pair_kernel, grid=(count,), in_specs=[x_spec, x_spec,...]
  transfers between devices with their start and end apart: 7 -> 7, of which waited for: 4 -> 4; matrix products, arithmetic and copies ran while one was open for 23% -> 23% of each run, Pallas kernels for 35% -> 33%
where the time goes in v14:
time: 144 us
  Pallas kernels  59.4 us (41%)
  other arithmetic  36.6 us (25%)
  starting transfers between devices  22.8 us (16%)
  local copies, waits for them, and re-layouts  15.7 us (11%)
  waiting for transfers between devices  8.13 us (6%)
    pallas_call x4, Pallas kernels, scan_group(): pl.pallas_call(kernel, grid=(1, blocks), in_specs=in_specs, out_specs=til...  30.9 us
    ppermute x5, starting transfers between devices, passed_along(): return lax.ppermute(x, axis, pairs)  22.7 us
    pallas_call x2, Pallas kernels, end_states(): pl.pallas_call(end_pair_kernel, grid=(count,), in_specs=[x_spec, x_spec,...  16.1 us
    pallas_call x1, Pallas kernels, per_device(): pl.pallas_call(out_kernel, grid=(set_groups, own // out_len), in_specs=[p...  12.4 us
    mul x1, other arithmetic, conv_rows(): return jax.nn.silu(total)  12.4 us
    ppermute x5, waiting for transfers between devices, passed_along(): return lax.ppermute(x, axis, pairs)  7.15 us
    mul x1, other arithmetic, conv_cols(): return jax.nn.silu(total)  5.47 us
    concatenate x1, other arithmetic, per_device(): x_pad = jnp.concatenate([x_rim, x_raw], 0)  4.98 us
  transfers between devices with their start and end apart: 7, of which 4 were waited for; matrix products, arithmetic and copies ran while one was open for 23% of the time, Pallas kernels for 33%

profile of v14, /device:TPU:0, one launch (start us, length us, event | category | flops | bytes accessed | tf_op | source)
XLA Modules:
  0.0 143.6 jit_solution(4667978943004730451)
XLA Ops:
  0.0 1.0 slice.124
  2.1 4.9 %collective-permute-start = (bf16[3,4608]{1,0:T(4,128)(2,1)S(1)}, bf16[3,4608]{1,0:T(4,128)(2,1)S(1)}, u32[]{:S(2)}, u32[]{:S(2)}) collective-permute-start(bf16[3,4608]{1,0:T(4,128)(2,1)S(1)} %pad_maximum_fusion.4), channel_id=1, source_target_pairs={{0,4},{4,8},{8,12},{1,5},{5,9},{9,13},{2,6},{6,10},{10,14},{3,7},{... | collective-permute-start | bytes 82952 | tf_op jit(solution)/shard_map/ppermute | solution.py:21
  7.7 1.2 broadcast_multiply_fusion
  14.7 1.3 copy.66
  16.9 5.5 %divide_multiply_fusion.2 = f32[2,4,64,1024]{3,2,1,0:T(8,128)S(1)} fusion(bf16[2,4,64,1024]{3,2,1,0:T(8,128)(2,1)} %param.13, bf16[2,4,64,3]{3,2,1,0:T(8,128)(2,1)S(1)} %bitcast.131, f32[2,4,64]{2,1,0:T(4,128)S(1)} %get-tuple-element.136, f32[2,4,64]{2,1,0:T(4,128)S(1)} %get-tuple-element.134, f32[2,4,64]{2,1,0:T(4,128)S(1)} %get-tuple-element.135, ...), kind=kLoop, calls=%fused_computation.11 | loop fusion | flops 13107200 | bytes 3159040 | tf_op jit(solution)/shard_map/jit(silu)/mul | solution.py:45
  22.4 1.1 constant_dynamic-slice_fusion.7
  23.5 5.0 %fusion = (bf16[515,4096]{1,0:T(8,128)(2,1)S(1)}, bf16[515,4096]{1,0:T(8,128)(2,1)S(1)}) fusion(s32[]{:T(128)S(6)} %select_n.146, bf16[1024,4096]{1,0:T(8,128)(2,1)} %param.12, bf16[3,4096]{1,0:T(4,128)(2,1)S(1)} %slice.156, s32[]{:T(128)S(6)} %select_n.145), kind=kLoop, calls=%fused_computation.6 | loop fusion | flops 16875520 | bytes 16850952 | tf_op jit(solution)/shard_map/concatenate | solution.py:193
  28.5 12.4 %divide_multiply_fusion = (f32[512,4096]{1,0:T(8,128)}, f32[512,4096]{1,0:T(8,128)}) fusion(bf16[515,4096]{1,0:T(8,128)(2,1)S(1)} %get-tuple-element.107, f32[4096]{0:T(1024)S(1)} %bitcast.136, f32[4096]{0:T(1024)S(1)} %bitcast.137, f32[4096]{0:T(1024)S(1)} %bitcast.135, f32[4096]{0:T(1024)S(1)} %bitcast.134, f32[4096]{0:T(1024)S(1)} %copy-done.7, ...), kind=kLoop, calls=%fused_computation.2 | loop fusion | flops 67108864 | bytes 50413568 | tf_op jit(solution)/shard_map/jit(silu)/mul | solution.py:35
  41.0 1.1 dynamic-slice_bitcast_fusion
  42.1 8.0 %shard_map.118 = (f32[2,8,64,128]{3,2,1,0:T(8,128)}, f32[2,8,64,128]{3,2,1,0:T(8,128)}) custom-call(f32[512,4096]{1,0:T(8,128)} %get-tuple-element.90.xa_ref.xc_ref.refs_0_, f32[512,4096]{1,0:T(8,128)} %get-tuple-element.64.xb_ref, f32[4,64,512]{2,1,0:T(8,128)} %get-tuple-element.120.ba_ref, f32[4,64,512]{2,1,0:T(8,128)} %get-tuple-element.119.bb_ref, ...), custom_call_target="tpu_custom_call" | custom-call | tf_op jit(solution)/shard_map/pallas_call | solution.py:257
  50.1 1.3 broadcast_select_fusion.1
  52.3 1.5 %select_bitcast_fusion.2 = (f32[2,4,1,64,512]{4,3,2,1,0:T(8,128)S(1)}, f32[2,4,1,64,512]{4,3,2,1,0:T(8,128)S(1)}) fusion(f32[2,4,64,512]{3,2,1,0:T(8,128)} %collective-permute-done.1, f32[2,4,64,1024]{3,2,1,0:T(8,128)S(1)} %divide_multiply_fusion.2, s32[]{:T(128)S(6)} %select_n.148, pred[]{:T(512)S(6)} %eq.2), kind=kLoop, calls=%fused_computation.29 | loop fusion | flops 524288 | bytes 4194309 | tf_op jit(solution)/shard_map/stack | solution.py:207
  53.8 1.2 pad_maximum_fusion.1
  55.0 1.4 copy.63
  56.3 3.7 %collective-permute-start.2 = (f32[16,64,128]{2,1,0:T(8,128)}, f32[16,64,128]{2,1,0:T(8,128)S(1)}, u32[]{:S(2)}, u32[]{:S(2)}) collective-permute-start(f32[16,64,128]{2,1,0:T(8,128)} %bitcast_add_fusion), channel_id=1, source_target_pairs={{0,4},{4,8},{8,12},{1,5},{5,9},{9,13},{2,6},{6,10},{10,14},{3,7},{... | collective-permute-start | bytes 1572872 | tf_op jit(solution)/shard_map/ppermute | solution.py:21
  60.3 8.1 %shard_map.120 = (f32[2,8,64,128]{3,2,1,0:T(8,128)}, f32[2,8,64,128]{3,2,1,0:T(8,128)}) custom-call(f32[512,4096]{1,0:T(8,128)} %get-tuple-element.90.xa_ref.xc_ref.refs_0_, f32[512,4096]{1,0:T(8,128)} %get-tuple-element.64.xb_ref, f32[4,64,512]{2,1,0:T(8,128)} %get-tuple-element.120.ba_ref, f32[4,64,512]{2,1,0:T(8,128)} %get-tuple-element.119.bb_ref, ...), custom_call_target="tpu_custom_call" | custom-call | tf_op jit(solution)/shard_map/pallas_call | solution.py:257
  68.4 7.8 %shard_map.119.refs_7_ = f32[512,4096]{1,0:T(8,128)} custom-call(f32[512,4096]{1,0:T(8,128)} %get-tuple-element.90.xa_ref.xc_ref.refs_0_, f32[4,512,128]{2,1,0:T(8,128)} %bitcast.105, f32[4,128,512]{2,1,0:T(8,128)} %bitcast.116, f32[4,16,512]{2,1,0:T(8,128)} %copy-done.2, f32[4,512,16]{2,1,0:T(8,128)} %bitcast.112, f32[4,16,512]{2,1,0:T(8,128)} %bitcast.126, ...), custom_call_target="tpu_custom_call" | custom-call | tf_op jit(solution)/shard_map/pallas_call | solution.py:314
  77.4 4.3 %collective-permute-start.3 = (f32[16,64,128]{2,1,0:T(8,128)S(1)}, f32[16,64,128]{2,1,0:T(8,128)}, u32[]{:S(2)}, u32[]{:S(2)}) collective-permute-start(f32[16,64,128]{2,1,0:T(8,128)S(1)} %fusion.12), channel_id=1, source_target_pairs={{0,4},{4,8},{8,12},{1,5},{5,9},{9,13},{2,6},{6,10},{10,14},{3,7},{... | collective-permute-start | bytes 1572872 | tf_op jit(solution)/shard_map/ppermute | solution.py:21
  81.7 7.7 %shard_map.121.refs_7_ = f32[512,4096]{1,0:T(8,128)} custom-call(f32[512,4096]{1,0:T(8,128)} %get-tuple-element.90.xa_ref.xc_ref.refs_0_, f32[4,512,128]{2,1,0:T(8,128)} %bitcast.106, f32[4,128,512]{2,1,0:T(8,128)} %bitcast.117, f32[4,16,512]{2,1,0:T(8,128)} %copy-done.2, f32[4,512,16]{2,1,0:T(8,128)} %bitcast.113, ...), custom_call_target="tpu_custom_call", output_to_operand_aliasing={{}: (7, {})} | custom-call | tf_op jit(solution)/shard_map/pallas_call | solution.py:314
  89.4 3.1 %collective-permute-done.3 = f32[16,64,128]{2,1,0:T(8,128)} collective-permute-done((f32[16,64,128]{2,1,0:T(8,128)S(1)}, f32[16,64,128]{2,1,0:T(8,128)}, u32[]{:S(2)}, u32[]{:S(2)}) %collective-permute-start.3) | collective-permute-done | bytes 524320 | tf_op jit(solution)/shard_map/ppermute | solution.py:21
  92.5 1.2 fusion.11
  93.7 5.3 %collective-permute-start.4 = (f32[16,64,128]{2,1,0:T(8,128)S(1)}, f32[16,64,128]{2,1,0:T(8,128)}, u32[]{:S(2)}, u32[]{:S(2)}) collective-permute-start(f32[16,64,128]{2,1,0:T(8,128)S(1)} %fusion.10), channel_id=1, source_target_pairs={{0,4},{4,8},{8,12},{1,5},{5,9},{9,13},{2,6},{6,10},{10,14},{3,7},{... | collective-permute-start | bytes 1572872 | tf_op jit(solution)/shard_map/ppermute | solution.py:21
  99.0 7.7 %shard_map.122.refs_7_ = f32[512,4096]{1,0:T(8,128)} custom-call(f32[512,4096]{1,0:T(8,128)} %get-tuple-element.90.xa_ref.xc_ref.refs_0_, f32[4,512,128]{2,1,0:T(8,128)} %bitcast.107, f32[4,128,512]{2,1,0:T(8,128)} %bitcast.118, f32[4,16,512]{2,1,0:T(8,128)} %copy-done.2, f32[4,512,16]{2,1,0:T(8,128)} %bitcast.114, ...), custom_call_target="tpu_custom_call", output_to_operand_aliasing={{}: (7, {})} | custom-call | tf_op jit(solution)/shard_map/pallas_call | solution.py:314
  106.7 2.2 %collective-permute-done.4 = f32[16,64,128]{2,1,0:T(8,128)} collective-permute-done((f32[16,64,128]{2,1,0:T(8,128)S(1)}, f32[16,64,128]{2,1,0:T(8,128)}, u32[]{:S(2)}, u32[]{:S(2)}) %collective-permute-start.4) | collective-permute-done | bytes 524320 | tf_op jit(solution)/shard_map/ppermute | solution.py:21
  109.0 1.2 fusion.9
  110.2 4.5 %collective-permute-start.5 = (f32[16,64,128]{2,1,0:T(8,128)S(1)}, f32[16,64,128]{2,1,0:T(8,128)S(1)}, u32[]{:S(2)}, u32[]{:S(2)}) collective-permute-start(f32[16,64,128]{2,1,0:T(8,128)S(1)} %fusion.8), channel_id=1, source_target_pairs={{0,4},{4,8},{8,12},{1,5},{5,9},{9,13},{2,6},{6,10},{10,14},{3,7},{... | collective-permute-start | bytes 1572872 | tf_op jit(solution)/shard_map/ppermute | solution.py:21
  115.0 7.7 %shard_map.123.y_ref = f32[512,4096]{1,0:T(8,128)} custom-call(f32[512,4096]{1,0:T(8,128)} %get-tuple-element.90.xa_ref.xc_ref.refs_0_, f32[4,512,128]{2,1,0:T(8,128)} %bitcast.108, f32[4,128,512]{2,1,0:T(8,128)} %bitcast.119, f32[4,16,512]{2,1,0:T(8,128)} %copy-done.2, f32[4,512,16]{2,1,0:T(8,128)} %bitcast.115, ...), custom_call_target="tpu_custom_call", output_to_operand_aliasing={{}: (7, {})} | custom-call | tf_op jit(solution)/shard_map/pallas_call | solution.py:314
  122.7 1.8 %collective-permute-done.5 = f32[16,64,128]{2,1,0:T(8,128)S(1)} collective-permute-done((f32[16,64,128]{2,1,0:T(8,128)S(1)}, f32[16,64,128]{2,1,0:T(8,128)S(1)}, u32[]{:S(2)}, u32[]{:S(2)}) %collective-permute-start.5) | collective-permute-done | bytes 524320 | tf_op jit(solution)/shard_map/ppermute | solution.py:21
  125.5 1.3 copy.68
  127.8 1.6 %select_bitcast_fusion.1 = (f32[4,8,1,64,128]{4,3,1,0,2:T(8,128)S(1)}, f32[4,8,1,64,128]{4,3,1,0,2:T(8,128)S(1)}) fusion(f32[4,8,64,128]{3,2,1,0:T(8,128)} %collective-permute-done.6, pred[]{:T(512)S(6)} %eq.2, f32[4,8,64,128]{3,2,1,0:T(8,128)S(1)} %bitcast.111, f32[2,8,64,128]{3,2,1,0:T(8,128)S(1)} %copy-done.3, ...), kind=kLoop, calls=%fused_computation.26 | loop fusion | flops 1572864 | bytes 5259265 | tf_op jit(solution)/shard_map/stack | solution.py:373
  129.7 1.5 %copy.69 = f32[4,8,2,64,128]{4,3,2,1,0:T(8,128)} copy(f32[4,8,2,64,128]{4,3,1,0,2:T(8,128)S(1)} %pad_maximum_fusion) | data formatting | bytes 4194304 | tf_op jit(solution)/shard_map/stack | solution.py:373
  131.2 12.4 %shard_map.124 = bf16[512,4096]{1,0:T(8,128)(2,1)} custom-call(f32[512,4096]{1,0:T(8,128)} %shard_map.123.y_ref, f32[4,512,128]{2,1,0:T(8,128)} %bitcast.109, f32[4,512,16]{2,1,0:T(8,128)} %bitcast.124, f32[4,8,128,128]{3,2,1,0:T(8,128)} %bitcast.120, bf16[512,4096]{1,0:T(8,128)(2,1)} %z_ref.1, f32[1,4096]{1,0:T(1,128)} %bitcast.139), custom_call_target="tpu_custom_call" | custom-call | tf_op jit(solution)/shard_map/pallas_call | solution.py:376
  (90 shorter events, 13.2 us)
Async XLA Ops:
  0.0 14.1 %copy-start = (f32[2,4,128]{2,1,0:T(4,128)S(1)}, f32[2,4,128]{2,1,0:T(4,128)}, u32[]{:S(2)}) copy-start(f32[2,4,128]{2,1,0:T(4,128)} %param.19) | copy-start | bytes 12292
  0.0 10.7 %copy-start.6 = (f32[4,4096]{1,0:T(4,128)S(1)}, f32[4,4096]{1,0:T(4,128)}, u32[]{:S(2)}) copy-start(f32[4,4096]{1,0:T(4,128)} %param.16) | copy-start | bytes 196612
  2.1 14.7 %collective-permute-start = (bf16[3,4608]{1,0:T(4,128)(2,1)S(1)}, bf16[3,4608]{1,0:T(4,128)(2,1)S(1)}, u32[]{:S(2)}, u32[]{:S(2)}) collective-permute-start(bf16[3,4608]{1,0:T(4,128)(2,1)S(1)} %pad_maximum_fusion.4), channel_id=1, source_target_pairs={{0,4},{4,8},{8,12},{1,5},{5,9},{9,13},{2,6},{6,10},{10,14},{3,7},{... | collective-permute-start | bytes 82952 | tf_op jit(solution)/shard_map/ppermute | solution.py:21
  7.7 6.4 %copy-start.8 = (f32[4,2,4,128]{3,2,1,0:T(4,128)S(1)}, f32[4,2,4,128]{3,2,1,0:T(4,128)}, u32[]{:S(2)}) copy-start(f32[4,2,4,128]{3,2,1,0:T(4,128)} %param.18) | copy-start | bytes 49156
  9.6 6.4 %copy-start.9 = (f32[64]{0:T(128)S(1)}, f32[64]{0:T(128)}, u32[]{:S(2)}) copy-start(f32[64]{0:T(128)} %param.22) | copy-start | bytes 772
  14.6 13.9 %copy-start.2 = (f32[4,16,512]{2,1,0:T(8,128)}, f32[4,16,512]{2,1,0:T(8,128)S(1)}, u32[]{:S(2)}) copy-start(f32[4,16,512]{2,1,0:T(8,128)S(1)} %reshape.107.cumr_ref.refs_3_) | copy-start | bytes 393220
  23.5 28.8 %collective-permute-start.1 = (f32[2,4,64,512]{3,2,1,0:T(8,128)}, f32[2,4,64,512]{3,2,1,0:T(8,128)}, u32[]{:S(2)}, u32[]{:S(2)}) collective-permute-start(f32[2,4,64,512]{3,2,1,0:T(8,128)} %constant_dynamic-slice_fusion.7), channel_id=1, source_target_pairs={{0,1},{1,0},{2,3},{3,2},{4,5},{5,4},{6,7},{7,6},{8,9},{9,8},{10,11... | collective-permute-start | bytes 3145736 | tf_op jit(solution)/shard_map/ppermute | solution.py:25
  23.5 5.0 %copy-start.7 = (f32[4096]{0:T(1024)S(1)}, f32[4096]{0:T(1024)}, u32[]{:S(2)}) copy-start(f32[4096]{0:T(1024)} %param.17) | copy-start | bytes 49156
  56.3 20.7 %collective-permute-start.2 = (f32[16,64,128]{2,1,0:T(8,128)}, f32[16,64,128]{2,1,0:T(8,128)S(1)}, u32[]{:S(2)}, u32[]{:S(2)}) collective-permute-start(f32[16,64,128]{2,1,0:T(8,128)} %bitcast_add_fusion), channel_id=1, source_target_pairs={{0,4},{4,8},{8,12},{1,5},{5,9},{9,13},{2,6},{6,10},{10,14},{3,7},{... | collective-permute-start | bytes 1572872 | tf_op jit(solution)/shard_map/ppermute | solution.py:21
  68.3 7.8 %copy-start.4 = (f32[2,8,64,128]{3,2,1,0:T(8,128)S(1)}, f32[2,8,64,128]{3,2,1,0:T(8,128)}, u32[]{:S(2)}) copy-start(f32[2,8,64,128]{3,2,1,0:T(8,128)} %get-tuple-element.65) | copy-start | bytes 1572868
  68.4 7.8 %copy-start.5 = (f32[2,8,64,128]{3,2,1,0:T(8,128)S(1)}, f32[2,8,64,128]{3,2,1,0:T(8,128)}, u32[]{:S(2)}) copy-start(f32[2,8,64,128]{3,2,1,0:T(8,128)} %get-tuple-element.66) | copy-start | bytes 1572868
  77.4 15.0 %collective-permute-start.3 = (f32[16,64,128]{2,1,0:T(8,128)S(1)}, f32[16,64,128]{2,1,0:T(8,128)}, u32[]{:S(2)}, u32[]{:S(2)}) collective-permute-start(f32[16,64,128]{2,1,0:T(8,128)S(1)} %fusion.12), channel_id=1, source_target_pairs={{0,4},{4,8},{8,12},{1,5},{5,9},{9,13},{2,6},{6,10},{10,14},{3,7},{... | collective-permute-start | bytes 1572872 | tf_op jit(solution)/shard_map/ppermute | solution.py:21
  93.7 15.2 %collective-permute-start.4 = (f32[16,64,128]{2,1,0:T(8,128)S(1)}, f32[16,64,128]{2,1,0:T(8,128)}, u32[]{:S(2)}, u32[]{:S(2)}) collective-permute-start(f32[16,64,128]{2,1,0:T(8,128)S(1)} %fusion.10), channel_id=1, source_target_pairs={{0,4},{4,8},{8,12},{1,5},{5,9},{9,13},{2,6},{6,10},{10,14},{3,7},{... | collective-permute-start | bytes 1572872 | tf_op jit(solution)/shard_map/ppermute | solution.py:21
  110.2 14.3 %collective-permute-start.5 = (f32[16,64,128]{2,1,0:T(8,128)S(1)}, f32[16,64,128]{2,1,0:T(8,128)S(1)}, u32[]{:S(2)}, u32[]{:S(2)}) collective-permute-start(f32[16,64,128]{2,1,0:T(8,128)S(1)} %fusion.8), channel_id=1, source_target_pairs={{0,4},{4,8},{8,12},{1,5},{5,9},{9,13},{2,6},{6,10},{10,14},{3,7},{... | collective-permute-start | bytes 1572872 | tf_op jit(solution)/shard_map/ppermute | solution.py:21
  115.0 9.7 %copy-start.3 = (f32[2,8,64,128]{3,2,1,0:T(8,128)S(1)}, f32[2,8,64,128]{3,2,1,0:T(8,128)}, u32[]{:S(2)}) copy-start(f32[2,8,64,128]{3,2,1,0:T(8,128)} %get-tuple-element.100) | copy-start | bytes 1572868
  124.9 2.9 %collective-permute-start.6 = (f32[4,8,64,128]{3,2,1,0:T(8,128)S(1)}, f32[4,8,64,128]{3,2,1,0:T(8,128)}, u32[]{:S(2)}, u32[]{:S(2)}) collective-permute-start(f32[4,8,64,128]{3,2,1,0:T(8,128)S(1)} %fusion.5), channel_id=1, source_target_pairs={{0,1},{1,0},{2,3},{3,2},{4,5},{5,4},{6,7},{7,6},{8,9},{9,8},{10,11... | collective-permute-start | bytes 3145736 | tf_op jit(solution)/shard_map/ppermute | solution.py:25
  131.2 12.4 %copy-start.1 = (f32[2,4,128]{2,1,0:T(4,128)S(1)}, f32[2,4,128]{2,1,0:T(4,128)}, u32[]{:S(2)}) copy-start(f32[2,4,128]{2,1,0:T(4,128)} %param.19) | copy-start | bytes 12292

commit v15 on v14

--- a/solution.py
+++ b/solution.py
@@ -70,9 +70,10 @@
     )
 
 
-def scan_kernel(xc_ref, ct_ref, b_ref, cumr_ref, cumc_ref, stp_ref, dsk_ref, y_ref, e_ref):
+def scan_kernel(xa_ref, xb_ref, flag_ref, ct_ref, b_ref, cumr_ref, cumc_ref, stp_ref, dsk_ref, y_ref, e_ref):
     chunk = pl.program_id(1)
-    block_len = xc_ref.shape[0]
+    block_len = xa_ref.shape[0]
+    first = flag_ref[0:1, 0:1] > 0.5
     pairs = e_ref.shape[0]
     heads = 2 * pairs
 
@@ -92,7 +93,7 @@
     left = lax.broadcasted_iota(jnp.int32, (1, 128), 1) < HEAD_DIM
     for pair in range(pairs):
         lanes = slice(pair * 128, (pair + 1) * 128)
-        xp = xc_ref[:, lanes]
+        xp = jnp.where(first, xa_ref[:, lanes], xb_ref[:, lanes])
         xs = split(xp)
         s_old = e_ref[pair]
         ys = []
@@ -190,15 +191,9 @@
     )
     x_rim = rims[:, :channels]
     bc_rim = rims[:, channels:].transpose(1, 0).reshape(bc_tail.shape)
-    x_pad = jnp.concatenate([x_rim, x_raw], 0)
-    x_own = conv_rows(
-        lax.dynamic_slice_in_dim(x_pad, sub_index * own, own + rim_len, 0), conv_x_w, conv_x_b
-    )
-    x_other = conv_rows(
-        lax.dynamic_slice_in_dim(x_pad, (1 - sub_index) * own, own + rim_len, 0),
-        conv_x_w,
-        conv_x_b,
-    )
+    x_first = conv_rows(jnp.concatenate([x_rim, x_raw[:own]], 0), conv_x_w, conv_x_b)
+    x_second = conv_rows(x_raw[own - rim_len :], conv_x_w, conv_x_b)
+    first_flag = jnp.full((8, 128), sub_index == 0, F32)
     bc_weights = lax.dynamic_slice_in_dim(conv_bc_w, sub_index * half, half, 3)
     bc_bias = lax.dynamic_slice_in_dim(conv_bc_b, sub_index * half, half, 2)
     bc_conv = conv_cols(jnp.concatenate([bc_rim, bc_raw], 3), bc_weights, bc_bias)
@@ -264,11 +259,11 @@
             *x_pair,
             *(
                 lax.dynamic_slice_in_dim(bc_conv[0], at * own, own, 2)
-                for at in (sub_index, 1 - sub_index)
+                for at in (0, 1)
             ),
             *(
                 lax.dynamic_slice_in_dim(to_end, at * own, own, 2)
-                for at in (sub_index, 1 - sub_index)
+                for at in (0, 1)
             ),
         )
 
@@ -280,17 +275,15 @@
     chip_decay = decay_first * decay_second
 
     def chip_ends(x_pair, start, count):
-        own_end, other_end = end_states(x_pair, start, count)
-        first = jnp.where(sub_index == 0, own_end, other_end)
-        second = jnp.where(sub_index == 0, other_end, own_end)
+        first, second = end_states(x_pair, start, count)
         return first, decay_second[start : start + count] * first + second
 
     pieces = 2 if (set_groups * pairs) % 2 == 0 else 1
     rounds = ctx_size + pieces - 2
     early = set_groups // 2 if (pieces == 2 and set_groups % 2 == 0 and rounds > 0) else set_groups
-    first_end, chip_end = chip_ends((x_own, x_other), 0, early)
+    first_end, chip_end = chip_ends((x_first, x_second), 0, early)
     ctx_index = lax.axis_index("ctx")
-    scan_inputs = (x_own, c_cols, b_rows, cum_rows, cum_cols, step_rows, skip_row)
+    scan_inputs = (x_first, x_second, first_flag, c_cols, b_rows, cum_rows, cum_cols, step_rows, skip_row)
 
     def scan_group(group, inputs, target):
         count = len(inputs)
@@ -298,6 +291,8 @@
         tile = pl.BlockSpec((block_len, group_width), lambda g, c: (c, group))
         in_specs = [
             tile,
+            tile,
+            pl.BlockSpec((8, 128), lambda g, c: (0, 0)),
             pl.BlockSpec((1, block_len, state), lambda g, c: (group, c, 0)),
             pl.BlockSpec((1, state, block_len), lambda g, c: (group, 0, c)),
             pl.BlockSpec((1, per_group, block_len), lambda g, c: (group, 0, c)),
@@ -339,7 +334,7 @@
             lax.dynamic_index_in_dim(received, send_at, 0, keepdims=False)
         )
         held = scan_inputs
-        x_pair = (x_own, x_other)
+        x_pair = (x_first, x_second)
         if any(p == step_index for p in placed):
             outgoing, held, x_pair = lax.optimization_barrier((outgoing, scan_inputs, x_pair))
         if rounds > 0:

time: 144 us -> 147 us (1.021)
  local copies, waits for them, and re-layouts: 15.7 us -> 18.3 us
  Pallas kernels: 59.4 us -> 61.6 us
  waiting for transfers between devices: 8.13 us -> 6.44 us
    mul x1, other arithmetic: 12.4 us -> 17.9 us  [conv_rows(): return jax.nn.silu(total)]
    concatenate x1 -> x0, other arithmetic: 4.98 us -> none  [per_device(): x_pad = jnp.concatenate([x_rim, x_raw], 0)]
    pallas_call x4, Pallas kernels: 30.9 us -> 33.1 us  [scan_group(): pl.pallas_call(kernel, grid=(1, blocks), in_specs=in_specs, out_specs=til...]
    ppermute x5, waiting for transfers between devices: 7.15 us -> 5.54 us  [passed_along(): return lax.ppermute(x, axis, pairs)]
  transfers between devices with their start and end apart: 7 -> 7, of which waited for: 4 -> 4; matrix products, arithmetic and copies ran while one was open for 23% -> 23% of each run, Pallas kernels for 33% -> 34%
where the time goes in v15:
time: 147 us; the launch traced here: 146 us
  Pallas kernels  61.6 us (42%)
  other arithmetic  35.2 us (24%)
  starting transfers between devices  23.8 us (16%)
  local copies, waits for them, and re-layouts  18.3 us (12%)
  waiting for transfers between devices  6.44 us (4%)
    pallas_call x4, Pallas kernels, scan_group(): pl.pallas_call(kernel, grid=(1, blocks), in_specs=in_specs, out_specs=til...  33.1 us
    ppermute x5, starting transfers between devices, passed_along(): return lax.ppermute(x, axis, pairs)  23.7 us
    mul x1, other arithmetic, conv_rows(): return jax.nn.silu(total)  17.9 us
    pallas_call x2, Pallas kernels, end_states(): pl.pallas_call(end_pair_kernel, grid=(count,), in_specs=[x_spec, x_spec,...  16.1 us
    pallas_call x1, Pallas kernels, per_device(): pl.pallas_call(out_kernel, grid=(set_groups, own // out_len), in_specs=[p...  12.4 us
    ppermute x5, waiting for transfers between devices, passed_along(): return lax.ppermute(x, axis, pairs)  5.54 us
    mul x1, other arithmetic, conv_cols(): return jax.nn.silu(total)  5.49 us
  transfers between devices with their start and end apart: 7, of which 4 were waited for; matrix products, arithmetic and copies ran while one was open for 23% of the time, Pallas kernels for 34%

profile of v15, /device:TPU:0, one launch (start us, length us, event | category | flops | bytes accessed | tf_op | source)
XLA Modules:
  0.0 146.4 jit_solution(7331310873321185874)
XLA Ops:
  0.0 1.0 slice.129
  2.1 4.9 %collective-permute-start = (bf16[3,4608]{1,0:T(4,128)(2,1)S(1)}, bf16[3,4608]{1,0:T(4,128)(2,1)S(1)}, u32[]{:S(2)}, u32[]{:S(2)}) collective-permute-start(bf16[3,4608]{1,0:T(4,128)(2,1)S(1)} %pad_maximum_fusion.5), channel_id=1, source_target_pairs={{0,4},{4,8},{8,12},{1,5},{5,9},{9,13},{2,6},{6,10},{10,14},{3,7},{... | collective-permute-start | bytes 82952 | tf_op jit(solution)/shard_map/ppermute | solution.py:21
  7.7 1.2 broadcast_multiply_fusion
  14.6 1.4 copy.69
  17.0 5.5 %divide_multiply_fusion.2 = f32[2,4,64,1024]{3,2,1,0:T(8,128)S(1)} fusion(bf16[2,4,64,1024]{3,2,1,0:T(8,128)(2,1)} %param.13, bf16[2,4,64,3]{3,2,1,0:T(8,128)(2,1)S(1)} %bitcast.127, f32[2,4,64]{2,1,0:T(4,128)S(1)} %get-tuple-element.146, f32[2,4,64]{2,1,0:T(4,128)S(1)} %get-tuple-element.144, f32[2,4,64]{2,1,0:T(4,128)S(1)} %get-tuple-element.145, ...), kind=kLoop, calls=%fused_computation.10 | loop fusion | flops 13107200 | bytes 3159040 | tf_op jit(solution)/shard_map/jit(silu)/mul | solution.py:45
  22.5 1.1 constant_dynamic-slice_fusion.4
  23.6 17.9 %divide_multiply_fusion = (f32[512,4096]{1,0:T(8,128)}, f32[512,4096]{1,0:T(8,128)}) fusion(bf16[1024,4096]{1,0:T(8,128)(2,1)} %param.12, f32[4096]{0:T(1024)S(1)} %bitcast.132, f32[4096]{0:T(1024)S(1)} %bitcast.133, f32[4096]{0:T(1024)S(1)} %bitcast.131, f32[4096]{0:T(1024)S(1)} %bitcast.130, f32[4096]{0:T(1024)S(1)} %copy-done.8, ...), kind=kLoop, calls=%fused_computation | loop fusion | flops 85983232 | bytes 37855232 | tf_op jit(solution)/shard_map/jit(silu)/mul | solution.py:35
  41.6 1.1 fusion.28
  42.7 8.0 %shard_map.118 = (f32[2,8,64,128]{3,2,1,0:T(8,128)}, f32[2,8,64,128]{3,2,1,0:T(8,128)}) custom-call(f32[512,4096]{1,0:T(8,128)} %get-tuple-element.104.xa_ref.refs_0_, f32[512,4096]{1,0:T(8,128)} %get-tuple-element.105.xb_ref.refs_1_, f32[4,64,512]{2,1,0:T(8,128)} %get-tuple-element.130.ba_ref, f32[4,64,512]{2,1,0:T(8,128)} %get-tuple-element.129.bb_ref, ...), custom_call_target="tpu_custom_call" | custom-call | tf_op jit(solution)/shard_map/pallas_call | solution.py:252
  50.8 1.3 multiply_add_fusion.1
  52.9 1.5 %select_bitcast_fusion.2 = (f32[2,4,1,64,512]{4,3,1,0,2:T(8,128)S(1)}, f32[2,4,1,64,512]{4,3,1,0,2:T(8,128)S(1)}) fusion(f32[2,4,64,512]{3,2,1,0:T(8,128)} %collective-permute-done.1, f32[2,4,64,1024]{3,2,1,0:T(8,128)S(1)} %divide_multiply_fusion.2, s32[]{:T(128)S(6)} %select_n.112, pred[]{:T(512)S(6)} %eq.2), kind=kLoop, calls=%fused_computation.29 | loop fusion | flops 524288 | bytes 4194309 | tf_op jit(solution)/shard_map/stack | solution.py:202
  54.7 1.3 copy.65
  56.0 1.1 copy.66
  57.7 3.7 %collective-permute-start.2 = (f32[16,64,128]{2,1,0:T(8,128)}, f32[16,64,128]{2,1,0:T(8,128)S(1)}, u32[]{:S(2)}, u32[]{:S(2)}) collective-permute-start(f32[16,64,128]{2,1,0:T(8,128)} %bitcast_add_fusion), channel_id=1, source_target_pairs={{0,4},{4,8},{8,12},{1,5},{5,9},{9,13},{2,6},{6,10},{10,14},{3,7},{... | collective-permute-start | bytes 1572872 | tf_op jit(solution)/shard_map/ppermute | solution.py:21
  61.6 8.1 %shard_map.120 = (f32[2,8,64,128]{3,2,1,0:T(8,128)}, f32[2,8,64,128]{3,2,1,0:T(8,128)}) custom-call(f32[512,4096]{1,0:T(8,128)} %get-tuple-element.104.xa_ref.refs_0_, f32[512,4096]{1,0:T(8,128)} %get-tuple-element.105.xb_ref.refs_1_, f32[4,64,512]{2,1,0:T(8,128)} %get-tuple-element.130.ba_ref, f32[4,64,512]{2,1,0:T(8,128)} %get-tuple-element.129.bb_ref, ...), custom_call_target="tpu_custom_call" | custom-call | tf_op jit(solution)/shard_map/pallas_call | solution.py:252
  69.7 8.3 %shard_map.119.refs_9_ = f32[512,4096]{1,0:T(8,128)} custom-call(f32[512,4096]{1,0:T(8,128)} %get-tuple-element.104.xa_ref.refs_0_, f32[512,4096]{1,0:T(8,128)} %get-tuple-element.105.xb_ref.refs_1_, f32[8,128]{1,0:T(8,128)} %broadcast_in_dim.47.flag_ref.refs_2_, f32[4,512,128]{2,1,0:T(8,128)} %bitcast.101, f32[4,128,512]{2,1,0:T(8,128)} %bitcast.112, ...), custom_call_target="tpu_custom_call" | custom-call | tf_op jit(solution)/shard_map/pallas_call | solution.py:309
  79.3 5.3 %collective-permute-start.3 = (f32[16,64,128]{2,1,0:T(8,128)S(1)}, f32[16,64,128]{2,1,0:T(8,128)}, u32[]{:S(2)}, u32[]{:S(2)}) collective-permute-start(f32[16,64,128]{2,1,0:T(8,128)S(1)} %fusion.12), channel_id=1, source_target_pairs={{0,4},{4,8},{8,12},{1,5},{5,9},{9,13},{2,6},{6,10},{10,14},{3,7},{... | collective-permute-start | bytes 1572872 | tf_op jit(solution)/shard_map/ppermute | solution.py:21
  84.6 8.2 %shard_map.121.refs_9_ = f32[512,4096]{1,0:T(8,128)} custom-call(f32[512,4096]{1,0:T(8,128)} %get-tuple-element.104.xa_ref.refs_0_, f32[512,4096]{1,0:T(8,128)} %get-tuple-element.105.xb_ref.refs_1_, f32[8,128]{1,0:T(8,128)} %broadcast_in_dim.47.flag_ref.refs_2_, f32[4,512,128]{2,1,0:T(8,128)} %bitcast.102, ...), custom_call_target="tpu_custom_call", output_to_operand_aliasing={{}: (9, {})} | custom-call | tf_op jit(solution)/shard_map/pallas_call | solution.py:309
  92.8 2.5 %collective-permute-done.3 = f32[16,64,128]{2,1,0:T(8,128)} collective-permute-done((f32[16,64,128]{2,1,0:T(8,128)S(1)}, f32[16,64,128]{2,1,0:T(8,128)}, u32[]{:S(2)}, u32[]{:S(2)}) %collective-permute-start.3) | collective-permute-done | bytes 524320 | tf_op jit(solution)/shard_map/ppermute | solution.py:21
  95.3 1.2 fusion.11
  96.6 5.3 %collective-permute-start.4 = (f32[16,64,128]{2,1,0:T(8,128)S(1)}, f32[16,64,128]{2,1,0:T(8,128)}, u32[]{:S(2)}, u32[]{:S(2)}) collective-permute-start(f32[16,64,128]{2,1,0:T(8,128)S(1)} %fusion.10), channel_id=1, source_target_pairs={{0,4},{4,8},{8,12},{1,5},{5,9},{9,13},{2,6},{6,10},{10,14},{3,7},{... | collective-permute-start | bytes 1572872 | tf_op jit(solution)/shard_map/ppermute | solution.py:21
  101.9 8.2 %shard_map.122.refs_9_ = f32[512,4096]{1,0:T(8,128)} custom-call(f32[512,4096]{1,0:T(8,128)} %get-tuple-element.104.xa_ref.refs_0_, f32[512,4096]{1,0:T(8,128)} %get-tuple-element.105.xb_ref.refs_1_, f32[8,128]{1,0:T(8,128)} %broadcast_in_dim.47.flag_ref.refs_2_, f32[4,512,128]{2,1,0:T(8,128)} %bitcast.103, ...), custom_call_target="tpu_custom_call", output_to_operand_aliasing={{}: (9, {})} | custom-call | tf_op jit(solution)/shard_map/pallas_call | solution.py:309
  110.2 1.7 %collective-permute-done.4 = f32[16,64,128]{2,1,0:T(8,128)} collective-permute-done((f32[16,64,128]{2,1,0:T(8,128)S(1)}, f32[16,64,128]{2,1,0:T(8,128)}, u32[]{:S(2)}, u32[]{:S(2)}) %collective-permute-start.4) | collective-permute-done | bytes 524320 | tf_op jit(solution)/shard_map/ppermute | solution.py:21
  111.9 1.2 fusion.9
  113.1 4.5 %collective-permute-start.5 = (f32[16,64,128]{2,1,0:T(8,128)S(1)}, f32[16,64,128]{2,1,0:T(8,128)S(1)}, u32[]{:S(2)}, u32[]{:S(2)}) collective-permute-start(f32[16,64,128]{2,1,0:T(8,128)S(1)} %fusion.8), channel_id=1, source_target_pairs={{0,4},{4,8},{8,12},{1,5},{5,9},{9,13},{2,6},{6,10},{10,14},{3,7},{... | collective-permute-start | bytes 1572872 | tf_op jit(solution)/shard_map/ppermute | solution.py:21
  117.8 8.3 %shard_map.123.y_ref = f32[512,4096]{1,0:T(8,128)} custom-call(f32[512,4096]{1,0:T(8,128)} %get-tuple-element.104.xa_ref.refs_0_, f32[512,4096]{1,0:T(8,128)} %get-tuple-element.105.xb_ref.refs_1_, f32[8,128]{1,0:T(8,128)} %broadcast_in_dim.47.flag_ref.refs_2_, f32[4,512,128]{2,1,0:T(8,128)} %bitcast.104, ...), custom_call_target="tpu_custom_call", output_to_operand_aliasing={{}: (9, {})} | custom-call | tf_op jit(solution)/shard_map/pallas_call | solution.py:309
  126.1 1.3 collective-permute-done.5
  128.4 1.4 copy.71
  129.8 0.9 collective-permute-done.6
  130.7 1.6 %select_bitcast_fusion.1 = (f32[4,8,1,64,128]{4,3,1,0,2:T(8,128)S(1)}, f32[4,8,1,64,128]{4,3,1,0,2:T(8,128)S(1)}) fusion(f32[4,8,64,128]{3,2,1,0:T(8,128)} %collective-permute-done.6, pred[]{:T(512)S(6)} %eq.2, f32[4,8,64,128]{3,2,1,0:T(8,128)S(1)} %bitcast.107, f32[2,8,64,128]{3,2,1,0:T(8,128)S(1)} %copy-done.4, f32[2,8,64,128]{3,2,1,0:T(8,128)S(1)} %copy-done.3, ...), kind=kLoop, calls=%fused_computation.26 | loop fusion | flops 1572864 | bytes 5259265 | tf_op jit(solution)/shard_map/stack | solution.py:368
  132.5 1.5 %copy.72 = f32[4,8,2,64,128]{4,3,2,1,0:T(8,128)} copy(f32[4,8,2,64,128]{4,3,1,0,2:T(8,128)S(1)} %pad_maximum_fusion.1) | data formatting | bytes 4194304 | tf_op jit(solution)/shard_map/stack | solution.py:368
  134.0 12.4 %shard_map.124 = bf16[512,4096]{1,0:T(8,128)(2,1)} custom-call(f32[512,4096]{1,0:T(8,128)} %shard_map.123.y_ref, f32[4,512,128]{2,1,0:T(8,128)} %bitcast.105, f32[4,512,16]{2,1,0:T(8,128)} %bitcast.120, f32[4,8,128,128]{3,2,1,0:T(8,128)} %bitcast.116, bf16[512,4096]{1,0:T(8,128)(2,1)} %z_ref.1, f32[1,4096]{1,0:T(1,128)} %bitcast.135), custom_call_target="tpu_custom_call" | custom-call | tf_op jit(solution)/shard_map/pallas_call | solution.py:371
  (96 shorter events, 12.9 us)
Async XLA Ops:
  0.0 14.1 %copy-start = (f32[2,4,128]{2,1,0:T(4,128)S(1)}, f32[2,4,128]{2,1,0:T(4,128)}, u32[]{:S(2)}) copy-start(f32[2,4,128]{2,1,0:T(4,128)} %param.19) | copy-start | bytes 12292
  0.0 10.7 %copy-start.7 = (f32[4,4096]{1,0:T(4,128)S(1)}, f32[4,4096]{1,0:T(4,128)}, u32[]{:S(2)}) copy-start(f32[4,4096]{1,0:T(4,128)} %param.16) | copy-start | bytes 196612
  2.1 14.7 %collective-permute-start = (bf16[3,4608]{1,0:T(4,128)(2,1)S(1)}, bf16[3,4608]{1,0:T(4,128)(2,1)S(1)}, u32[]{:S(2)}, u32[]{:S(2)}) collective-permute-start(bf16[3,4608]{1,0:T(4,128)(2,1)S(1)} %pad_maximum_fusion.5), channel_id=1, source_target_pairs={{0,4},{4,8},{8,12},{1,5},{5,9},{9,13},{2,6},{6,10},{10,14},{3,7},{... | collective-permute-start | bytes 82952 | tf_op jit(solution)/shard_map/ppermute | solution.py:21
  7.7 6.4 %copy-start.9 = (f32[4,2,4,128]{3,2,1,0:T(4,128)S(1)}, f32[4,2,4,128]{3,2,1,0:T(4,128)}, u32[]{:S(2)}) copy-start(f32[4,2,4,128]{3,2,1,0:T(4,128)} %param.18) | copy-start | bytes 49156
  14.2 1.8 %copy-start.10 = (f32[64]{0:T(128)S(1)}, f32[64]{0:T(128)}, u32[]{:S(2)}) copy-start(f32[64]{0:T(128)} %param.22) | copy-start | bytes 772
  14.2 9.4 %copy-start.8 = (f32[4096]{0:T(1024)S(1)}, f32[4096]{0:T(1024)}, u32[]{:S(2)}) copy-start(f32[4096]{0:T(1024)} %param.17) | copy-start | bytes 49156
  14.6 26.9 %copy-start.2 = (f32[4,16,512]{2,1,0:T(8,128)}, f32[4,16,512]{2,1,0:T(8,128)S(1)}, u32[]{:S(2)}) copy-start(f32[4,16,512]{2,1,0:T(8,128)S(1)} %reshape.105.cumr_ref.refs_5_) | copy-start | bytes 393220
  17.0 6.6 %slice-start = ((bf16[1024,4096]{1,0:T(8,128)(2,1)}), bf16[512,4096]{1,0:T(8,128)(2,1)S(1)}, s32[]{:S(2)}) async-start(bf16[1024,4096]{1,0:T(8,128)(2,1)} %param.12), calls=%async_computation | async-start | bytes 8388608 | tf_op jit(solution)/shard_map/slice | solution.py:194
  23.6 29.3 %collective-permute-start.1 = (f32[2,4,64,512]{3,2,1,0:T(8,128)}, f32[2,4,64,512]{3,2,1,0:T(8,128)}, u32[]{:S(2)}, u32[]{:S(2)}) collective-permute-start(f32[2,4,64,512]{3,2,1,0:T(8,128)} %constant_dynamic-slice_fusion.4), channel_id=1, source_target_pairs={{0,1},{1,0},{2,3},{3,2},{4,5},{5,4},{6,7},{7,6},{8,9},{9,8},{10,11... | collective-permute-start | bytes 3145736 | tf_op jit(solution)/shard_map/ppermute | solution.py:25
  57.7 20.4 %collective-permute-start.2 = (f32[16,64,128]{2,1,0:T(8,128)}, f32[16,64,128]{2,1,0:T(8,128)S(1)}, u32[]{:S(2)}, u32[]{:S(2)}) collective-permute-start(f32[16,64,128]{2,1,0:T(8,128)} %bitcast_add_fusion), channel_id=1, source_target_pairs={{0,4},{4,8},{8,12},{1,5},{5,9},{9,13},{2,6},{6,10},{10,14},{3,7},{... | collective-permute-start | bytes 1572872 | tf_op jit(solution)/shard_map/ppermute | solution.py:21
  69.7 8.3 %copy-start.4 = (f32[2,8,64,128]{3,2,1,0:T(8,128)S(1)}, f32[2,8,64,128]{3,2,1,0:T(8,128)}, u32[]{:S(2)}) copy-start(f32[2,8,64,128]{3,2,1,0:T(8,128)} %get-tuple-element.116) | copy-start | bytes 1572868
  69.7 8.3 %copy-start.5 = (f32[2,8,64,128]{3,2,1,0:T(8,128)S(1)}, f32[2,8,64,128]{3,2,1,0:T(8,128)}, u32[]{:S(2)}) copy-start(f32[2,8,64,128]{3,2,1,0:T(8,128)} %get-tuple-element.76) | copy-start | bytes 1572868
  78.1 0.8 copy-start.6
  79.3 16.0 %collective-permute-start.3 = (f32[16,64,128]{2,1,0:T(8,128)S(1)}, f32[16,64,128]{2,1,0:T(8,128)}, u32[]{:S(2)}, u32[]{:S(2)}) collective-permute-start(f32[16,64,128]{2,1,0:T(8,128)S(1)} %fusion.12), channel_id=1, source_target_pairs={{0,4},{4,8},{8,12},{1,5},{5,9},{9,13},{2,6},{6,10},{10,14},{3,7},{... | collective-permute-start | bytes 1572872 | tf_op jit(solution)/shard_map/ppermute | solution.py:21
  96.6 15.2 %collective-permute-start.4 = (f32[16,64,128]{2,1,0:T(8,128)S(1)}, f32[16,64,128]{2,1,0:T(8,128)}, u32[]{:S(2)}, u32[]{:S(2)}) collective-permute-start(f32[16,64,128]{2,1,0:T(8,128)S(1)} %fusion.10), channel_id=1, source_target_pairs={{0,4},{4,8},{8,12},{1,5},{5,9},{9,13},{2,6},{6,10},{10,14},{3,7},{... | collective-permute-start | bytes 1572872 | tf_op jit(solution)/shard_map/ppermute | solution.py:21
  113.1 14.3 %collective-permute-start.5 = (f32[16,64,128]{2,1,0:T(8,128)S(1)}, f32[16,64,128]{2,1,0:T(8,128)S(1)}, u32[]{:S(2)}, u32[]{:S(2)}) collective-permute-start(f32[16,64,128]{2,1,0:T(8,128)S(1)} %fusion.8), channel_id=1, source_target_pairs={{0,4},{4,8},{8,12},{1,5},{5,9},{9,13},{2,6},{6,10},{10,14},{3,7},{... | collective-permute-start | bytes 1572872 | tf_op jit(solution)/shard_map/ppermute | solution.py:21
  117.8 9.7 %copy-start.3 = (f32[2,8,64,128]{3,2,1,0:T(8,128)S(1)}, f32[2,8,64,128]{3,2,1,0:T(8,128)}, u32[]{:S(2)}) copy-start(f32[2,8,64,128]{3,2,1,0:T(8,128)} %get-tuple-element.61) | copy-start | bytes 1572868
  127.8 2.9 %collective-permute-start.6 = (f32[4,8,64,128]{3,2,1,0:T(8,128)S(1)}, f32[4,8,64,128]{3,2,1,0:T(8,128)}, u32[]{:S(2)}, u32[]{:S(2)}) collective-permute-start(f32[4,8,64,128]{3,2,1,0:T(8,128)S(1)} %fusion.5), channel_id=1, source_target_pairs={{0,1},{1,0},{2,3},{3,2},{4,5},{5,4},{6,7},{7,6},{8,9},{9,8},{10,11... | collective-permute-start | bytes 3145736 | tf_op jit(solution)/shard_map/ppermute | solution.py:25
  134.0 12.4 %copy-start.1 = (f32[2,4,128]{2,1,0:T(4,128)S(1)}, f32[2,4,128]{2,1,0:T(4,128)}, u32[]{:S(2)}) copy-start(f32[2,4,128]{2,1,0:T(4,128)} %param.19) | copy-start | bytes 12292

commit v16 on v14

--- a/solution.py
+++ b/solution.py
@@ -372,7 +372,7 @@
     high = jnp.where(sub_index == 0, got, keep)
     incoming = jnp.stack([low, high], 2).reshape(set_groups, pairs, state, 128)
 
-    out_len = min(256, own)
+    out_len = min(512, own)
     return pl.pallas_call(
         out_kernel,
         grid=(set_groups, own // out_len),

time: 144 us -> 143 us (level)
  no operation moved by 1% of the time
where the time goes in v16:
time: 143 us; the launch traced here: 142 us
  Pallas kernels  58 us (41%)
  other arithmetic  36.6 us (26%)
  starting transfers between devices  23 us (16%)
  local copies, waits for them, and re-layouts  15.7 us (11%)
  waiting for transfers between devices  7.91 us (6%)
    pallas_call x4, Pallas kernels, scan_group(): pl.pallas_call(kernel, grid=(1, blocks), in_specs=in_specs, out_specs=til...  30.9 us
    ppermute x5, starting transfers between devices, passed_along(): return lax.ppermute(x, axis, pairs)  22.9 us
    pallas_call x2, Pallas kernels, end_states(): pl.pallas_call(end_pair_kernel, grid=(count,), in_specs=[x_spec, x_spec,...  16.1 us
    mul x1, other arithmetic, conv_rows(): return jax.nn.silu(total)  12.4 us
    pallas_call x1, Pallas kernels, per_device(): pl.pallas_call(out_kernel, grid=(set_groups, own // out_len), in_specs=[p...  11 us
    ppermute x5, waiting for transfers between devices, passed_along(): return lax.ppermute(x, axis, pairs)  6.93 us
    mul x1, other arithmetic, conv_cols(): return jax.nn.silu(total)  5.47 us
    concatenate x1, other arithmetic, per_device(): x_pad = jnp.concatenate([x_rim, x_raw], 0)  4.98 us
  transfers between devices with their start and end apart: 7, of which 4 were waited for; matrix products, arithmetic and copies ran while one was open for 23% of the time, Pallas kernels for 33%

profile of v16, /device:TPU:0, one launch (start us, length us, event | category | flops | bytes accessed | tf_op | source)
XLA Modules:
  0.0 142.2 jit_solution(10808586022983744505)
XLA Ops:
  0.0 1.0 slice.124
  2.1 4.9 %collective-permute-start = (bf16[3,4608]{1,0:T(4,128)(2,1)S(1)}, bf16[3,4608]{1,0:T(4,128)(2,1)S(1)}, u32[]{:S(2)}, u32[]{:S(2)}) collective-permute-start(bf16[3,4608]{1,0:T(4,128)(2,1)S(1)} %pad_maximum_fusion.4), channel_id=1, source_target_pairs={{0,4},{4,8},{8,12},{1,5},{5,9},{9,13},{2,6},{6,10},{10,14},{3,7},{... | collective-permute-start | bytes 82952 | tf_op jit(solution)/shard_map/ppermute | solution.py:21
  7.7 1.2 broadcast_multiply_fusion
  14.7 1.3 copy.66
  16.9 5.5 %divide_multiply_fusion.2 = f32[2,4,64,1024]{3,2,1,0:T(8,128)S(1)} fusion(bf16[2,4,64,1024]{3,2,1,0:T(8,128)(2,1)} %param.13, bf16[2,4,64,3]{3,2,1,0:T(8,128)(2,1)S(1)} %bitcast.131, f32[2,4,64]{2,1,0:T(4,128)S(1)} %get-tuple-element.136, f32[2,4,64]{2,1,0:T(4,128)S(1)} %get-tuple-element.134, f32[2,4,64]{2,1,0:T(4,128)S(1)} %get-tuple-element.135, ...), kind=kLoop, calls=%fused_computation.11 | loop fusion | flops 13107200 | bytes 3159040 | tf_op jit(solution)/shard_map/jit(silu)/mul | solution.py:45
  22.4 1.1 constant_dynamic-slice_fusion.7
  23.5 5.0 %fusion = (bf16[515,4096]{1,0:T(8,128)(2,1)S(1)}, bf16[515,4096]{1,0:T(8,128)(2,1)S(1)}) fusion(s32[]{:T(128)S(6)} %select_n.146, bf16[1024,4096]{1,0:T(8,128)(2,1)} %param.12, bf16[3,4096]{1,0:T(4,128)(2,1)S(1)} %slice.156, s32[]{:T(128)S(6)} %select_n.145), kind=kLoop, calls=%fused_computation.6 | loop fusion | flops 16875520 | bytes 16850952 | tf_op jit(solution)/shard_map/concatenate | solution.py:193
  28.5 12.4 %divide_multiply_fusion = (f32[512,4096]{1,0:T(8,128)}, f32[512,4096]{1,0:T(8,128)}) fusion(bf16[515,4096]{1,0:T(8,128)(2,1)S(1)} %get-tuple-element.107, f32[4096]{0:T(1024)S(1)} %bitcast.136, f32[4096]{0:T(1024)S(1)} %bitcast.137, f32[4096]{0:T(1024)S(1)} %bitcast.135, f32[4096]{0:T(1024)S(1)} %bitcast.134, f32[4096]{0:T(1024)S(1)} %copy-done.7, ...), kind=kLoop, calls=%fused_computation.2 | loop fusion | flops 67108864 | bytes 50413568 | tf_op jit(solution)/shard_map/jit(silu)/mul | solution.py:35
  41.0 1.1 dynamic-slice_bitcast_fusion
  42.1 8.0 %shard_map.118 = (f32[2,8,64,128]{3,2,1,0:T(8,128)}, f32[2,8,64,128]{3,2,1,0:T(8,128)}) custom-call(f32[512,4096]{1,0:T(8,128)} %get-tuple-element.90.xa_ref.xc_ref.refs_0_, f32[512,4096]{1,0:T(8,128)} %get-tuple-element.64.xb_ref, f32[4,64,512]{2,1,0:T(8,128)} %get-tuple-element.120.ba_ref, f32[4,64,512]{2,1,0:T(8,128)} %get-tuple-element.119.bb_ref, ...), custom_call_target="tpu_custom_call" | custom-call | tf_op jit(solution)/shard_map/pallas_call | solution.py:257
  50.1 1.3 broadcast_select_fusion.1
  52.3 1.5 %select_bitcast_fusion.2 = (f32[2,4,1,64,512]{4,3,2,1,0:T(8,128)S(1)}, f32[2,4,1,64,512]{4,3,2,1,0:T(8,128)S(1)}) fusion(f32[2,4,64,512]{3,2,1,0:T(8,128)} %collective-permute-done.1, f32[2,4,64,1024]{3,2,1,0:T(8,128)S(1)} %divide_multiply_fusion.2, s32[]{:T(128)S(6)} %select_n.148, pred[]{:T(512)S(6)} %eq.2), kind=kLoop, calls=%fused_computation.29 | loop fusion | flops 524288 | bytes 4194309 | tf_op jit(solution)/shard_map/stack | solution.py:207
  53.8 1.2 pad_maximum_fusion.1
  55.0 1.4 copy.63
  56.3 3.7 %collective-permute-start.2 = (f32[16,64,128]{2,1,0:T(8,128)}, f32[16,64,128]{2,1,0:T(8,128)S(1)}, u32[]{:S(2)}, u32[]{:S(2)}) collective-permute-start(f32[16,64,128]{2,1,0:T(8,128)} %bitcast_add_fusion), channel_id=1, source_target_pairs={{0,4},{4,8},{8,12},{1,5},{5,9},{9,13},{2,6},{6,10},{10,14},{3,7},{... | collective-permute-start | bytes 1572872 | tf_op jit(solution)/shard_map/ppermute | solution.py:21
  60.3 8.1 %shard_map.120 = (f32[2,8,64,128]{3,2,1,0:T(8,128)}, f32[2,8,64,128]{3,2,1,0:T(8,128)}) custom-call(f32[512,4096]{1,0:T(8,128)} %get-tuple-element.90.xa_ref.xc_ref.refs_0_, f32[512,4096]{1,0:T(8,128)} %get-tuple-element.64.xb_ref, f32[4,64,512]{2,1,0:T(8,128)} %get-tuple-element.120.ba_ref, f32[4,64,512]{2,1,0:T(8,128)} %get-tuple-element.119.bb_ref, ...), custom_call_target="tpu_custom_call" | custom-call | tf_op jit(solution)/shard_map/pallas_call | solution.py:257
  68.4 7.8 %shard_map.119.refs_7_ = f32[512,4096]{1,0:T(8,128)} custom-call(f32[512,4096]{1,0:T(8,128)} %get-tuple-element.90.xa_ref.xc_ref.refs_0_, f32[4,512,128]{2,1,0:T(8,128)} %bitcast.105, f32[4,128,512]{2,1,0:T(8,128)} %bitcast.116, f32[4,16,512]{2,1,0:T(8,128)} %copy-done.2, f32[4,512,16]{2,1,0:T(8,128)} %bitcast.112, f32[4,16,512]{2,1,0:T(8,128)} %bitcast.126, ...), custom_call_target="tpu_custom_call" | custom-call | tf_op jit(solution)/shard_map/pallas_call | solution.py:314
  77.4 4.3 %collective-permute-start.3 = (f32[16,64,128]{2,1,0:T(8,128)S(1)}, f32[16,64,128]{2,1,0:T(8,128)}, u32[]{:S(2)}, u32[]{:S(2)}) collective-permute-start(f32[16,64,128]{2,1,0:T(8,128)S(1)} %fusion.12), channel_id=1, source_target_pairs={{0,4},{4,8},{8,12},{1,5},{5,9},{9,13},{2,6},{6,10},{10,14},{3,7},{... | collective-permute-start | bytes 1572872 | tf_op jit(solution)/shard_map/ppermute | solution.py:21
  81.7 7.7 %shard_map.121.refs_7_ = f32[512,4096]{1,0:T(8,128)} custom-call(f32[512,4096]{1,0:T(8,128)} %get-tuple-element.90.xa_ref.xc_ref.refs_0_, f32[4,512,128]{2,1,0:T(8,128)} %bitcast.106, f32[4,128,512]{2,1,0:T(8,128)} %bitcast.117, f32[4,16,512]{2,1,0:T(8,128)} %copy-done.2, f32[4,512,16]{2,1,0:T(8,128)} %bitcast.113, ...), custom_call_target="tpu_custom_call", output_to_operand_aliasing={{}: (7, {})} | custom-call | tf_op jit(solution)/shard_map/pallas_call | solution.py:314
  89.4 3.1 %collective-permute-done.3 = f32[16,64,128]{2,1,0:T(8,128)} collective-permute-done((f32[16,64,128]{2,1,0:T(8,128)S(1)}, f32[16,64,128]{2,1,0:T(8,128)}, u32[]{:S(2)}, u32[]{:S(2)}) %collective-permute-start.3) | collective-permute-done | bytes 524320 | tf_op jit(solution)/shard_map/ppermute | solution.py:21
  92.5 1.2 fusion.11
  93.7 5.3 %collective-permute-start.4 = (f32[16,64,128]{2,1,0:T(8,128)S(1)}, f32[16,64,128]{2,1,0:T(8,128)}, u32[]{:S(2)}, u32[]{:S(2)}) collective-permute-start(f32[16,64,128]{2,1,0:T(8,128)S(1)} %fusion.10), channel_id=1, source_target_pairs={{0,4},{4,8},{8,12},{1,5},{5,9},{9,13},{2,6},{6,10},{10,14},{3,7},{... | collective-permute-start | bytes 1572872 | tf_op jit(solution)/shard_map/ppermute | solution.py:21
  99.0 7.7 %shard_map.122.refs_7_ = f32[512,4096]{1,0:T(8,128)} custom-call(f32[512,4096]{1,0:T(8,128)} %get-tuple-element.90.xa_ref.xc_ref.refs_0_, f32[4,512,128]{2,1,0:T(8,128)} %bitcast.107, f32[4,128,512]{2,1,0:T(8,128)} %bitcast.118, f32[4,16,512]{2,1,0:T(8,128)} %copy-done.2, f32[4,512,16]{2,1,0:T(8,128)} %bitcast.114, ...), custom_call_target="tpu_custom_call", output_to_operand_aliasing={{}: (7, {})} | custom-call | tf_op jit(solution)/shard_map/pallas_call | solution.py:314
  106.7 2.2 %collective-permute-done.4 = f32[16,64,128]{2,1,0:T(8,128)} collective-permute-done((f32[16,64,128]{2,1,0:T(8,128)S(1)}, f32[16,64,128]{2,1,0:T(8,128)}, u32[]{:S(2)}, u32[]{:S(2)}) %collective-permute-start.4) | collective-permute-done | bytes 524320 | tf_op jit(solution)/shard_map/ppermute | solution.py:21
  109.0 1.2 fusion.9
  110.2 4.7 %collective-permute-start.5 = (f32[16,64,128]{2,1,0:T(8,128)S(1)}, f32[16,64,128]{2,1,0:T(8,128)S(1)}, u32[]{:S(2)}, u32[]{:S(2)}) collective-permute-start(f32[16,64,128]{2,1,0:T(8,128)S(1)} %fusion.8), channel_id=1, source_target_pairs={{0,4},{4,8},{8,12},{1,5},{5,9},{9,13},{2,6},{6,10},{10,14},{3,7},{... | collective-permute-start | bytes 1572872 | tf_op jit(solution)/shard_map/ppermute | solution.py:21
  115.2 7.7 %shard_map.123.y_ref = f32[512,4096]{1,0:T(8,128)} custom-call(f32[512,4096]{1,0:T(8,128)} %get-tuple-element.90.xa_ref.xc_ref.refs_0_, f32[4,512,128]{2,1,0:T(8,128)} %bitcast.108, f32[4,128,512]{2,1,0:T(8,128)} %bitcast.119, f32[4,16,512]{2,1,0:T(8,128)} %copy-done.2, f32[4,512,16]{2,1,0:T(8,128)} %bitcast.115, ...), custom_call_target="tpu_custom_call", output_to_operand_aliasing={{}: (7, {})} | custom-call | tf_op jit(solution)/shard_map/pallas_call | solution.py:314
  122.9 1.6 %collective-permute-done.5 = f32[16,64,128]{2,1,0:T(8,128)S(1)} collective-permute-done((f32[16,64,128]{2,1,0:T(8,128)S(1)}, f32[16,64,128]{2,1,0:T(8,128)S(1)}, u32[]{:S(2)}, u32[]{:S(2)}) %collective-permute-start.5) | collective-permute-done | bytes 524320 | tf_op jit(solution)/shard_map/ppermute | solution.py:21
  125.5 1.3 copy.68
  127.8 1.6 %select_bitcast_fusion.1 = (f32[4,8,1,64,128]{4,3,1,0,2:T(8,128)S(1)}, f32[4,8,1,64,128]{4,3,1,0,2:T(8,128)S(1)}) fusion(f32[4,8,64,128]{3,2,1,0:T(8,128)} %collective-permute-done.6, pred[]{:T(512)S(6)} %eq.2, f32[4,8,64,128]{3,2,1,0:T(8,128)S(1)} %bitcast.111, f32[2,8,64,128]{3,2,1,0:T(8,128)S(1)} %copy-done.3, ...), kind=kLoop, calls=%fused_computation.26 | loop fusion | flops 1572864 | bytes 5259265 | tf_op jit(solution)/shard_map/stack | solution.py:373
  129.7 1.5 %copy.69 = f32[4,8,2,64,128]{4,3,2,1,0:T(8,128)} copy(f32[4,8,2,64,128]{4,3,1,0,2:T(8,128)S(1)} %pad_maximum_fusion) | data formatting | bytes 4194304 | tf_op jit(solution)/shard_map/stack | solution.py:373
  131.2 11.0 %shard_map.124 = bf16[512,4096]{1,0:T(8,128)(2,1)} custom-call(f32[512,4096]{1,0:T(8,128)} %shard_map.123.y_ref, f32[4,512,128]{2,1,0:T(8,128)} %bitcast.109, f32[4,512,16]{2,1,0:T(8,128)} %bitcast.124, f32[4,8,128,128]{3,2,1,0:T(8,128)} %bitcast.120, bf16[512,4096]{1,0:T(8,128)(2,1)} %z_ref.1, f32[1,4096]{1,0:T(1,128)} %bitcast.139), custom_call_target="tpu_custom_call" | custom-call | tf_op jit(solution)/shard_map/pallas_call | solution.py:376
  (90 shorter events, 13.2 us)
Async XLA Ops:
  0.0 14.1 %copy-start = (f32[2,4,128]{2,1,0:T(4,128)S(1)}, f32[2,4,128]{2,1,0:T(4,128)}, u32[]{:S(2)}) copy-start(f32[2,4,128]{2,1,0:T(4,128)} %param.19) | copy-start | bytes 12292
  0.0 10.7 %copy-start.6 = (f32[4,4096]{1,0:T(4,128)S(1)}, f32[4,4096]{1,0:T(4,128)}, u32[]{:S(2)}) copy-start(f32[4,4096]{1,0:T(4,128)} %param.16) | copy-start | bytes 196612
  2.1 14.7 %collective-permute-start = (bf16[3,4608]{1,0:T(4,128)(2,1)S(1)}, bf16[3,4608]{1,0:T(4,128)(2,1)S(1)}, u32[]{:S(2)}, u32[]{:S(2)}) collective-permute-start(bf16[3,4608]{1,0:T(4,128)(2,1)S(1)} %pad_maximum_fusion.4), channel_id=1, source_target_pairs={{0,4},{4,8},{8,12},{1,5},{5,9},{9,13},{2,6},{6,10},{10,14},{3,7},{... | collective-permute-start | bytes 82952 | tf_op jit(solution)/shard_map/ppermute | solution.py:21
  7.7 6.4 %copy-start.8 = (f32[4,2,4,128]{3,2,1,0:T(4,128)S(1)}, f32[4,2,4,128]{3,2,1,0:T(4,128)}, u32[]{:S(2)}) copy-start(f32[4,2,4,128]{3,2,1,0:T(4,128)} %param.18) | copy-start | bytes 49156
  9.6 6.4 %copy-start.9 = (f32[64]{0:T(128)S(1)}, f32[64]{0:T(128)}, u32[]{:S(2)}) copy-start(f32[64]{0:T(128)} %param.22) | copy-start | bytes 772
  14.6 13.9 %copy-start.2 = (f32[4,16,512]{2,1,0:T(8,128)}, f32[4,16,512]{2,1,0:T(8,128)S(1)}, u32[]{:S(2)}) copy-start(f32[4,16,512]{2,1,0:T(8,128)S(1)} %reshape.107.cumr_ref.refs_3_) | copy-start | bytes 393220
  23.5 28.8 %collective-permute-start.1 = (f32[2,4,64,512]{3,2,1,0:T(8,128)}, f32[2,4,64,512]{3,2,1,0:T(8,128)}, u32[]{:S(2)}, u32[]{:S(2)}) collective-permute-start(f32[2,4,64,512]{3,2,1,0:T(8,128)} %constant_dynamic-slice_fusion.7), channel_id=1, source_target_pairs={{0,1},{1,0},{2,3},{3,2},{4,5},{5,4},{6,7},{7,6},{8,9},{9,8},{10,11... | collective-permute-start | bytes 3145736 | tf_op jit(solution)/shard_map/ppermute | solution.py:25
  23.5 5.0 %copy-start.7 = (f32[4096]{0:T(1024)S(1)}, f32[4096]{0:T(1024)}, u32[]{:S(2)}) copy-start(f32[4096]{0:T(1024)} %param.17) | copy-start | bytes 49156
  56.3 20.7 %collective-permute-start.2 = (f32[16,64,128]{2,1,0:T(8,128)}, f32[16,64,128]{2,1,0:T(8,128)S(1)}, u32[]{:S(2)}, u32[]{:S(2)}) collective-permute-start(f32[16,64,128]{2,1,0:T(8,128)} %bitcast_add_fusion), channel_id=1, source_target_pairs={{0,4},{4,8},{8,12},{1,5},{5,9},{9,13},{2,6},{6,10},{10,14},{3,7},{... | collective-permute-start | bytes 1572872 | tf_op jit(solution)/shard_map/ppermute | solution.py:21
  68.3 7.8 %copy-start.4 = (f32[2,8,64,128]{3,2,1,0:T(8,128)S(1)}, f32[2,8,64,128]{3,2,1,0:T(8,128)}, u32[]{:S(2)}) copy-start(f32[2,8,64,128]{3,2,1,0:T(8,128)} %get-tuple-element.65) | copy-start | bytes 1572868
  68.4 7.8 %copy-start.5 = (f32[2,8,64,128]{3,2,1,0:T(8,128)S(1)}, f32[2,8,64,128]{3,2,1,0:T(8,128)}, u32[]{:S(2)}) copy-start(f32[2,8,64,128]{3,2,1,0:T(8,128)} %get-tuple-element.66) | copy-start | bytes 1572868
  77.4 15.0 %collective-permute-start.3 = (f32[16,64,128]{2,1,0:T(8,128)S(1)}, f32[16,64,128]{2,1,0:T(8,128)}, u32[]{:S(2)}, u32[]{:S(2)}) collective-permute-start(f32[16,64,128]{2,1,0:T(8,128)S(1)} %fusion.12), channel_id=1, source_target_pairs={{0,4},{4,8},{8,12},{1,5},{5,9},{9,13},{2,6},{6,10},{10,14},{3,7},{... | collective-permute-start | bytes 1572872 | tf_op jit(solution)/shard_map/ppermute | solution.py:21
  93.7 15.2 %collective-permute-start.4 = (f32[16,64,128]{2,1,0:T(8,128)S(1)}, f32[16,64,128]{2,1,0:T(8,128)}, u32[]{:S(2)}, u32[]{:S(2)}) collective-permute-start(f32[16,64,128]{2,1,0:T(8,128)S(1)} %fusion.10), channel_id=1, source_target_pairs={{0,4},{4,8},{8,12},{1,5},{5,9},{9,13},{2,6},{6,10},{10,14},{3,7},{... | collective-permute-start | bytes 1572872 | tf_op jit(solution)/shard_map/ppermute | solution.py:21
  110.2 14.3 %collective-permute-start.5 = (f32[16,64,128]{2,1,0:T(8,128)S(1)}, f32[16,64,128]{2,1,0:T(8,128)S(1)}, u32[]{:S(2)}, u32[]{:S(2)}) collective-permute-start(f32[16,64,128]{2,1,0:T(8,128)S(1)} %fusion.8), channel_id=1, source_target_pairs={{0,4},{4,8},{8,12},{1,5},{5,9},{9,13},{2,6},{6,10},{10,14},{3,7},{... | collective-permute-start | bytes 1572872 | tf_op jit(solution)/shard_map/ppermute | solution.py:21
  115.2 9.5 %copy-start.3 = (f32[2,8,64,128]{3,2,1,0:T(8,128)S(1)}, f32[2,8,64,128]{3,2,1,0:T(8,128)}, u32[]{:S(2)}) copy-start(f32[2,8,64,128]{3,2,1,0:T(8,128)} %get-tuple-element.100) | copy-start | bytes 1572868
  124.9 2.9 %collective-permute-start.6 = (f32[4,8,64,128]{3,2,1,0:T(8,128)S(1)}, f32[4,8,64,128]{3,2,1,0:T(8,128)}, u32[]{:S(2)}, u32[]{:S(2)}) collective-permute-start(f32[4,8,64,128]{3,2,1,0:T(8,128)S(1)} %fusion.5), channel_id=1, source_target_pairs={{0,1},{1,0},{2,3},{3,2},{4,5},{5,4},{6,7},{7,6},{8,9},{9,8},{10,11... | collective-permute-start | bytes 3145736 | tf_op jit(solution)/shard_map/ppermute | solution.py:25
  131.2 11.0 %copy-start.1 = (f32[2,4,128]{2,1,0:T(4,128)S(1)}, f32[2,4,128]{2,1,0:T(4,128)}, u32[]{:S(2)}) copy-start(f32[2,4,128]{2,1,0:T(4,128)} %param.19) | copy-start | bytes 12292

commit v17 on v16

--- a/solution.py
+++ b/solution.py
@@ -9,6 +9,7 @@
 HEAD_DIM = 64
 GROUPS = 8
 CONV_K = 4
+SUB_LEN = 128
 
 
 HIGHEST = lax.Precision.HIGHEST
@@ -72,47 +73,48 @@
 
 def scan_kernel(xc_ref, ct_ref, b_ref, cumr_ref, cumc_ref, stp_ref, dsk_ref, y_ref, e_ref):
     chunk = pl.program_id(1)
-    block_len = xc_ref.shape[0]
     pairs = e_ref.shape[0]
-    heads = 2 * pairs
+    block_len = SUB_LEN
 
     @pl.when(chunk == 0)
     def _():
         e_ref[...] = jnp.zeros_like(e_ref)
 
-    ct = split(ct_ref[0])
-    bm = b_ref[0]
-    scores = dot3(ct, split(bm))
     rows = lax.broadcasted_iota(jnp.int32, (block_len, block_len), 0)
     cols = lax.broadcasted_iota(jnp.int32, (block_len, block_len), 1)
     causal = rows >= cols
-    cumr = cumr_ref[0]
-    cumc = cumc_ref[0]
-    stp = stp_ref[0]
     left = lax.broadcasted_iota(jnp.int32, (1, 128), 1) < HEAD_DIM
-    for pair in range(pairs):
-        lanes = slice(pair * 128, (pair + 1) * 128)
-        xp = xc_ref[:, lanes]
-        xs = split(xp)
-        s_old = e_ref[pair]
-        ys = []
-        us = []
-        for side in range(2):
-            head = 2 * pair + side
-            dq = jnp.broadcast_to(cumc[:, head : head + 1], (block_len, block_len))
-            ck = cumr[head : head + 1, :]
-            sk = stp[head : head + 1, :]
-            dec = jnp.exp(jnp.where(causal, dq - ck, -jnp.inf))
-            ys.append(dot3(split(scores * dec * sk), xs))
-            wk = jnp.exp(dq[block_len - 1 : block_len, :] - ck) * sk
-            us.append(dot3(split(bm * wk), xs))
-        cq = pair_columns(cumc, pair, block_len)
-        inflow = dot3(ct, split(s_old)) * jnp.exp(cq)
-        y = jnp.where(left, ys[0], ys[1]) + inflow
-        y_ref[:, lanes] = y + xp * dsk_ref[:, lanes]
-        e_ref[pair] = jnp.exp(cq[block_len - 1 : block_len, :]) * s_old + jnp.where(
-            left, us[0], us[1]
-        )
+    for start in range(0, xc_ref.shape[0], block_len):
+        span = slice(start, start + block_len)
+        ct = split(ct_ref[0, span, :])
+        bm = b_ref[0, :, span]
+        scores = dot3(ct, split(bm))
+        cumr = cumr_ref[0, :, span]
+        cumc = cumc_ref[0, span, :]
+        stp = stp_ref[0, :, span]
+        for pair in range(pairs):
+            lanes = slice(pair * 128, (pair + 1) * 128)
+            xp = xc_ref[span, lanes]
+            xs = split(xp)
+            s_old = e_ref[pair]
+            ys = []
+            us = []
+            for side in range(2):
+                head = 2 * pair + side
+                dq = jnp.broadcast_to(cumc[:, head : head + 1], (block_len, block_len))
+                ck = cumr[head : head + 1, :]
+                sk = stp[head : head + 1, :]
+                dec = jnp.exp(jnp.where(causal, dq - ck, -jnp.inf))
+                ys.append(dot3(split(scores * dec * sk), xs))
+                wk = jnp.exp(dq[block_len - 1 : block_len, :] - ck) * sk
+                us.append(dot3(split(bm * wk), xs))
+            cq = pair_columns(cumc, pair, block_len)
+            inflow = dot3(ct, split(s_old)) * jnp.exp(cq)
+            y = jnp.where(left, ys[0], ys[1]) + inflow
+            y_ref[span, lanes] = y + xp * dsk_ref[:, lanes]
+            e_ref[pair] = jnp.exp(cq[block_len - 1 : block_len, :]) * s_old + jnp.where(
+                left, us[0], us[1]
+            )
 
 
 def end_kernel(xc_ref, b_ref, wk_ref, e_ref):
@@ -292,17 +294,19 @@
     ctx_index = lax.axis_index("ctx")
     scan_inputs = (x_own, c_cols, b_rows, cum_rows, cum_cols, step_rows, skip_row)
 
+    step_len = min(2 * block_len, own)
+
     def scan_group(group, inputs, target):
         count = len(inputs)
         extra = {} if target is None else {"input_output_aliases": {count: 0}}
-        tile = pl.BlockSpec((block_len, group_width), lambda g, c: (c, group))
+        tile = pl.BlockSpec((step_len, group_width), lambda g, c: (c, group))
         in_specs = [
             tile,
-            pl.BlockSpec((1, block_len, state), lambda g, c: (group, c, 0)),
-            pl.BlockSpec((1, state, block_len), lambda g, c: (group, 0, c)),
-            pl.BlockSpec((1, per_group, block_len), lambda g, c: (group, 0, c)),
-            pl.BlockSpec((1, block_len, per_group), lambda g, c: (group, c, 0)),
-            pl.BlockSpec((1, per_group, block_len), lambda g, c: (group, 0, c)),
+            pl.BlockSpec((1, step_len, state), lambda g, c: (group, c, 0)),
+            pl.BlockSpec((1, state, step_len), lambda g, c: (group, 0, c)),
+            pl.BlockSpec((1, per_group, step_len), lambda g, c: (group, 0, c)),
+            pl.BlockSpec((1, step_len, per_group), lambda g, c: (group, c, 0)),
+            pl.BlockSpec((1, per_group, step_len), lambda g, c: (group, 0, c)),
             pl.BlockSpec((1, group_width), lambda g, c: (0, group)),
         ]
         operands = tuple(inputs)
@@ -313,7 +317,7 @@
             kernel = lambda *refs: scan_kernel(*refs[:count], *refs[count + 1 :])
         return pl.pallas_call(
             kernel,
-            grid=(1, blocks),
+            grid=(1, own // step_len),
             in_specs=in_specs,
             out_specs=tile,
             out_shape=jax.ShapeDtypeStruct((own, channels), F32),

time: 143 us -> 143 us (level)
  no operation moved by 1% of the time
where the time goes in v17:
time: 143 us; the launch traced here: 142 us
  Pallas kernels  57.8 us (40%)
  other arithmetic  36.6 us (26%)
  starting transfers between devices  23 us (16%)
  local copies, waits for them, and re-layouts  15.7 us (11%)
  waiting for transfers between devices  8.05 us (6%)
    pallas_call x4, Pallas kernels, scan_group(): pl.pallas_call(kernel, grid=(1, own // step_len), in_specs=in_specs, out_...  30.7 us
    ppermute x5, starting transfers between devices, passed_along(): return lax.ppermute(x, axis, pairs)  22.9 us
    pallas_call x2, Pallas kernels, end_states(): pl.pallas_call(end_pair_kernel, grid=(count,), in_specs=[x_spec, x_spec,...  16.1 us
    mul x1, other arithmetic, conv_rows(): return jax.nn.silu(total)  12.4 us
    pallas_call x1, Pallas kernels, per_device(): pl.pallas_call(out_kernel, grid=(set_groups, own // out_len), in_specs=[p...  11 us
    ppermute x5, waiting for transfers between devices, passed_along(): return lax.ppermute(x, axis, pairs)  7.07 us
    mul x1, other arithmetic, conv_cols(): return jax.nn.silu(total)  5.47 us
    concatenate x1, other arithmetic, per_device(): x_pad = jnp.concatenate([x_rim, x_raw], 0)  4.98 us
  transfers between devices with their start and end apart: 7, of which 4 were waited for; matrix products, arithmetic and copies ran while one was open for 23% of the time, Pallas kernels for 33%

profile of v17, /device:TPU:0, one launch (start us, length us, event | category | flops | bytes accessed | tf_op | source)
XLA Modules:
  0.0 142.2 jit_solution(16714165862824413141)
XLA Ops:
  0.0 1.0 slice.124
  2.1 4.9 %collective-permute-start = (bf16[3,4608]{1,0:T(4,128)(2,1)S(1)}, bf16[3,4608]{1,0:T(4,128)(2,1)S(1)}, u32[]{:S(2)}, u32[]{:S(2)}) collective-permute-start(bf16[3,4608]{1,0:T(4,128)(2,1)S(1)} %pad_maximum_fusion.4), channel_id=1, source_target_pairs={{0,4},{4,8},{8,12},{1,5},{5,9},{9,13},{2,6},{6,10},{10,14},{3,7},{... | collective-permute-start | bytes 82952 | tf_op jit(solution)/shard_map/ppermute | solution.py:22
  7.7 1.2 broadcast_multiply_fusion
  14.7 1.3 copy.66
  16.9 5.5 %divide_multiply_fusion.2 = f32[2,4,64,1024]{3,2,1,0:T(8,128)S(1)} fusion(bf16[2,4,64,1024]{3,2,1,0:T(8,128)(2,1)} %param.13, bf16[2,4,64,3]{3,2,1,0:T(8,128)(2,1)S(1)} %bitcast.131, f32[2,4,64]{2,1,0:T(4,128)S(1)} %get-tuple-element.136, f32[2,4,64]{2,1,0:T(4,128)S(1)} %get-tuple-element.134, f32[2,4,64]{2,1,0:T(4,128)S(1)} %get-tuple-element.135, ...), kind=kLoop, calls=%fused_computation.11 | loop fusion | flops 13107200 | bytes 3159040 | tf_op jit(solution)/shard_map/jit(silu)/mul | solution.py:46
  22.4 1.1 constant_dynamic-slice_fusion.7
  23.5 5.0 %fusion = (bf16[515,4096]{1,0:T(8,128)(2,1)S(1)}, bf16[515,4096]{1,0:T(8,128)(2,1)S(1)}) fusion(s32[]{:T(128)S(6)} %select_n.146, bf16[1024,4096]{1,0:T(8,128)(2,1)} %param.12, bf16[3,4096]{1,0:T(4,128)(2,1)S(1)} %slice.156, s32[]{:T(128)S(6)} %select_n.145), kind=kLoop, calls=%fused_computation.6 | loop fusion | flops 16875520 | bytes 16850952 | tf_op jit(solution)/shard_map/concatenate | solution.py:195
  28.5 12.4 %divide_multiply_fusion = (f32[512,4096]{1,0:T(8,128)}, f32[512,4096]{1,0:T(8,128)}) fusion(bf16[515,4096]{1,0:T(8,128)(2,1)S(1)} %get-tuple-element.107, f32[4096]{0:T(1024)S(1)} %bitcast.136, f32[4096]{0:T(1024)S(1)} %bitcast.137, f32[4096]{0:T(1024)S(1)} %bitcast.135, f32[4096]{0:T(1024)S(1)} %bitcast.134, f32[4096]{0:T(1024)S(1)} %copy-done.7, ...), kind=kLoop, calls=%fused_computation.2 | loop fusion | flops 67108864 | bytes 50413568 | tf_op jit(solution)/shard_map/jit(silu)/mul | solution.py:36
  41.0 1.1 dynamic-slice_bitcast_fusion
  42.1 8.0 %shard_map.118 = (f32[2,8,64,128]{3,2,1,0:T(8,128)}, f32[2,8,64,128]{3,2,1,0:T(8,128)}) custom-call(f32[512,4096]{1,0:T(8,128)} %get-tuple-element.90.xa_ref.xc_ref.refs_0_, f32[512,4096]{1,0:T(8,128)} %get-tuple-element.64.xb_ref, f32[4,64,512]{2,1,0:T(8,128)} %get-tuple-element.120.ba_ref, f32[4,64,512]{2,1,0:T(8,128)} %get-tuple-element.119.bb_ref, ...), custom_call_target="tpu_custom_call" | custom-call | tf_op jit(solution)/shard_map/pallas_call | solution.py:259
  50.1 1.3 broadcast_select_fusion.1
  52.3 1.5 %select_bitcast_fusion.2 = (f32[2,4,1,64,512]{4,3,2,1,0:T(8,128)S(1)}, f32[2,4,1,64,512]{4,3,2,1,0:T(8,128)S(1)}) fusion(f32[2,4,64,512]{3,2,1,0:T(8,128)} %collective-permute-done.1, f32[2,4,64,1024]{3,2,1,0:T(8,128)S(1)} %divide_multiply_fusion.2, s32[]{:T(128)S(6)} %select_n.148, pred[]{:T(512)S(6)} %eq.2), kind=kLoop, calls=%fused_computation.29 | loop fusion | flops 524288 | bytes 4194309 | tf_op jit(solution)/shard_map/stack | solution.py:209
  53.8 1.2 pad_maximum_fusion.1
  55.0 1.4 copy.63
  56.3 3.7 %collective-permute-start.2 = (f32[16,64,128]{2,1,0:T(8,128)}, f32[16,64,128]{2,1,0:T(8,128)S(1)}, u32[]{:S(2)}, u32[]{:S(2)}) collective-permute-start(f32[16,64,128]{2,1,0:T(8,128)} %bitcast_add_fusion), channel_id=1, source_target_pairs={{0,4},{4,8},{8,12},{1,5},{5,9},{9,13},{2,6},{6,10},{10,14},{3,7},{... | collective-permute-start | bytes 1572872 | tf_op jit(solution)/shard_map/ppermute | solution.py:22
  60.3 8.1 %shard_map.120 = (f32[2,8,64,128]{3,2,1,0:T(8,128)}, f32[2,8,64,128]{3,2,1,0:T(8,128)}) custom-call(f32[512,4096]{1,0:T(8,128)} %get-tuple-element.90.xa_ref.xc_ref.refs_0_, f32[512,4096]{1,0:T(8,128)} %get-tuple-element.64.xb_ref, f32[4,64,512]{2,1,0:T(8,128)} %get-tuple-element.120.ba_ref, f32[4,64,512]{2,1,0:T(8,128)} %get-tuple-element.119.bb_ref, ...), custom_call_target="tpu_custom_call" | custom-call | tf_op jit(solution)/shard_map/pallas_call | solution.py:259
  68.4 7.7 %shard_map.119.refs_7_ = f32[512,4096]{1,0:T(8,128)} custom-call(f32[512,4096]{1,0:T(8,128)} %get-tuple-element.90.xa_ref.xc_ref.refs_0_, f32[4,512,128]{2,1,0:T(8,128)} %bitcast.105, f32[4,128,512]{2,1,0:T(8,128)} %bitcast.116, f32[4,16,512]{2,1,0:T(8,128)} %copy-done.2, f32[4,512,16]{2,1,0:T(8,128)} %bitcast.112, f32[4,16,512]{2,1,0:T(8,128)} %bitcast.126, ...), custom_call_target="tpu_custom_call" | custom-call | tf_op jit(solution)/shard_map/pallas_call | solution.py:318
  77.4 4.3 %collective-permute-start.3 = (f32[16,64,128]{2,1,0:T(8,128)S(1)}, f32[16,64,128]{2,1,0:T(8,128)}, u32[]{:S(2)}, u32[]{:S(2)}) collective-permute-start(f32[16,64,128]{2,1,0:T(8,128)S(1)} %fusion.12), channel_id=1, source_target_pairs={{0,4},{4,8},{8,12},{1,5},{5,9},{9,13},{2,6},{6,10},{10,14},{3,7},{... | collective-permute-start | bytes 1572872 | tf_op jit(solution)/shard_map/ppermute | solution.py:22
  81.7 7.6 %shard_map.121.refs_7_ = f32[512,4096]{1,0:T(8,128)} custom-call(f32[512,4096]{1,0:T(8,128)} %get-tuple-element.90.xa_ref.xc_ref.refs_0_, f32[4,512,128]{2,1,0:T(8,128)} %bitcast.106, f32[4,128,512]{2,1,0:T(8,128)} %bitcast.117, f32[4,16,512]{2,1,0:T(8,128)} %copy-done.2, f32[4,512,16]{2,1,0:T(8,128)} %bitcast.113, ...), custom_call_target="tpu_custom_call", output_to_operand_aliasing={{}: (7, {})} | custom-call | tf_op jit(solution)/shard_map/pallas_call | solution.py:318
  89.3 3.1 %collective-permute-done.3 = f32[16,64,128]{2,1,0:T(8,128)} collective-permute-done((f32[16,64,128]{2,1,0:T(8,128)S(1)}, f32[16,64,128]{2,1,0:T(8,128)}, u32[]{:S(2)}, u32[]{:S(2)}) %collective-permute-start.3) | collective-permute-done | bytes 524320 | tf_op jit(solution)/shard_map/ppermute | solution.py:22
  92.4 1.2 fusion.11
  93.7 5.3 %collective-permute-start.4 = (f32[16,64,128]{2,1,0:T(8,128)S(1)}, f32[16,64,128]{2,1,0:T(8,128)}, u32[]{:S(2)}, u32[]{:S(2)}) collective-permute-start(f32[16,64,128]{2,1,0:T(8,128)S(1)} %fusion.10), channel_id=1, source_target_pairs={{0,4},{4,8},{8,12},{1,5},{5,9},{9,13},{2,6},{6,10},{10,14},{3,7},{... | collective-permute-start | bytes 1572872 | tf_op jit(solution)/shard_map/ppermute | solution.py:22
  99.0 7.6 %shard_map.122.refs_7_ = f32[512,4096]{1,0:T(8,128)} custom-call(f32[512,4096]{1,0:T(8,128)} %get-tuple-element.90.xa_ref.xc_ref.refs_0_, f32[4,512,128]{2,1,0:T(8,128)} %bitcast.107, f32[4,128,512]{2,1,0:T(8,128)} %bitcast.118, f32[4,16,512]{2,1,0:T(8,128)} %copy-done.2, f32[4,512,16]{2,1,0:T(8,128)} %bitcast.114, ...), custom_call_target="tpu_custom_call", output_to_operand_aliasing={{}: (7, {})} | custom-call | tf_op jit(solution)/shard_map/pallas_call | solution.py:318
  106.6 2.3 %collective-permute-done.4 = f32[16,64,128]{2,1,0:T(8,128)} collective-permute-done((f32[16,64,128]{2,1,0:T(8,128)S(1)}, f32[16,64,128]{2,1,0:T(8,128)}, u32[]{:S(2)}, u32[]{:S(2)}) %collective-permute-start.4) | collective-permute-done | bytes 524320 | tf_op jit(solution)/shard_map/ppermute | solution.py:22
  108.9 1.2 fusion.9
  110.2 4.7 %collective-permute-start.5 = (f32[16,64,128]{2,1,0:T(8,128)S(1)}, f32[16,64,128]{2,1,0:T(8,128)S(1)}, u32[]{:S(2)}, u32[]{:S(2)}) collective-permute-start(f32[16,64,128]{2,1,0:T(8,128)S(1)} %fusion.8), channel_id=1, source_target_pairs={{0,4},{4,8},{8,12},{1,5},{5,9},{9,13},{2,6},{6,10},{10,14},{3,7},{... | collective-permute-start | bytes 1572872 | tf_op jit(solution)/shard_map/ppermute | solution.py:22
  115.1 7.7 %shard_map.123.y_ref = f32[512,4096]{1,0:T(8,128)} custom-call(f32[512,4096]{1,0:T(8,128)} %get-tuple-element.90.xa_ref.xc_ref.refs_0_, f32[4,512,128]{2,1,0:T(8,128)} %bitcast.108, f32[4,128,512]{2,1,0:T(8,128)} %bitcast.119, f32[4,16,512]{2,1,0:T(8,128)} %copy-done.2, f32[4,512,16]{2,1,0:T(8,128)} %bitcast.115, ...), custom_call_target="tpu_custom_call", output_to_operand_aliasing={{}: (7, {})} | custom-call | tf_op jit(solution)/shard_map/pallas_call | solution.py:318
  122.8 1.6 %collective-permute-done.5 = f32[16,64,128]{2,1,0:T(8,128)S(1)} collective-permute-done((f32[16,64,128]{2,1,0:T(8,128)S(1)}, f32[16,64,128]{2,1,0:T(8,128)S(1)}, u32[]{:S(2)}, u32[]{:S(2)}) %collective-permute-start.5) | collective-permute-done | bytes 524320 | tf_op jit(solution)/shard_map/ppermute | solution.py:22
  125.5 1.3 copy.68
  127.8 1.6 %select_bitcast_fusion.1 = (f32[4,8,1,64,128]{4,3,1,0,2:T(8,128)S(1)}, f32[4,8,1,64,128]{4,3,1,0,2:T(8,128)S(1)}) fusion(f32[4,8,64,128]{3,2,1,0:T(8,128)} %collective-permute-done.6, pred[]{:T(512)S(6)} %eq.2, f32[4,8,64,128]{3,2,1,0:T(8,128)S(1)} %bitcast.111, f32[2,8,64,128]{3,2,1,0:T(8,128)S(1)} %copy-done.3, ...), kind=kLoop, calls=%fused_computation.26 | loop fusion | flops 1572864 | bytes 5259265 | tf_op jit(solution)/shard_map/stack | solution.py:377
  129.6 1.5 %copy.69 = f32[4,8,2,64,128]{4,3,2,1,0:T(8,128)} copy(f32[4,8,2,64,128]{4,3,1,0,2:T(8,128)S(1)} %pad_maximum_fusion) | data formatting | bytes 4194304 | tf_op jit(solution)/shard_map/stack | solution.py:377
  131.1 11.0 %shard_map.124 = bf16[512,4096]{1,0:T(8,128)(2,1)} custom-call(f32[512,4096]{1,0:T(8,128)} %shard_map.123.y_ref, f32[4,512,128]{2,1,0:T(8,128)} %bitcast.109, f32[4,512,16]{2,1,0:T(8,128)} %bitcast.124, f32[4,8,128,128]{3,2,1,0:T(8,128)} %bitcast.120, bf16[512,4096]{1,0:T(8,128)(2,1)} %z_ref.1, f32[1,4096]{1,0:T(1,128)} %bitcast.139), custom_call_target="tpu_custom_call" | custom-call | tf_op jit(solution)/shard_map/pallas_call | solution.py:380
  (90 shorter events, 13.2 us)
Async XLA Ops:
  0.0 14.1 %copy-start = (f32[2,4,128]{2,1,0:T(4,128)S(1)}, f32[2,4,128]{2,1,0:T(4,128)}, u32[]{:S(2)}) copy-start(f32[2,4,128]{2,1,0:T(4,128)} %param.19) | copy-start | bytes 12292
  0.0 10.7 %copy-start.6 = (f32[4,4096]{1,0:T(4,128)S(1)}, f32[4,4096]{1,0:T(4,128)}, u32[]{:S(2)}) copy-start(f32[4,4096]{1,0:T(4,128)} %param.16) | copy-start | bytes 196612
  2.1 14.7 %collective-permute-start = (bf16[3,4608]{1,0:T(4,128)(2,1)S(1)}, bf16[3,4608]{1,0:T(4,128)(2,1)S(1)}, u32[]{:S(2)}, u32[]{:S(2)}) collective-permute-start(bf16[3,4608]{1,0:T(4,128)(2,1)S(1)} %pad_maximum_fusion.4), channel_id=1, source_target_pairs={{0,4},{4,8},{8,12},{1,5},{5,9},{9,13},{2,6},{6,10},{10,14},{3,7},{... | collective-permute-start | bytes 82952 | tf_op jit(solution)/shard_map/ppermute | solution.py:22
  7.7 6.4 %copy-start.8 = (f32[4,2,4,128]{3,2,1,0:T(4,128)S(1)}, f32[4,2,4,128]{3,2,1,0:T(4,128)}, u32[]{:S(2)}) copy-start(f32[4,2,4,128]{3,2,1,0:T(4,128)} %param.18) | copy-start | bytes 49156
  9.6 6.4 %copy-start.9 = (f32[64]{0:T(128)S(1)}, f32[64]{0:T(128)}, u32[]{:S(2)}) copy-start(f32[64]{0:T(128)} %param.22) | copy-start | bytes 772
  14.6 13.9 %copy-start.2 = (f32[4,16,512]{2,1,0:T(8,128)}, f32[4,16,512]{2,1,0:T(8,128)S(1)}, u32[]{:S(2)}) copy-start(f32[4,16,512]{2,1,0:T(8,128)S(1)} %reshape.107.cumr_ref.refs_3_) | copy-start | bytes 393220
  23.5 28.8 %collective-permute-start.1 = (f32[2,4,64,512]{3,2,1,0:T(8,128)}, f32[2,4,64,512]{3,2,1,0:T(8,128)}, u32[]{:S(2)}, u32[]{:S(2)}) collective-permute-start(f32[2,4,64,512]{3,2,1,0:T(8,128)} %constant_dynamic-slice_fusion.7), channel_id=1, source_target_pairs={{0,1},{1,0},{2,3},{3,2},{4,5},{5,4},{6,7},{7,6},{8,9},{9,8},{10,11... | collective-permute-start | bytes 3145736 | tf_op jit(solution)/shard_map/ppermute | solution.py:26
  23.5 5.0 %copy-start.7 = (f32[4096]{0:T(1024)S(1)}, f32[4096]{0:T(1024)}, u32[]{:S(2)}) copy-start(f32[4096]{0:T(1024)} %param.17) | copy-start | bytes 49156
  56.3 20.7 %collective-permute-start.2 = (f32[16,64,128]{2,1,0:T(8,128)}, f32[16,64,128]{2,1,0:T(8,128)S(1)}, u32[]{:S(2)}, u32[]{:S(2)}) collective-permute-start(f32[16,64,128]{2,1,0:T(8,128)} %bitcast_add_fusion), channel_id=1, source_target_pairs={{0,4},{4,8},{8,12},{1,5},{5,9},{9,13},{2,6},{6,10},{10,14},{3,7},{... | collective-permute-start | bytes 1572872 | tf_op jit(solution)/shard_map/ppermute | solution.py:22
  68.3 7.7 %copy-start.4 = (f32[2,8,64,128]{3,2,1,0:T(8,128)S(1)}, f32[2,8,64,128]{3,2,1,0:T(8,128)}, u32[]{:S(2)}) copy-start(f32[2,8,64,128]{3,2,1,0:T(8,128)} %get-tuple-element.65) | copy-start | bytes 1572868
  68.4 7.7 %copy-start.5 = (f32[2,8,64,128]{3,2,1,0:T(8,128)S(1)}, f32[2,8,64,128]{3,2,1,0:T(8,128)}, u32[]{:S(2)}) copy-start(f32[2,8,64,128]{3,2,1,0:T(8,128)} %get-tuple-element.66) | copy-start | bytes 1572868
  77.4 15.0 %collective-permute-start.3 = (f32[16,64,128]{2,1,0:T(8,128)S(1)}, f32[16,64,128]{2,1,0:T(8,128)}, u32[]{:S(2)}, u32[]{:S(2)}) collective-permute-start(f32[16,64,128]{2,1,0:T(8,128)S(1)} %fusion.12), channel_id=1, source_target_pairs={{0,4},{4,8},{8,12},{1,5},{5,9},{9,13},{2,6},{6,10},{10,14},{3,7},{... | collective-permute-start | bytes 1572872 | tf_op jit(solution)/shard_map/ppermute | solution.py:22
  93.7 15.2 %collective-permute-start.4 = (f32[16,64,128]{2,1,0:T(8,128)S(1)}, f32[16,64,128]{2,1,0:T(8,128)}, u32[]{:S(2)}, u32[]{:S(2)}) collective-permute-start(f32[16,64,128]{2,1,0:T(8,128)S(1)} %fusion.10), channel_id=1, source_target_pairs={{0,4},{4,8},{8,12},{1,5},{5,9},{9,13},{2,6},{6,10},{10,14},{3,7},{... | collective-permute-start | bytes 1572872 | tf_op jit(solution)/shard_map/ppermute | solution.py:22
  110.2 14.3 %collective-permute-start.5 = (f32[16,64,128]{2,1,0:T(8,128)S(1)}, f32[16,64,128]{2,1,0:T(8,128)S(1)}, u32[]{:S(2)}, u32[]{:S(2)}) collective-permute-start(f32[16,64,128]{2,1,0:T(8,128)S(1)} %fusion.8), channel_id=1, source_target_pairs={{0,4},{4,8},{8,12},{1,5},{5,9},{9,13},{2,6},{6,10},{10,14},{3,7},{... | collective-permute-start | bytes 1572872 | tf_op jit(solution)/shard_map/ppermute | solution.py:22
  115.1 9.5 %copy-start.3 = (f32[2,8,64,128]{3,2,1,0:T(8,128)S(1)}, f32[2,8,64,128]{3,2,1,0:T(8,128)}, u32[]{:S(2)}) copy-start(f32[2,8,64,128]{3,2,1,0:T(8,128)} %get-tuple-element.100) | copy-start | bytes 1572868
  124.9 2.9 %collective-permute-start.6 = (f32[4,8,64,128]{3,2,1,0:T(8,128)S(1)}, f32[4,8,64,128]{3,2,1,0:T(8,128)}, u32[]{:S(2)}, u32[]{:S(2)}) collective-permute-start(f32[4,8,64,128]{3,2,1,0:T(8,128)S(1)} %fusion.5), channel_id=1, source_target_pairs={{0,1},{1,0},{2,3},{3,2},{4,5},{5,4},{6,7},{7,6},{8,9},{9,8},{10,11... | collective-permute-start | bytes 3145736 | tf_op jit(solution)/shard_map/ppermute | solution.py:26
  131.1 11.0 %copy-start.1 = (f32[2,4,128]{2,1,0:T(4,128)S(1)}, f32[2,4,128]{2,1,0:T(4,128)}, u32[]{:S(2)}) copy-start(f32[2,4,128]{2,1,0:T(4,128)} %param.19) | copy-start | bytes 12292

commit v18 on v16

--- a/solution.py
+++ b/solution.py
@@ -330,7 +330,7 @@
         end_pieces = chip_end.reshape((1,) + piece_shape[1:])
     received = jnp.zeros(piece_shape, F32)
     y_local = None
-    placed = [min(group, max(rounds, 1) - 1) for group in range(set_groups)]
+    placed = [min(max(group, 1), max(rounds, 1) - 1) for group in range(set_groups)]
     for step_index in range(max(rounds, 1)):
         send_at = jnp.clip(step_index - ctx_index, 0, pieces - 1)
         outgoing = lax.dynamic_index_in_dim(
@@ -340,7 +340,7 @@
         )
         held = scan_inputs
         x_pair = (x_own, x_other)
-        if any(p == step_index for p in placed):
+        if any(p == step_index for p in placed) or (step_index == 0 and early < set_groups):
             outgoing, held, x_pair = lax.optimization_barrier((outgoing, scan_inputs, x_pair))
         if rounds > 0:
             arrived = passed_along(outgoing, "ctx", 1)
@@ -352,7 +352,7 @@
             late = chip_ends(x_pair, early, set_groups - early)
         if rounds == 0:
             break
-        if any(p == step_index for p in placed):
+        if any(p == step_index for p in placed) or (step_index == 0 and early < set_groups):
             arrived, y_local, late = lax.optimization_barrier((arrived, y_local, late))
         if late is not None:
             first_end = jnp.concatenate([first_end, late[0]], 0)

time: 143 us -> 142 us (level)
  waiting for transfers between devices: 7.91 us -> 6.01 us
    ppermute x5, waiting for transfers between devices: 6.93 us -> 5.04 us  [passed_along(): return lax.ppermute(x, axis, pairs)]
  transfers between devices with their start and end apart: 7 -> 7, of which waited for: 4 -> 4; matrix products, arithmetic and copies ran while one was open for 23% -> 25% of each run, Pallas kernels for 33% -> 33%
where the time goes in v18:
time: 142 us; the launch traced here: 141 us
  Pallas kernels  58.1 us (41%)
  other arithmetic  37.9 us (27%)
  starting transfers between devices  22.2 us (16%)
  local copies, waits for them, and re-layouts  15.8 us (11%)
  waiting for transfers between devices  6.01 us (4%)
    pallas_call x4, Pallas kernels, scan_group(): pl.pallas_call(kernel, grid=(1, blocks), in_specs=in_specs, out_specs=til...  30.9 us
    ppermute x5, starting transfers between devices, passed_along(): return lax.ppermute(x, axis, pairs)  22.1 us
    pallas_call x2, Pallas kernels, end_states(): pl.pallas_call(end_pair_kernel, grid=(count,), in_specs=[x_spec, x_spec,...  16.1 us
    mul x1, other arithmetic, conv_rows(): return jax.nn.silu(total)  12.4 us
    pallas_call x1, Pallas kernels, per_device(): pl.pallas_call(out_kernel, grid=(set_groups, own // out_len), in_specs=[p...  11 us
    mul x1, other arithmetic, conv_cols(): return jax.nn.silu(total)  5.59 us
    ppermute x5, waiting for transfers between devices, passed_along(): return lax.ppermute(x, axis, pairs)  5.04 us
    concatenate x1, other arithmetic, per_device(): x_pad = jnp.concatenate([x_rim, x_raw], 0)  4.98 us
  transfers between devices with their start and end apart: 7, of which 4 were waited for; matrix products, arithmetic and copies ran while one was open for 25% of the time, Pallas kernels for 33%

profile of v18, /device:TPU:0, one launch (start us, length us, event | category | flops | bytes accessed | tf_op | source)
XLA Modules:
  0.0 140.9 jit_solution(17324225107768617236)
XLA Ops:
  2.1 4.9 %collective-permute-start = (bf16[3,4608]{1,0:T(4,128)(2,1)S(1)}, bf16[3,4608]{1,0:T(4,128)(2,1)S(1)}, u32[]{:S(2)}, u32[]{:S(2)}) collective-permute-start(bf16[3,4608]{1,0:T(4,128)(2,1)S(1)} %pad_maximum_fusion.4), channel_id=1, source_target_pairs={{0,4},{4,8},{8,12},{1,5},{5,9},{9,13},{2,6},{6,10},{10,14},{3,7},{... | collective-permute-start | bytes 82952 | tf_op jit(solution)/shard_map/ppermute | solution.py:21
  7.7 1.2 broadcast_multiply_fusion
  14.7 1.3 copy.66
  16.9 5.6 %divide_multiply_fusion.2 = f32[2,4,64,1024]{3,2,1,0:T(8,128)S(1)} fusion(bf16[2,4,64,1024]{3,2,1,0:T(8,128)(2,1)} %param.13, bf16[2,4,64,3]{3,2,1,0:T(8,128)(2,1)S(1)} %bitcast.131, f32[2,4,64]{2,1,0:T(4,128)S(1)} %get-tuple-element.120, f32[2,4,64]{2,1,0:T(4,128)S(1)} %get-tuple-element.118, f32[2,4,64]{2,1,0:T(4,128)S(1)} %get-tuple-element.119, ...), kind=kLoop, calls=%fused_computation.11 | loop fusion | flops 13107200 | bytes 3159040 | tf_op jit(solution)/shard_map/jit(silu)/mul | solution.py:45
  22.5 1.1 constant_dynamic-slice_fusion.7
  23.6 5.0 %fusion = (bf16[515,4096]{1,0:T(8,128)(2,1)S(1)}, bf16[515,4096]{1,0:T(8,128)(2,1)S(1)}) fusion(s32[]{:T(128)S(6)} %select_n.146, bf16[1024,4096]{1,0:T(8,128)(2,1)} %param.12, bf16[3,4096]{1,0:T(4,128)(2,1)S(1)} %slice.156, s32[]{:T(128)S(6)} %select_n.145), kind=kLoop, calls=%fused_computation.6 | loop fusion | flops 16875520 | bytes 16850952 | tf_op jit(solution)/shard_map/concatenate | solution.py:193
  28.7 12.4 %divide_multiply_fusion = (f32[512,4096]{1,0:T(8,128)}, f32[512,4096]{1,0:T(8,128)}) fusion(bf16[515,4096]{1,0:T(8,128)(2,1)S(1)} %get-tuple-element.91, f32[4096]{0:T(1024)S(1)} %bitcast.136, f32[4096]{0:T(1024)S(1)} %bitcast.137, f32[4096]{0:T(1024)S(1)} %bitcast.135, f32[4096]{0:T(1024)S(1)} %bitcast.134, f32[4096]{0:T(1024)S(1)} %copy-done.6, ...), kind=kLoop, calls=%fused_computation.2 | loop fusion | flops 67108864 | bytes 50413568 | tf_op jit(solution)/shard_map/jit(silu)/mul | solution.py:35
  41.1 1.1 dynamic-slice_bitcast_fusion
  42.2 8.0 %shard_map.118 = (f32[2,8,64,128]{3,2,1,0:T(8,128)}, f32[2,8,64,128]{3,2,1,0:T(8,128)}) custom-call(f32[512,4096]{1,0:T(8,128)} %get-tuple-element.74.xa_ref.xc_ref.refs_0_, f32[512,4096]{1,0:T(8,128)} %get-tuple-element.49.xb_ref, f32[4,64,512]{2,1,0:T(8,128)} %get-tuple-element.104.ba_ref, f32[4,64,512]{2,1,0:T(8,128)} %get-tuple-element.103.bb_ref, ...), custom_call_target="tpu_custom_call" | custom-call | tf_op jit(solution)/shard_map/pallas_call | solution.py:257
  50.3 1.3 broadcast_select_fusion.1
  52.4 1.5 %select_bitcast_fusion.2 = (f32[2,4,1,64,512]{4,3,2,1,0:T(8,128)S(1)}, f32[2,4,1,64,512]{4,3,2,1,0:T(8,128)S(1)}) fusion(f32[2,4,64,512]{3,2,1,0:T(8,128)} %collective-permute-done.1, f32[2,4,64,1024]{3,2,1,0:T(8,128)S(1)} %divide_multiply_fusion.2, s32[]{:T(128)S(6)} %select_n.148, pred[]{:T(512)S(6)} %eq.2), kind=kLoop, calls=%fused_computation.29 | loop fusion | flops 524288 | bytes 4194309 | tf_op jit(solution)/shard_map/stack | solution.py:207
  54.0 1.2 pad_maximum_fusion.1
  55.1 1.4 copy.63
  56.5 3.7 %collective-permute-start.2 = (f32[16,64,128]{2,1,0:T(8,128)S(1)}, f32[16,64,128]{2,1,0:T(8,128)S(1)}, u32[]{:S(2)}, u32[]{:S(2)}) collective-permute-start(f32[16,64,128]{2,1,0:T(8,128)S(1)} %copy-done.4), channel_id=1, source_target_pairs={{0,4},{4,8},{8,12},{1,5},{5,9},{9,13},{2,6},{6,10},{10,14},{3,7},{... | collective-permute-start | bytes 1572872 | tf_op jit(solution)/shard_map/ppermute | solution.py:21
  60.5 8.0 %shard_map.119 = (f32[2,8,64,128]{3,2,1,0:T(8,128)}, f32[2,8,64,128]{3,2,1,0:T(8,128)}) custom-call(f32[512,4096]{1,0:T(8,128)} %get-tuple-element.74.xa_ref.xc_ref.refs_0_, f32[512,4096]{1,0:T(8,128)} %get-tuple-element.49.xb_ref, f32[4,64,512]{2,1,0:T(8,128)} %get-tuple-element.104.ba_ref, f32[4,64,512]{2,1,0:T(8,128)} %get-tuple-element.103.bb_ref, ...), custom_call_target="tpu_custom_call" | custom-call | tf_op jit(solution)/shard_map/pallas_call | solution.py:257
  68.5 2.1 %select_add_fusion = (f32[2,8,64,128]{3,2,1,0:T(8,128)S(1)}, f32[2,8,64,128]{3,2,1,0:T(8,128)}) fusion(f32[2,8,64,128]{3,2,1,0:T(8,128)} %get-tuple-element.51, f32[2,8,64,128]{3,2,1,0:T(8,128)} %get-tuple-element.50, f32[2,8,128]{2,1,0:T(8,128)S(1)} %mul.251, pred[]{:T(512)S(6)} %eq.2), kind=kLoop, calls=%fused_computation.46 | loop fusion | flops 524288 | bytes 2105345 | tf_op jit(solution)/shard_map/add | solution.py:286
  70.7 1.2 collective-permute-done.2
  72.2 5.2 %collective-permute-start.3 = (f32[16,64,128]{2,1,0:T(8,128)S(1)}, f32[16,64,128]{2,1,0:T(8,128)}, u32[]{:S(2)}, u32[]{:S(2)}) collective-permute-start(f32[16,64,128]{2,1,0:T(8,128)S(1)} %fusion.12), channel_id=1, source_target_pairs={{0,4},{4,8},{8,12},{1,5},{5,9},{9,13},{2,6},{6,10},{10,14},{3,7},{... | collective-permute-start | bytes 1572872 | tf_op jit(solution)/shard_map/ppermute | solution.py:21
  77.4 7.7 %shard_map.120.refs_7_ = f32[512,4096]{1,0:T(8,128)} custom-call(f32[512,4096]{1,0:T(8,128)} %get-tuple-element.74.xa_ref.xc_ref.refs_0_, f32[4,512,128]{2,1,0:T(8,128)} %bitcast.105, f32[4,128,512]{2,1,0:T(8,128)} %bitcast.116, f32[4,16,512]{2,1,0:T(8,128)} %copy-done.2, f32[4,512,16]{2,1,0:T(8,128)} %bitcast.112, f32[4,16,512]{2,1,0:T(8,128)} %bitcast.126, ...), custom_call_target="tpu_custom_call" | custom-call | tf_op jit(solution)/shard_map/pallas_call | solution.py:314
  85.1 7.8 %shard_map.121.refs_7_ = f32[512,4096]{1,0:T(8,128)} custom-call(f32[512,4096]{1,0:T(8,128)} %get-tuple-element.74.xa_ref.xc_ref.refs_0_, f32[4,512,128]{2,1,0:T(8,128)} %bitcast.106, f32[4,128,512]{2,1,0:T(8,128)} %bitcast.117, f32[4,16,512]{2,1,0:T(8,128)} %copy-done.2, f32[4,512,16]{2,1,0:T(8,128)} %bitcast.113, ...), custom_call_target="tpu_custom_call", output_to_operand_aliasing={{}: (7, {})} | custom-call | tf_op jit(solution)/shard_map/pallas_call | solution.py:314
  92.9 1.2 fusion.11
  94.2 3.5 %collective-permute-start.4 = (f32[16,64,128]{2,1,0:T(8,128)S(1)}, f32[16,64,128]{2,1,0:T(8,128)}, u32[]{:S(2)}, u32[]{:S(2)}) collective-permute-start(f32[16,64,128]{2,1,0:T(8,128)S(1)} %fusion.10), channel_id=1, source_target_pairs={{0,4},{4,8},{8,12},{1,5},{5,9},{9,13},{2,6},{6,10},{10,14},{3,7},{... | collective-permute-start | bytes 1572872 | tf_op jit(solution)/shard_map/ppermute | solution.py:21
  97.7 7.7 %shard_map.122.refs_7_ = f32[512,4096]{1,0:T(8,128)} custom-call(f32[512,4096]{1,0:T(8,128)} %get-tuple-element.74.xa_ref.xc_ref.refs_0_, f32[4,512,128]{2,1,0:T(8,128)} %bitcast.107, f32[4,128,512]{2,1,0:T(8,128)} %bitcast.118, f32[4,16,512]{2,1,0:T(8,128)} %copy-done.2, f32[4,512,16]{2,1,0:T(8,128)} %bitcast.114, ...), custom_call_target="tpu_custom_call", output_to_operand_aliasing={{}: (7, {})} | custom-call | tf_op jit(solution)/shard_map/pallas_call | solution.py:314
  105.4 2.2 %collective-permute-done.4 = f32[16,64,128]{2,1,0:T(8,128)} collective-permute-done((f32[16,64,128]{2,1,0:T(8,128)S(1)}, f32[16,64,128]{2,1,0:T(8,128)}, u32[]{:S(2)}, u32[]{:S(2)}) %collective-permute-start.4) | collective-permute-done | bytes 524320 | tf_op jit(solution)/shard_map/ppermute | solution.py:21
  107.6 1.2 fusion.9
  108.9 4.7 %collective-permute-start.5 = (f32[16,64,128]{2,1,0:T(8,128)S(1)}, f32[16,64,128]{2,1,0:T(8,128)S(1)}, u32[]{:S(2)}, u32[]{:S(2)}) collective-permute-start(f32[16,64,128]{2,1,0:T(8,128)S(1)} %fusion.8), channel_id=1, source_target_pairs={{0,4},{4,8},{8,12},{1,5},{5,9},{9,13},{2,6},{6,10},{10,14},{3,7},{... | collective-permute-start | bytes 1572872 | tf_op jit(solution)/shard_map/ppermute | solution.py:21
  113.8 7.8 %shard_map.123.y_ref = f32[512,4096]{1,0:T(8,128)} custom-call(f32[512,4096]{1,0:T(8,128)} %get-tuple-element.74.xa_ref.xc_ref.refs_0_, f32[4,512,128]{2,1,0:T(8,128)} %bitcast.108, f32[4,128,512]{2,1,0:T(8,128)} %bitcast.119, f32[4,16,512]{2,1,0:T(8,128)} %copy-done.2, f32[4,512,16]{2,1,0:T(8,128)} %bitcast.115, ...), custom_call_target="tpu_custom_call", output_to_operand_aliasing={{}: (7, {})} | custom-call | tf_op jit(solution)/shard_map/pallas_call | solution.py:314
  121.6 1.6 %collective-permute-done.5 = f32[16,64,128]{2,1,0:T(8,128)S(1)} collective-permute-done((f32[16,64,128]{2,1,0:T(8,128)S(1)}, f32[16,64,128]{2,1,0:T(8,128)S(1)}, u32[]{:S(2)}, u32[]{:S(2)}) %collective-permute-start.5) | collective-permute-done | bytes 524320 | tf_op jit(solution)/shard_map/ppermute | solution.py:21
  124.2 1.3 copy.68
  126.5 1.6 %select_bitcast_fusion.1 = (f32[4,8,1,64,128]{4,3,1,0,2:T(8,128)S(1)}, f32[4,8,1,64,128]{4,3,1,0,2:T(8,128)S(1)}) fusion(f32[4,8,64,128]{3,2,1,0:T(8,128)} %collective-permute-done.6, pred[]{:T(512)S(6)} %eq.2, f32[4,8,64,128]{3,2,1,0:T(8,128)S(1)} %bitcast.111, f32[2,8,64,128]{3,2,1,0:T(8,128)S(1)} %copy-done.3, ...), kind=kLoop, calls=%fused_computation.26 | loop fusion | flops 1572864 | bytes 5259265 | tf_op jit(solution)/shard_map/stack | solution.py:373
  128.4 1.5 %copy.69 = f32[4,8,2,64,128]{4,3,2,1,0:T(8,128)} copy(f32[4,8,2,64,128]{4,3,1,0,2:T(8,128)S(1)} %pad_maximum_fusion) | data formatting | bytes 4194304 | tf_op jit(solution)/shard_map/stack | solution.py:373
  129.9 11.0 %shard_map.124 = bf16[512,4096]{1,0:T(8,128)(2,1)} custom-call(f32[512,4096]{1,0:T(8,128)} %shard_map.123.y_ref, f32[4,512,128]{2,1,0:T(8,128)} %bitcast.109, f32[4,512,16]{2,1,0:T(8,128)} %bitcast.124, f32[4,8,128,128]{3,2,1,0:T(8,128)} %bitcast.120, bf16[512,4096]{1,0:T(8,128)(2,1)} %z_ref.1, f32[1,4096]{1,0:T(1,128)} %bitcast.139), custom_call_target="tpu_custom_call" | custom-call | tf_op jit(solution)/shard_map/pallas_call | solution.py:376
  (88 shorter events, 13.3 us)
Async XLA Ops:
  0.0 14.1 %copy-start = (f32[2,4,128]{2,1,0:T(4,128)S(1)}, f32[2,4,128]{2,1,0:T(4,128)}, u32[]{:S(2)}) copy-start(f32[2,4,128]{2,1,0:T(4,128)} %param.19) | copy-start | bytes 12292
  0.0 10.7 %copy-start.5 = (f32[4,4096]{1,0:T(4,128)S(1)}, f32[4,4096]{1,0:T(4,128)}, u32[]{:S(2)}) copy-start(f32[4,4096]{1,0:T(4,128)} %param.16) | copy-start | bytes 196612
  2.1 14.7 %collective-permute-start = (bf16[3,4608]{1,0:T(4,128)(2,1)S(1)}, bf16[3,4608]{1,0:T(4,128)(2,1)S(1)}, u32[]{:S(2)}, u32[]{:S(2)}) collective-permute-start(bf16[3,4608]{1,0:T(4,128)(2,1)S(1)} %pad_maximum_fusion.4), channel_id=1, source_target_pairs={{0,4},{4,8},{8,12},{1,5},{5,9},{9,13},{2,6},{6,10},{10,14},{3,7},{... | collective-permute-start | bytes 82952 | tf_op jit(solution)/shard_map/ppermute | solution.py:21
  7.7 6.4 %copy-start.7 = (f32[4,2,4,128]{3,2,1,0:T(4,128)S(1)}, f32[4,2,4,128]{3,2,1,0:T(4,128)}, u32[]{:S(2)}) copy-start(f32[4,2,4,128]{3,2,1,0:T(4,128)} %param.18) | copy-start | bytes 49156
  9.6 6.4 %copy-start.8 = (f32[64]{0:T(128)S(1)}, f32[64]{0:T(128)}, u32[]{:S(2)}) copy-start(f32[64]{0:T(128)} %param.22) | copy-start | bytes 772
  14.6 14.0 %copy-start.2 = (f32[4,16,512]{2,1,0:T(8,128)}, f32[4,16,512]{2,1,0:T(8,128)S(1)}, u32[]{:S(2)}) copy-start(f32[4,16,512]{2,1,0:T(8,128)S(1)} %reshape.107.cumr_ref.refs_3_) | copy-start | bytes 393220
  23.6 28.8 %collective-permute-start.1 = (f32[2,4,64,512]{3,2,1,0:T(8,128)}, f32[2,4,64,512]{3,2,1,0:T(8,128)}, u32[]{:S(2)}, u32[]{:S(2)}) collective-permute-start(f32[2,4,64,512]{3,2,1,0:T(8,128)} %constant_dynamic-slice_fusion.7), channel_id=1, source_target_pairs={{0,1},{1,0},{2,3},{3,2},{4,5},{5,4},{6,7},{7,6},{8,9},{9,8},{10,11... | collective-permute-start | bytes 3145736 | tf_op jit(solution)/shard_map/ppermute | solution.py:25
  23.6 5.0 %copy-start.6 = (f32[4096]{0:T(1024)S(1)}, f32[4096]{0:T(1024)}, u32[]{:S(2)}) copy-start(f32[4096]{0:T(1024)} %param.17) | copy-start | bytes 49156
  53.9 2.6 %copy-start.4 = (f32[16,64,128]{2,1,0:T(8,128)S(1)}, f32[16,64,128]{2,1,0:T(8,128)}, u32[]{:S(2)}) copy-start(f32[16,64,128]{2,1,0:T(8,128)} %bitcast_add_fusion) | copy-start | bytes 1572868
  56.5 15.3 %collective-permute-start.2 = (f32[16,64,128]{2,1,0:T(8,128)S(1)}, f32[16,64,128]{2,1,0:T(8,128)S(1)}, u32[]{:S(2)}, u32[]{:S(2)}) collective-permute-start(f32[16,64,128]{2,1,0:T(8,128)S(1)} %copy-done.4), channel_id=1, source_target_pairs={{0,4},{4,8},{8,12},{1,5},{5,9},{9,13},{2,6},{6,10},{10,14},{3,7},{... | collective-permute-start | bytes 1572872 | tf_op jit(solution)/shard_map/ppermute | solution.py:21
  72.2 20.7 %collective-permute-start.3 = (f32[16,64,128]{2,1,0:T(8,128)S(1)}, f32[16,64,128]{2,1,0:T(8,128)}, u32[]{:S(2)}, u32[]{:S(2)}) collective-permute-start(f32[16,64,128]{2,1,0:T(8,128)S(1)} %fusion.12), channel_id=1, source_target_pairs={{0,4},{4,8},{8,12},{1,5},{5,9},{9,13},{2,6},{6,10},{10,14},{3,7},{... | collective-permute-start | bytes 1572872 | tf_op jit(solution)/shard_map/ppermute | solution.py:21
  94.2 13.5 %collective-permute-start.4 = (f32[16,64,128]{2,1,0:T(8,128)S(1)}, f32[16,64,128]{2,1,0:T(8,128)}, u32[]{:S(2)}, u32[]{:S(2)}) collective-permute-start(f32[16,64,128]{2,1,0:T(8,128)S(1)} %fusion.10), channel_id=1, source_target_pairs={{0,4},{4,8},{8,12},{1,5},{5,9},{9,13},{2,6},{6,10},{10,14},{3,7},{... | collective-permute-start | bytes 1572872 | tf_op jit(solution)/shard_map/ppermute | solution.py:21
  108.9 14.3 %collective-permute-start.5 = (f32[16,64,128]{2,1,0:T(8,128)S(1)}, f32[16,64,128]{2,1,0:T(8,128)S(1)}, u32[]{:S(2)}, u32[]{:S(2)}) collective-permute-start(f32[16,64,128]{2,1,0:T(8,128)S(1)} %fusion.8), channel_id=1, source_target_pairs={{0,4},{4,8},{8,12},{1,5},{5,9},{9,13},{2,6},{6,10},{10,14},{3,7},{... | collective-permute-start | bytes 1572872 | tf_op jit(solution)/shard_map/ppermute | solution.py:21
  113.8 9.5 %copy-start.3 = (f32[2,8,64,128]{3,2,1,0:T(8,128)S(1)}, f32[2,8,64,128]{3,2,1,0:T(8,128)}, u32[]{:S(2)}) copy-start(f32[2,8,64,128]{3,2,1,0:T(8,128)} %get-tuple-element.84) | copy-start | bytes 1572868
  123.7 2.9 %collective-permute-start.6 = (f32[4,8,64,128]{3,2,1,0:T(8,128)S(1)}, f32[4,8,64,128]{3,2,1,0:T(8,128)}, u32[]{:S(2)}, u32[]{:S(2)}) collective-permute-start(f32[4,8,64,128]{3,2,1,0:T(8,128)S(1)} %fusion.5), channel_id=1, source_target_pairs={{0,1},{1,0},{2,3},{3,2},{4,5},{5,4},{6,7},{7,6},{8,9},{9,8},{10,11... | collective-permute-start | bytes 3145736 | tf_op jit(solution)/shard_map/ppermute | solution.py:25
  129.9 11.1 %copy-start.1 = (f32[2,4,128]{2,1,0:T(4,128)S(1)}, f32[2,4,128]{2,1,0:T(4,128)}, u32[]{:S(2)}) copy-start(f32[2,4,128]{2,1,0:T(4,128)} %param.19) | copy-start | bytes 12292
